TPU v7x, 32 devices: a whole 2x2x4 slice. The times are simulated.
32 devices in a mesh: dp: 8 (over z, y), tensor: 4 (over x, core).
Axes of the slice: x: 2, y: 2, z: 4, core: 2. Of those that a mesh axis runs over, the one named last changes fastest.
Arguments:
- tokens: bfloat16 [8192, 2048], P('dp'), may hold values from -6 to 6
- attn_gain: float32 [2048], replicated, may hold values from 0.25 to 1.75
- w_query: bfloat16 [2048, 2048], P(None, 'tensor'), may hold values from -0.125 to 0.125
- key_matrix: bfloat16 [2048, 1024], P(None, 'tensor'), may hold values from -0.125 to 0.125
- value_matrix: bfloat16 [2048, 1024], P(None, 'tensor'), may hold values from -0.125 to 0.125
- query_gain: float32 [128], replicated, may hold values from 0.25 to 1.75
- key_gain: float32 [128], replicated, may hold values from 0.25 to 1.75
- w_out: bfloat16 [2048, 2048], P('tensor'), may hold values from -0.5 to 0.5
- mlp_gain: float32 [2048], replicated, may hold values from 0.25 to 1.75
- w_gate: bfloat16 [2048, 6144], P(None, 'tensor'), may hold values from -0.125 to 0.125
- w_up: bfloat16 [2048, 6144], P(None, 'tensor'), may hold values from -0.125 to 0.125
- w_down: bfloat16 [6144, 2048], P('tensor'), may hold values from -0.15625 to 0.15625
- cotangent: bfloat16 [8192, 2048], P('dp'), may hold values from -6 to 6
Outputs:
- mixed: bfloat16 [8192, 2048], P('dp')
- input_grad: float32 [8192, 2048], P('dp')
- attn_gain_grad: float32 [2048], replicated
- mlp_gain_grad: float32 [2048], replicated
- query_gain_grad: float32 [128], replicated
- key_gain_grad: float32 [128], replicated
- w_query_grad: float32 [2048, 2048], P('dp', 'tensor')
- w_key_grad: float32 [2048, 1024], P('dp', 'tensor')
- w_value_grad: float32 [2048, 1024], P('dp', 'tensor')
- w_out_grad: float32 [2048, 2048], P('tensor', 'dp')
- w_gate_grad: float32 [2048, 6144], P('dp', 'tensor')
- w_up_grad: float32 [2048, 6144], P('dp', 'tensor')
- w_down_grad: float32 [6144, 2048], P('tensor', 'dp')
All inputs are finite; a program needn't handle non-finite values.
Results may differ from a plain program's by a relative error of at most 0.025.
Values may be sent and summed in bfloat16 or wider, within the bound.
No kernel may reach another device: no remote copies, remote signals or barrier semaphores. Data moves between devices by JAX's collectives and lax.ppermute only.
A program may use at most 320 MiB of HBM per device.

v0:
```python
import math

import jax
import jax.numpy as jnp
from jax import lax
from jax.sharding import PartitionSpec as P

HEAD_SIZE = 128
LEN = 128


EPS = 1e-06
THETA = 1000000.0


def product(form, left, right):
    return jnp.einsum(form, left, right, preferred_element_type=jnp.float32)


def matmul(left, right):
    return jnp.dot(left, right, preferred_element_type=jnp.float32)


def inner_rows(left, right):
    return lax.dot_general(
        left, right, (((0,), (0,)), ((), ())), preferred_element_type=jnp.float32
    )


def outer_cols(left, right):
    return lax.dot_general(
        left, right, (((1,), (1,)), ((), ())), preferred_element_type=jnp.float32
    )


def rms_scale(values, gain):
    return values * lax.rsqrt(jnp.mean(values * values, -1, keepdims=True) + EPS) * gain


def norm_back(values, gain, upstream):
    factor = lax.rsqrt(jnp.mean(values * values, -1, keepdims=True) + EPS)
    scaled = gain * upstream
    return factor * scaled - values * factor**3 * jnp.mean(scaled * values, -1, keepdims=True)


def gain_term(values, upstream):
    factor = lax.rsqrt(jnp.mean(values * values, -1, keepdims=True) + EPS)
    return jnp.sum(upstream * values * factor, 0)


def swiglu(gate, upper):
    return jax.nn.silu(gate) * upper


def rope_tables(length, width):
    position = jnp.arange(length).astype(jnp.float32)
    freqs = jnp.exp(jnp.arange(width // 2).astype(jnp.float32) * (-2.0 * math.log(THETA) / width))
    angles = position[:, None] * freqs[None, :]
    cosine = jnp.cos(angles)
    sine = jnp.sin(angles)
    return (jnp.concatenate([cosine, cosine], -1), jnp.concatenate([sine, sine], -1))


def head_prep(values, gain, cosine, sine):
    normed = values * lax.rsqrt(jnp.mean(values * values, -1, keepdims=True) + EPS) * gain
    half = normed.shape[-1] // 2
    turned = jnp.concatenate([-normed[..., half:], normed[..., :half]], -1)
    return normed * cosine[:, None, :] + turned * sine[:, None, :]


def causal_scores(queries, keys_rot, length):
    scores = product("sqgrd,skgd->sgrqk", queries, keys_rot) * (1.0 / math.sqrt(HEAD_SIZE))
    allowed = jnp.arange(length)[:, None] >= jnp.arange(length)[None, :]
    return jnp.where(allowed, scores, -1e30)


def attend(q_raw, k_raw, v_raw, query_gain, key_gain, seqs):
    total = q_raw.shape[0]
    length = total // seqs
    heads = q_raw.shape[1] // HEAD_SIZE
    kv_heads = k_raw.shape[1] // HEAD_SIZE
    repeat = heads // kv_heads
    cosine, sine = rope_tables(length, HEAD_SIZE)
    queries = head_prep(q_raw.reshape(seqs, length, heads, HEAD_SIZE), query_gain, cosine, sine)
    queries = queries.astype(jnp.bfloat16).reshape(seqs, length, kv_heads, repeat, HEAD_SIZE)
    keys_rot = head_prep(
        k_raw.reshape(seqs, length, kv_heads, HEAD_SIZE), key_gain, cosine, sine
    ).astype(jnp.bfloat16)
    values = v_raw.astype(jnp.bfloat16).reshape(seqs, length, kv_heads, HEAD_SIZE)
    scores = causal_scores(queries, keys_rot, length)
    top = jnp.max(scores, -1, keepdims=True)
    logsum = top + jnp.log(jnp.sum(jnp.exp(scores - top), -1, keepdims=True))
    weights = jnp.exp(scores - logsum).astype(jnp.bfloat16)
    attended = (
        product("sgrqk,skgd->sqgrd", weights, values)
        .astype(jnp.bfloat16)
        .reshape(total, heads * HEAD_SIZE)
    )
    return (attended, logsum, queries, keys_rot, values)


def attend_back(
    upstream, q_raw, k_raw, query_gain, key_gain, queries, keys_rot, values, logsum, seqs
):
    total = q_raw.shape[0]
    length = total // seqs
    heads = q_raw.shape[1] // HEAD_SIZE
    kv_heads = k_raw.shape[1] // HEAD_SIZE
    repeat = heads // kv_heads
    cosine, sine = rope_tables(length, HEAD_SIZE)
    grad_out = upstream.reshape(seqs, length, kv_heads, repeat, HEAD_SIZE)
    scores = causal_scores(queries, keys_rot, length)
    probs = jnp.exp(scores - logsum)
    value_grad = product("sgrqk,sqgrd->skgd", probs.astype(jnp.bfloat16), grad_out)
    prob_grad = product("sqgrd,skgd->sgrqk", grad_out, values)
    center = jnp.sum(probs * prob_grad, -1, keepdims=True)
    score_grad = (probs * (prob_grad - center) * (1.0 / math.sqrt(HEAD_SIZE))).astype(jnp.bfloat16)
    query_rot_grad = product("sgrqk,skgd->sqgrd", score_grad, keys_rot).reshape(
        seqs, length, heads, HEAD_SIZE
    )
    key_rot_grad = product("sgrqk,sqgrd->skgd", score_grad, queries)
    query_in = q_raw.reshape(seqs, length, heads, HEAD_SIZE)
    key_in = k_raw.reshape(seqs, length, kv_heads, HEAD_SIZE)
    _, pull_query = jax.vjp(
        lambda inner, gain: head_prep(inner, gain, cosine, sine), query_in, query_gain
    )
    query_grad, query_gain_grad = pull_query(query_rot_grad)
    _, pull_key = jax.vjp(
        lambda inner, gain: head_prep(inner, gain, cosine, sine), key_in, key_gain
    )
    key_grad, key_gain_grad = pull_key(key_rot_grad)
    return (
        query_grad.astype(jnp.bfloat16).reshape(total, heads * HEAD_SIZE),
        key_grad.astype(jnp.bfloat16).reshape(total, kv_heads * HEAD_SIZE),
        value_grad.astype(jnp.bfloat16).reshape(total, kv_heads * HEAD_SIZE),
        query_gain_grad,
        key_gain_grad,
    )


def on_device(
    tokens,
    attn_gain,
    w_query,
    key_matrix,
    value_matrix,
    query_gain,
    key_gain,
    w_out,
    mlp_gain,
    w_gate,
    w_up,
    w_down,
    cotangent,
):
    count = tokens.shape[0]
    seqs = count // LEN
    share = count // lax.axis_size("tensor")
    offset = lax.axis_index("tensor") * share
    stream = tokens.astype(jnp.float32)
    stream_rows = lax.dynamic_slice_in_dim(stream, offset, share, 0)
    normed_in = rms_scale(stream, attn_gain).astype(jnp.bfloat16)
    q_raw = matmul(normed_in, w_query)
    k_raw = matmul(normed_in, key_matrix)
    v_raw = matmul(normed_in, value_matrix)
    attended, logsum, queries, keys_rot, values = attend(
        q_raw, k_raw, v_raw, query_gain, key_gain, seqs
    )
    attn_part = matmul(attended, w_out).astype(jnp.bfloat16)
    resid = stream + lax.psum(attn_part, "tensor").astype(jnp.float32)
    resid_rows = lax.dynamic_slice_in_dim(resid, offset, share, 0)
    normed_mid = rms_scale(resid, mlp_gain).astype(jnp.bfloat16)
    gate = matmul(normed_mid, w_gate)
    upper = matmul(normed_mid, w_up)
    hidden = swiglu(gate, upper).astype(jnp.bfloat16)
    mlp_part = matmul(hidden, w_down).astype(jnp.bfloat16)
    mixed = (resid + lax.psum(mlp_part, "tensor").astype(jnp.float32)).astype(jnp.bfloat16)
    down_grad = inner_rows(hidden, cotangent)
    hidden_grad = outer_cols(cotangent, w_down)
    _, pull = jax.vjp(swiglu, gate, upper)
    gate_grad, upper_grad = pull(hidden_grad)
    gate_grad = gate_grad.astype(jnp.bfloat16)
    upper_grad = upper_grad.astype(jnp.bfloat16)
    gate_w_grad = inner_rows(normed_mid, gate_grad)
    up_w_grad = inner_rows(normed_mid, upper_grad)
    mid_part = (outer_cols(gate_grad, w_gate) + outer_cols(upper_grad, w_up)).astype(jnp.bfloat16)
    mid_grad = lax.psum(mid_part, "tensor").astype(jnp.float32)
    resid_grad = cotangent.astype(jnp.float32) + norm_back(resid, mlp_gain, mid_grad)
    mlp_gain_part = gain_term(resid_rows, lax.dynamic_slice_in_dim(mid_grad, offset, share, 0))
    resid_low = resid_grad.astype(jnp.bfloat16)
    out_w_grad = inner_rows(attended, resid_low)
    attended_grad = outer_cols(resid_low, w_out).astype(jnp.bfloat16)
    q_grad, k_grad, v_grad, qg_part, kg_part = attend_back(
        attended_grad, q_raw, k_raw, query_gain, key_gain, queries, keys_rot, values, logsum, seqs
    )
    query_w_grad = inner_rows(normed_in, q_grad)
    key_w_grad = inner_rows(normed_in, k_grad)
    value_w_grad = inner_rows(normed_in, v_grad)
    in_part = (
        outer_cols(q_grad, w_query)
        + outer_cols(k_grad, key_matrix)
        + outer_cols(v_grad, value_matrix)
    ).astype(jnp.bfloat16)
    in_grad = lax.psum(in_part, "tensor").astype(jnp.float32)
    input_grad = resid_grad + norm_back(stream, attn_gain, in_grad)
    attn_gain_part = gain_term(stream_rows, lax.dynamic_slice_in_dim(in_grad, offset, share, 0))
    attn_gain_grad, mlp_gain_grad, query_gain_grad, key_gain_grad = lax.psum(
        (attn_gain_part, mlp_gain_part, qg_part, kg_part), ("dp", "tensor")
    )
    summed = (
        lax.psum_scatter(
            query_w_grad.astype(jnp.bfloat16), "dp", scatter_dimension=0, tiled=True
        ).astype(jnp.float32),
        lax.psum_scatter(
            key_w_grad.astype(jnp.bfloat16), "dp", scatter_dimension=0, tiled=True
        ).astype(jnp.float32),
        lax.psum_scatter(
            value_w_grad.astype(jnp.bfloat16), "dp", scatter_dimension=0, tiled=True
        ).astype(jnp.float32),
        lax.psum_scatter(
            out_w_grad.astype(jnp.bfloat16), "dp", scatter_dimension=1, tiled=True
        ).astype(jnp.float32),
        lax.psum_scatter(
            gate_w_grad.astype(jnp.bfloat16), "dp", scatter_dimension=0, tiled=True
        ).astype(jnp.float32),
        lax.psum_scatter(
            up_w_grad.astype(jnp.bfloat16), "dp", scatter_dimension=0, tiled=True
        ).astype(jnp.float32),
        lax.psum_scatter(
            down_grad.astype(jnp.bfloat16), "dp", scatter_dimension=1, tiled=True
        ).astype(jnp.float32),
    )
    return (
        mixed,
        input_grad,
        attn_gain_grad,
        mlp_gain_grad,
        query_gain_grad,
        key_gain_grad,
        summed[0],
        summed[1],
        summed[2],
        summed[3],
        summed[4],
        summed[5],
        summed[6],
    )


def solution(mesh):
    placed = (
        P("dp", None),
        P(),
        P(None, "tensor"),
        P(None, "tensor"),
        P(None, "tensor"),
        P(),
        P(),
        P("tensor", None),
        P(),
        P(None, "tensor"),
        P(None, "tensor"),
        P("tensor", None),
        P("dp", None),
    )
    return jax.shard_map(
        on_device,
        mesh=mesh,
        in_specs=placed,
        out_specs=(
            P("dp", None),
            P("dp", None),
            P(),
            P(),
            P(),
            P(),
            P("dp", "tensor"),
            P("dp", "tensor"),
            P("dp", "tensor"),
            P("tensor", "dp"),
            P("dp", "tensor"),
            P("dp", "tensor"),
            P("tensor", "dp"),
        ),
        check_vma=False,
    )
```

profile of v0, /device:TPU:0, one launch (start us, length us, event | category | flops | bytes accessed | tf_op | source)
XLA Modules:
  0.0 1163.3 jit_solution(15609509962232079448)
XLA Ops:
  7.3 3.2 fusion.1
  22.7 6.5 fusion.77
  29.2 2.9 reshape.201
  32.1 3.5 copy.223
  35.6 2.9 copy.185
  38.5 3.5 reshape.187
  47.8 4.1 copy.183
  67.8 4.4 convolution_convert_fusion.4
  72.5 88.1 %all-reduce.10.cloned.1.call-done = bf16[1024,2048]{1,0:T(8,128)(2,1)} async-done(((bf16[1024,2048]{1,0:T(8,128)(2,1)}), bf16[1024,2048]{1,0:T(8,128)(2,1)}) %all-reduce.10.cloned.1.call-update) | async-done | bytes 4194320 | tf_op jit(solution)/shard_map/psum | solution.py:170
  160.6 8.3 convert_add_fusion
  169.0 2.8 multiply_convert_fusion
  171.8 12.0 %fusion.78 = f32[1024,1536]{1,0:T(8,128)} fusion(bf16[1024,2048]{1,0:T(8,128)(2,1)S(1)} %multiply_convert_fusion, bf16[2048,1536]{1,0:T(8,128)(2,1)} %param.22), kind=kOutput, calls=%fused_computation.149 | convolution fusion | flops 6442450944 | bytes 16777216 | tf_op jit(solution)/shard_map/dot_general | solution.py:21
  183.9 8.6 fusion.79
  192.5 15.9 %multiply_convert_fusion.1 = (bf16[1024,1536]{1,0:T(8,128)(2,1)}, bf16[1024,1536]{1,0:T(8,128)(2,1)}, bf16[1024,1536]{1,0:T(8,128)(2,1)}) fusion(f32[1024,1536]{1,0:T(8,128)} %fusion.78, f32[1024,1536]{1,0:T(8,128)} %fusion.79, bf16[1024,2048]{1,0:T(8,128)(2,1)S(1)} %copy-done.26, bf16[1536,2048]{1,0:T(8,128)(2,1)} %param.24), kind=kOutput, calls=%fused_computation.27 | convolution fusion | flops 6467616768 | bytes 32505856 | tf_op jit(solution)/shard_map/dot_general | solution.py:31
  208.4 10.4 fusion.80
  218.7 11.1 add_convert_fusion.1
  229.9 11.1 convolution_convert_fusion.3
  241.1 74.6 %all-reduce.12.cloned.1.call-done = bf16[1024,2048]{1,0:T(8,128)(2,1)} async-done(((bf16[1024,2048]{1,0:T(8,128)(2,1)}), bf16[1024,2048]{1,0:T(8,128)(2,1)}) %all-reduce.12.cloned.1.call-update) | async-done | bytes 4194320 | tf_op jit(solution)/shard_map/psum | solution.py:187
  315.7 6.8 multiply_reduce_fusion
  324.0 7.0 subtract_add_fusion
  331.0 6.7 fusion.25
  340.0 3.8 copy.205
  345.6 2.8 fusion.61
  349.6 4.9 broadcast_multiply_fusion.1
  355.9 2.7 multiply_reduce_fusion.9
  363.0 4.7 fusion.24
  383.7 3.4 add_convert_fusion
  388.4 7.1 convolution_convert_fusion.5
  395.5 5.9 convolution_convert_fusion.6
  401.9 11.6 convolution_convert_fusion.2
  413.6 11.5 convolution_convert_fusion.1
  425.4 11.3 convolution_convert_fusion
  436.7 6.5 convert_element_type.159
  451.7 40.9 %reduce-scatter.10.cloned.1.call-done = bf16[256,256]{1,0:T(8,128)(2,1)} async-done(((bf16[2048,256]{1,0:T(8,128)(2,1)}), bf16[256,256]{1,0:T(8,128)(2,1)}) %reduce-scatter.10.cloned.1.call-update) | async-done | bytes 131088 | tf_op jit(solution)/shard_map/reduce_scatter | solution.py:214
  494.2 152.6 %all-reduce.14.cloned.1.call-done = (bf16[1024,2048]{1,0:T(8,128)(2,1)}, bf16[1024,2048]{1,0:T(8,128)(2,1)}) async-done(((bf16[1024,2048]{1,0:T(8,128)(2,1)}, bf16[1024,2048]{1,0:T(8,128)(2,1)}), (bf16[1024,2048]{1,0:T(8,128)(2,1)}, bf16[1024,2048]{1,0:T(8,128)(2,1)})) %all-reduce.14.cloned.1.call-update) | async-done | bytes 8388624 | tf_op jit(solution)/shard_map/psum | solution.py:177
  646.8 6.7 convert_element_type.189
  653.5 65.8 %reduce-scatter.14.cloned.1.call-done = bf16[512,256]{1,0:T(8,128)(2,1)} async-done(((bf16[512,2048]{1,0:T(8,128)(2,1)}), bf16[512,256]{1,0:T(8,128)(2,1)}) %reduce-scatter.14.cloned.1.call-update) | async-done | bytes 262160 | tf_op jit(solution)/shard_map/reduce_scatter | solution.py:220
  721.1 69.1 %reduce-scatter.8.cloned.1.call-done = bf16[256,512]{1,0:T(8,128)(2,1)} async-done(((bf16[2048,512]{1,0:T(8,128)(2,1)}), bf16[256,512]{1,0:T(8,128)(2,1)}) %reduce-scatter.8.cloned.1.call-update) | async-done | bytes 262160 | tf_op jit(solution)/shard_map/reduce_scatter | solution.py:211
  792.0 2.5 multiply_reduce_fusion.5
  794.5 43.1 %all-reduce.4 = (f32[2048]{0:T(1024)}, f32[2048]{0:T(1024)}, f32[128]{0:T(128)}, f32[128]{0:T(128)}) all-reduce(f32[2048]{0:T(1024)S(1)} %multiply_reduce_fusion.5, f32[2048]{0:T(1024)S(1)} %multiply_reduce_fusion.3, f32[128]{0:T(128)S(1)} %get-tuple-element.13, ...), channel_id=1, replica_groups=mesh['dp'=8,'tensor'=4] {'dp','tensor'}, use_global_device_ids=true, to_apply=%region_17.18 | all-reduce | flops 4352 | bytes 34816 | tf_op jit(solution)/shard_map/psum | solution.py:207
  837.6 5.1 fusion.7
  843.7 10.6 fusion.6
  854.2 57.6 %reduce-scatter.16.cloned.1.call-done = bf16[256,1536]{1,0:T(8,128)(2,1)} async-done(((bf16[2048,1536]{1,0:T(8,128)(2,1)}), bf16[256,1536]{1,0:T(8,128)(2,1)}) %reduce-scatter.16.cloned.1.call-update) | async-done | bytes 786448 | tf_op jit(solution)/shard_map/reduce_scatter | solution.py:223
  911.8 2.5 convert_element_type.199
  914.3 118.4 %reduce-scatter.18.cloned.1.call-done = bf16[256,1536]{1,0:T(8,128)(2,1)} async-done(((bf16[2048,1536]{1,0:T(8,128)(2,1)}), bf16[256,1536]{1,0:T(8,128)(2,1)}) %reduce-scatter.18.cloned.1.call-update) | async-done | bytes 786448 | tf_op jit(solution)/shard_map/reduce_scatter | solution.py:226
  1032.7 2.5 convert_element_type.201
  1035.2 118.7 %reduce-scatter.20.cloned.1.call-done = bf16[1536,256]{1,0:T(8,128)(2,1)} async-done(((bf16[1536,2048]{1,0:T(8,128)(2,1)}), bf16[1536,256]{1,0:T(8,128)(2,1)}) %reduce-scatter.20.cloned.1.call-update) | async-done | bytes 786448 | tf_op jit(solution)/shard_map/reduce_scatter | solution.py:229
  1153.9 2.4 convert_element_type.203
  (185 shorter events, 79.0 us)
Async XLA Ops:
  7.2 60.6 %copy-start = (bf16[512,2048]{1,0:T(8,128)(2,1)S(1)}, bf16[512,2048]{1,0:T(8,128)(2,1)}, u32[]{:S(2)}) copy-start(bf16[512,2048]{1,0:T(8,128)(2,1)} %param.20) | copy-start | bytes 6291460
  7.2 3.9 copy-start.39
  7.2 153.4 %all-reduce.10.cloned.1.call-start = ((), (), s32[]{:S(2)}) async-start(), calls=%async_computation.7 | async-start | bytes 8388608 | tf_op jit(solution)/shard_map/psum | solution.py:170
  7.3 3.8 copy-start.2
  11.1 3.1 copy-start.30
  35.6 7.7 copy-start.44
  42.1 3.4 copy-start.45
  43.3 2.6 copy-start.13
  53.8 2.9 copy-start.29
  56.1 3.3 copy-start.22
  56.2 3.6 copy-start.32
  72.2 96.7 %copy-start.38 = (f32[2048]{0:T(1024)S(1)}, f32[2048]{0:T(1024)}, u32[]{:S(2)}) copy-start(f32[2048]{0:T(1024)} %param.21) | copy-start | bytes 24580
  72.2 243.5 %all-reduce.12.cloned.1.call-start = ((), (), s32[]{:S(2)}) async-start(), calls=%async_computation.8 | async-start | bytes 8388608 | tf_op jit(solution)/shard_map/psum | solution.py:187
  160.6 8.3 copy-start.3
  160.6 8.4 copy-start.6
  169.0 14.9 %slice-start = ((s8[6291456]{0:T(1024)(128)(4,1)}), s8[4194304]{0:T(1024)(128)(4,1)S(1)}, s32[]{:S(2)}) async-start(s8[6291456]{0:T(1024)(128)(4,1)} %bitcast.150), calls=%async_computation.17 | async-start | bytes 8388608
  171.8 12.1 %copy-start.20 = (bf16[1024,2048]{1,0:T(8,128)(2,1)}, bf16[1024,2048]{1,0:T(8,128)(2,1)S(1)}, u32[]{:S(2)}) copy-start(bf16[1024,2048]{1,0:T(8,128)(2,1)S(1)} %multiply_convert_fusion) | copy-start | bytes 12582916
  171.8 12.1 %slice-start.1 = ((s8[6291456]{0:T(1024)(128)(4,1)}), s8[2097152]{0:T(1024)(128)(4,1)S(1)}, s32[]{:S(2)}) async-start(s8[6291456]{0:T(1024)(128)(4,1)} %bitcast.150), calls=%async_computation.18 | async-start | bytes 4194304
  183.9 8.6 copy-start.26
  208.4 10.4 copy-start.47
  229.9 220.2 %reduce-scatter.12.cloned.1.call-start = ((), (), s32[]{:S(2)}) async-start(), calls=%async_computation.11 | async-start | bytes 1179648 | tf_op jit(solution)/shard_map/reduce_scatter | solution.py:217
  315.7 6.8 copy-start.4
  315.7 7.1 copy-start.7
  315.7 8.3 copy-start.9
  337.7 6.1 copy-start.12
  354.5 4.2 copy-start.23
  354.5 4.2 copy-start.27
  361.1 131.5 %reduce-scatter.10.cloned.1.call-start = ((), (), s32[]{:S(2)}) async-start(), calls=%async_computation.10 | async-start | bytes 1179648 | tf_op jit(solution)/shard_map/reduce_scatter | solution.py:214
  367.8 2.3 copy-start.14
  367.8 2.9 copy-start.17
  370.7 2.9 copy-start.24
  376.0 270.8 %all-reduce.14.cloned.1.call-start = ((), (), s32[]{:S(2)}) async-start(), calls=%async_computation.16 | async-start | bytes 16777216 | tf_op jit(solution)/shard_map/psum | solution.py:177
  376.3 3.0 copy-start.31
  381.3 2.4 copy-start.28
  381.3 2.4 copy-start.33
  387.2 8.4 copy-start.37
  387.2 332.1 %reduce-scatter.14.cloned.1.call-start = ((), (), s32[]{:S(2)}) async-start(), calls=%async_computation.12 | async-start | bytes 2359296 | tf_op jit(solution)/shard_map/reduce_scatter | solution.py:220
  395.5 394.7 %reduce-scatter.8.cloned.1.call-start = ((), (), s32[]{:S(2)}) async-start(), calls=%async_computation.9 | async-start | bytes 2359296 | tf_op jit(solution)/shard_map/reduce_scatter | solution.py:211
  401.5 510.4 %reduce-scatter.16.cloned.1.call-start = ((), (), s32[]{:S(2)}) async-start(), calls=%async_computation.13 | async-start | bytes 7077888 | tf_op jit(solution)/shard_map/reduce_scatter | solution.py:223
  413.5 619.2 %reduce-scatter.18.cloned.1.call-start = ((), (), s32[]{:S(2)}) async-start(), calls=%async_computation.14 | async-start | bytes 7077888 | tf_op jit(solution)/shard_map/reduce_scatter | solution.py:226
  425.1 728.8 %reduce-scatter.20.cloned.1.call-start = ((), (), s32[]{:S(2)}) async-start(), calls=%async_computation.15 | async-start | bytes 7077888 | tf_op jit(solution)/shard_map/reduce_scatter | solution.py:229
  443.2 3.8 copy-start.10
  653.5 184.1 %copy-start.40 = (f32[2048]{0:T(1024)S(1)}, f32[2048]{0:T(1024)}, u32[]{:S(2)}) copy-start(f32[2048]{0:T(1024)} %param.14) | copy-start | bytes 24580
  837.6 5.1 copy-start.5
  837.6 6.1 copy-start.8
  837.6 6.1 copy-start.42
  837.6 6.1 copy-start.43
  843.7 312.7 %copy-start.1 = (bf16[512,2048]{1,0:T(8,128)(2,1)S(1)}, bf16[512,2048]{1,0:T(8,128)(2,1)}, u32[]{:S(2)}) copy-start(bf16[512,2048]{1,0:T(8,128)(2,1)} %param.20) | copy-start | bytes 6291460
  (12 other events, 18.9 us)
Sparse Core Ops, SparseCore 0:
  72.3 88.2 all-reduce.9
  230.0 85.6 all-reduce.11
  361.2 64.3 reduce-scatter.11
  429.5 63.0 reduce-scatter.9
  495.0 151.7 all-reduce.13
  650.2 69.0 reduce-scatter.13
  722.8 67.2 reduce-scatter.7
  793.7 118.0 reduce-scatter.15
  915.4 117.2 reduce-scatter.17
  1036.2 117.6 reduce-scatter.19
where the time goes:
time: 1170 us; the launch traced here: 1160 us
  waiting for transfers between devices  786 us (67%)
  matrix products  167 us (14%)
  other arithmetic  104 us (9%)
  local copies, waits for them, and re-layouts  46.2 us (4%)
  blocking collectives  43.1 us (4%)
  between operations  15 us (1%)
    psum x1, waiting for transfers between devices, on_device(): lax.psum(mlp_part, 'tensor').astype(jnp.float32)  153 us
    reduce_scatter x1, waiting for transfers between devices, on_device(): lax.psum_scatter(down_grad.astype(jnp.bfloat16), 'dp', scatter_dimension=...  119 us
    reduce_scatter x1, waiting for transfers between devices, on_device(): lax.psum_scatter(up_w_grad.astype(jnp.bfloat16), 'dp', scatter_dimension=...  118 us
    psum x1, waiting for transfers between devices, on_device(): resid = stream + lax.psum(attn_part, 'tensor').astype(jnp.float32)  88.1 us
    psum x1, waiting for transfers between devices, on_device(): mid_grad = lax.psum(mid_part, 'tensor').astype(jnp.float32)  74.6 us
    reduce_scatter x1, waiting for transfers between devices, on_device(): lax.psum_scatter(query_w_grad.astype(jnp.bfloat16), 'dp', scatter_dimensi...  69.1 us
    reduce_scatter x1, waiting for transfers between devices, on_device(): lax.psum_scatter(out_w_grad.astype(jnp.bfloat16), 'dp', scatter_dimension...  65.8 us
    reduce_scatter x1, waiting for transfers between devices, on_device(): lax.psum_scatter(gate_w_grad.astype(jnp.bfloat16), 'dp', scatter_dimensio...  57.6 us
  transfers between devices with their start and end apart: 10, of which 9 were waited for; matrix products, arithmetic and copies ran while one was open for 11% of the time, Pallas kernels for 0%

commit v1 on v0

--- a/solution.py
+++ b/solution.py
@@ -1,7 +1,9 @@
+import itertools
 import math
 
 import jax
 import jax.numpy as jnp
+import numpy as np
 from jax import lax
 from jax.sharding import PartitionSpec as P
 
@@ -138,116 +140,228 @@
     )
 
 
-def on_device(
-    tokens,
-    attn_gain,
-    w_query,
-    key_matrix,
-    value_matrix,
-    query_gain,
-    key_gain,
-    w_out,
-    mlp_gain,
-    w_gate,
-    w_up,
-    w_down,
-    cotangent,
-):
-    count = tokens.shape[0]
-    seqs = count // LEN
-    share = count // lax.axis_size("tensor")
-    offset = lax.axis_index("tensor") * share
-    stream = tokens.astype(jnp.float32)
-    stream_rows = lax.dynamic_slice_in_dim(stream, offset, share, 0)
-    normed_in = rms_scale(stream, attn_gain).astype(jnp.bfloat16)
-    q_raw = matmul(normed_in, w_query)
-    k_raw = matmul(normed_in, key_matrix)
-    v_raw = matmul(normed_in, value_matrix)
-    attended, logsum, queries, keys_rot, values = attend(
-        q_raw, k_raw, v_raw, query_gain, key_gain, seqs
-    )
-    attn_part = matmul(attended, w_out).astype(jnp.bfloat16)
-    resid = stream + lax.psum(attn_part, "tensor").astype(jnp.float32)
-    resid_rows = lax.dynamic_slice_in_dim(resid, offset, share, 0)
-    normed_mid = rms_scale(resid, mlp_gain).astype(jnp.bfloat16)
-    gate = matmul(normed_mid, w_gate)
-    upper = matmul(normed_mid, w_up)
-    hidden = swiglu(gate, upper).astype(jnp.bfloat16)
-    mlp_part = matmul(hidden, w_down).astype(jnp.bfloat16)
-    mixed = (resid + lax.psum(mlp_part, "tensor").astype(jnp.float32)).astype(jnp.bfloat16)
-    down_grad = inner_rows(hidden, cotangent)
-    hidden_grad = outer_cols(cotangent, w_down)
-    _, pull = jax.vjp(swiglu, gate, upper)
-    gate_grad, upper_grad = pull(hidden_grad)
-    gate_grad = gate_grad.astype(jnp.bfloat16)
-    upper_grad = upper_grad.astype(jnp.bfloat16)
-    gate_w_grad = inner_rows(normed_mid, gate_grad)
-    up_w_grad = inner_rows(normed_mid, upper_grad)
-    mid_part = (outer_cols(gate_grad, w_gate) + outer_cols(upper_grad, w_up)).astype(jnp.bfloat16)
-    mid_grad = lax.psum(mid_part, "tensor").astype(jnp.float32)
-    resid_grad = cotangent.astype(jnp.float32) + norm_back(resid, mlp_gain, mid_grad)
-    mlp_gain_part = gain_term(resid_rows, lax.dynamic_slice_in_dim(mid_grad, offset, share, 0))
-    resid_low = resid_grad.astype(jnp.bfloat16)
-    out_w_grad = inner_rows(attended, resid_low)
-    attended_grad = outer_cols(resid_low, w_out).astype(jnp.bfloat16)
-    q_grad, k_grad, v_grad, qg_part, kg_part = attend_back(
-        attended_grad, q_raw, k_raw, query_gain, key_gain, queries, keys_rot, values, logsum, seqs
-    )
-    query_w_grad = inner_rows(normed_in, q_grad)
-    key_w_grad = inner_rows(normed_in, k_grad)
-    value_w_grad = inner_rows(normed_in, v_grad)
-    in_part = (
-        outer_cols(q_grad, w_query)
-        + outer_cols(k_grad, key_matrix)
-        + outer_cols(v_grad, value_matrix)
-    ).astype(jnp.bfloat16)
-    in_grad = lax.psum(in_part, "tensor").astype(jnp.float32)
-    input_grad = resid_grad + norm_back(stream, attn_gain, in_grad)
-    attn_gain_part = gain_term(stream_rows, lax.dynamic_slice_in_dim(in_grad, offset, share, 0))
-    attn_gain_grad, mlp_gain_grad, query_gain_grad, key_gain_grad = lax.psum(
-        (attn_gain_part, mlp_gain_part, qg_part, kg_part), ("dp", "tensor")
-    )
-    summed = (
-        lax.psum_scatter(
-            query_w_grad.astype(jnp.bfloat16), "dp", scatter_dimension=0, tiled=True
-        ).astype(jnp.float32),
-        lax.psum_scatter(
-            key_w_grad.astype(jnp.bfloat16), "dp", scatter_dimension=0, tiled=True
-        ).astype(jnp.float32),
-        lax.psum_scatter(
-            value_w_grad.astype(jnp.bfloat16), "dp", scatter_dimension=0, tiled=True
-        ).astype(jnp.float32),
-        lax.psum_scatter(
-            out_w_grad.astype(jnp.bfloat16), "dp", scatter_dimension=1, tiled=True
-        ).astype(jnp.float32),
-        lax.psum_scatter(
-            gate_w_grad.astype(jnp.bfloat16), "dp", scatter_dimension=0, tiled=True
-        ).astype(jnp.float32),
-        lax.psum_scatter(
-            up_w_grad.astype(jnp.bfloat16), "dp", scatter_dimension=0, tiled=True
-        ).astype(jnp.float32),
-        lax.psum_scatter(
-            down_grad.astype(jnp.bfloat16), "dp", scatter_dimension=1, tiled=True
-        ).astype(jnp.float32),
-    )
-    return (
-        mixed,
-        input_grad,
-        attn_gain_grad,
-        mlp_gain_grad,
-        query_gain_grad,
-        key_gain_grad,
-        summed[0],
-        summed[1],
-        summed[2],
-        summed[3],
-        summed[4],
-        summed[5],
-        summed[6],
-    )
+def snake_ring(coords):
+    coords = [tuple(c) for c in coords]
+    dims = [d for d in range(len(coords[0])) if len({c[d] for c in coords}) > 1]
+    if not dims:
+        return list(range(len(coords)))
+    values = [sorted({c[d] for c in coords}) for d in dims]
+    where = {tuple(c[d] for d in dims): i for i, c in enumerate(coords)}
+    best = None
+    for perm in itertools.permutations(range(len(dims))):
+        def walk(level):
+            if level == len(perm):
+                return [()]
+            inner = walk(level + 1)
+            out = []
+            for i, value in enumerate(values[perm[level]]):
+                seq = inner if i % 2 == 0 else inner[::-1]
+                out += [((perm[level], value),) + t for t in seq]
+            return out
+
+        order = []
+        for path in walk(0):
+            key = dict(path)
+            point = tuple(key[k] for k in range(len(dims)))
+            if point in where:
+                order.append(where[point])
+        if len(order) != len(coords):
+            continue
+        cost = sum(
+            sum(abs(a - b) for a, b in zip(coords[order[i]], coords[order[(i + 1) % len(order)]]))
+            for i in range(len(order))
+        )
+        if best is None or cost < best[0]:
+            best = (cost, order)
+    return best[1] if best else list(range(len(coords)))
+
+
+class Plan:
+    def __init__(self, mesh):
+        names = mesh.axis_names
+        devices = np.asarray(mesh.devices)
+        dp_axis, tp_axis = names.index("dp"), names.index("tensor")
+        devices = np.transpose(devices, (dp_axis, tp_axis))
+        self.n_dp, self.n_tp = devices.shape
+        dp_coords = [tuple(devices[d, 0].coords) for d in range(self.n_dp)]
+        self.ring = snake_ring(dp_coords)
+        self.pos = [self.ring.index(d) for d in range(self.n_dp)]
+        n = self.n_dp
+        self.cw = [(self.ring[i], self.ring[(i + 1) % n]) for i in range(n)]
+        self.ccw = [(b, a) for a, b in self.cw]
+        group = [devices[0, t] for t in range(self.n_tp)]
+        self.tp_ok = False
+        if self.n_tp == 4:
+            chip = [tuple(g.coords) for g in group]
+            core = [g.core_on_chip for g in group]
+            same = [[u for u in range(4) if u != t and chip[u] == chip[t]] for t in range(4)]
+            cross = [
+                [u for u in range(4) if chip[u] != chip[t] and core[u] == core[t]] for t in range(4)
+            ]
+            if all(len(s) == 1 for s in same) and all(len(c) == 1 for c in cross):
+                self.core_pairs = [(t, same[t][0]) for t in range(4)]
+                self.chip_pairs = [(t, cross[t][0]) for t in range(4)]
+                self.half_of = [0 if t < same[t][0] else 1 for t in range(4)]
+                self.tp_ok = True
+
+    def tp_sum(self, part):
+        if not self.tp_ok:
+            return lax.psum(part.astype(jnp.float32), "tensor").astype(jnp.bfloat16)
+        rows = part.shape[0]
+        h = rows // 2
+        t = lax.axis_index("tensor")
+        half = jnp.array(self.half_of, jnp.int32)[t]
+        keep = lax.dynamic_slice_in_dim(part, half * h, h, 0)
+        give = lax.dynamic_slice_in_dim(part, (1 - half) * h, h, 0)
+        got = lax.ppermute(give, "tensor", self.core_pairs)
+        chip_sum = (keep.astype(jnp.float32) + got.astype(jnp.float32)).astype(jnp.bfloat16)
+        other = lax.ppermute(chip_sum, "tensor", self.chip_pairs)
+        done = (chip_sum.astype(jnp.float32) + other.astype(jnp.float32)).astype(jnp.bfloat16)
+        partner = lax.ppermute(done, "tensor", self.core_pairs)
+        first = jnp.where(half == 0, done, partner)
+        second = jnp.where(half == 0, partner, done)
+        return jnp.concatenate([first, second], 0)
+
+    def dp_rs(self, grads):
+        n = self.n_dp
+        me = lax.axis_index("dp")
+        pos = jnp.array(self.pos, jnp.int32)[me]
+        ring = jnp.array(self.ring, jnp.int32)
+        blocks = [g.reshape(n, 2, g.shape[0] // n // 2, g.shape[1]) for g in grads]
+        acc_a = acc_b = None
+        for s in range(n - 1):
+            ia = ring[(pos - 1 - s) % n]
+            ib = ring[(pos + 1 + s) % n]
+            own_a = [lax.dynamic_index_in_dim(b, ia, 0, keepdims=False)[0] for b in blocks]
+            own_b = [lax.dynamic_index_in_dim(b, ib, 0, keepdims=False)[1] for b in blocks]
+            if acc_a is None:
+                send_a, send_b = own_a, own_b
+            else:
+                send_a = [x + y for x, y in zip(acc_a, own_a)]
+                send_b = [x + y for x, y in zip(acc_b, own_b)]
+            send_a = [x.astype(jnp.bfloat16) for x in send_a]
+            send_b = [x.astype(jnp.bfloat16) for x in send_b]
+            acc_a = [x.astype(jnp.float32) for x in lax.ppermute(send_a, "dp", self.cw)]
+            acc_b = [x.astype(jnp.float32) for x in lax.ppermute(send_b, "dp", self.ccw)]
+        out = []
+        for b, xa, xb in zip(blocks, acc_a, acc_b):
+            mine = lax.dynamic_index_in_dim(b, me, 0, keepdims=False)
+            out.append(jnp.concatenate([xa + mine[0], xb + mine[1]], 0))
+        return out
+
+    def all_sum(self, x):
+        for axis, size in (("tensor", self.n_tp), ("dp", self.n_dp)):
+            if size & (size - 1):
+                x = lax.psum(x, axis)
+                continue
+            bit = 1
+            while bit < size:
+                x = x + lax.ppermute(x, axis, [(i, i ^ bit) for i in range(size)])
+                bit *= 2
+        return x
+
+
+def make_on_device(plan):
+    def on_device(
+        tokens,
+        attn_gain,
+        w_query,
+        key_matrix,
+        value_matrix,
+        query_gain,
+        key_gain,
+        w_out,
+        mlp_gain,
+        w_gate,
+        w_up,
+        w_down,
+        cotangent,
+    ):
+        count = tokens.shape[0]
+        seqs = count // LEN
+        share = count // lax.axis_size("tensor")
+        offset = lax.axis_index("tensor") * share
+        stream = tokens.astype(jnp.float32)
+        stream_rows = lax.dynamic_slice_in_dim(stream, offset, share, 0)
+        normed_in = rms_scale(stream, attn_gain).astype(jnp.bfloat16)
+        q_raw = matmul(normed_in, w_query)
+        k_raw = matmul(normed_in, key_matrix)
+        v_raw = matmul(normed_in, value_matrix)
+        attended, logsum, queries, keys_rot, values = attend(
+            q_raw, k_raw, v_raw, query_gain, key_gain, seqs
+        )
+        attn_part = matmul(attended, w_out).astype(jnp.bfloat16)
+        resid = stream + plan.tp_sum(attn_part).astype(jnp.float32)
+        resid_rows = lax.dynamic_slice_in_dim(resid, offset, share, 0)
+        normed_mid = rms_scale(resid, mlp_gain).astype(jnp.bfloat16)
+        gate = matmul(normed_mid, w_gate)
+        upper = matmul(normed_mid, w_up)
+        hidden = swiglu(gate, upper).astype(jnp.bfloat16)
+        mlp_part = matmul(hidden, w_down).astype(jnp.bfloat16)
+        mixed = (resid + plan.tp_sum(mlp_part).astype(jnp.float32)).astype(jnp.bfloat16)
+        down_grad_t = inner_rows(cotangent, hidden)
+        hidden_grad = outer_cols(cotangent, w_down)
+        _, pull = jax.vjp(swiglu, gate, upper)
+        gate_grad, upper_grad = pull(hidden_grad)
+        gate_grad = gate_grad.astype(jnp.bfloat16)
+        upper_grad = upper_grad.astype(jnp.bfloat16)
+        gate_w_grad = inner_rows(normed_mid, gate_grad)
+        up_w_grad = inner_rows(normed_mid, upper_grad)
+        mlp_sums = plan.dp_rs([down_grad_t, gate_w_grad, up_w_grad])
+        mid_part = (outer_cols(gate_grad, w_gate) + outer_cols(upper_grad, w_up)).astype(
+            jnp.bfloat16
+        )
+        mid_grad = plan.tp_sum(mid_part).astype(jnp.float32)
+        resid_grad = cotangent.astype(jnp.float32) + norm_back(resid, mlp_gain, mid_grad)
+        mlp_gain_part = gain_term(resid_rows, lax.dynamic_slice_in_dim(mid_grad, offset, share, 0))
+        resid_low = resid_grad.astype(jnp.bfloat16)
+        out_w_grad_t = inner_rows(resid_low, attended)
+        attended_grad = outer_cols(resid_low, w_out).astype(jnp.bfloat16)
+        q_grad, k_grad, v_grad, qg_part, kg_part = attend_back(
+            attended_grad, q_raw, k_raw, query_gain, key_gain, queries, keys_rot, values, logsum, seqs
+        )
+        query_w_grad = inner_rows(normed_in, q_grad)
+        key_w_grad = inner_rows(normed_in, k_grad)
+        value_w_grad = inner_rows(normed_in, v_grad)
+        attn_sums = plan.dp_rs([out_w_grad_t, query_w_grad, key_w_grad, value_w_grad])
+        in_part = (
+            outer_cols(q_grad, w_query)
+            + outer_cols(k_grad, key_matrix)
+            + outer_cols(v_grad, value_matrix)
+        ).astype(jnp.bfloat16)
+        in_grad = plan.tp_sum(in_part).astype(jnp.float32)
+        input_grad = resid_grad + norm_back(stream, attn_gain, in_grad)
+        attn_gain_part = gain_term(stream_rows, lax.dynamic_slice_in_dim(in_grad, offset, share, 0))
+        gains = plan.all_sum(jnp.concatenate([attn_gain_part, mlp_gain_part, qg_part, kg_part]))
+        width = attn_gain_part.shape[0]
+        head = qg_part.shape[0]
+        attn_gain_grad = gains[:width]
+        mlp_gain_grad = gains[width : 2 * width]
+        query_gain_grad = gains[2 * width : 2 * width + head]
+        key_gain_grad = gains[2 * width + head :]
+        down_sum, gate_sum, up_sum = mlp_sums
+        out_sum, query_sum, key_sum, value_sum = attn_sums
+        return (
+            mixed,
+            input_grad,
+            attn_gain_grad,
+            mlp_gain_grad,
+            query_gain_grad,
+            key_gain_grad,
+            query_sum,
+            key_sum,
+            value_sum,
+            out_sum.T,
+            gate_sum,
+            up_sum,
+            down_sum.T,
+        )
+
+    return on_device
 
 
 def solution(mesh):
+    plan = Plan(mesh)
     placed = (
         P("dp", None),
         P(),
@@ -264,7 +378,7 @@
         P("dp", None),
     )
     return jax.shard_map(
-        on_device,
+        make_on_device(plan),
         mesh=mesh,
         in_specs=placed,
         out_specs=(

time: 1170 us -> 847 us (0.72)
  waiting for transfers between devices: 786 us -> 261 us
  starting transfers between devices: 1.42 us -> 124 us
  local copies, waits for them, and re-layouts: 46.2 us -> 105 us
  blocking collectives: 43.1 us -> 0 us
  other arithmetic: 104 us -> 140 us
  between operations: 15 us -> 40.4 us
    reduce_scatter x7 -> x0, waiting for transfers between devices: 471 us -> none  [the longest x1 119 us: on_device(): lax.psum_scatter(down_grad.astype(jnp.bfloat16), 'dp', scatter_dimension=...]
    psum x3 -> x0, waiting for transfers between devices: 315 us -> none  [the longest x1 153 us: on_device(): lax.psum(mlp_part, 'tensor').astype(jnp.float32)]
    ppermute x0 -> x115, waiting for transfers between devices: none -> 261 us  [the longest x4 119 us: tp_sum(): other = lax.ppermute(chip_sum, 'tensor', self.chip_pairs)]
    ppermute x0 -> x115, starting transfers between devices: none -> 124 us  [the longest x49 68.9 us: dp_rs(): acc_a = [x.astype(jnp.float32) for x in lax.ppermute(send_a, 'dp', self.cw)]]
    psum x1 -> x0, blocking collectives: 43.1 us -> none  [on_device(): lax.psum((attn_gain_part, mlp_gain_part, qg_part, kg_part), ('dp', 'tenso...]
    dot_general x0 -> x2, other arithmetic: none -> 25.5 us  [inner_rows(): lax.dot_general(left, right, (((0,), (0,)), ((), ())), preferred_element_...]
    reshape x0 -> x1, local copies, waits for them, and re-layouts: none -> 16.9 us  [dp_rs(): blocks = [g.reshape(n, 2, g.shape[0] // n // 2, g.shape[1]) for g in grads]]
    convert_element_type x10 -> x58, other arithmetic: 22.9 us -> 38.7 us  [the longest x42 17.9 us: dp_rs(): send_a = [x.astype(jnp.bfloat16) for x in send_a]]
  transfers between devices with their start and end apart: 10 -> 115, of which waited for: 9 -> 61; matrix products, arithmetic and copies ran while one was open for 11% -> 24% of each run, Pallas kernels for 0% -> 0%
where the time goes in v1:
time: 847 us; the launch traced here: 838 us
  waiting for transfers between devices  261 us (31%)
  matrix products  167 us (20%)
  other arithmetic  140 us (17%)
  starting transfers between devices  124 us (15%)
  local copies, waits for them, and re-layouts  105 us (12%)
  between operations  40.4 us (5%)
    ppermute x4, waiting for transfers between devices, tp_sum(): other = lax.ppermute(chip_sum, 'tensor', self.chip_pairs)  119 us
    ppermute x49, waiting for transfers between devices, dp_rs(): acc_a = [x.astype(jnp.float32) for x in lax.ppermute(send_a, 'dp', self.cw)]  89.6 us
    ppermute x49, starting transfers between devices, dp_rs(): acc_a = [x.astype(jnp.float32) for x in lax.ppermute(send_a, 'dp', self.cw)]  68.9 us
    dot_general x7, matrix products, outer_cols(): lax.dot_general(left, right, (((1,), (1,)), ((), ())), preferred_element_...  53 us
    dot_general x7, matrix products, matmul(): return jnp.dot(left, right, preferred_element_type=jnp.float32)  50.6 us
    dot_general x7, matrix products, inner_rows(): lax.dot_general(left, right, (((0,), (0,)), ((), ())), preferred_element_...  42.5 us
    ppermute x49, starting transfers between devices, dp_rs(): lax.ppermute(send_b, 'dp', self.ccw)  39.9 us
    ppermute x49, waiting for transfers between devices, dp_rs(): lax.ppermute(send_b, 'dp', self.ccw)  39.8 us
  transfers between devices with their start and end apart: 115, of which 61 were waited for; matrix products, arithmetic and copies ran while one was open for 24% of the time, Pallas kernels for 0%

profile of v1, /device:TPU:0, one launch (start us, length us, event | category | flops | bytes accessed | tf_op | source)
XLA Modules:
  0.0 837.5 jit_solution(12904182960194125535)
XLA Ops:
  14.2 6.9 fusion.244
  40.5 4.4 copy.327
  59.6 5.6 convolution_convert_fusion.1
  73.0 4.4 add_convert_fusion.10
  80.3 6.4 convert_element_type.791
  88.6 38.0 %collective-permute-done.1 = bf16[512,2048]{1,0:T(8,128)(2,1)} collective-permute-done((bf16[512,2048]{1,0:T(8,128)(2,1)}, bf16[512,2048]{1,0:T(8,128)(2,1)}, u32[]{:S(2)}, u32[]{:S(2)}) %collective-permute-start.1) | collective-permute-done | bytes 2097184 | tf_op jit(solution)/shard_map/ppermute | solution.py:218
  126.5 4.4 add_convert_fusion.9
  169.3 12.4 %fusion.256 = f32[1024,1536]{1,0:T(8,128)} fusion(bf16[1024,2048]{1,0:T(8,128)(2,1)} %param.33, bf16[1536,2048]{1,0:T(8,128)(2,1)} %param.32), kind=kOutput, calls=%fused_computation.481 | convolution fusion | flops 6442450944 | bytes 16777216 | tf_op jit(solution)/shard_map/dot_general | solution.py:33
  185.1 4.7 convert_add_fusion
  190.4 5.7 multiply_convert_fusion
  196.2 8.6 %fusion.255 = f32[1024,1536]{1,0:T(8,128)} fusion(bf16[1024,2048]{1,0:T(8,128)(2,1)S(1)} %multiply_convert_fusion, bf16[2048,1536]{1,0:T(8,128)(2,1)S(1)} %bitcast.806), kind=kOutput, calls=%fused_computation.480 | convolution fusion | flops 6442450944 | bytes 16777216 | tf_op jit(solution)/shard_map/dot_general | solution.py:23
  204.8 16.4 %multiply_convert_fusion.1 = (bf16[1024,1536]{1,0:T(8,128)(2,1)}, bf16[1024,1536]{1,0:T(8,128)(2,1)}, bf16[1024,1536]{1,0:T(8,128)(2,1)}) fusion(f32[1024,1536]{1,0:T(8,128)} %fusion.256, f32[1024,1536]{1,0:T(8,128)} %fusion.255, bf16[1024,2048]{1,0:T(8,128)(2,1)S(1)} %multiply_convert_fusion, bf16[2048,1536]{1,0:T(8,128)(2,1)} %param.30), kind=kOutput, calls=%fused_computation.25 | convolution fusion | flops 6467616768 | bytes 32505856 | tf_op jit(solution)/shard_map/dot_general | solution.py:23
  221.2 11.6 %convolution_bitcast_fusion = f32[2048,1536]{0,1:T(8,128)} fusion(bf16[1024,1536]{1,0:T(8,128)(2,1)} %get-tuple-element.158, bf16[1024,2048]{1,0:T(8,128)(2,1)S(1)} %copy-done.31), kind=kOutput, calls=%fused_computation.7 | convolution fusion | flops 6442450944 | bytes 19922944 | tf_op jit(solution)/shard_map/dot_general | solution.py:27
  232.9 8.2 convolution_convert_fusion
  241.1 9.4 %fusion.258 = f32[2048,1536]{1,0:T(8,128)} fusion(bf16[1024,2048]{1,0:T(8,128)(2,1)S(1)} %multiply_convert_fusion, bf16[1024,1536]{1,0:T(8,128)(2,1)S(1)} %copy-done.95), kind=kOutput, calls=%fused_computation.483 | convolution fusion | flops 6442450944 | bytes 19922944 | tf_op jit(solution)/shard_map/dot_general | solution.py:27
  250.6 9.1 %fusion.257 = f32[1024,2048]{1,0:T(8,128)} fusion(bf16[1024,1536]{1,0:T(8,128)(2,1)S(1)} %copy-done.95, bf16[2048,1536]{1,0:T(8,128)(2,1)S(1)} %bitcast.804), kind=kOutput, calls=%fused_computation.482 | convolution fusion | flops 6442450944 | bytes 17825792 | tf_op jit(solution)/shard_map/dot_general | solution.py:33
  259.6 16.9 %reshape.540 = f32[8,2,128,1536]{2,1,0,3:T(2,128)} reshape(f32[2048,1536]{0,1:T(8,128)} %convolution_bitcast_fusion) | data formatting | bytes 25165824 | tf_op jit(solution)/shard_map/reshape | solution.py:230
  283.7 9.0 %fusion.259 = f32[2048,1536]{1,0:T(8,128)S(1)} fusion(bf16[1024,2048]{1,0:T(8,128)(2,1)S(1)} %copy-done.33, bf16[1024,1536]{1,0:T(8,128)(2,1)} %get-tuple-element.156), kind=kOutput, calls=%fused_computation.484 | convolution fusion | flops 6442450944 | bytes 19922944 | tf_op jit(solution)/shard_map/dot_general | solution.py:27
  302.7 13.5 %add_convert_fusion.1 = bf16[1024,2048]{1,0:T(8,128)(2,1)} fusion(f32[1024,2048]{1,0:T(8,128)} %fusion.257, bf16[1024,1536]{1,0:T(8,128)(2,1)} %get-tuple-element.156, bf16[2048,1536]{1,0:T(8,128)(2,1)} %param.31), kind=kOutput, calls=%fused_computation.18 | convolution fusion | flops 6446645248 | bytes 22020096 | tf_op jit(solution)/shard_map/dot_general | solution.py:33
  318.0 10.4 %constant_dynamic-slice_fusion.1 = (f32[1,1,128,1536]{2,1,0,3:T(1,128)}, f32[1,1,128,1536]{2,1,0,3:T(1,128)}, f32[1,1,128,1536]{2,1,0,3:T(1,128)}, f32[1,1,128,1...) fusion(f32[8,2,128,1536]{2,1,0,3:T(2,128)S(1)} %bitcast.746, ...), kind=kLoop, calls=%fused_computation.427 | loop fusion | bytes 22020152 | tf_op jit(solution)/shard_map/slice | solution.py:235
  338.8 7.9 collective-permute-done.102
  348.0 8.8 %collective-permute-done.109 = bf16[128,1536]{0,1:T(8,128)(2,1)S(1)} collective-permute-done((bf16[128,1536]{0,1:T(8,128)(2,1)S(1)}, bf16[128,1536]{0,1:T(8,128)(2,1)S(1)}, u32[]{:S(2)}, u32[]{:S(2)}) %collective-permute-start.109) | collective-permute-done | bytes 393248 | tf_op jit(solution)/shard_map/ppermute | solution.py:245
  360.3 8.5 %collective-permute-done.88 = bf16[128,1536]{1,0:T(8,128)(2,1)S(1)} collective-permute-done((bf16[128,1536]{1,0:T(8,128)(2,1)S(1)}, bf16[128,1536]{1,0:T(8,128)(2,1)S(1)}, u32[]{:S(2)}, u32[]{:S(2)}) %collective-permute-start.88) | collective-permute-done | bytes 393248 | tf_op jit(solution)/shard_map/ppermute | solution.py:244
  372.4 4.8 collective-permute-done.74
  380.5 5.1 collective-permute-done.103
  387.9 6.1 collective-permute-done.89
  398.9 3.6 collective-permute-done.75
  406.0 4.9 collective-permute-done.104
  414.3 5.0 collective-permute-done.90
  424.2 3.6 collective-permute-done.76
  431.2 4.9 collective-permute-done.105
  441.0 3.6 collective-permute-done.91
  457.7 3.8 collective-permute-done.106
  467.5 29.2 %collective-permute-done.7 = bf16[512,2048]{1,0:T(8,128)(2,1)S(1)} collective-permute-done((bf16[512,2048]{1,0:T(8,128)(2,1)S(1)}, bf16[512,2048]{1,0:T(8,128)(2,1)S(1)}, u32[]{:S(2)}, u32[]{:S(2)}) %collective-permute-start.7) | collective-permute-done | bytes 2097184 | tf_op jit(solution)/shard_map/ppermute | solution.py:218
  507.3 25.8 %collective-permute-done.4 = bf16[512,2048]{1,0:T(8,128)(2,1)S(1)} collective-permute-done((bf16[512,2048]{1,0:T(8,128)(2,1)S(1)}, bf16[512,2048]{1,0:T(8,128)(2,1)S(1)}, u32[]{:S(2)}, u32[]{:S(2)}) %collective-permute-start.4) | collective-permute-done | bytes 2097184 | tf_op jit(solution)/shard_map/ppermute | solution.py:218
  535.9 4.9 collective-permute-done.99
  553.3 16.1 %convert_bitcast_fusion = (bf16[2048,1024]{0,1:T(8,128)(2,1)}, f32[1024,2048]{1,0:T(8,128)}, bf16[1024,2048]{1,0:T(8,128)(2,1)}) fusion(f32[1024]{0:T(1024)S(1)} %broadcast_multiply_fusion.3, f32[1024]{0:T(1024)S(1)} %copy-done.86, bf16[512,2048]{1,0:T(8,128)(2,1)S(1)} %copy-done.9, bf16[512,2048]{1,0:T(8,128)(2,1)S(1)} %copy-done.7, ...), kind=kLoop, calls=%fused_computation.59 | loop fusion | flops 50331648 | bytes 37769216 | tf_op jit(solution)/shard_map/dot_general | solution.py:27
  569.4 5.7 fusion.24
  584.7 6.4 broadcast_multiply_fusion.1
  591.1 6.1 fusion.23
  608.7 5.6 fusion.32
  614.3 5.5 add_convert_fusion
  630.5 6.4 copy.404
  636.9 5.0 fusion.36
  667.7 26.0 %collective-permute-done.10 = bf16[512,2048]{1,0:T(8,128)(2,1)S(1)} collective-permute-done((bf16[512,2048]{1,0:T(8,128)(2,1)S(1)}, bf16[512,2048]{1,0:T(8,128)(2,1)S(1)}, u32[]{:S(2)}, u32[]{:S(2)}) %collective-permute-start.10) | collective-permute-done | bytes 2097184 | tf_op jit(solution)/shard_map/ppermute | solution.py:218
  721.2 9.4 %fusion.243 = (bf16[2048,1024]{0,1:T(8,128)(2,1)}, f32[1024,2048]{1,0:T(8,128)}) fusion(f32[2048]{0:T(1024)S(1)} %copy-done.82, f32[1024]{0:T(1024)S(1)} %copy-done.85, bf16[1024,2048]{1,0:T(8,128)(2,1)S(1)} %copy-done.5, f32[1024,2048]{1,0:T(8,128)} %get-tuple-element.109, f32[1024]{0:T(1024)S(1)} %broadcast_multiply_fusion.2, f32[1024]{0:T(1024)S(1)} %copy-done.83, ...), kind=kLoop, calls=%fused_computation.471 | loop fusion | flops 29360128 | bytes 29380608 | tf_op jit(solution)/shard_map/dot_general | solution.py:27
  730.7 6.4 copy.406
  737.1 3.6 fusion.103
  (609 shorter events, 358.4 us)
Async XLA Ops:
  77.4 49.1 %collective-permute-start.1 = (bf16[512,2048]{1,0:T(8,128)(2,1)}, bf16[512,2048]{1,0:T(8,128)(2,1)}, u32[]{:S(2)}, u32[]{:S(2)}) collective-permute-start(bf16[512,2048]{1,0:T(8,128)(2,1)} %add_convert_fusion.10), channel_id=1, source_target_pairs={{0,2},{1,3},{2,0},{3,1},{4,6},{5,7},{6,4},{7,5},{8,10},{9,11},{10,... | collective-permute-start | bytes 6291464 | tf_op jit(solution)/shard_map/ppermute | solution.py:218
  131.0 50.7 %collective-permute-start.2 = (bf16[512,2048]{1,0:T(8,128)(2,1)}, bf16[512,2048]{1,0:T(8,128)(2,1)}, u32[]{:S(2)}, u32[]{:S(2)}) collective-permute-start(bf16[512,2048]{1,0:T(8,128)(2,1)} %add_convert_fusion.9), channel_id=1, source_target_pairs={{0,1},{1,0},{2,3},{3,2},{4,5},{5,4},{6,7},{7,6},{8,9},{9,8},{10,11... | collective-permute-start | bytes 6291464 | tf_op jit(solution)/shard_map/ppermute | solution.py:220
  280.0 50.5 %collective-permute-start.101 = (bf16[128,1536]{0,1:T(8,128)(2,1)}, bf16[128,1536]{0,1:T(8,128)(2,1)}, u32[]{:S(2)}, u32[]{:S(2)}) collective-permute-start(bf16[128,1536]{0,1:T(8,128)(2,1)} %bitcast.742), channel_id=1, source_target_pairs={{0,8},{8,16},{16,24},{24,28},{28,20},{20,12},{12,4},{4,0},{1,9},{9... | collective-permute-start | bytes 1179656 | tf_op jit(solution)/shard_map/ppermute | solution.py:244
  283.5 48.9 %collective-permute-start.108 = (bf16[128,1536]{0,1:T(8,128)(2,1)}, bf16[128,1536]{0,1:T(8,128)(2,1)}, u32[]{:S(2)}, u32[]{:S(2)}) collective-permute-start(bf16[128,1536]{0,1:T(8,128)(2,1)} %bitcast.743), channel_id=1, source_target_pairs={{8,0},{16,8},{24,16},{28,24},{20,28},{12,20},{4,12},{0,4},{9,1},{1... | collective-permute-start | bytes 1179656 | tf_op jit(solution)/shard_map/ppermute | solution.py:245
  293.8 39.8 %collective-permute-start.87 = (bf16[128,1536]{1,0:T(8,128)(2,1)}, bf16[128,1536]{1,0:T(8,128)(2,1)}, u32[]{:S(2)}, u32[]{:S(2)}) collective-permute-start(bf16[128,1536]{1,0:T(8,128)(2,1)} %get-tuple-element.140), channel_id=1, source_target_pairs={{0,8},{8,16},{16,24},{24,28},{28,20},{20,12},{12,4},{4,0},{1,9},{9... | collective-permute-start | bytes 1179656 | tf_op jit(solution)/shard_map/ppermute | solution.py:244
  295.7 63.0 %collective-permute-start.94 = (bf16[128,1536]{1,0:T(8,128)(2,1)}, bf16[128,1536]{1,0:T(8,128)(2,1)S(1)}, u32[]{:S(2)}, u32[]{:S(2)}) collective-permute-start(bf16[128,1536]{1,0:T(8,128)(2,1)} %get-tuple-element.141), channel_id=1, source_target_pairs={{8,0},{16,8},{24,16},{28,24},{20,28},{12,20},{4,12},{0,4},{9,1},{1... | collective-permute-start | bytes 1179656 | tf_op jit(solution)/shard_map/ppermute | solution.py:245
  299.4 36.4 %collective-permute-start.73 = (bf16[128,1536]{1,0:T(8,128)(2,1)}, bf16[128,1536]{1,0:T(8,128)(2,1)}, u32[]{:S(2)}, u32[]{:S(2)}) collective-permute-start(bf16[128,1536]{1,0:T(8,128)(2,1)} %get-tuple-element.154), channel_id=1, source_target_pairs={{0,8},{8,16},{16,24},{24,28},{28,20},{20,12},{12,4},{4,0},{1,9},{9... | collective-permute-start | bytes 1179656 | tf_op jit(solution)/shard_map/ppermute | solution.py:244
  330.4 41.6 %collective-permute-start.80 = (bf16[128,1536]{1,0:T(8,128)(2,1)S(1)}, bf16[128,1536]{1,0:T(8,128)(2,1)S(1)}, u32[]{:S(2)}, u32[]{:S(2)}) collective-permute-start(bf16[128,1536]{1,0:T(8,128)(2,1)S(1)} %copy-done.66), channel_id=1, source_target_pairs={{8,0},{16,8},{24,16},{28,24},{20,28},{12,20},{4,12},{0,4},{9,1},{1... | collective-permute-start | bytes 1179656 | tf_op jit(solution)/shard_map/ppermute | solution.py:245
  332.4 124.1 %collective-permute-start.3 = (bf16[512,2048]{1,0:T(8,128)(2,1)S(1)}, bf16[512,2048]{1,0:T(8,128)(2,1)S(1)}, u32[]{:S(2)}, u32[]{:S(2)}) collective-permute-start(bf16[512,2048]{1,0:T(8,128)(2,1)S(1)} %copy-done.55), channel_id=1, source_target_pairs={{0,1},{1,0},{2,3},{3,2},{4,5},{5,4},{6,7},{7,6},{8,9},{9,8},{10,11... | collective-permute-start | bytes 6291464 | tf_op jit(solution)/shard_map/ppermute | solution.py:216
  333.6 106.0 %collective-permute-start.6 = (bf16[512,2048]{1,0:T(8,128)(2,1)S(1)}, bf16[512,2048]{1,0:T(8,128)(2,1)S(1)}, u32[]{:S(2)}, u32[]{:S(2)}) collective-permute-start(bf16[512,2048]{1,0:T(8,128)(2,1)S(1)} %constant_dynamic-slice_fusion.13), channel_id=1, source_target_pairs={{0,1},{1,0},{2,3},{3,2},{4,5},{5,4},{6,7},{7,6},{8,9},{9,8},{10,11... | collective-permute-start | bytes 6291464 | tf_op jit(solution)/shard_map/ppermute | solution.py:216
  358.6 18.6 %collective-permute-start.74 = (bf16[128,1536]{1,0:T(8,128)(2,1)S(1)}, bf16[128,1536]{1,0:T(8,128)(2,1)S(1)}, u32[]{:S(2)}, u32[]{:S(2)}) collective-permute-start(bf16[128,1536]{1,0:T(8,128)(2,1)S(1)} %fusion.100), channel_id=1, source_target_pairs={{0,8},{8,16},{16,24},{24,28},{28,20},{20,12},{12,4},{4,0},{1,9},{9... | collective-permute-start | bytes 1179656 | tf_op jit(solution)/shard_map/ppermute | solution.py:244
  368.8 16.9 %collective-permute-start.103 = (bf16[128,1536]{0,1:T(8,128)(2,1)S(1)}, bf16[128,1536]{0,1:T(8,128)(2,1)S(1)}, u32[]{:S(2)}, u32[]{:S(2)}) collective-permute-start(bf16[128,1536]{0,1:T(8,128)(2,1)S(1)} %add_convert_fusion.21), channel_id=1, source_target_pairs={{0,8},{8,16},{16,24},{24,28},{28,20},{20,12},{12,4},{4,0},{1,9},{9... | collective-permute-start | bytes 1179656 | tf_op jit(solution)/shard_map/ppermute | solution.py:244
  372.1 14.8 %collective-permute-start.110 = (bf16[128,1536]{0,1:T(8,128)(2,1)S(1)}, bf16[128,1536]{0,1:T(8,128)(2,1)S(1)}, u32[]{:S(2)}, u32[]{:S(2)}) collective-permute-start(bf16[128,1536]{0,1:T(8,128)(2,1)S(1)} %add_convert_fusion.15), channel_id=1, source_target_pairs={{8,0},{16,8},{24,16},{28,24},{20,28},{12,20},{4,12},{0,4},{9,1},{1... | collective-permute-start | bytes 1179656 | tf_op jit(solution)/shard_map/ppermute | solution.py:245
  377.2 16.9 %collective-permute-start.89 = (bf16[128,1536]{1,0:T(8,128)(2,1)S(1)}, bf16[128,1536]{1,0:T(8,128)(2,1)S(1)}, u32[]{:S(2)}, u32[]{:S(2)}) collective-permute-start(bf16[128,1536]{1,0:T(8,128)(2,1)S(1)} %get-tuple-element.138), channel_id=1, source_target_pairs={{0,8},{8,16},{16,24},{24,28},{28,20},{20,12},{12,4},{4,0},{1,9},{9... | collective-permute-start | bytes 1179656 | tf_op jit(solution)/shard_map/ppermute | solution.py:244
  386.9 15.6 %collective-permute-start.75 = (bf16[128,1536]{1,0:T(8,128)(2,1)S(1)}, bf16[128,1536]{1,0:T(8,128)(2,1)S(1)}, u32[]{:S(2)}, u32[]{:S(2)}) collective-permute-start(bf16[128,1536]{1,0:T(8,128)(2,1)S(1)} %get-tuple-element.152), channel_id=1, source_target_pairs={{0,8},{8,16},{16,24},{24,28},{28,20},{20,12},{12,4},{4,0},{1,9},{9... | collective-permute-start | bytes 1179656 | tf_op jit(solution)/shard_map/ppermute | solution.py:244
  395.6 15.3 %collective-permute-start.104 = (bf16[128,1536]{0,1:T(8,128)(2,1)S(1)}, bf16[128,1536]{0,1:T(8,128)(2,1)S(1)}, u32[]{:S(2)}, u32[]{:S(2)}) collective-permute-start(bf16[128,1536]{0,1:T(8,128)(2,1)S(1)} %add_convert_fusion.20), channel_id=1, source_target_pairs={{0,8},{8,16},{16,24},{24,28},{28,20},{20,12},{12,4},{4,0},{1,9},{9... | collective-permute-start | bytes 1179656 | tf_op jit(solution)/shard_map/ppermute | solution.py:244
  404.0 15.3 %collective-permute-start.90 = (bf16[128,1536]{1,0:T(8,128)(2,1)S(1)}, bf16[128,1536]{1,0:T(8,128)(2,1)S(1)}, u32[]{:S(2)}, u32[]{:S(2)}) collective-permute-start(bf16[128,1536]{1,0:T(8,128)(2,1)S(1)} %get-tuple-element.136), channel_id=1, source_target_pairs={{0,8},{8,16},{16,24},{24,28},{28,20},{20,12},{12,4},{4,0},{1,9},{9... | collective-permute-start | bytes 1179656 | tf_op jit(solution)/shard_map/ppermute | solution.py:244
  412.5 15.3 %collective-permute-start.76 = (bf16[128,1536]{1,0:T(8,128)(2,1)S(1)}, bf16[128,1536]{1,0:T(8,128)(2,1)S(1)}, u32[]{:S(2)}, u32[]{:S(2)}) collective-permute-start(bf16[128,1536]{1,0:T(8,128)(2,1)S(1)} %get-tuple-element.150), channel_id=1, source_target_pairs={{0,8},{8,16},{16,24},{24,28},{28,20},{20,12},{12,4},{4,0},{1,9},{9... | collective-permute-start | bytes 1179656 | tf_op jit(solution)/shard_map/ppermute | solution.py:244
  420.9 15.3 %collective-permute-start.105 = (bf16[128,1536]{0,1:T(8,128)(2,1)S(1)}, bf16[128,1536]{0,1:T(8,128)(2,1)S(1)}, u32[]{:S(2)}, u32[]{:S(2)}) collective-permute-start(bf16[128,1536]{0,1:T(8,128)(2,1)S(1)} %add_convert_fusion.19), channel_id=1, source_target_pairs={{0,8},{8,16},{16,24},{24,28},{28,20},{20,12},{12,4},{4,0},{1,9},{9... | collective-permute-start | bytes 1179656 | tf_op jit(solution)/shard_map/ppermute | solution.py:244
  429.3 15.3 %collective-permute-start.91 = (bf16[128,1536]{1,0:T(8,128)(2,1)S(1)}, bf16[128,1536]{1,0:T(8,128)(2,1)S(1)}, u32[]{:S(2)}, u32[]{:S(2)}) collective-permute-start(bf16[128,1536]{1,0:T(8,128)(2,1)S(1)} %get-tuple-element.134), channel_id=1, source_target_pairs={{0,8},{8,16},{16,24},{24,28},{28,20},{20,12},{12,4},{4,0},{1,9},{9... | collective-permute-start | bytes 1179656 | tf_op jit(solution)/shard_map/ppermute | solution.py:244
  437.7 15.3 %collective-permute-start.77 = (bf16[128,1536]{1,0:T(8,128)(2,1)S(1)}, bf16[128,1536]{1,0:T(8,128)(2,1)S(1)}, u32[]{:S(2)}, u32[]{:S(2)}) collective-permute-start(bf16[128,1536]{1,0:T(8,128)(2,1)S(1)} %get-tuple-element.148), channel_id=1, source_target_pairs={{0,8},{8,16},{16,24},{24,28},{28,20},{20,12},{12,4},{4,0},{1,9},{9... | collective-permute-start | bytes 1179656 | tf_op jit(solution)/shard_map/ppermute | solution.py:244
  439.6 15.0 %collective-permute-start.83 = (bf16[128,1536]{1,0:T(8,128)(2,1)S(1)}, bf16[128,1536]{1,0:T(8,128)(2,1)S(1)}, u32[]{:S(2)}, u32[]{:S(2)}) collective-permute-start(bf16[128,1536]{1,0:T(8,128)(2,1)S(1)} %get-tuple-element.149), channel_id=1, source_target_pairs={{8,0},{16,8},{24,16},{28,24},{20,28},{12,20},{4,12},{0,4},{9,1},{1... | collective-permute-start | bytes 1179656 | tf_op jit(solution)/shard_map/ppermute | solution.py:245
  444.6 16.9 %collective-permute-start.106 = (bf16[128,1536]{0,1:T(8,128)(2,1)S(1)}, bf16[128,1536]{0,1:T(8,128)(2,1)S(1)}, u32[]{:S(2)}, u32[]{:S(2)}) collective-permute-start(bf16[128,1536]{0,1:T(8,128)(2,1)S(1)} %add_convert_fusion.18), channel_id=1, source_target_pairs={{0,8},{8,16},{16,24},{24,28},{28,20},{20,12},{12,4},{4,0},{1,9},{9... | collective-permute-start | bytes 1179656 | tf_op jit(solution)/shard_map/ppermute | solution.py:244
  448.2 48.5 %collective-permute-start.7 = (bf16[512,2048]{1,0:T(8,128)(2,1)S(1)}, bf16[512,2048]{1,0:T(8,128)(2,1)S(1)}, u32[]{:S(2)}, u32[]{:S(2)}) collective-permute-start(bf16[512,2048]{1,0:T(8,128)(2,1)S(1)} %add_convert_fusion.6), channel_id=1, source_target_pairs={{0,2},{1,3},{2,0},{3,1},{4,6},{5,7},{6,4},{7,5},{8,10},{9,11},{10,... | collective-permute-start | bytes 6291464 | tf_op jit(solution)/shard_map/ppermute | solution.py:218
  454.6 44.1 %collective-permute-start.92 = (bf16[128,1536]{1,0:T(8,128)(2,1)S(1)}, bf16[128,1536]{1,0:T(8,128)(2,1)S(1)}, u32[]{:S(2)}, u32[]{:S(2)}) collective-permute-start(bf16[128,1536]{1,0:T(8,128)(2,1)S(1)} %get-tuple-element.132), channel_id=1, source_target_pairs={{0,8},{8,16},{16,24},{24,28},{28,20},{20,12},{12,4},{4,0},{1,9},{9... | collective-permute-start | bytes 1179656 | tf_op jit(solution)/shard_map/ppermute | solution.py:244
  456.5 43.1 %collective-permute-start.98 = (bf16[128,1536]{1,0:T(8,128)(2,1)S(1)}, bf16[128,1536]{1,0:T(8,128)(2,1)S(1)}, u32[]{:S(2)}, u32[]{:S(2)}) collective-permute-start(bf16[128,1536]{1,0:T(8,128)(2,1)S(1)} %get-tuple-element.133), channel_id=1, source_target_pairs={{8,0},{16,8},{24,16},{28,24},{20,28},{12,20},{4,12},{0,4},{9,1},{1... | collective-permute-start | bytes 1179656 | tf_op jit(solution)/shard_map/ppermute | solution.py:245
  461.5 39.8 %collective-permute-start.78 = (bf16[128,1536]{1,0:T(8,128)(2,1)S(1)}, bf16[128,1536]{1,0:T(8,128)(2,1)S(1)}, u32[]{:S(2)}, u32[]{:S(2)}) collective-permute-start(bf16[128,1536]{1,0:T(8,128)(2,1)S(1)} %get-tuple-element.146), channel_id=1, source_target_pairs={{0,8},{8,16},{16,24},{24,28},{28,20},{20,12},{12,4},{4,0},{1,9},{9... | collective-permute-start | bytes 1179656 | tf_op jit(solution)/shard_map/ppermute | solution.py:244
  465.0 68.0 %collective-permute-start.4 = (bf16[512,2048]{1,0:T(8,128)(2,1)S(1)}, bf16[512,2048]{1,0:T(8,128)(2,1)S(1)}, u32[]{:S(2)}, u32[]{:S(2)}) collective-permute-start(bf16[512,2048]{1,0:T(8,128)(2,1)S(1)} %add_convert_fusion.8), channel_id=1, source_target_pairs={{0,2},{1,3},{2,0},{3,1},{4,6},{5,7},{6,4},{7,5},{8,10},{9,11},{10,... | collective-permute-start | bytes 6291464 | tf_op jit(solution)/shard_map/ppermute | solution.py:218
  498.7 127.8 %collective-permute-start.107 = (bf16[128,1536]{0,1:T(8,128)(2,1)}, bf16[128,1536]{0,1:T(8,128)(2,1)}, u32[]{:S(2)}, u32[]{:S(2)}) collective-permute-start(bf16[128,1536]{0,1:T(8,128)(2,1)} %add_convert_fusion.17), channel_id=1, source_target_pairs={{0,8},{8,16},{16,24},{24,28},{28,20},{20,12},{12,4},{4,0},{1,9},{9... | collective-permute-start | bytes 1179656 | tf_op jit(solution)/shard_map/ppermute | solution.py:244
  499.7 43.7 %collective-permute-start.8 = (bf16[512,2048]{1,0:T(8,128)(2,1)S(1)}, bf16[512,2048]{1,0:T(8,128)(2,1)S(1)}, u32[]{:S(2)}, u32[]{:S(2)}) collective-permute-start(bf16[512,2048]{1,0:T(8,128)(2,1)S(1)} %add_convert_fusion.5), channel_id=1, source_target_pairs={{0,1},{1,0},{2,3},{3,2},{4,5},{5,4},{6,7},{7,6},{8,9},{9,8},{10,11... | collective-permute-start | bytes 6291464 | tf_op jit(solution)/shard_map/ppermute | solution.py:220
  501.2 127.3 %collective-permute-start.114 = (bf16[128,1536]{0,1:T(8,128)(2,1)}, bf16[128,1536]{0,1:T(8,128)(2,1)}, u32[]{:S(2)}, u32[]{:S(2)}) collective-permute-start(bf16[128,1536]{0,1:T(8,128)(2,1)} %add_convert_fusion.11), channel_id=1, source_target_pairs={{8,0},{16,8},{24,16},{28,24},{20,28},{12,20},{4,12},{0,4},{9,1},{1... | collective-permute-start | bytes 1179656 | tf_op jit(solution)/shard_map/ppermute | solution.py:245
  504.4 29.8 %collective-permute-start.93 = (bf16[128,1536]{1,0:T(8,128)(2,1)S(1)}, bf16[128,1536]{1,0:T(8,128)(2,1)S(1)}, u32[]{:S(2)}, u32[]{:S(2)}) collective-permute-start(bf16[128,1536]{1,0:T(8,128)(2,1)S(1)} %get-tuple-element.130), channel_id=1, source_target_pairs={{0,8},{8,16},{16,24},{24,28},{28,20},{20,12},{12,4},{4,0},{1,9},{9... | collective-permute-start | bytes 1179656 | tf_op jit(solution)/shard_map/ppermute | solution.py:244
  534.3 87.0 %collective-permute-start.79 = (bf16[128,1536]{1,0:T(8,128)(2,1)}, bf16[128,1536]{1,0:T(8,128)(2,1)}, u32[]{:S(2)}, u32[]{:S(2)}) collective-permute-start(bf16[128,1536]{1,0:T(8,128)(2,1)} %get-tuple-element.144), channel_id=1, source_target_pairs={{0,8},{8,16},{16,24},{24,28},{28,20},{20,12},{12,4},{4,0},{1,9},{9... | collective-permute-start | bytes 1179656 | tf_op jit(solution)/shard_map/ppermute | solution.py:244
  543.4 78.3 %collective-permute-start.85 = (bf16[128,1536]{1,0:T(8,128)(2,1)}, bf16[128,1536]{1,0:T(8,128)(2,1)}, u32[]{:S(2)}, u32[]{:S(2)}) collective-permute-start(bf16[128,1536]{1,0:T(8,128)(2,1)} %get-tuple-element.145), channel_id=1, source_target_pairs={{8,0},{16,8},{24,16},{28,24},{20,28},{12,20},{4,12},{0,4},{9,1},{1... | collective-permute-start | bytes 1179656 | tf_op jit(solution)/shard_map/ppermute | solution.py:245
  550.5 104.7 %collective-permute-start.100 = (bf16[128,1536]{1,0:T(8,128)(2,1)}, bf16[128,1536]{1,0:T(8,128)(2,1)}, u32[]{:S(2)}, u32[]{:S(2)}) collective-permute-start(bf16[128,1536]{1,0:T(8,128)(2,1)} %get-tuple-element.129), channel_id=1, source_target_pairs={{8,0},{16,8},{24,16},{28,24},{20,28},{12,20},{4,12},{0,4},{9,1},{1... | collective-permute-start | bytes 1179656 | tf_op jit(solution)/shard_map/ppermute | solution.py:245
  621.3 22.8 %collective-permute-start.9 = (bf16[512,2048]{1,0:T(8,128)(2,1)}, bf16[512,2048]{1,0:T(8,128)(2,1)}, u32[]{:S(2)}, u32[]{:S(2)}) collective-permute-start(bf16[512,2048]{1,0:T(8,128)(2,1)} %constant_dynamic-slice_fusion.10), channel_id=1, source_target_pairs={{0,1},{1,0},{2,3},{3,2},{4,5},{5,4},{6,7},{7,6},{8,9},{9,8},{10,11... | collective-permute-start | bytes 6291464 | tf_op jit(solution)/shard_map/ppermute | solution.py:216
  624.9 35.9 %collective-permute-start.86 = (bf16[128,1536]{1,0:T(8,128)(2,1)}, bf16[128,1536]{1,0:T(8,128)(2,1)}, u32[]{:S(2)}, u32[]{:S(2)}) collective-permute-start(bf16[128,1536]{1,0:T(8,128)(2,1)} %get-tuple-element.143), channel_id=1, source_target_pairs={{8,0},{16,8},{24,16},{28,24},{20,28},{12,20},{4,12},{0,4},{9,1},{1... | collective-permute-start | bytes 1179656 | tf_op jit(solution)/shard_map/ppermute | solution.py:245
  646.4 47.2 %collective-permute-start.10 = (bf16[512,2048]{1,0:T(8,128)(2,1)S(1)}, bf16[512,2048]{1,0:T(8,128)(2,1)S(1)}, u32[]{:S(2)}, u32[]{:S(2)}) collective-permute-start(bf16[512,2048]{1,0:T(8,128)(2,1)S(1)} %add_convert_fusion.4), channel_id=1, source_target_pairs={{0,2},{1,3},{2,0},{3,1},{4,6},{5,7},{6,4},{7,5},{8,10},{9,11},{10,... | collective-permute-start | bytes 6291464 | tf_op jit(solution)/shard_map/ppermute | solution.py:218
  665.6 31.4 %collective-permute-start.63 = (bf16[128,512]{1,0:T(8,128)(2,1)S(1)}, bf16[128,512]{1,0:T(8,128)(2,1)S(1)}, u32[]{:S(2)}, u32[]{:S(2)}) collective-permute-start(bf16[128,512]{1,0:T(8,128)(2,1)S(1)} %get-tuple-element.170), channel_id=1, source_target_pairs={{0,8},{8,16},{16,24},{24,28},{28,20},{20,12},{12,4},{4,0},{1,9},{9... | collective-permute-start | bytes 393224 | tf_op jit(solution)/shard_map/ppermute | solution.py:244
  667.2 29.7 %collective-permute-start.69 = (bf16[128,512]{1,0:T(8,128)(2,1)S(1)}, bf16[128,512]{1,0:T(8,128)(2,1)S(1)}, u32[]{:S(2)}, u32[]{:S(2)}) collective-permute-start(bf16[128,512]{1,0:T(8,128)(2,1)S(1)} %get-tuple-element.171), channel_id=1, source_target_pairs={{8,0},{16,8},{24,16},{28,24},{20,28},{12,20},{4,12},{0,4},{9,1},{1... | collective-permute-start | bytes 393224 | tf_op jit(solution)/shard_map/ppermute | solution.py:245
  695.7 20.3 %collective-permute-start.11 = (bf16[512,2048]{1,0:T(8,128)(2,1)}, bf16[512,2048]{1,0:T(8,128)(2,1)}, u32[]{:S(2)}, u32[]{:S(2)}) collective-permute-start(bf16[512,2048]{1,0:T(8,128)(2,1)} %add_convert_fusion.3), channel_id=1, source_target_pairs={{0,1},{1,0},{2,3},{3,2},{4,5},{5,4},{6,7},{7,6},{8,9},{9,8},{10,11... | collective-permute-start | bytes 6291464 | tf_op jit(solution)/shard_map/ppermute | solution.py:220
  749.1 22.1 %collective-permute-start.52 = (bf16[128,256]{1,0:T(8,128)(2,1)S(1)}, bf16[128,256]{1,0:T(8,128)(2,1)S(1)}, u32[]{:S(2)}, u32[]{:S(2)}) collective-permute-start(bf16[128,256]{1,0:T(8,128)(2,1)S(1)} %get-tuple-element.213), channel_id=1, source_target_pairs={{8,0},{16,8},{24,16},{28,24},{20,28},{12,20},{4,12},{0,4},{9,1},{1... | collective-permute-start | bytes 196616 | tf_op jit(solution)/shard_map/ppermute | solution.py:245
  752.8 22.1 %collective-permute-start.38 = (bf16[128,256]{1,0:T(8,128)(2,1)S(1)}, bf16[128,256]{1,0:T(8,128)(2,1)S(1)}, u32[]{:S(2)}, u32[]{:S(2)}) collective-permute-start(bf16[128,256]{1,0:T(8,128)(2,1)S(1)} %get-tuple-element.227), channel_id=1, source_target_pairs={{8,0},{16,8},{24,16},{28,24},{20,28},{12,20},{4,12},{0,4},{9,1},{1... | collective-permute-start | bytes 196616 | tf_op jit(solution)/shard_map/ppermute | solution.py:245
  757.2 20.0 %collective-permute-start.17 = (bf16[128,512]{1,0:T(8,128)(2,1)S(1)}, bf16[128,512]{1,0:T(8,128)(2,1)S(1)}, u32[]{:S(2)}, u32[]{:S(2)}) collective-permute-start(bf16[128,512]{1,0:T(8,128)(2,1)S(1)} %get-tuple-element.190), channel_id=1, source_target_pairs={{0,8},{8,16},{16,24},{24,28},{28,20},{20,12},{12,4},{4,0},{1,9},{9... | collective-permute-start | bytes 393224 | tf_op jit(solution)/shard_map/ppermute | solution.py:244
  762.9 28.2 %collective-permute-start.24 = (bf16[128,512]{1,0:T(8,128)(2,1)S(1)}, bf16[128,512]{1,0:T(8,128)(2,1)S(1)}, u32[]{:S(2)}, u32[]{:S(2)}) collective-permute-start(bf16[128,512]{1,0:T(8,128)(2,1)S(1)} %get-tuple-element.191), channel_id=1, source_target_pairs={{8,0},{16,8},{24,16},{28,24},{20,28},{12,20},{4,12},{0,4},{9,1},{1... | collective-permute-start | bytes 393224 | tf_op jit(solution)/shard_map/ppermute | solution.py:245
  778.3 13.3 %collective-permute-start.18 = (bf16[128,512]{1,0:T(8,128)(2,1)S(1)}, bf16[128,512]{1,0:T(8,128)(2,1)S(1)}, u32[]{:S(2)}, u32[]{:S(2)}) collective-permute-start(bf16[128,512]{1,0:T(8,128)(2,1)S(1)} %fusion.173), channel_id=1, source_target_pairs={{0,8},{8,16},{16,24},{24,28},{28,20},{20,12},{12,4},{4,0},{1,9},{9... | collective-permute-start | bytes 393224 | tf_op jit(solution)/shard_map/ppermute | solution.py:244
  791.7 13.1 %collective-permute-start.19 = (bf16[128,512]{1,0:T(8,128)(2,1)S(1)}, bf16[128,512]{1,0:T(8,128)(2,1)S(1)}, u32[]{:S(2)}, u32[]{:S(2)}) collective-permute-start(bf16[128,512]{1,0:T(8,128)(2,1)S(1)} %get-tuple-element.188), channel_id=1, source_target_pairs={{0,8},{8,16},{16,24},{24,28},{28,20},{20,12},{12,4},{4,0},{1,9},{9... | collective-permute-start | bytes 393224 | tf_op jit(solution)/shard_map/ppermute | solution.py:244
  808.0 13.6 %collective-permute-start.58 = (bf16[128,256]{1,0:T(8,128)(2,1)S(1)}, bf16[128,256]{1,0:T(8,128)(2,1)S(1)}, u32[]{:S(2)}, u32[]{:S(2)}) collective-permute-start(bf16[128,256]{1,0:T(8,128)(2,1)S(1)} %get-tuple-element.201), channel_id=1, source_target_pairs={{8,0},{16,8},{24,16},{28,24},{20,28},{12,20},{4,12},{0,4},{9,1},{1... | collective-permute-start | bytes 196616 | tf_op jit(solution)/shard_map/ppermute | solution.py:245
  (176 other events, 1752.8 us)

commit v2 on v1

--- a/solution.py
+++ b/solution.py
@@ -223,31 +223,10 @@
         return jnp.concatenate([first, second], 0)
 
     def dp_rs(self, grads):
-        n = self.n_dp
-        me = lax.axis_index("dp")
-        pos = jnp.array(self.pos, jnp.int32)[me]
-        ring = jnp.array(self.ring, jnp.int32)
-        blocks = [g.reshape(n, 2, g.shape[0] // n // 2, g.shape[1]) for g in grads]
-        acc_a = acc_b = None
-        for s in range(n - 1):
-            ia = ring[(pos - 1 - s) % n]
-            ib = ring[(pos + 1 + s) % n]
-            own_a = [lax.dynamic_index_in_dim(b, ia, 0, keepdims=False)[0] for b in blocks]
-            own_b = [lax.dynamic_index_in_dim(b, ib, 0, keepdims=False)[1] for b in blocks]
-            if acc_a is None:
-                send_a, send_b = own_a, own_b
-            else:
-                send_a = [x + y for x, y in zip(acc_a, own_a)]
-                send_b = [x + y for x, y in zip(acc_b, own_b)]
-            send_a = [x.astype(jnp.bfloat16) for x in send_a]
-            send_b = [x.astype(jnp.bfloat16) for x in send_b]
-            acc_a = [x.astype(jnp.float32) for x in lax.ppermute(send_a, "dp", self.cw)]
-            acc_b = [x.astype(jnp.float32) for x in lax.ppermute(send_b, "dp", self.ccw)]
-        out = []
-        for b, xa, xb in zip(blocks, acc_a, acc_b):
-            mine = lax.dynamic_index_in_dim(b, me, 0, keepdims=False)
-            out.append(jnp.concatenate([xa + mine[0], xb + mine[1]], 0))
-        return out
+        ring = Ring(self, grads)
+        for _ in range(ring.steps):
+            ring.step()
+        return ring.result()
 
     def all_sum(self, x):
         for axis, size in (("tensor", self.n_tp), ("dp", self.n_dp)):
@@ -259,6 +238,46 @@
                 x = x + lax.ppermute(x, axis, [(i, i ^ bit) for i in range(size)])
                 bit *= 2
         return x
+
+
+class Ring:
+    def __init__(self, plan, grads):
+        self.plan = plan
+        self.n = n = plan.n_dp
+        self.me = lax.axis_index("dp")
+        self.pos = jnp.array(plan.pos, jnp.int32)[self.me]
+        self.order = jnp.array(plan.ring, jnp.int32)
+        self.widths = [g.shape[1] for g in grads]
+        self.blocks = [g.reshape(n, 2, g.shape[0] // n // 2, g.shape[1]) for g in grads]
+        self.steps = n - 1
+        self.done = 0
+        self.state = None
+
+    def piece(self, index, side):
+        parts = [lax.dynamic_index_in_dim(b, index, 0, keepdims=False)[side] for b in self.blocks]
+        return parts[0] if len(parts) == 1 else jnp.concatenate(parts, 1)
+
+    def step(self):
+        n, s = self.n, self.done
+        own_a = self.piece(self.order[(self.pos - 1 - s) % n], 0)
+        own_b = self.piece(self.order[(self.pos + 1 + s) % n], 1)
+        if self.state is None:
+            send_a, send_b = own_a, own_b
+        else:
+            send_a, send_b = self.state[0] + own_a, self.state[1] + own_b
+        got_a = lax.ppermute(send_a.astype(jnp.bfloat16), "dp", self.plan.cw)
+        got_b = lax.ppermute(send_b.astype(jnp.bfloat16), "dp", self.plan.ccw)
+        self.state = (got_a.astype(jnp.float32), got_b.astype(jnp.float32))
+        self.done += 1
+
+    def result(self):
+        acc_a, acc_b = self.state
+        total = jnp.concatenate([acc_a + self.piece(self.me, 0), acc_b + self.piece(self.me, 1)], 0)
+        out, start = [], 0
+        for w in self.widths:
+            out.append(total[:, start : start + w])
+            start += w
+        return out
 
 
 def make_on_device(plan):
@@ -307,29 +326,65 @@
         upper_grad = upper_grad.astype(jnp.bfloat16)
         gate_w_grad = inner_rows(normed_mid, gate_grad)
         up_w_grad = inner_rows(normed_mid, upper_grad)
-        mlp_sums = plan.dp_rs([down_grad_t, gate_w_grad, up_w_grad])
         mid_part = (outer_cols(gate_grad, w_gate) + outer_cols(upper_grad, w_up)).astype(
             jnp.bfloat16
         )
-        mid_grad = plan.tp_sum(mid_part).astype(jnp.float32)
+        mid_sum = plan.tp_sum(mid_part)
+        mid_sum, down_grad_t, gate_w_grad, up_w_grad = lax.optimization_barrier(
+            (mid_sum, down_grad_t, gate_w_grad, up_w_grad)
+        )
+        mid_grad = mid_sum.astype(jnp.float32)
         resid_grad = cotangent.astype(jnp.float32) + norm_back(resid, mlp_gain, mid_grad)
         mlp_gain_part = gain_term(resid_rows, lax.dynamic_slice_in_dim(mid_grad, offset, share, 0))
         resid_low = resid_grad.astype(jnp.bfloat16)
         out_w_grad_t = inner_rows(resid_low, attended)
         attended_grad = outer_cols(resid_low, w_out).astype(jnp.bfloat16)
-        q_grad, k_grad, v_grad, qg_part, kg_part = attend_back(
-            attended_grad, q_raw, k_raw, query_gain, key_gain, queries, keys_rot, values, logsum, seqs
-        )
+        big = Ring(plan, [down_grad_t, gate_w_grad, up_w_grad, out_w_grad_t])
+        big.step()
+        chunks = 4 if seqs % 4 == 0 else 1
+        per = seqs // chunks
+        rows = per * LEN
+        plan_steps = [big.steps * (c + 1) // (chunks + 1) for c in range(chunks)]
+        q_parts, k_parts, v_parts, in_parts = [], [], [], []
+        qg_part = kg_part = 0.0
+        for c in range(chunks):
+            span = slice(c * rows, (c + 1) * rows)
+            seq_span = slice(c * per, (c + 1) * per)
+            qc, kc, vc, qgc, kgc = attend_back(
+                attended_grad[span],
+                q_raw[span],
+                k_raw[span],
+                query_gain,
+                key_gain,
+                queries[seq_span],
+                keys_rot[seq_span],
+                values[seq_span],
+                logsum[seq_span],
+                per,
+            )
+            in_c = (
+                outer_cols(qc, w_query) + outer_cols(kc, key_matrix) + outer_cols(vc, value_matrix)
+            ).astype(jnp.bfloat16)
+            while big.done < plan_steps[c]:
+                big.step()
+            big.state, qc, kc, vc, in_c = lax.optimization_barrier((big.state, qc, kc, vc, in_c))
+            in_parts.append(plan.tp_sum(in_c))
+            q_parts.append(qc)
+            k_parts.append(kc)
+            v_parts.append(vc)
+            qg_part = qg_part + qgc
+            kg_part = kg_part + kgc
+        q_grad = jnp.concatenate(q_parts, 0)
+        k_grad = jnp.concatenate(k_parts, 0)
+        v_grad = jnp.concatenate(v_parts, 0)
         query_w_grad = inner_rows(normed_in, q_grad)
         key_w_grad = inner_rows(normed_in, k_grad)
         value_w_grad = inner_rows(normed_in, v_grad)
-        attn_sums = plan.dp_rs([out_w_grad_t, query_w_grad, key_w_grad, value_w_grad])
-        in_part = (
-            outer_cols(q_grad, w_query)
-            + outer_cols(k_grad, key_matrix)
-            + outer_cols(v_grad, value_matrix)
-        ).astype(jnp.bfloat16)
-        in_grad = plan.tp_sum(in_part).astype(jnp.float32)
+        while big.done < big.steps:
+            big.step()
+        down_sum, gate_sum, up_sum, out_sum = big.result()
+        query_sum, key_sum, value_sum = plan.dp_rs([query_w_grad, key_w_grad, value_w_grad])
+        in_grad = jnp.concatenate(in_parts, 0).astype(jnp.float32)
         input_grad = resid_grad + norm_back(stream, attn_gain, in_grad)
         attn_gain_part = gain_term(stream_rows, lax.dynamic_slice_in_dim(in_grad, offset, share, 0))
         gains = plan.all_sum(jnp.concatenate([attn_gain_part, mlp_gain_part, qg_part, kg_part]))
@@ -339,8 +394,6 @@
         mlp_gain_grad = gains[width : 2 * width]
         query_gain_grad = gains[2 * width : 2 * width + head]
         key_gain_grad = gains[2 * width + head :]
-        down_sum, gate_sum, up_sum = mlp_sums
-        out_sum, query_sum, key_sum, value_sum = attn_sums
         return (
             mixed,
             input_grad,

time: 847 us -> 986 us (1.16)
  local copies, waits for them, and re-layouts: 105 us -> 272 us
  starting transfers between devices: 124 us -> 47.6 us
  matrix products: 167 us -> 192 us
  other arithmetic: 140 us -> 161 us
    unnamed x221 -> x522, local copies, waits for them, and re-layouts: 15.7 us -> 94.8 us
    ppermute x98 -> x28, starting transfers between devices: 109 us -> 33.9 us  [the longest x14 22.8 us: step(): got_a = lax.ppermute(send_a.astype(jnp.bfloat16), 'dp', self.plan.cw)]
    slice x2 -> x22, local copies, waits for them, and re-layouts: 11.3 us -> 50 us  [the longest x8 33.7 us: piece(): lax.dynamic_index_in_dim(b, index, 0, keepdims=False)[side]]
    squeeze x0 -> x22, local copies, waits for them, and re-layouts: none -> 30.3 us  [piece(): lax.dynamic_index_in_dim(b, index, 0, keepdims=False)[side]]
    reshape x1 -> x17, local copies, waits for them, and re-layouts: 16.9 us -> 32.9 us  [the longest x1 16.9 us: __init__(): g.reshape(n, 2, g.shape[0] // n // 2, g.shape[1])]
    dot_general x7 -> x16, matrix products: 53 us -> 68.5 us  [outer_cols(): lax.dot_general(left, right, (((1,), (1,)), ((), ())), preferred_element_...]
    ppermute x5, waiting for transfers between devices: 9.02 us -> 22.7 us  [all_sum(): x = x + lax.ppermute(x, axis, [(i, i ^ bit) for i in range(size)])]
    dot_general x6 -> x22, matrix products: 21 us -> 34.2 us  [product(): return jnp.einsum(form, left, right, preferred_element_type=jnp.float32)]
  transfers between devices with their start and end apart: 115 -> 54, of which waited for: 61 -> 20; matrix products, arithmetic and copies ran while one was open for 24% -> 37% of each run, Pallas kernels for 0% -> 0%
where the time goes in v2:
time: 986 us; the launch traced here: 975 us
  local copies, waits for them, and re-layouts  272 us (28%)
  waiting for transfers between devices  261 us (26%)
  matrix products  192 us (19%)
  other arithmetic  161 us (16%)
  starting transfers between devices  47.6 us (5%)
  between operations  42.2 us (4%)
    ppermute x7, waiting for transfers between devices, tp_sum(): other = lax.ppermute(chip_sum, 'tensor', self.chip_pairs)  120 us
    ppermute x14, waiting for transfers between devices, step(): got_a = lax.ppermute(send_a.astype(jnp.bfloat16), 'dp', self.plan.cw)  114 us
    unnamed x522, local copies, waits for them, and re-layouts  94.8 us
    dot_general x16, matrix products, outer_cols(): lax.dot_general(left, right, (((1,), (1,)), ((), ())), preferred_element_...  68.5 us
    dot_general x7, matrix products, matmul(): return jnp.dot(left, right, preferred_element_type=jnp.float32)  46.1 us
    dot_general x7, matrix products, inner_rows(): lax.dot_general(left, right, (((0,), (0,)), ((), ())), preferred_element_...  42.9 us
    dot_general x22, matrix products, product(): return jnp.einsum(form, left, right, preferred_element_type=jnp.float32)  34.2 us
    slice x8, local copies, waits for them, and re-layouts, piece(): lax.dynamic_index_in_dim(b, index, 0, keepdims=False)[side]  33.7 us
  transfers between devices with their start and end apart: 54, of which 20 were waited for; matrix products, arithmetic and copies ran while one was open for 37% of the time, Pallas kernels for 0%

profile of v2, /device:TPU:0, one launch (start us, length us, event | category | flops | bytes accessed | tf_op | source)
XLA Modules:
  0.0 975.4 jit_solution(16756524555202610558)
XLA Ops:
  0.7 3.2 fusion.4
  7.5 3.6 fusion.253
  14.1 3.5 reshape.769
  50.8 5.9 convolution_convert_fusion.1
  56.7 3.3 constant_dynamic-slice_fusion.54
  62.8 3.3 fusion.38
  76.0 6.5 convert_element_type.476
  124.8 38.8 %collective-permute-done.1 = bf16[512,2048]{1,0:T(8,128)(2,1)S(1)} collective-permute-done((bf16[512,2048]{1,0:T(8,128)(2,1)S(1)}, bf16[512,2048]{1,0:T(8,128)(2,1)S(1)}, u32[]{:S(2)}, u32[]{:S(2)}) %collective-permute-start.1) | collective-permute-done | bytes 2097184 | tf_op jit(solution)/shard_map/ppermute | solution.py:218
  217.3 12.4 %fusion.255 = f32[1024,1536]{1,0:T(8,128)} fusion(bf16[1024,2048]{1,0:T(8,128)(2,1)} %param.36, bf16[1536,2048]{1,0:T(8,128)(2,1)} %param.35), kind=kOutput, calls=%fused_computation.609 | convolution fusion | flops 6442450944 | bytes 16777216 | tf_op jit(solution)/shard_map/dot_general | solution.py:33
  233.2 4.5 convert_add_fusion
  237.7 5.5 multiply_convert_fusion
  243.2 8.6 fusion.254
  251.8 15.7 %multiply_convert_fusion.1 = (bf16[1024,1536]{1,0:T(8,128)(2,1)}, bf16[1024,1536]{1,0:T(8,128)(2,1)S(1)}, bf16[1024,1536]{1,0:T(8,128)(2,1)}) fusion(f32[1024,1536]{1,0:T(8,128)} %fusion.255, f32[1024,1536]{1,0:T(8,128)} %fusion.254, bf16[1024,2048]{1,0:T(8,128)(2,1)S(1)} %multiply_convert_fusion, bf16[2048,1536]{1,0:T(8,128)(2,1)} %param.33), kind=kOutput, calls=%fused_computation.27 | convolution fusion | flops 6467616768 | bytes 32505856 | tf_op jit(solution)/shard_map/dot_general | solution.py:23
  267.5 11.9 %fusion.256 = f32[1024,2048]{1,0:T(8,128)} fusion(bf16[1024,1536]{1,0:T(8,128)(2,1)S(1)} %get-tuple-element.222, bf16[2048,1536]{1,0:T(8,128)(2,1)} %param.33), kind=kOutput, calls=%fused_computation.610 | convolution fusion | flops 6442450944 | bytes 17825792 | tf_op jit(solution)/shard_map/dot_general | solution.py:33
  279.4 11.0 %add_convert_fusion = bf16[1024,2048]{1,0:T(8,128)(2,1)S(1)} fusion(f32[1024,2048]{1,0:T(8,128)} %fusion.256, bf16[1024,1536]{1,0:T(8,128)(2,1)} %get-tuple-element.221, bf16[2048,1536]{1,0:T(8,128)(2,1)} %param.34), kind=kOutput, calls=%fused_computation.20 | convolution fusion | flops 6446645248 | bytes 22020096 | tf_op jit(solution)/shard_map/dot_general | solution.py:33
  293.1 8.7 convolution_convert_fusion
  304.8 11.7 %convolution_bitcast_fusion = f32[2048,1536]{0,1:T(8,128)} fusion(bf16[1024,1536]{1,0:T(8,128)(2,1)} %get-tuple-element.223, bf16[1024,2048]{1,0:T(8,128)(2,1)S(1)} %copy-done.45), kind=kOutput, calls=%fused_computation.10 | convolution fusion | flops 6442450944 | bytes 19922944 | tf_op jit(solution)/shard_map/dot_general | solution.py:27
  319.1 11.5 %fusion.257 = f32[2048,1536]{1,0:T(8,128)} fusion(bf16[1024,2048]{1,0:T(8,128)(2,1)S(1)} %multiply_convert_fusion, bf16[1024,1536]{1,0:T(8,128)(2,1)} %copy-done.227), kind=kOutput, calls=%fused_computation.611 | convolution fusion | flops 6442450944 | bytes 19922944 | tf_op jit(solution)/shard_map/dot_general | solution.py:27
  331.8 34.1 %collective-permute-done.7 = bf16[512,2048]{1,0:T(8,128)(2,1)S(1)} collective-permute-done((bf16[512,2048]{1,0:T(8,128)(2,1)S(1)}, bf16[512,2048]{1,0:T(8,128)(2,1)S(1)}, u32[]{:S(2)}, u32[]{:S(2)}) %collective-permute-start.7) | collective-permute-done | bytes 2097184 | tf_op jit(solution)/shard_map/ppermute | solution.py:218
  366.8 9.6 fusion.258
  376.4 33.7 %collective-permute-done.4 = bf16[512,2048]{1,0:T(8,128)(2,1)S(1)} collective-permute-done((bf16[512,2048]{1,0:T(8,128)(2,1)S(1)}, bf16[512,2048]{1,0:T(8,128)(2,1)S(1)}, u32[]{:S(2)}, u32[]{:S(2)}) %collective-permute-start.4) | collective-permute-done | bytes 2097184 | tf_op jit(solution)/shard_map/ppermute | solution.py:218
  417.5 15.3 %convert_bitcast_fusion = (bf16[2048,1024]{0,1:T(8,128)(2,1)}, f32[1024,2048]{1,0:T(8,128)}, bf16[1024,2048]{1,0:T(8,128)(2,1)}) fusion(f32[1024]{0:T(1024)S(1)} %broadcast_multiply_fusion.9, f32[1024]{0:T(1024)S(1)} %get-tuple-element.372, bf16[512,2048]{1,0:T(8,128)(2,1)} %copy-done.7, bf16[512,2048]{1,0:T(8,128)(2,1)S(1)} %get-tuple-element.266, ...), kind=kLoop, calls=%fused_computation.95 | loop fusion | flops 44040192 | bytes 37769216 | tf_op jit(solution)/shard_map/dot_general | solution.py:27
  432.7 5.7 fusion.44
  474.5 6.5 copy.964
  481.0 5.0 fusion.90
  486.1 3.2 constant_dynamic-slice_fusion.43
  491.1 8.3 constant_dynamic-slice_fusion.5
  499.5 3.3 constant_dynamic-slice_fusion.44
  502.7 8.4 constant_dynamic-slice_fusion.4
  517.8 16.9 %reshape.772 = f32[8,2,128,1536]{2,1,0,3:T(2,128)} reshape(f32[2048,1536]{0,1:T(8,128)} %convolution_bitcast_fusion) | data formatting | bytes 25165824 | tf_op jit(solution)/shard_map/reshape | solution.py:251
  534.7 3.3 constant_dynamic-slice_fusion.45
  560.8 7.7 multiply_reduce_fusion.12
  573.7 8.0 fusion.132
  613.3 3.2 fusion.31
  616.5 3.7 fusion.32
  624.0 10.5 %constant_dynamic-slice_fusion.3 = (f32[1,1,128,1536]{2,1,0,3:T(1,128)}, f32[1,1,128,1536]{2,1,0,3:T(1,128)}, f32[1,1,128,1536]{2,1,0,3:T(1,128)}, f32[1,1,128,1...) fusion(f32[8,2,128,1536]{2,1,0,3:T(2,128)S(1)} %bitcast.584, ...), kind=kLoop, calls=%fused_computation.467 | loop fusion | bytes 22020152 | tf_op jit(solution)/shard_map/slice | solution.py:257
  651.0 4.4 convert_element_type.515
  745.3 27.2 %collective-permute-done.19 = bf16[128,5120]{0,1:T(8,128)(2,1)S(1)} collective-permute-done((bf16[128,5120]{0,1:T(8,128)(2,1)S(1)}, bf16[128,5120]{0,1:T(8,128)(2,1)S(1)}, u32[]{:S(2)}, u32[]{:S(2)}) %collective-permute-start.19) | collective-permute-done | bytes 1310752 | tf_op jit(solution)/shard_map/ppermute | solution.py:268
  776.7 26.6 %collective-permute-done.20 = bf16[128,5120]{0,1:T(8,128)(2,1)S(1)} collective-permute-done((bf16[128,5120]{0,1:T(8,128)(2,1)S(1)}, bf16[128,5120]{0,1:T(8,128)(2,1)S(1)}, u32[]{:S(2)}, u32[]{:S(2)}) %collective-permute-start.20) | collective-permute-done | bytes 1310752 | tf_op jit(solution)/shard_map/ppermute | solution.py:268
  810.1 13.2 %collective-permute-done.24 = bf16[128,2048]{1,0:T(8,128)(2,1)S(1)} collective-permute-done((bf16[128,2048]{1,0:T(8,128)(2,1)S(1)}, bf16[128,2048]{1,0:T(8,128)(2,1)S(1)}, u32[]{:S(2)}, u32[]{:S(2)}) %collective-permute-start.24) | collective-permute-done | bytes 524320 | tf_op jit(solution)/shard_map/ppermute | solution.py:218
  823.5 13.4 %collective-permute-done.26 = bf16[128,5120]{0,1:T(8,128)(2,1)S(1)} collective-permute-done((bf16[128,5120]{0,1:T(8,128)(2,1)S(1)}, bf16[128,5120]{0,1:T(8,128)(2,1)S(1)}, u32[]{:S(2)}, u32[]{:S(2)}) %collective-permute-start.26) | collective-permute-done | bytes 1310752 | tf_op jit(solution)/shard_map/ppermute | solution.py:268
  859.2 31.5 %collective-permute-done.37 = bf16[128,1024]{1,0:T(8,128)(2,1)S(1)} collective-permute-done((bf16[128,1024]{1,0:T(8,128)(2,1)S(1)}, bf16[128,1024]{1,0:T(8,128)(2,1)S(1)}, u32[]{:S(2)}, u32[]{:S(2)}) %collective-permute-start.37) | collective-permute-done | bytes 262176 | tf_op jit(solution)/shard_map/ppermute | solution.py:268
  893.7 4.1 collective-permute-done.38
  900.1 4.3 collective-permute-done.39
  907.2 3.8 collective-permute-done.40
  919.9 3.6 multiply_reduce_fusion.2
  931.7 17.8 %collective-permute-done.33 = f32[4352]{0:T(1024)S(1)} collective-permute-done((f32[4352]{0:T(1024)S(1)}, f32[4352]{0:T(1024)S(1)}, u32[]{:S(2)}, u32[]{:S(2)}) %collective-permute-start.33) | collective-permute-done | bytes 17440 | tf_op jit(solution)/shard_map/ppermute | solution.py:238
  954.4 4.7 fusion.9
  (918 shorter events, 422.5 us)
Async XLA Ops:
  60.1 51.7 %collective-permute-start = (bf16[512,2048]{1,0:T(8,128)(2,1)}, bf16[512,2048]{1,0:T(8,128)(2,1)}, u32[]{:S(2)}, u32[]{:S(2)}) collective-permute-start(bf16[512,2048]{1,0:T(8,128)(2,1)} %constant_dynamic-slice_fusion.54), channel_id=1, source_target_pairs={{0,1},{1,0},{2,3},{3,2},{4,5},{5,4},{6,7},{7,6},{8,9},{9,8},{10,11... | collective-permute-start | bytes 6291464 | tf_op jit(solution)/shard_map/ppermute | solution.py:216
  114.9 48.7 %collective-permute-start.1 = (bf16[512,2048]{1,0:T(8,128)(2,1)S(1)}, bf16[512,2048]{1,0:T(8,128)(2,1)S(1)}, u32[]{:S(2)}, u32[]{:S(2)}) collective-permute-start(bf16[512,2048]{1,0:T(8,128)(2,1)S(1)} %add_convert_fusion.7), channel_id=1, source_target_pairs={{0,2},{1,3},{2,0},{3,1},{4,6},{5,7},{6,4},{7,5},{8,10},{9,11},{10,... | collective-permute-start | bytes 6291464 | tf_op jit(solution)/shard_map/ppermute | solution.py:218
  165.7 64.0 %collective-permute-start.2 = (bf16[512,2048]{1,0:T(8,128)(2,1)}, bf16[512,2048]{1,0:T(8,128)(2,1)}, u32[]{:S(2)}, u32[]{:S(2)}) collective-permute-start(bf16[512,2048]{1,0:T(8,128)(2,1)} %add_convert_fusion.6), channel_id=1, source_target_pairs={{0,1},{1,0},{2,3},{3,2},{4,5},{5,4},{6,7},{7,6},{8,9},{9,8},{10,11... | collective-permute-start | bytes 6291464 | tf_op jit(solution)/shard_map/ppermute | solution.py:220
  292.0 24.5 %collective-permute-start.6 = (bf16[512,2048]{1,0:T(8,128)(2,1)}, bf16[512,2048]{1,0:T(8,128)(2,1)S(1)}, u32[]{:S(2)}, u32[]{:S(2)}) collective-permute-start(bf16[512,2048]{1,0:T(8,128)(2,1)} %constant_dynamic-slice_fusion.49), channel_id=1, source_target_pairs={{0,1},{1,0},{2,3},{3,2},{4,5},{5,4},{6,7},{7,6},{8,9},{9,8},{10,11... | collective-permute-start | bytes 6291464 | tf_op jit(solution)/shard_map/ppermute | solution.py:216
  302.1 28.6 %collective-permute-start.3 = (bf16[512,2048]{1,0:T(8,128)(2,1)S(1)}, bf16[512,2048]{1,0:T(8,128)(2,1)S(1)}, u32[]{:S(2)}, u32[]{:S(2)}) collective-permute-start(bf16[512,2048]{1,0:T(8,128)(2,1)S(1)} %constant_dynamic-slice_fusion.52), channel_id=1, source_target_pairs={{0,1},{1,0},{2,3},{3,2},{4,5},{5,4},{6,7},{7,6},{8,9},{9,8},{10,11... | collective-permute-start | bytes 6291464 | tf_op jit(solution)/shard_map/ppermute | solution.py:216
  317.3 48.6 %collective-permute-start.7 = (bf16[512,2048]{1,0:T(8,128)(2,1)S(1)}, bf16[512,2048]{1,0:T(8,128)(2,1)S(1)}, u32[]{:S(2)}, u32[]{:S(2)}) collective-permute-start(bf16[512,2048]{1,0:T(8,128)(2,1)S(1)} %add_convert_fusion.3), channel_id=1, source_target_pairs={{0,2},{1,3},{2,0},{3,1},{4,6},{5,7},{6,4},{7,5},{8,10},{9,11},{10,... | collective-permute-start | bytes 6291464 | tf_op jit(solution)/shard_map/ppermute | solution.py:218
  331.5 78.6 %collective-permute-start.4 = (bf16[512,2048]{1,0:T(8,128)(2,1)S(1)}, bf16[512,2048]{1,0:T(8,128)(2,1)S(1)}, u32[]{:S(2)}, u32[]{:S(2)}) collective-permute-start(bf16[512,2048]{1,0:T(8,128)(2,1)S(1)} %add_convert_fusion.5), channel_id=1, source_target_pairs={{0,2},{1,3},{2,0},{3,1},{4,6},{5,7},{6,4},{7,5},{8,10},{9,11},{10,... | collective-permute-start | bytes 6291464 | tf_op jit(solution)/shard_map/ppermute | solution.py:218
  366.7 44.9 %collective-permute-start.8 = (bf16[512,2048]{1,0:T(8,128)(2,1)S(1)}, bf16[512,2048]{1,0:T(8,128)(2,1)S(1)}, u32[]{:S(2)}, u32[]{:S(2)}) collective-permute-start(bf16[512,2048]{1,0:T(8,128)(2,1)S(1)} %add_convert_fusion.2), channel_id=1, source_target_pairs={{0,1},{1,0},{2,3},{3,2},{4,5},{5,4},{6,7},{7,6},{8,9},{9,8},{10,11... | collective-permute-start | bytes 6291464 | tf_op jit(solution)/shard_map/ppermute | solution.py:220
  539.2 95.3 %collective-permute-start.9 = (bf16[128,5120]{0,1:T(8,128)(2,1)}, bf16[128,5120]{0,1:T(8,128)(2,1)}, u32[]{:S(2)}, u32[]{:S(2)}) collective-permute-start(bf16[128,5120]{0,1:T(8,128)(2,1)} %pad_maximum_fusion.4), channel_id=1, source_target_pairs={{0,8},{8,16},{16,24},{24,28},{28,20},{20,12},{12,4},{4,0},{1,9},{9... | collective-permute-start | bytes 3932168 | tf_op jit(solution)/shard_map/ppermute | solution.py:268
  550.0 86.0 %collective-permute-start.10 = (bf16[128,5120]{0,1:T(8,128)(2,1)}, bf16[128,5120]{0,1:T(8,128)(2,1)}, u32[]{:S(2)}, u32[]{:S(2)}) collective-permute-start(bf16[128,5120]{0,1:T(8,128)(2,1)} %pad_maximum_fusion.5), channel_id=1, source_target_pairs={{8,0},{16,8},{24,16},{28,24},{20,28},{12,20},{4,12},{0,4},{9,1},{1... | collective-permute-start | bytes 3932168 | tf_op jit(solution)/shard_map/ppermute | solution.py:269
  637.7 5.3 collective-permute-start.11
  639.1 98.0 %collective-permute-start.14 = (bf16[128,5120]{0,1:T(8,128)(2,1)}, bf16[128,5120]{0,1:T(8,128)(2,1)}, u32[]{:S(2)}, u32[]{:S(2)}) collective-permute-start(bf16[128,5120]{0,1:T(8,128)(2,1)} %fusion.19), channel_id=1, source_target_pairs={{0,8},{8,16},{16,24},{24,28},{28,20},{20,12},{12,4},{4,0},{1,9},{9... | collective-permute-start | bytes 3932168 | tf_op jit(solution)/shard_map/ppermute | solution.py:268
  642.4 96.3 %collective-permute-start.15 = (bf16[128,5120]{0,1:T(8,128)(2,1)}, bf16[128,5120]{0,1:T(8,128)(2,1)}, u32[]{:S(2)}, u32[]{:S(2)}) collective-permute-start(bf16[128,5120]{0,1:T(8,128)(2,1)} %fusion.20), channel_id=1, source_target_pairs={{8,0},{16,8},{24,16},{28,24},{20,28},{12,20},{4,12},{0,4},{9,1},{1... | collective-permute-start | bytes 3932168 | tf_op jit(solution)/shard_map/ppermute | solution.py:269
  643.9 91.8 %collective-permute-start.12 = (bf16[128,2048]{1,0:T(8,128)(2,1)}, bf16[128,2048]{1,0:T(8,128)(2,1)}, u32[]{:S(2)}, u32[]{:S(2)}) collective-permute-start(bf16[128,2048]{1,0:T(8,128)(2,1)} %add_convert_fusion.15), channel_id=1, source_target_pairs={{0,2},{1,3},{2,0},{3,1},{4,6},{5,7},{6,4},{7,5},{8,10},{9,11},{10,... | collective-permute-start | bytes 1572872 | tf_op jit(solution)/shard_map/ppermute | solution.py:218
  737.1 39.1 %collective-permute-start.13 = (bf16[128,2048]{1,0:T(8,128)(2,1)S(1)}, bf16[128,2048]{1,0:T(8,128)(2,1)S(1)}, u32[]{:S(2)}, u32[]{:S(2)}) collective-permute-start(bf16[128,2048]{1,0:T(8,128)(2,1)S(1)} %add_convert_fusion.14), channel_id=1, source_target_pairs={{0,1},{1,0},{2,3},{3,2},{4,5},{5,4},{6,7},{7,6},{8,9},{9,8},{10,11... | collective-permute-start | bytes 1572872 | tf_op jit(solution)/shard_map/ppermute | solution.py:220
  741.3 31.2 %collective-permute-start.19 = (bf16[128,5120]{0,1:T(8,128)(2,1)S(1)}, bf16[128,5120]{0,1:T(8,128)(2,1)S(1)}, u32[]{:S(2)}, u32[]{:S(2)}) collective-permute-start(bf16[128,5120]{0,1:T(8,128)(2,1)S(1)} %fusion.21), channel_id=1, source_target_pairs={{0,8},{8,16},{16,24},{24,28},{28,20},{20,12},{12,4},{4,0},{1,9},{9... | collective-permute-start | bytes 3932168 | tf_op jit(solution)/shard_map/ppermute | solution.py:268
  743.2 31.3 %collective-permute-start.21 = (bf16[128,5120]{0,1:T(8,128)(2,1)S(1)}, bf16[128,5120]{0,1:T(8,128)(2,1)S(1)}, u32[]{:S(2)}, u32[]{:S(2)}) collective-permute-start(bf16[128,5120]{0,1:T(8,128)(2,1)S(1)} %fusion.23), channel_id=1, source_target_pairs={{8,0},{16,8},{24,16},{28,24},{20,28},{12,20},{4,12},{0,4},{9,1},{1... | collective-permute-start | bytes 3932168 | tf_op jit(solution)/shard_map/ppermute | solution.py:269
  744.7 31.7 %collective-permute-start.17 = (bf16[128,2048]{1,0:T(8,128)(2,1)S(1)}, bf16[128,2048]{1,0:T(8,128)(2,1)S(1)}, u32[]{:S(2)}, u32[]{:S(2)}) collective-permute-start(bf16[128,2048]{1,0:T(8,128)(2,1)S(1)} %add_convert_fusion.13), channel_id=1, source_target_pairs={{0,2},{1,3},{2,0},{3,1},{4,6},{5,7},{6,4},{7,5},{8,10},{9,11},{10,... | collective-permute-start | bytes 1572872 | tf_op jit(solution)/shard_map/ppermute | solution.py:218
  772.9 30.4 %collective-permute-start.20 = (bf16[128,5120]{0,1:T(8,128)(2,1)S(1)}, bf16[128,5120]{0,1:T(8,128)(2,1)S(1)}, u32[]{:S(2)}, u32[]{:S(2)}) collective-permute-start(bf16[128,5120]{0,1:T(8,128)(2,1)S(1)} %fusion.22), channel_id=1, source_target_pairs={{0,8},{8,16},{16,24},{24,28},{28,20},{20,12},{12,4},{4,0},{1,9},{9... | collective-permute-start | bytes 3932168 | tf_op jit(solution)/shard_map/ppermute | solution.py:268
  774.9 30.1 %collective-permute-start.22 = (bf16[128,5120]{0,1:T(8,128)(2,1)S(1)}, bf16[128,5120]{0,1:T(8,128)(2,1)S(1)}, u32[]{:S(2)}, u32[]{:S(2)}) collective-permute-start(bf16[128,5120]{0,1:T(8,128)(2,1)S(1)} %fusion.24), channel_id=1, source_target_pairs={{8,0},{16,8},{24,16},{28,24},{20,28},{12,20},{4,12},{0,4},{9,1},{1... | collective-permute-start | bytes 3932168 | tf_op jit(solution)/shard_map/ppermute | solution.py:269
  776.6 33.2 %collective-permute-start.18 = (bf16[128,2048]{1,0:T(8,128)(2,1)S(1)}, bf16[128,2048]{1,0:T(8,128)(2,1)S(1)}, u32[]{:S(2)}, u32[]{:S(2)}) collective-permute-start(bf16[128,2048]{1,0:T(8,128)(2,1)S(1)} %add_convert_fusion.12), channel_id=1, source_target_pairs={{0,1},{1,0},{2,3},{3,2},{4,5},{5,4},{6,7},{7,6},{8,9},{9,8},{10,11... | collective-permute-start | bytes 1572872 | tf_op jit(solution)/shard_map/ppermute | solution.py:220
  805.7 31.2 %collective-permute-start.26 = (bf16[128,5120]{0,1:T(8,128)(2,1)S(1)}, bf16[128,5120]{0,1:T(8,128)(2,1)S(1)}, u32[]{:S(2)}, u32[]{:S(2)}) collective-permute-start(bf16[128,5120]{0,1:T(8,128)(2,1)S(1)} %fusion.25), channel_id=1, source_target_pairs={{0,8},{8,16},{16,24},{24,28},{28,20},{20,12},{12,4},{4,0},{1,9},{9... | collective-permute-start | bytes 3932168 | tf_op jit(solution)/shard_map/ppermute | solution.py:268
  807.6 31.1 %collective-permute-start.27 = (bf16[128,5120]{0,1:T(8,128)(2,1)S(1)}, bf16[128,5120]{0,1:T(8,128)(2,1)S(1)}, u32[]{:S(2)}, u32[]{:S(2)}) collective-permute-start(bf16[128,5120]{0,1:T(8,128)(2,1)S(1)} %fusion.26), channel_id=1, source_target_pairs={{8,0},{16,8},{24,16},{28,24},{20,28},{12,20},{4,12},{0,4},{9,1},{1... | collective-permute-start | bytes 3932168 | tf_op jit(solution)/shard_map/ppermute | solution.py:269
  809.2 14.1 %collective-permute-start.24 = (bf16[128,2048]{1,0:T(8,128)(2,1)S(1)}, bf16[128,2048]{1,0:T(8,128)(2,1)S(1)}, u32[]{:S(2)}, u32[]{:S(2)}) collective-permute-start(bf16[128,2048]{1,0:T(8,128)(2,1)S(1)} %add_convert_fusion.11), channel_id=1, source_target_pairs={{0,2},{1,3},{2,0},{3,1},{4,6},{5,7},{6,4},{7,5},{8,10},{9,11},{10,... | collective-permute-start | bytes 1572872 | tf_op jit(solution)/shard_map/ppermute | solution.py:218
  823.4 35.1 %collective-permute-start.25 = (bf16[128,2048]{1,0:T(8,128)(2,1)S(1)}, bf16[128,2048]{1,0:T(8,128)(2,1)S(1)}, u32[]{:S(2)}, u32[]{:S(2)}) collective-permute-start(bf16[128,2048]{1,0:T(8,128)(2,1)S(1)} %add_convert_fusion.10), channel_id=1, source_target_pairs={{0,1},{1,0},{2,3},{3,2},{4,5},{5,4},{6,7},{7,6},{8,9},{9,8},{10,11... | collective-permute-start | bytes 1572872 | tf_op jit(solution)/shard_map/ppermute | solution.py:220
  843.4 49.5 %collective-permute-start.28 = (bf16[128,2048]{1,0:T(8,128)(2,1)S(1)}, bf16[128,2048]{1,0:T(8,128)(2,1)S(1)}, u32[]{:S(2)}, u32[]{:S(2)}) collective-permute-start(bf16[128,2048]{1,0:T(8,128)(2,1)S(1)} %constant_dynamic-slice_fusion.15), channel_id=1, source_target_pairs={{0,1},{1,0},{2,3},{3,2},{4,5},{5,4},{6,7},{7,6},{8,9},{9,8},{10,11... | collective-permute-start | bytes 1572872 | tf_op jit(solution)/shard_map/ppermute | solution.py:216
  846.0 8.7 collective-permute-start.36
  847.7 9.2 collective-permute-start.43
  848.6 65.9 %collective-permute-start.52 = (bf16[128,5120]{0,1:T(8,128)(2,1)S(1)}, bf16[128,5120]{0,1:T(8,128)(2,1)S(1)}, u32[]{:S(2)}, u32[]{:S(2)}) collective-permute-start(bf16[128,5120]{0,1:T(8,128)(2,1)S(1)} %fusion.29), channel_id=1, source_target_pairs={{8,0},{16,8},{24,16},{28,24},{20,28},{12,20},{4,12},{0,4},{9,1},{1... | collective-permute-start | bytes 3932168 | tf_op jit(solution)/shard_map/ppermute | solution.py:269
  854.7 61.7 %collective-permute-start.50 = (bf16[128,5120]{0,1:T(8,128)(2,1)S(1)}, bf16[128,5120]{0,1:T(8,128)(2,1)S(1)}, u32[]{:S(2)}, u32[]{:S(2)}) collective-permute-start(bf16[128,5120]{0,1:T(8,128)(2,1)S(1)} %fusion.27), channel_id=1, source_target_pairs={{0,8},{8,16},{16,24},{24,28},{28,20},{20,12},{12,4},{4,0},{1,9},{9... | collective-permute-start | bytes 3932168 | tf_op jit(solution)/shard_map/ppermute | solution.py:268
  856.9 33.7 %collective-permute-start.37 = (bf16[128,1024]{1,0:T(8,128)(2,1)S(1)}, bf16[128,1024]{1,0:T(8,128)(2,1)S(1)}, u32[]{:S(2)}, u32[]{:S(2)}) collective-permute-start(bf16[128,1024]{1,0:T(8,128)(2,1)S(1)} %fusion.150), channel_id=1, source_target_pairs={{0,8},{8,16},{16,24},{24,28},{28,20},{20,12},{12,4},{4,0},{1,9},{9... | collective-permute-start | bytes 786440 | tf_op jit(solution)/shard_map/ppermute | solution.py:268
  858.5 33.8 %collective-permute-start.44 = (bf16[128,1024]{1,0:T(8,128)(2,1)S(1)}, bf16[128,1024]{1,0:T(8,128)(2,1)S(1)}, u32[]{:S(2)}, u32[]{:S(2)}) collective-permute-start(bf16[128,1024]{1,0:T(8,128)(2,1)S(1)} %fusion.156), channel_id=1, source_target_pairs={{8,0},{16,8},{24,16},{28,24},{20,28},{12,20},{4,12},{0,4},{9,1},{1... | collective-permute-start | bytes 786440 | tf_op jit(solution)/shard_map/ppermute | solution.py:269
  890.7 7.0 collective-permute-start.38
  892.4 7.0 collective-permute-start.45
  893.1 13.9 %collective-permute-start.29 = (bf16[128,2048]{1,0:T(8,128)(2,1)S(1)}, bf16[128,2048]{1,0:T(8,128)(2,1)S(1)}, u32[]{:S(2)}, u32[]{:S(2)}) collective-permute-start(bf16[128,2048]{1,0:T(8,128)(2,1)S(1)} %add_convert_fusion.9), channel_id=1, source_target_pairs={{0,2},{1,3},{2,0},{3,1},{4,6},{5,7},{6,4},{7,5},{8,10},{9,11},{10,... | collective-permute-start | bytes 1572872 | tf_op jit(solution)/shard_map/ppermute | solution.py:218
  897.8 6.6 collective-permute-start.39
  899.5 6.9 collective-permute-start.46
  904.5 6.4 collective-permute-start.40
  906.5 6.8 collective-permute-start.47
  907.1 11.3 %collective-permute-start.30 = (bf16[128,2048]{1,0:T(8,128)(2,1)S(1)}, bf16[128,2048]{1,0:T(8,128)(2,1)S(1)}, u32[]{:S(2)}, u32[]{:S(2)}) collective-permute-start(bf16[128,2048]{1,0:T(8,128)(2,1)S(1)} %add_convert_fusion.8), channel_id=1, source_target_pairs={{0,1},{1,0},{2,3},{3,2},{4,5},{5,4},{6,7},{7,6},{8,9},{9,8},{10,11... | collective-permute-start | bytes 1572872 | tf_op jit(solution)/shard_map/ppermute | solution.py:220
  911.7 14.4 %collective-permute-start.41 = (bf16[128,1024]{1,0:T(8,128)(2,1)}, bf16[128,1024]{1,0:T(8,128)(2,1)}, u32[]{:S(2)}, u32[]{:S(2)}) collective-permute-start(bf16[128,1024]{1,0:T(8,128)(2,1)} %fusion.154), channel_id=1, source_target_pairs={{0,8},{8,16},{16,24},{24,28},{28,20},{20,12},{12,4},{4,0},{1,9},{9... | collective-permute-start | bytes 786440 | tf_op jit(solution)/shard_map/ppermute | solution.py:268
  914.1 35.4 %collective-permute-start.48 = (bf16[128,1024]{1,0:T(8,128)(2,1)}, bf16[128,1024]{1,0:T(8,128)(2,1)}, u32[]{:S(2)}, u32[]{:S(2)}) collective-permute-start(bf16[128,1024]{1,0:T(8,128)(2,1)} %fusion.160), channel_id=1, source_target_pairs={{8,0},{16,8},{24,16},{28,24},{20,28},{12,20},{4,12},{0,4},{9,1},{1... | collective-permute-start | bytes 786440 | tf_op jit(solution)/shard_map/ppermute | solution.py:269
  914.9 47.2 %collective-permute-start.53 = (bf16[128,5120]{0,1:T(8,128)(2,1)S(1)}, bf16[128,5120]{0,1:T(8,128)(2,1)}, u32[]{:S(2)}, u32[]{:S(2)}) collective-permute-start(bf16[128,5120]{0,1:T(8,128)(2,1)S(1)} %fusion.30), channel_id=1, source_target_pairs={{8,0},{16,8},{24,16},{28,24},{20,28},{12,20},{4,12},{0,4},{9,1},{1... | collective-permute-start | bytes 3932168 | tf_op jit(solution)/shard_map/ppermute | solution.py:269
  916.8 47.1 %collective-permute-start.51 = (bf16[128,5120]{0,1:T(8,128)(2,1)S(1)}, bf16[128,5120]{0,1:T(8,128)(2,1)}, u32[]{:S(2)}, u32[]{:S(2)}) collective-permute-start(bf16[128,5120]{0,1:T(8,128)(2,1)S(1)} %fusion.28), channel_id=1, source_target_pairs={{0,8},{8,16},{16,24},{24,28},{28,20},{20,12},{12,4},{4,0},{1,9},{9... | collective-permute-start | bytes 3932168 | tf_op jit(solution)/shard_map/ppermute | solution.py:268
  929.4 20.1 %collective-permute-start.33 = (f32[4352]{0:T(1024)S(1)}, f32[4352]{0:T(1024)S(1)}, u32[]{:S(2)}, u32[]{:S(2)}) collective-permute-start(f32[4352]{0:T(1024)S(1)} %add.1095), channel_id=1, source_target_pairs={{0,4},{4,0},{8,12},{12,8},{16,20},{20,16},{24,28},{28,24},{1,5},{5... | collective-permute-start | bytes 52232 | tf_op jit(solution)/shard_map/ppermute | solution.py:238
  930.1 30.2 %collective-permute-start.42 = (bf16[128,1024]{1,0:T(8,128)(2,1)S(1)}, bf16[128,1024]{1,0:T(8,128)(2,1)S(1)}, u32[]{:S(2)}, u32[]{:S(2)}) collective-permute-start(bf16[128,1024]{1,0:T(8,128)(2,1)S(1)} %fusion.155), channel_id=1, source_target_pairs={{0,8},{8,16},{16,24},{24,28},{28,20},{20,12},{12,4},{4,0},{1,9},{9... | collective-permute-start | bytes 786440 | tf_op jit(solution)/shard_map/ppermute | solution.py:268
  950.6 9.8 %collective-permute-start.49 = (bf16[128,1024]{1,0:T(8,128)(2,1)S(1)}, bf16[128,1024]{1,0:T(8,128)(2,1)S(1)}, u32[]{:S(2)}, u32[]{:S(2)}) collective-permute-start(bf16[128,1024]{1,0:T(8,128)(2,1)S(1)} %fusion.161), channel_id=1, source_target_pairs={{8,0},{16,8},{24,16},{28,24},{20,28},{12,20},{4,12},{0,4},{9,1},{1... | collective-permute-start | bytes 786440 | tf_op jit(solution)/shard_map/ppermute | solution.py:269
  953.3 5.9 collective-permute-start.35
  (243 other events, 2179.1 us)

commit v3 on v2

--- a/solution.py
+++ b/solution.py
@@ -6,6 +6,7 @@
 import numpy as np
 from jax import lax
 from jax.sharding import PartitionSpec as P
+
 
 HEAD_SIZE = 128
 LEN = 128
@@ -281,7 +282,7 @@
 
 
 def make_on_device(plan):
-    def on_device(
+    def body(
         tokens,
         attn_gain,
         w_query,
@@ -324,67 +325,40 @@
         gate_grad, upper_grad = pull(hidden_grad)
         gate_grad = gate_grad.astype(jnp.bfloat16)
         upper_grad = upper_grad.astype(jnp.bfloat16)
-        gate_w_grad = inner_rows(normed_mid, gate_grad)
-        up_w_grad = inner_rows(normed_mid, upper_grad)
         mid_part = (outer_cols(gate_grad, w_gate) + outer_cols(upper_grad, w_up)).astype(
             jnp.bfloat16
         )
         mid_sum = plan.tp_sum(mid_part)
-        mid_sum, down_grad_t, gate_w_grad, up_w_grad = lax.optimization_barrier(
-            (mid_sum, down_grad_t, gate_w_grad, up_w_grad)
-        )
+        gate_w_grad = inner_rows(normed_mid, gate_grad)
+        up_w_grad = inner_rows(normed_mid, upper_grad)
+        big = Ring(plan, [down_grad_t, gate_w_grad, up_w_grad])
+        big.step()
         mid_grad = mid_sum.astype(jnp.float32)
         resid_grad = cotangent.astype(jnp.float32) + norm_back(resid, mlp_gain, mid_grad)
         mlp_gain_part = gain_term(resid_rows, lax.dynamic_slice_in_dim(mid_grad, offset, share, 0))
         resid_low = resid_grad.astype(jnp.bfloat16)
         out_w_grad_t = inner_rows(resid_low, attended)
         attended_grad = outer_cols(resid_low, w_out).astype(jnp.bfloat16)
-        big = Ring(plan, [down_grad_t, gate_w_grad, up_w_grad, out_w_grad_t])
-        big.step()
-        chunks = 4 if seqs % 4 == 0 else 1
-        per = seqs // chunks
-        rows = per * LEN
-        plan_steps = [big.steps * (c + 1) // (chunks + 1) for c in range(chunks)]
-        q_parts, k_parts, v_parts, in_parts = [], [], [], []
-        qg_part = kg_part = 0.0
-        for c in range(chunks):
-            span = slice(c * rows, (c + 1) * rows)
-            seq_span = slice(c * per, (c + 1) * per)
-            qc, kc, vc, qgc, kgc = attend_back(
-                attended_grad[span],
-                q_raw[span],
-                k_raw[span],
-                query_gain,
-                key_gain,
-                queries[seq_span],
-                keys_rot[seq_span],
-                values[seq_span],
-                logsum[seq_span],
-                per,
-            )
-            in_c = (
-                outer_cols(qc, w_query) + outer_cols(kc, key_matrix) + outer_cols(vc, value_matrix)
-            ).astype(jnp.bfloat16)
-            while big.done < plan_steps[c]:
-                big.step()
-            big.state, qc, kc, vc, in_c = lax.optimization_barrier((big.state, qc, kc, vc, in_c))
-            in_parts.append(plan.tp_sum(in_c))
-            q_parts.append(qc)
-            k_parts.append(kc)
-            v_parts.append(vc)
-            qg_part = qg_part + qgc
-            kg_part = kg_part + kgc
-        q_grad = jnp.concatenate(q_parts, 0)
-        k_grad = jnp.concatenate(k_parts, 0)
-        v_grad = jnp.concatenate(v_parts, 0)
+        small = Ring(plan, [out_w_grad_t])
+        for _ in range(big.steps - 1):
+            big.step()
+            small.step()
+        q_grad, k_grad, v_grad, qg_part, kg_part = attend_back(
+            attended_grad, q_raw, k_raw, query_gain, key_gain, queries, keys_rot, values, logsum, seqs
+        )
+        in_part = (
+            outer_cols(q_grad, w_query)
+            + outer_cols(k_grad, key_matrix)
+            + outer_cols(v_grad, value_matrix)
+        ).astype(jnp.bfloat16)
         query_w_grad = inner_rows(normed_in, q_grad)
         key_w_grad = inner_rows(normed_in, k_grad)
         value_w_grad = inner_rows(normed_in, v_grad)
-        while big.done < big.steps:
-            big.step()
-        down_sum, gate_sum, up_sum, out_sum = big.result()
+        small.step()
+        in_grad = plan.tp_sum(in_part).astype(jnp.float32)
+        down_sum, gate_sum, up_sum = big.result()
+        (out_sum,) = small.result()
         query_sum, key_sum, value_sum = plan.dp_rs([query_w_grad, key_w_grad, value_w_grad])
-        in_grad = jnp.concatenate(in_parts, 0).astype(jnp.float32)
         input_grad = resid_grad + norm_back(stream, attn_gain, in_grad)
         attn_gain_part = gain_term(stream_rows, lax.dynamic_slice_in_dim(in_grad, offset, share, 0))
         gains = plan.all_sum(jnp.concatenate([attn_gain_part, mlp_gain_part, qg_part, kg_part]))
@@ -410,7 +384,7 @@
             down_sum.T,
         )
 
-    return on_device
+    return body
 
 
 def solution(mesh):

time: 986 us -> 826 us (0.84)
  local copies, waits for them, and re-layouts: 272 us -> 215 us
  waiting for transfers between devices: 261 us -> 217 us
  other arithmetic: 161 us -> 121 us
  matrix products: 192 us -> 159 us
  starting transfers between devices: 47.6 us -> 62.4 us
    ppermute x14 -> x21, waiting for transfers between devices: 3.95 us -> 58.9 us  [step(): got_b = lax.ppermute(send_b.astype(jnp.bfloat16), 'dp', self.plan.ccw)]
    ppermute x14 -> x21, waiting for transfers between devices: 114 us -> 61.3 us  [step(): got_a = lax.ppermute(send_a.astype(jnp.bfloat16), 'dp', self.plan.cw)]
    ppermute x7 -> x4, waiting for transfers between devices: 120 us -> 92.3 us  [tp_sum(): other = lax.ppermute(chip_sum, 'tensor', self.chip_pairs)]
    squeeze x22 -> x4, local copies, waits for them, and re-layouts: 30.3 us -> 3.49 us  [piece(): lax.dynamic_index_in_dim(b, index, 0, keepdims=False)[side]]
    ppermute x5, waiting for transfers between devices: 22.7 us -> 0.82 us  [all_sum(): x = x + lax.ppermute(x, axis, [(i, i ^ bit) for i in range(size)])]
    dot_general x16 -> x7, matrix products: 68.5 us -> 49.6 us  [outer_cols(): lax.dot_general(left, right, (((1,), (1,)), ((), ())), preferred_element_...]
    slice x16 -> x2, local copies, waits for them, and re-layouts: 17.4 us -> 1.12 us  [the longest x1 0.6 us: body(): mlp_gain_grad = gains[width:2 * width]]
    dot_general x22 -> x6, matrix products: 34.2 us -> 18.2 us  [product(): return jnp.einsum(form, left, right, preferred_element_type=jnp.float32)]
  transfers between devices with their start and end apart: 54 -> 59, of which waited for: 20 -> 22; matrix products, arithmetic and copies ran while one was open for 37% -> 40% of each run, Pallas kernels for 0% -> 0%
where the time goes in v3:
time: 826 us; the launch traced here: 815 us
  waiting for transfers between devices  217 us (26%)
  local copies, waits for them, and re-layouts  215 us (26%)
  matrix products  159 us (19%)
  other arithmetic  121 us (15%)
  starting transfers between devices  62.4 us (8%)
  between operations  41 us (5%)
    unnamed x345, local copies, waits for them, and re-layouts  99.3 us
    ppermute x4, waiting for transfers between devices, tp_sum(): other = lax.ppermute(chip_sum, 'tensor', self.chip_pairs)  92.3 us
    ppermute x21, waiting for transfers between devices, step(): got_a = lax.ppermute(send_a.astype(jnp.bfloat16), 'dp', self.plan.cw)  61.3 us
    ppermute x21, waiting for transfers between devices, step(): got_b = lax.ppermute(send_b.astype(jnp.bfloat16), 'dp', self.plan.ccw)  58.9 us
    dot_general x7, matrix products, matmul(): return jnp.dot(left, right, preferred_element_type=jnp.float32)  50.7 us
    dot_general x7, matrix products, outer_cols(): lax.dot_general(left, right, (((1,), (1,)), ((), ())), preferred_element_...  49.6 us
    dot_general x7, matrix products, inner_rows(): lax.dot_general(left, right, (((0,), (0,)), ((), ())), preferred_element_...  40.6 us
    slice x7, local copies, waits for them, and re-layouts, piece(): lax.dynamic_index_in_dim(b, index, 0, keepdims=False)[side]  37.2 us
  transfers between devices with their start and end apart: 59, of which 22 were waited for; matrix products, arithmetic and copies ran while one was open for 40% of the time, Pallas kernels for 0%

profile of v3, /device:TPU:0, one launch (start us, length us, event | category | flops | bytes accessed | tf_op | source)
XLA Modules:
  0.0 815.1 jit_solution(6551976949709251309)
XLA Ops:
  0.7 3.2 fusion.1
  4.6 3.5 fusion.141
  14.2 6.9 fusion.139
  24.0 3.5 reshape.546
  30.5 3.5 copy.621
  35.5 4.6 convolution_convert_fusion.3
  45.4 4.3 copy.521
  64.9 3.5 collective-permute-done
  68.4 4.4 add_convert_fusion.10
  75.7 6.5 convert_element_type.435
  84.0 37.9 %collective-permute-done.1 = bf16[512,2048]{1,0:T(8,128)(2,1)} collective-permute-done((bf16[512,2048]{1,0:T(8,128)(2,1)}, bf16[512,2048]{1,0:T(8,128)(2,1)}, u32[]{:S(2)}, u32[]{:S(2)}) %collective-permute-start.1) | collective-permute-done | bytes 2097184 | tf_op jit(solution)/shard_map/ppermute | solution.py:219
  121.9 4.4 add_convert_fusion.9
  164.6 11.9 %fusion.151 = f32[1024,1536]{1,0:T(8,128)} fusion(bf16[1024,2048]{1,0:T(8,128)(2,1)} %param.35, bf16[1536,2048]{1,0:T(8,128)(2,1)} %param.34), kind=kOutput, calls=%fused_computation.402 | convolution fusion | flops 6442450944 | bytes 16777216 | tf_op jit(solution)/shard_map/dot_general | solution.py:34
  182.9 5.7 multiply_convert_fusion
  188.7 8.7 %fusion.150 = f32[1024,1536]{1,0:T(8,128)} fusion(bf16[1024,2048]{1,0:T(8,128)(2,1)S(1)} %multiply_convert_fusion, bf16[2048,1536]{1,0:T(8,128)(2,1)S(1)} %bitcast.538), kind=kOutput, calls=%fused_computation.401 | convolution fusion | flops 6442450944 | bytes 16777216 | tf_op jit(solution)/shard_map/dot_general | solution.py:24
  197.3 16.0 %multiply_convert_fusion.1 = (bf16[1024,1536]{1,0:T(8,128)(2,1)}, bf16[1024,1536]{1,0:T(8,128)(2,1)S(1)}, bf16[1024,1536]{1,0:T(8,128)(2,1)}) fusion(f32[1024,1536]{1,0:T(8,128)} %fusion.151, f32[1024,1536]{1,0:T(8,128)} %fusion.150, bf16[1024,2048]{1,0:T(8,128)(2,1)S(1)} %multiply_convert_fusion, bf16[2048,1536]{1,0:T(8,128)(2,1)} %param.32), kind=kOutput, calls=%fused_computation.25 | convolution fusion | flops 6467616768 | bytes 32505856 | tf_op jit(solution)/shard_map/dot_general | solution.py:24
  213.3 10.9 %fusion.152 = f32[1024,2048]{1,0:T(8,128)} fusion(bf16[1024,1536]{1,0:T(8,128)(2,1)S(1)} %get-tuple-element.161, bf16[2048,1536]{1,0:T(8,128)(2,1)} %param.32), kind=kOutput, calls=%fused_computation.403 | convolution fusion | flops 6442450944 | bytes 17825792 | tf_op jit(solution)/shard_map/dot_general | solution.py:34
  224.3 9.5 %fusion.153 = f32[2048,1536]{1,0:T(8,128)} fusion(bf16[1024,2048]{1,0:T(8,128)(2,1)S(1)} %multiply_convert_fusion, bf16[1024,1536]{1,0:T(8,128)(2,1)S(1)} %get-tuple-element.161), kind=kOutput, calls=%fused_computation.404 | convolution fusion | flops 6442450944 | bytes 19922944 | tf_op jit(solution)/shard_map/dot_general | solution.py:28
  233.8 8.6 %convolution_convert_fusion = bf16[1024,2048]{1,0:T(8,128)(2,1)S(1)} fusion(bf16[1024,1536]{1,0:T(8,128)(2,1)} %get-tuple-element.162, bf16[1536,2048]{1,0:T(8,128)(2,1)S(1)} %bitcast.536), kind=kOutput, calls=%fused_computation.43 | convolution fusion | flops 6444548096 | bytes 13631488 | tf_op jit(solution)/shard_map/dot_general | solution.py:24
  242.4 9.6 %convolution_bitcast_fusion = f32[2048,1536]{0,1:T(8,128)} fusion(bf16[1024,1536]{1,0:T(8,128)(2,1)S(1)} %copy-done.144, bf16[1024,2048]{1,0:T(8,128)(2,1)S(1)} %copy-done.28), kind=kOutput, calls=%fused_computation.7 | convolution fusion | flops 6442450944 | bytes 19922944 | tf_op jit(solution)/shard_map/dot_general | solution.py:28
  254.7 9.4 %fusion.154 = f32[2048,1536]{1,0:T(8,128)} fusion(bf16[1024,2048]{1,0:T(8,128)(2,1)S(1)} %multiply_convert_fusion, bf16[1024,1536]{1,0:T(8,128)(2,1)S(1)} %copy-done.145), kind=kOutput, calls=%fused_computation.405 | convolution fusion | flops 6442450944 | bytes 19922944 | tf_op jit(solution)/shard_map/dot_general | solution.py:28
  264.2 8.9 %add_convert_fusion.1 = bf16[1024,2048]{1,0:T(8,128)(2,1)S(1)} fusion(f32[1024,2048]{1,0:T(8,128)S(1)} %bitcast.540, bf16[1024,1536]{1,0:T(8,128)(2,1)S(1)} %copy-done.145, bf16[2048,1536]{1,0:T(8,128)(2,1)} %param.33), kind=kOutput, calls=%fused_computation.18 | convolution fusion | flops 6446645248 | bytes 22020096 | tf_op jit(solution)/shard_map/dot_general | solution.py:34
  277.1 15.6 %constant_dynamic-slice_fusion.9 = (f32[1,1,128,1536]{3,2,1,0:T(8,128)}, f32[1,1,128,1536]{3,2,1,0:T(8,128)}, f32[1,1,128,1536]{3,2,1,0:T(8,128)}, f32[1,1,128,1...) fusion(f32[8,2,128,1536]{3,2,1,0:T(8,128)} %bitcast.463, ...), kind=kLoop, calls=%fused_computation.324 | loop fusion | bytes 44040248 | tf_op jit(solution)/shard_map/slice | solution.py:258
  295.1 4.3 constant_dynamic-slice_fusion.1
  372.6 17.1 %reshape.554 = f32[8,2,128,1536]{2,1,0,3:T(2,128)} reshape(f32[2048,1536]{0,1:T(8,128)} %convolution_bitcast_fusion) | data formatting | bytes 25165824 | tf_op jit(solution)/shard_map/reshape | solution.py:252
  396.4 14.6 %constant_dynamic-slice_fusion.8 = (f32[1,1,128,1536]{2,1,0,3:T(1,128)S(1)}, f32[1,1,128,1536]{2,1,0,3:T(1,128)}, f32[1,1,128,1536]{2,1,0,3:T(1,128)}, f32[1,1,1...) fusion(f32[8,2,128,1536]{2,1,0,3:T(2,128)} %reshape.554, ...), kind=kLoop, calls=%fused_computation.323 | loop fusion | bytes 22020152 | tf_op jit(solution)/shard_map/slice | solution.py:258
  411.0 10.7 %collective-permute-done.45 = bf16[128,4608]{0,1:T(8,128)(2,1)S(1)} collective-permute-done((bf16[128,4608]{0,1:T(8,128)(2,1)S(1)}, bf16[128,4608]{0,1:T(8,128)(2,1)S(1)}, u32[]{:S(2)}, u32[]{:S(2)}) %collective-permute-start.45) | collective-permute-done | bytes 1179680 | tf_op jit(solution)/shard_map/ppermute | solution.py:269
  433.3 16.1 %collective-permute-done.46 = bf16[128,4608]{0,1:T(8,128)(2,1)S(1)} collective-permute-done((bf16[128,4608]{0,1:T(8,128)(2,1)S(1)}, bf16[128,4608]{0,1:T(8,128)(2,1)S(1)}, u32[]{:S(2)}, u32[]{:S(2)}) %collective-permute-start.46) | collective-permute-done | bytes 1179680 | tf_op jit(solution)/shard_map/ppermute | solution.py:269
  452.5 23.7 %collective-permute-done.47 = bf16[128,4608]{0,1:T(8,128)(2,1)S(1)} collective-permute-done((bf16[128,4608]{0,1:T(8,128)(2,1)S(1)}, bf16[128,4608]{0,1:T(8,128)(2,1)S(1)}, u32[]{:S(2)}, u32[]{:S(2)}) %collective-permute-start.47) | collective-permute-done | bytes 1179680 | tf_op jit(solution)/shard_map/ppermute | solution.py:269
  477.8 42.4 %collective-permute-done.7 = bf16[512,2048]{1,0:T(8,128)(2,1)S(1)} collective-permute-done((bf16[512,2048]{1,0:T(8,128)(2,1)S(1)}, bf16[512,2048]{1,0:T(8,128)(2,1)S(1)}, u32[]{:S(2)}, u32[]{:S(2)}) %collective-permute-start.7) | collective-permute-done | bytes 2097184 | tf_op jit(solution)/shard_map/ppermute | solution.py:219
  535.8 16.1 %convert_bitcast_fusion = (bf16[2048,1024]{0,1:T(8,128)(2,1)}, f32[1024,2048]{1,0:T(8,128)}, bf16[1024,2048]{1,0:T(8,128)(2,1)}) fusion(f32[1024]{0:T(1024)S(1)} %broadcast_multiply_fusion.3, f32[1024]{0:T(1024)S(1)} %copy-done.135, bf16[512,2048]{1,0:T(8,128)(2,1)S(1)} %copy-done.8, bf16[512,2048]{1,0:T(8,128)(2,1)S(1)} %copy-done.6, ...), kind=kLoop, calls=%fused_computation.89 | loop fusion | flops 50331648 | bytes 37769216 | tf_op jit(solution)/shard_map/dot_general | solution.py:28
  551.9 5.7 fusion.39
  566.0 6.3 broadcast_multiply_fusion.1
  572.3 6.0 fusion.35
  578.3 6.6 copy.630
  585.0 4.7 fusion.51
  599.9 5.7 fusion.47
  607.0 5.0 add_convert_fusion
  614.1 4.1 collective-permute-done.32
  631.6 20.6 %collective-permute-done.40 = bf16[128,512]{1,0:T(8,128)(2,1)S(1)} collective-permute-done((bf16[128,512]{1,0:T(8,128)(2,1)S(1)}, bf16[128,512]{1,0:T(8,128)(2,1)S(1)}, u32[]{:S(2)}, u32[]{:S(2)}) %collective-permute-start.40) | collective-permute-done | bytes 131104 | tf_op jit(solution)/shard_map/ppermute | solution.py:270
  662.0 4.2 maximum_convert_fusion
  666.2 20.5 %collective-permute-done.42 = bf16[128,512]{1,0:T(8,128)(2,1)S(1)} collective-permute-done((bf16[128,512]{1,0:T(8,128)(2,1)S(1)}, bf16[128,512]{1,0:T(8,128)(2,1)S(1)}, u32[]{:S(2)}, u32[]{:S(2)}) %collective-permute-start.42) | collective-permute-done | bytes 131104 | tf_op jit(solution)/shard_map/ppermute | solution.py:270
  688.9 12.0 %collective-permute-done.10 = bf16[512,2048]{1,0:T(8,128)(2,1)S(1)} collective-permute-done((bf16[512,2048]{1,0:T(8,128)(2,1)S(1)}, bf16[512,2048]{1,0:T(8,128)(2,1)S(1)}, u32[]{:S(2)}, u32[]{:S(2)}) %collective-permute-start.10) | collective-permute-done | bytes 2097184 | tf_op jit(solution)/shard_map/ppermute | solution.py:219
  712.1 3.4 copy-done.4
  717.1 7.2 fusion.138
  724.3 6.4 copy.632
  730.7 3.6 fusion.67
  746.0 3.4 multiply_reduce_fusion.3
  (600 shorter events, 302.3 us)
Async XLA Ops:
  72.8 49.1 %collective-permute-start.1 = (bf16[512,2048]{1,0:T(8,128)(2,1)}, bf16[512,2048]{1,0:T(8,128)(2,1)}, u32[]{:S(2)}, u32[]{:S(2)}) collective-permute-start(bf16[512,2048]{1,0:T(8,128)(2,1)} %add_convert_fusion.10), channel_id=1, source_target_pairs={{0,2},{1,3},{2,0},{3,1},{4,6},{5,7},{6,4},{7,5},{8,10},{9,11},{10,... | collective-permute-start | bytes 6291464 | tf_op jit(solution)/shard_map/ppermute | solution.py:219
  126.4 50.2 %collective-permute-start.2 = (bf16[512,2048]{1,0:T(8,128)(2,1)}, bf16[512,2048]{1,0:T(8,128)(2,1)}, u32[]{:S(2)}, u32[]{:S(2)}) collective-permute-start(bf16[512,2048]{1,0:T(8,128)(2,1)} %add_convert_fusion.9), channel_id=1, source_target_pairs={{0,1},{1,0},{2,3},{3,2},{4,5},{5,4},{6,7},{7,6},{8,9},{9,8},{10,11... | collective-permute-start | bytes 6291464 | tf_op jit(solution)/shard_map/ppermute | solution.py:221
  254.0 171.2 %collective-permute-start.3 = (bf16[512,2048]{1,0:T(8,128)(2,1)}, bf16[512,2048]{1,0:T(8,128)(2,1)}, u32[]{:S(2)}, u32[]{:S(2)}) collective-permute-start(bf16[512,2048]{1,0:T(8,128)(2,1)} %constant_dynamic-slice_fusion.48), channel_id=1, source_target_pairs={{0,1},{1,0},{2,3},{3,2},{4,5},{5,4},{6,7},{7,6},{8,9},{9,8},{10,11... | collective-permute-start | bytes 6291464 | tf_op jit(solution)/shard_map/ppermute | solution.py:217
  276.6 153.6 %collective-permute-start.6 = (bf16[512,2048]{1,0:T(8,128)(2,1)}, bf16[512,2048]{1,0:T(8,128)(2,1)}, u32[]{:S(2)}, u32[]{:S(2)}) collective-permute-start(bf16[512,2048]{1,0:T(8,128)(2,1)} %constant_dynamic-slice_fusion.46), channel_id=1, source_target_pairs={{0,1},{1,0},{2,3},{3,2},{4,5},{5,4},{6,7},{7,6},{8,9},{9,8},{10,11... | collective-permute-start | bytes 6291464 | tf_op jit(solution)/shard_map/ppermute | solution.py:217
  393.4 28.3 %collective-permute-start.45 = (bf16[128,4608]{0,1:T(8,128)(2,1)S(1)}, bf16[128,4608]{0,1:T(8,128)(2,1)S(1)}, u32[]{:S(2)}, u32[]{:S(2)}) collective-permute-start(bf16[128,4608]{0,1:T(8,128)(2,1)S(1)} %pad_maximum_fusion.1), channel_id=1, source_target_pairs={{0,8},{8,16},{16,24},{24,28},{28,20},{20,12},{12,4},{4,0},{1,9},{9... | collective-permute-start | bytes 3538952 | tf_op jit(solution)/shard_map/ppermute | solution.py:269
  395.7 28.1 %collective-permute-start.52 = (bf16[128,4608]{0,1:T(8,128)(2,1)S(1)}, bf16[128,4608]{0,1:T(8,128)(2,1)S(1)}, u32[]{:S(2)}, u32[]{:S(2)}) collective-permute-start(bf16[128,4608]{0,1:T(8,128)(2,1)S(1)} %pad_maximum_fusion.2), channel_id=1, source_target_pairs={{8,0},{16,8},{24,16},{28,24},{20,28},{12,20},{4,12},{0,4},{9,1},{1... | collective-permute-start | bytes 3538952 | tf_op jit(solution)/shard_map/ppermute | solution.py:270
  422.0 27.3 %collective-permute-start.46 = (bf16[128,4608]{0,1:T(8,128)(2,1)S(1)}, bf16[128,4608]{0,1:T(8,128)(2,1)S(1)}, u32[]{:S(2)}, u32[]{:S(2)}) collective-permute-start(bf16[128,4608]{0,1:T(8,128)(2,1)S(1)} %fusion.12), channel_id=1, source_target_pairs={{0,8},{8,16},{16,24},{24,28},{28,20},{20,12},{12,4},{4,0},{1,9},{9... | collective-permute-start | bytes 3538952 | tf_op jit(solution)/shard_map/ppermute | solution.py:269
  424.1 27.1 %collective-permute-start.53 = (bf16[128,4608]{0,1:T(8,128)(2,1)S(1)}, bf16[128,4608]{0,1:T(8,128)(2,1)S(1)}, u32[]{:S(2)}, u32[]{:S(2)}) collective-permute-start(bf16[128,4608]{0,1:T(8,128)(2,1)S(1)} %fusion.18), channel_id=1, source_target_pairs={{8,0},{16,8},{24,16},{28,24},{20,28},{12,20},{4,12},{0,4},{9,1},{1... | collective-permute-start | bytes 3538952 | tf_op jit(solution)/shard_map/ppermute | solution.py:270
  428.7 95.3 %collective-permute-start.4 = (bf16[512,2048]{1,0:T(8,128)(2,1)S(1)}, bf16[512,2048]{1,0:T(8,128)(2,1)S(1)}, u32[]{:S(2)}, u32[]{:S(2)}) collective-permute-start(bf16[512,2048]{1,0:T(8,128)(2,1)S(1)} %add_convert_fusion.8), channel_id=1, source_target_pairs={{0,2},{1,3},{2,0},{3,1},{4,6},{5,7},{6,4},{7,5},{8,10},{9,11},{10,... | collective-permute-start | bytes 6291464 | tf_op jit(solution)/shard_map/ppermute | solution.py:219
  432.7 87.5 %collective-permute-start.7 = (bf16[512,2048]{1,0:T(8,128)(2,1)S(1)}, bf16[512,2048]{1,0:T(8,128)(2,1)S(1)}, u32[]{:S(2)}, u32[]{:S(2)}) collective-permute-start(bf16[512,2048]{1,0:T(8,128)(2,1)S(1)} %add_convert_fusion.6), channel_id=1, source_target_pairs={{0,2},{1,3},{2,0},{3,1},{4,6},{5,7},{6,4},{7,5},{8,10},{9,11},{10,... | collective-permute-start | bytes 6291464 | tf_op jit(solution)/shard_map/ppermute | solution.py:219
  449.7 26.5 %collective-permute-start.47 = (bf16[128,4608]{0,1:T(8,128)(2,1)S(1)}, bf16[128,4608]{0,1:T(8,128)(2,1)S(1)}, u32[]{:S(2)}, u32[]{:S(2)}) collective-permute-start(bf16[128,4608]{0,1:T(8,128)(2,1)S(1)} %fusion.13), channel_id=1, source_target_pairs={{0,8},{8,16},{16,24},{24,28},{28,20},{20,12},{12,4},{4,0},{1,9},{9... | collective-permute-start | bytes 3538952 | tf_op jit(solution)/shard_map/ppermute | solution.py:269
  451.5 69.5 %collective-permute-start.54 = (bf16[128,4608]{0,1:T(8,128)(2,1)S(1)}, bf16[128,4608]{0,1:T(8,128)(2,1)S(1)}, u32[]{:S(2)}, u32[]{:S(2)}) collective-permute-start(bf16[128,4608]{0,1:T(8,128)(2,1)S(1)} %fusion.19), channel_id=1, source_target_pairs={{8,0},{16,8},{24,16},{28,24},{20,28},{12,20},{4,12},{0,4},{9,1},{1... | collective-permute-start | bytes 3538952 | tf_op jit(solution)/shard_map/ppermute | solution.py:270
  476.4 48.6 %collective-permute-start.48 = (bf16[128,4608]{0,1:T(8,128)(2,1)S(1)}, bf16[128,4608]{0,1:T(8,128)(2,1)S(1)}, u32[]{:S(2)}, u32[]{:S(2)}) collective-permute-start(bf16[128,4608]{0,1:T(8,128)(2,1)S(1)} %fusion.14), channel_id=1, source_target_pairs={{0,8},{8,16},{16,24},{24,28},{28,20},{20,12},{12,4},{4,0},{1,9},{9... | collective-permute-start | bytes 3538952 | tf_op jit(solution)/shard_map/ppermute | solution.py:269
  522.3 98.1 %collective-permute-start.55 = (bf16[128,4608]{0,1:T(8,128)(2,1)}, bf16[128,4608]{0,1:T(8,128)(2,1)}, u32[]{:S(2)}, u32[]{:S(2)}) collective-permute-start(bf16[128,4608]{0,1:T(8,128)(2,1)} %fusion.20), channel_id=1, source_target_pairs={{8,0},{16,8},{24,16},{28,24},{20,28},{12,20},{4,12},{0,4},{9,1},{1... | collective-permute-start | bytes 3538952 | tf_op jit(solution)/shard_map/ppermute | solution.py:270
  524.8 8.7 %collective-permute-start.5 = (bf16[512,2048]{1,0:T(8,128)(2,1)S(1)}, bf16[512,2048]{1,0:T(8,128)(2,1)S(1)}, u32[]{:S(2)}, u32[]{:S(2)}) collective-permute-start(bf16[512,2048]{1,0:T(8,128)(2,1)S(1)} %add_convert_fusion.7), channel_id=1, source_target_pairs={{0,1},{1,0},{2,3},{3,2},{4,5},{5,4},{6,7},{7,6},{8,9},{9,8},{10,11... | collective-permute-start | bytes 6291464 | tf_op jit(solution)/shard_map/ppermute | solution.py:221
  526.3 101.0 %collective-permute-start.49 = (bf16[128,4608]{0,1:T(8,128)(2,1)}, bf16[128,4608]{0,1:T(8,128)(2,1)}, u32[]{:S(2)}, u32[]{:S(2)}) collective-permute-start(bf16[128,4608]{0,1:T(8,128)(2,1)} %fusion.15), channel_id=1, source_target_pairs={{0,8},{8,16},{16,24},{24,28},{28,20},{20,12},{12,4},{4,0},{1,9},{9... | collective-permute-start | bytes 3538952 | tf_op jit(solution)/shard_map/ppermute | solution.py:269
  590.5 21.6 %collective-permute-start.31 = (bf16[128,512]{1,0:T(8,128)(2,1)}, bf16[128,512]{1,0:T(8,128)(2,1)}, u32[]{:S(2)}, u32[]{:S(2)}) collective-permute-start(bf16[128,512]{1,0:T(8,128)(2,1)} %get-tuple-element.183), channel_id=1, source_target_pairs={{0,8},{8,16},{16,24},{24,28},{28,20},{20,12},{12,4},{4,0},{1,9},{9... | collective-permute-start | bytes 393224 | tf_op jit(solution)/shard_map/ppermute | solution.py:269
  591.2 22.8 %collective-permute-start.38 = (bf16[128,512]{1,0:T(8,128)(2,1)S(1)}, bf16[128,512]{1,0:T(8,128)(2,1)S(1)}, u32[]{:S(2)}, u32[]{:S(2)}) collective-permute-start(bf16[128,512]{1,0:T(8,128)(2,1)S(1)} %get-tuple-element.184), channel_id=1, source_target_pairs={{8,0},{16,8},{24,16},{28,24},{20,28},{12,20},{4,12},{0,4},{9,1},{1... | collective-permute-start | bytes 393224 | tf_op jit(solution)/shard_map/ppermute | solution.py:270
  614.0 40.5 %collective-permute-start.9 = (bf16[512,2048]{1,0:T(8,128)(2,1)S(1)}, bf16[512,2048]{1,0:T(8,128)(2,1)S(1)}, u32[]{:S(2)}, u32[]{:S(2)}) collective-permute-start(bf16[512,2048]{1,0:T(8,128)(2,1)S(1)} %constant_dynamic-slice_fusion.44), channel_id=1, source_target_pairs={{0,1},{1,0},{2,3},{3,2},{4,5},{5,4},{6,7},{7,6},{8,9},{9,8},{10,11... | collective-permute-start | bytes 6291464 | tf_op jit(solution)/shard_map/ppermute | solution.py:217
  622.1 34.8 %collective-permute-start.56 = (bf16[128,4608]{0,1:T(8,128)(2,1)S(1)}, bf16[128,4608]{0,1:T(8,128)(2,1)S(1)}, u32[]{:S(2)}, u32[]{:S(2)}) collective-permute-start(bf16[128,4608]{0,1:T(8,128)(2,1)S(1)} %fusion.21), channel_id=1, source_target_pairs={{8,0},{16,8},{24,16},{28,24},{20,28},{12,20},{4,12},{0,4},{9,1},{1... | collective-permute-start | bytes 3538952 | tf_op jit(solution)/shard_map/ppermute | solution.py:270
  627.1 25.1 %collective-permute-start.40 = (bf16[128,512]{1,0:T(8,128)(2,1)S(1)}, bf16[128,512]{1,0:T(8,128)(2,1)S(1)}, u32[]{:S(2)}, u32[]{:S(2)}) collective-permute-start(bf16[128,512]{1,0:T(8,128)(2,1)S(1)} %get-tuple-element.180), channel_id=1, source_target_pairs={{8,0},{16,8},{24,16},{28,24},{20,28},{12,20},{4,12},{0,4},{9,1},{1... | collective-permute-start | bytes 393224 | tf_op jit(solution)/shard_map/ppermute | solution.py:270
  628.8 73.0 %collective-permute-start.50 = (bf16[128,4608]{0,1:T(8,128)(2,1)S(1)}, bf16[128,4608]{0,1:T(8,128)(2,1)S(1)}, u32[]{:S(2)}, u32[]{:S(2)}) collective-permute-start(bf16[128,4608]{0,1:T(8,128)(2,1)S(1)} %fusion.16), channel_id=1, source_target_pairs={{0,8},{8,16},{16,24},{24,28},{28,20},{20,12},{12,4},{4,0},{1,9},{9... | collective-permute-start | bytes 3538952 | tf_op jit(solution)/shard_map/ppermute | solution.py:269
  655.4 45.5 %collective-permute-start.10 = (bf16[512,2048]{1,0:T(8,128)(2,1)S(1)}, bf16[512,2048]{1,0:T(8,128)(2,1)S(1)}, u32[]{:S(2)}, u32[]{:S(2)}) collective-permute-start(bf16[512,2048]{1,0:T(8,128)(2,1)S(1)} %add_convert_fusion.4), channel_id=1, source_target_pairs={{0,2},{1,3},{2,0},{3,1},{4,6},{5,7},{6,4},{7,5},{8,10},{9,11},{10,... | collective-permute-start | bytes 6291464 | tf_op jit(solution)/shard_map/ppermute | solution.py:219
  657.2 48.7 %collective-permute-start.57 = (bf16[128,4608]{0,1:T(8,128)(2,1)S(1)}, bf16[128,4608]{0,1:T(8,128)(2,1)S(1)}, u32[]{:S(2)}, u32[]{:S(2)}) collective-permute-start(bf16[128,4608]{0,1:T(8,128)(2,1)S(1)} %fusion.22), channel_id=1, source_target_pairs={{8,0},{16,8},{24,16},{28,24},{20,28},{12,20},{4,12},{0,4},{9,1},{1... | collective-permute-start | bytes 3538952 | tf_op jit(solution)/shard_map/ppermute | solution.py:270
  661.7 25.1 %collective-permute-start.42 = (bf16[128,512]{1,0:T(8,128)(2,1)S(1)}, bf16[128,512]{1,0:T(8,128)(2,1)S(1)}, u32[]{:S(2)}, u32[]{:S(2)}) collective-permute-start(bf16[128,512]{1,0:T(8,128)(2,1)S(1)} %get-tuple-element.176), channel_id=1, source_target_pairs={{8,0},{16,8},{24,16},{28,24},{20,28},{12,20},{4,12},{0,4},{9,1},{1... | collective-permute-start | bytes 393224 | tf_op jit(solution)/shard_map/ppermute | solution.py:270
  686.8 17.4 %collective-permute-start.37 = (bf16[128,512]{1,0:T(8,128)(2,1)S(1)}, bf16[128,512]{1,0:T(8,128)(2,1)S(1)}, u32[]{:S(2)}, u32[]{:S(2)}) collective-permute-start(bf16[128,512]{1,0:T(8,128)(2,1)S(1)} %get-tuple-element.173), channel_id=1, source_target_pairs={{0,8},{8,16},{16,24},{24,28},{28,20},{20,12},{12,4},{4,0},{1,9},{9... | collective-permute-start | bytes 393224 | tf_op jit(solution)/shard_map/ppermute | solution.py:269
  688.1 16.0 %collective-permute-start.43 = (bf16[128,512]{1,0:T(8,128)(2,1)S(1)}, bf16[128,512]{1,0:T(8,128)(2,1)S(1)}, u32[]{:S(2)}, u32[]{:S(2)}) collective-permute-start(bf16[128,512]{1,0:T(8,128)(2,1)S(1)} %get-tuple-element.174), channel_id=1, source_target_pairs={{8,0},{16,8},{24,16},{28,24},{20,28},{12,20},{4,12},{0,4},{9,1},{1... | collective-permute-start | bytes 393224 | tf_op jit(solution)/shard_map/ppermute | solution.py:270
  701.7 10.1 %collective-permute-start.11 = (bf16[512,2048]{1,0:T(8,128)(2,1)S(1)}, bf16[512,2048]{1,0:T(8,128)(2,1)S(1)}, u32[]{:S(2)}, u32[]{:S(2)}) collective-permute-start(bf16[512,2048]{1,0:T(8,128)(2,1)S(1)} %add_convert_fusion.3), channel_id=1, source_target_pairs={{0,1},{1,0},{2,3},{3,2},{4,5},{5,4},{6,7},{7,6},{8,9},{9,8},{10,11... | collective-permute-start | bytes 6291464 | tf_op jit(solution)/shard_map/ppermute | solution.py:221
  703.1 66.0 %collective-permute-start.51 = (bf16[128,4608]{0,1:T(8,128)(2,1)}, bf16[128,4608]{0,1:T(8,128)(2,1)}, u32[]{:S(2)}, u32[]{:S(2)}) collective-permute-start(bf16[128,4608]{0,1:T(8,128)(2,1)} %fusion.17), channel_id=1, source_target_pairs={{0,8},{8,16},{16,24},{24,28},{28,20},{20,12},{12,4},{4,0},{1,9},{9... | collective-permute-start | bytes 3538952 | tf_op jit(solution)/shard_map/ppermute | solution.py:269
  707.3 69.1 %collective-permute-start.58 = (bf16[128,4608]{0,1:T(8,128)(2,1)}, bf16[128,4608]{0,1:T(8,128)(2,1)}, u32[]{:S(2)}, u32[]{:S(2)}) collective-permute-start(bf16[128,4608]{0,1:T(8,128)(2,1)} %fusion.23), channel_id=1, source_target_pairs={{8,0},{16,8},{24,16},{28,24},{20,28},{12,20},{4,12},{0,4},{9,1},{1... | collective-permute-start | bytes 3538952 | tf_op jit(solution)/shard_map/ppermute | solution.py:270
  744.2 8.5 %collective-permute-start.17 = (bf16[128,1024]{1,0:T(8,128)(2,1)S(1)}, bf16[128,1024]{1,0:T(8,128)(2,1)S(1)}, u32[]{:S(2)}, u32[]{:S(2)}) collective-permute-start(bf16[128,1024]{1,0:T(8,128)(2,1)S(1)} %pad_maximum_fusion.4), channel_id=1, source_target_pairs={{0,8},{8,16},{16,24},{24,28},{28,20},{20,12},{12,4},{4,0},{1,9},{9... | collective-permute-start | bytes 786440 | tf_op jit(solution)/shard_map/ppermute | solution.py:269
  749.5 8.8 %collective-permute-start.24 = (bf16[128,1024]{1,0:T(8,128)(2,1)S(1)}, bf16[128,1024]{1,0:T(8,128)(2,1)S(1)}, u32[]{:S(2)}, u32[]{:S(2)}) collective-permute-start(bf16[128,1024]{1,0:T(8,128)(2,1)S(1)} %pad_maximum_fusion.5), channel_id=1, source_target_pairs={{8,0},{16,8},{24,16},{28,24},{20,28},{12,20},{4,12},{0,4},{9,1},{1... | collective-permute-start | bytes 786440 | tf_op jit(solution)/shard_map/ppermute | solution.py:270
  751.3 9.1 %collective-permute-start.13 = (f32[4352]{0:T(1024)}, f32[4352]{0:T(1024)}, u32[]{:S(2)}, u32[]{:S(2)}) collective-permute-start(f32[4352]{0:T(1024)} %fusion.137), channel_id=1, source_target_pairs={{0,2},{1,3},{2,0},{3,1},{4,6},{5,7},{6,4},{7,5},{8,10},{9,11},{10,... | collective-permute-start | bytes 52232 | tf_op jit(solution)/shard_map/ppermute | solution.py:239
  753.5 8.8 %collective-permute-start.18 = (bf16[128,1024]{1,0:T(8,128)(2,1)}, bf16[128,1024]{1,0:T(8,128)(2,1)}, u32[]{:S(2)}, u32[]{:S(2)}) collective-permute-start(bf16[128,1024]{1,0:T(8,128)(2,1)} %fusion.71), channel_id=1, source_target_pairs={{0,8},{8,16},{16,24},{24,28},{28,20},{20,12},{12,4},{4,0},{1,9},{9... | collective-permute-start | bytes 786440 | tf_op jit(solution)/shard_map/ppermute | solution.py:269
  759.0 8.3 %collective-permute-start.25 = (bf16[128,1024]{1,0:T(8,128)(2,1)}, bf16[128,1024]{1,0:T(8,128)(2,1)}, u32[]{:S(2)}, u32[]{:S(2)}) collective-permute-start(bf16[128,1024]{1,0:T(8,128)(2,1)} %fusion.77), channel_id=1, source_target_pairs={{8,0},{16,8},{24,16},{28,24},{20,28},{12,20},{4,12},{0,4},{9,1},{1... | collective-permute-start | bytes 786440 | tf_op jit(solution)/shard_map/ppermute | solution.py:270
  761.2 9.6 %collective-permute-start.14 = (f32[4352]{0:T(1024)S(1)}, f32[4352]{0:T(1024)S(1)}, u32[]{:S(2)}, u32[]{:S(2)}) collective-permute-start(f32[4352]{0:T(1024)S(1)} %add.1066), channel_id=1, source_target_pairs={{0,4},{4,0},{8,12},{12,8},{16,20},{20,16},{24,28},{28,24},{1,5},{5... | collective-permute-start | bytes 52232 | tf_op jit(solution)/shard_map/ppermute | solution.py:239
  763.5 8.9 %collective-permute-start.19 = (bf16[128,1024]{1,0:T(8,128)(2,1)S(1)}, bf16[128,1024]{1,0:T(8,128)(2,1)S(1)}, u32[]{:S(2)}, u32[]{:S(2)}) collective-permute-start(bf16[128,1024]{1,0:T(8,128)(2,1)S(1)} %fusion.72), channel_id=1, source_target_pairs={{0,8},{8,16},{16,24},{24,28},{28,20},{20,12},{12,4},{4,0},{1,9},{9... | collective-permute-start | bytes 786440 | tf_op jit(solution)/shard_map/ppermute | solution.py:269
  768.5 7.4 collective-permute-start.26
  770.8 7.2 collective-permute-start.15
  772.5 9.0 %collective-permute-start.20 = (bf16[128,1024]{1,0:T(8,128)(2,1)S(1)}, bf16[128,1024]{1,0:T(8,128)(2,1)S(1)}, u32[]{:S(2)}, u32[]{:S(2)}) collective-permute-start(bf16[128,1024]{1,0:T(8,128)(2,1)S(1)} %fusion.73), channel_id=1, source_target_pairs={{0,8},{8,16},{16,24},{24,28},{28,20},{20,12},{12,4},{4,0},{1,9},{9... | collective-permute-start | bytes 786440 | tf_op jit(solution)/shard_map/ppermute | solution.py:269
  776.0 7.9 collective-permute-start.27
  778.6 14.9 %collective-permute-start.16 = (f32[4352]{0:T(1024)}, f32[4352]{0:T(1024)}, u32[]{:S(2)}, u32[]{:S(2)}) collective-permute-start(f32[4352]{0:T(1024)} %add.1068), channel_id=1, source_target_pairs={{0,16},{4,20},{8,24},{12,28},{16,0},{20,4},{24,8},{28,12},{1,17},{... | collective-permute-start | bytes 52232 | tf_op jit(solution)/shard_map/ppermute | solution.py:239
  782.3 12.1 %collective-permute-start.21 = (bf16[128,1024]{1,0:T(8,128)(2,1)}, bf16[128,1024]{1,0:T(8,128)(2,1)}, u32[]{:S(2)}, u32[]{:S(2)}) collective-permute-start(bf16[128,1024]{1,0:T(8,128)(2,1)} %fusion.74), channel_id=1, source_target_pairs={{0,8},{8,16},{16,24},{24,28},{28,20},{20,12},{12,4},{4,0},{1,9},{9... | collective-permute-start | bytes 786440 | tf_op jit(solution)/shard_map/ppermute | solution.py:269
  784.6 12.5 %collective-permute-start.28 = (bf16[128,1024]{1,0:T(8,128)(2,1)}, bf16[128,1024]{1,0:T(8,128)(2,1)}, u32[]{:S(2)}, u32[]{:S(2)}) collective-permute-start(bf16[128,1024]{1,0:T(8,128)(2,1)} %fusion.80), channel_id=1, source_target_pairs={{8,0},{16,8},{24,16},{28,24},{20,28},{12,20},{4,12},{0,4},{9,1},{1... | collective-permute-start | bytes 786440 | tf_op jit(solution)/shard_map/ppermute | solution.py:270
  795.5 7.0 collective-permute-start.22
  798.3 8.1 collective-permute-start.29
  803.5 6.4 collective-permute-start.23
  806.5 6.4 collective-permute-start.30
  (165 other events, 1374.3 us)

commit v4 on v3

--- a/solution.py
+++ b/solution.py
@@ -6,7 +6,6 @@
 import numpy as np
 from jax import lax
 from jax.sharding import PartitionSpec as P
-
 
 HEAD_SIZE = 128
 LEN = 128
@@ -103,7 +102,7 @@
 
 
 def attend_back(
-    upstream, q_raw, k_raw, query_gain, key_gain, queries, keys_rot, values, logsum, seqs
+    upstream, q_raw, k_raw, query_gain, key_gain, queries, keys_rot, values, logsum, seqs, hook
 ):
     total = q_raw.shape[0]
     length = total // seqs
@@ -114,14 +113,18 @@
     grad_out = upstream.reshape(seqs, length, kv_heads, repeat, HEAD_SIZE)
     scores = causal_scores(queries, keys_rot, length)
     probs = jnp.exp(scores - logsum)
+    probs = hook(probs)
     value_grad = product("sgrqk,sqgrd->skgd", probs.astype(jnp.bfloat16), grad_out)
     prob_grad = product("sqgrd,skgd->sgrqk", grad_out, values)
+    value_grad, prob_grad = hook((value_grad, prob_grad))
     center = jnp.sum(probs * prob_grad, -1, keepdims=True)
     score_grad = (probs * (prob_grad - center) * (1.0 / math.sqrt(HEAD_SIZE))).astype(jnp.bfloat16)
+    score_grad = hook(score_grad)
     query_rot_grad = product("sgrqk,skgd->sqgrd", score_grad, keys_rot).reshape(
         seqs, length, heads, HEAD_SIZE
     )
     key_rot_grad = product("sgrqk,sqgrd->skgd", score_grad, queries)
+    query_rot_grad, key_rot_grad = hook((query_rot_grad, key_rot_grad))
     query_in = q_raw.reshape(seqs, length, heads, HEAD_SIZE)
     key_in = k_raw.reshape(seqs, length, kv_heads, HEAD_SIZE)
     _, pull_query = jax.vjp(
@@ -132,6 +135,7 @@
         lambda inner, gain: head_prep(inner, gain, cosine, sine), key_in, key_gain
     )
     key_grad, key_gain_grad = pull_key(key_rot_grad)
+    query_grad, key_grad = hook((query_grad, key_grad))
     return (
         query_grad.astype(jnp.bfloat16).reshape(total, heads * HEAD_SIZE),
         key_grad.astype(jnp.bfloat16).reshape(total, kv_heads * HEAD_SIZE),
@@ -249,13 +253,16 @@
         self.pos = jnp.array(plan.pos, jnp.int32)[self.me]
         self.order = jnp.array(plan.ring, jnp.int32)
         self.widths = [g.shape[1] for g in grads]
-        self.blocks = [g.reshape(n, 2, g.shape[0] // n // 2, g.shape[1]) for g in grads]
+        self.grads = grads
+        self.rows = grads[0].shape[0] // n
         self.steps = n - 1
         self.done = 0
         self.state = None
 
     def piece(self, index, side):
-        parts = [lax.dynamic_index_in_dim(b, index, 0, keepdims=False)[side] for b in self.blocks]
+        half = self.rows // 2
+        start = index * self.rows + side * half
+        parts = [lax.dynamic_slice_in_dim(g, start, half, 0) for g in self.grads]
         return parts[0] if len(parts) == 1 else jnp.concatenate(parts, 1)
 
     def step(self):
@@ -340,11 +347,30 @@
         out_w_grad_t = inner_rows(resid_low, attended)
         attended_grad = outer_cols(resid_low, w_out).astype(jnp.bfloat16)
         small = Ring(plan, [out_w_grad_t])
-        for _ in range(big.steps - 1):
-            big.step()
-            small.step()
+
+        def hook(values):
+            if big.done < big.steps:
+                big.step()
+            if small.done < small.steps:
+                small.step()
+            big.state, small.state, values = lax.optimization_barrier(
+                (big.state, small.state, values)
+            )
+            return values
+
+        resid_grad, attended_grad = hook((resid_grad, attended_grad))
         q_grad, k_grad, v_grad, qg_part, kg_part = attend_back(
-            attended_grad, q_raw, k_raw, query_gain, key_gain, queries, keys_rot, values, logsum, seqs
+            attended_grad,
+            q_raw,
+            k_raw,
+            query_gain,
+            key_gain,
+            queries,
+            keys_rot,
+            values,
+            logsum,
+            seqs,
+            hook,
         )
         in_part = (
             outer_cols(q_grad, w_query)
@@ -354,7 +380,10 @@
         query_w_grad = inner_rows(normed_in, q_grad)
         key_w_grad = inner_rows(normed_in, k_grad)
         value_w_grad = inner_rows(normed_in, v_grad)
-        small.step()
+        while big.done < big.steps:
+            big.step()
+        while small.done < small.steps:
+            small.step()
         in_grad = plan.tp_sum(in_part).astype(jnp.float32)
         down_sum, gate_sum, up_sum = big.result()
         (out_sum,) = small.result()

time: 826 us -> 755 us (0.914)
  local copies, waits for them, and re-layouts: 215 us -> 98.5 us
  waiting for transfers between devices: 217 us -> 270 us
  other arithmetic: 121 us -> 143 us
  between operations: 41 us -> 23.4 us
  matrix products: 159 us -> 147 us
    unnamed x345 -> x300, local copies, waits for them, and re-layouts: 99.3 us -> 30.1 us
    ppermute x4, waiting for transfers between devices: 92.3 us -> 148 us  [tp_sum(): other = lax.ppermute(chip_sum, 'tensor', self.chip_pairs)]
    slice x7 -> x0, local copies, waits for them, and re-layouts: 37.2 us -> none  [piece(): lax.dynamic_index_in_dim(b, index, 0, keepdims=False)[side]]
    dynamic_slice x2 -> x7, local copies, waits for them, and re-layouts: 6.85 us -> 31 us  [piece(): parts = [lax.dynamic_slice_in_dim(g, start, half, 0) for g in self.grads]]
    dot_general x2 -> x0, other arithmetic: 23.3 us -> none  [inner_rows(): lax.dot_general(left, right, (((0,), (0,)), ((), ())), preferred_element_...]
    ppermute x21, waiting for transfers between devices: 61.3 us -> 38.6 us  [step(): got_a = lax.ppermute(send_a.astype(jnp.bfloat16), 'dp', self.plan.cw)]
    add x0 -> x2, other arithmetic: none -> 22.3 us  [the longest x1 14.5 us: body(): cotangent.astype(jnp.float32) + norm_back(resid, mlp_gain, mid_grad)]
    ppermute x21, waiting for transfers between devices: 58.9 us -> 76.4 us  [step(): got_b = lax.ppermute(send_b.astype(jnp.bfloat16), 'dp', self.plan.ccw)]
  transfers between devices with their start and end apart: 59 -> 59, of which waited for: 22 -> 25; matrix products, arithmetic and copies ran while one was open for 40% -> 23% of each run, Pallas kernels for 0% -> 0%
where the time goes in v4:
time: 755 us; the launch traced here: 745 us
  waiting for transfers between devices  270 us (36%)
  matrix products  147 us (19%)
  other arithmetic  143 us (19%)
  local copies, waits for them, and re-layouts  98.5 us (13%)
  starting transfers between devices  63.6 us (8%)
  between operations  23.4 us (3%)
    ppermute x4, waiting for transfers between devices, tp_sum(): other = lax.ppermute(chip_sum, 'tensor', self.chip_pairs)  148 us
    ppermute x21, waiting for transfers between devices, step(): got_b = lax.ppermute(send_b.astype(jnp.bfloat16), 'dp', self.plan.ccw)  76.4 us
    dot_general x7, matrix products, outer_cols(): lax.dot_general(left, right, (((1,), (1,)), ((), ())), preferred_element_...  50.8 us
    dot_general x7, matrix products, matmul(): return jnp.dot(left, right, preferred_element_type=jnp.float32)  49.3 us
    dot_general x7, matrix products, inner_rows(): lax.dot_general(left, right, (((0,), (0,)), ((), ())), preferred_element_...  43.3 us
    ppermute x21, waiting for transfers between devices, step(): got_a = lax.ppermute(send_a.astype(jnp.bfloat16), 'dp', self.plan.cw)  38.6 us
    dynamic_slice x7, local copies, waits for them, and re-layouts, piece(): parts = [lax.dynamic_slice_in_dim(g, start, half, 0) for g in self.grads]  31 us
    unnamed x300, local copies, waits for them, and re-layouts  30.1 us
  transfers between devices with their start and end apart: 59, of which 25 were waited for; matrix products, arithmetic and copies ran while one was open for 23% of the time, Pallas kernels for 0%

profile of v4, /device:TPU:0, one launch (start us, length us, event | category | flops | bytes accessed | tf_op | source)
XLA Modules:
  0.0 745.4 jit_solution(14773820533480845926)
XLA Ops:
  0.7 3.2 fusion.1
  15.9 6.9 fusion.98
  25.7 3.5 reshape.471
  32.1 3.5 copy.275
  36.8 4.5 convolution_convert_fusion.3
  46.6 4.6 copy.229
  67.6 3.5 collective-permute-done
  71.0 3.0 add_convert_fusion.10
  74.1 2.9 collective-permute-start.1
  77.0 45.9 %collective-permute-done.1 = bf16[512,2048]{1,0:T(8,128)(2,1)S(1)} collective-permute-done((bf16[512,2048]{1,0:T(8,128)(2,1)S(1)}, bf16[512,2048]{1,0:T(8,128)(2,1)S(1)}, u32[]{:S(2)}, u32[]{:S(2)}) %collective-permute-start.1) | collective-permute-done | bytes 2097184 | tf_op jit(solution)/shard_map/ppermute | solution.py:223
  145.3 12.0 %fusion.101 = f32[1024,1536]{1,0:T(8,128)} fusion(bf16[1024,2048]{1,0:T(8,128)(2,1)} %param.35, bf16[1536,2048]{1,0:T(8,128)(2,1)} %param.34), kind=kOutput, calls=%fused_computation.347 | convolution fusion | flops 6442450944 | bytes 16777216 | tf_op jit(solution)/shard_map/dot_general | solution.py:33
  160.8 4.2 convert_add_fusion
  165.0 5.4 multiply_convert_fusion
  170.5 8.6 %fusion.99 = f32[1024,1536]{1,0:T(8,128)} fusion(bf16[1024,2048]{1,0:T(8,128)(2,1)S(1)} %multiply_convert_fusion, bf16[2048,1536]{1,0:T(8,128)(2,1)S(1)} %bitcast.197), kind=kOutput, calls=%fused_computation.345 | convolution fusion | flops 6442450944 | bytes 16777216 | tf_op jit(solution)/shard_map/dot_general | solution.py:23
  179.1 16.1 %fusion.10 = (bf16[1024,1536]{1,0:T(8,128)(2,1)}, bf16[1024,1536]{1,0:T(8,128)(2,1)}, bf16[1024,1536]{1,0:T(8,128)(2,1)}) fusion(f32[1024,1536]{1,0:T(8,128)} %fusion.101, f32[1024,1536]{1,0:T(8,128)} %fusion.99, bf16[1024,2048]{1,0:T(8,128)(2,1)S(1)} %multiply_convert_fusion, bf16[2048,1536]{1,0:T(8,128)(2,1)} %param.32), kind=kOutput, calls=%fused_computation.23 | convolution fusion | flops 6467616768 | bytes 32505856 | tf_op jit(solution)/shard_map/dot_general | solution.py:23
  195.2 12.0 %fusion.104 = f32[1024,2048]{1,0:T(8,128)} fusion(bf16[1024,1536]{1,0:T(8,128)(2,1)} %get-tuple-element.226, bf16[2048,1536]{1,0:T(8,128)(2,1)} %param.32), kind=kOutput, calls=%fused_computation.350 | convolution fusion | flops 6442450944 | bytes 17825792 | tf_op jit(solution)/shard_map/dot_general | solution.py:33
  207.1 9.8 %fusion.102 = f32[2048,1536]{0,1:T(8,128)} fusion(bf16[1024,2048]{1,0:T(8,128)(2,1)S(1)} %multiply_convert_fusion, bf16[1024,1536]{1,0:T(8,128)(2,1)S(1)} %copy-done.141), kind=kOutput, calls=%fused_computation.348 | convolution fusion | flops 6442450944 | bytes 19922944 | tf_op jit(solution)/shard_map/dot_general | solution.py:27
  216.9 8.6 %convolution_convert_fusion = bf16[1024,2048]{1,0:T(8,128)(2,1)S(1)} fusion(bf16[1024,1536]{1,0:T(8,128)(2,1)} %get-tuple-element.228, bf16[1536,2048]{1,0:T(8,128)(2,1)S(1)} %bitcast.195), kind=kOutput, calls=%fused_computation.42 | convolution fusion | flops 6444548096 | bytes 13631488 | tf_op jit(solution)/shard_map/dot_general | solution.py:23
  225.6 13.1 %fusion.100 = f32[1536,2048]{1,0:T(8,128)} fusion(bf16[1024,1536]{1,0:T(8,128)(2,1)} %get-tuple-element.228, bf16[1024,2048]{1,0:T(8,128)(2,1)S(1)} %copy-done.33), kind=kOutput, calls=%fused_computation.346 | convolution fusion | flops 6442450944 | bytes 19922944 | tf_op jit(solution)/shard_map/dot_general | solution.py:27
  241.3 9.5 %fusion.103 = f32[2048,1536]{0,1:T(8,128)} fusion(bf16[1024,2048]{1,0:T(8,128)(2,1)S(1)} %multiply_convert_fusion, bf16[1024,1536]{1,0:T(8,128)(2,1)S(1)} %copy-done.142), kind=kOutput, calls=%fused_computation.349 | convolution fusion | flops 6442450944 | bytes 19922944 | tf_op jit(solution)/shard_map/dot_general | solution.py:27
  250.8 11.4 %add_convert_fusion.1 = bf16[1024,2048]{1,0:T(8,128)(2,1)S(1)} fusion(f32[1024,2048]{1,0:T(8,128)} %fusion.104, bf16[1024,1536]{1,0:T(8,128)(2,1)} %get-tuple-element.227, bf16[2048,1536]{1,0:T(8,128)(2,1)} %param.33), kind=kOutput, calls=%fused_computation.17 | convolution fusion | flops 6446645248 | bytes 22020096 | tf_op jit(solution)/shard_map/dot_general | solution.py:33
  272.4 8.5 %constant_dynamic-slice_fusion.72 = (f32[128,1536]{0,1:T(8,128)}, f32[128,1536]{0,1:T(8,128)}, f32[128,1536]{0,1:T(8,128)}, f32[128,1536]{0,1:T(8,128)}, f32[128...) fusion(f32[2048,1536]{0,1:T(8,128)} %fusion.103, ...), kind=kLoop, calls=%fused_computation.314 | loop fusion | bytes 22020152 | tf_op jit(solution)/shard_map/dynamic_slice | solution.py:265
  280.9 8.5 %constant_dynamic-slice_fusion.71 = (f32[128,1536]{0,1:T(8,128)}, f32[128,1536]{0,1:T(8,128)}, f32[128,1536]{0,1:T(8,128)}, f32[128,1536]{0,1:T(8,128)}, f32[128...) fusion(f32[2048,1536]{0,1:T(8,128)} %fusion.102, ...), kind=kLoop, calls=%fused_computation.313 | loop fusion | bytes 22020152 | tf_op jit(solution)/shard_map/dynamic_slice | solution.py:265
  289.3 3.1 add_convert_fusion.6
  294.3 8.4 %dynamic-slice_bitcast_fusion = (f32[128,1536]{0,1:T(8,128)}, f32[128,1536]{0,1:T(8,128)}, f32[128,1536]{0,1:T(8,128)}, f32[128,1536]{0,1:T(8,128)}, f32[128,153...) fusion(f32[1536,2048]{1,0:T(8,128)} %fusion.100, ...), kind=kLoop, calls=%fused_computation.144 | loop fusion | bytes 22020152 | tf_op jit(solution)/shard_map/dynamic_slice | solution.py:265
  302.8 3.2 add_convert_fusion.8
  309.7 31.4 %collective-permute-done.11 = bf16[512,2048]{1,0:T(8,128)(2,1)} collective-permute-done((bf16[512,2048]{1,0:T(8,128)(2,1)S(1)}, bf16[512,2048]{1,0:T(8,128)(2,1)}, u32[]{:S(2)}, u32[]{:S(2)}) %collective-permute-start.11) | collective-permute-done | bytes 2097184 | tf_op jit(solution)/shard_map/ppermute | solution.py:223
  347.0 38.1 %collective-permute-done.4 = bf16[512,2048]{1,0:T(8,128)(2,1)S(1)} collective-permute-done((bf16[512,2048]{1,0:T(8,128)(2,1)S(1)}, bf16[512,2048]{1,0:T(8,128)(2,1)S(1)}, u32[]{:S(2)}, u32[]{:S(2)}) %collective-permute-start.4) | collective-permute-done | bytes 2097184 | tf_op jit(solution)/shard_map/ppermute | solution.py:223
  394.2 14.5 %subtract_add_fusion = (f32[1024,2048]{1,0:T(8,128)}, bf16[1024,2048]{1,0:T(8,128)(2,1)}) fusion(bf16[1024,2048]{1,0:T(8,128)(2,1)} %param.35, f32[1024]{0:T(1024)S(1)} %broadcast_multiply_fusion.3, f32[1024]{0:T(1024)S(1)} %get-tuple-element.324, f32[2048]{0:T(1024)S(1)} %copy-done.129, f32[1024]{0:T(1024)S(1)} %get-tuple-element.325, ...), kind=kLoop, calls=%fused_computation.15 | loop fusion | flops 48234496 | bytes 33574912 | tf_op jit(solution)/shard_map/add | solution.py:344
  408.7 6.0 fusion.29
  416.9 3.4 fusion.36
  430.7 6.5 convert_element_type.432
  439.1 17.5 %collective-permute-done.18 = bf16[128,512]{1,0:T(8,128)(2,1)} collective-permute-done((bf16[128,512]{1,0:T(8,128)(2,1)S(1)}, bf16[128,512]{1,0:T(8,128)(2,1)}, u32[]{:S(2)}, u32[]{:S(2)}) %collective-permute-start.18) | collective-permute-done | bytes 131104 | tf_op jit(solution)/shard_map/ppermute | solution.py:277
  475.2 18.7 %collective-permute-done.22 = bf16[128,512]{1,0:T(8,128)(2,1)S(1)} collective-permute-done((bf16[128,512]{1,0:T(8,128)(2,1)S(1)}, bf16[128,512]{1,0:T(8,128)(2,1)S(1)}, u32[]{:S(2)}, u32[]{:S(2)}) %collective-permute-start.22) | collective-permute-done | bytes 131104 | tf_op jit(solution)/shard_map/ppermute | solution.py:277
  508.3 17.8 %collective-permute-done.26 = bf16[128,512]{1,0:T(8,128)(2,1)S(1)} collective-permute-done((bf16[128,512]{1,0:T(8,128)(2,1)S(1)}, bf16[128,512]{1,0:T(8,128)(2,1)S(1)}, u32[]{:S(2)}, u32[]{:S(2)}) %collective-permute-start.26) | collective-permute-done | bytes 131104 | tf_op jit(solution)/shard_map/ppermute | solution.py:277
  540.0 18.8 %collective-permute-done.30 = bf16[128,512]{1,0:T(8,128)(2,1)S(1)} collective-permute-done((bf16[128,512]{1,0:T(8,128)(2,1)S(1)}, bf16[128,512]{1,0:T(8,128)(2,1)S(1)}, u32[]{:S(2)}, u32[]{:S(2)}) %collective-permute-start.30) | collective-permute-done | bytes 131104 | tf_op jit(solution)/shard_map/ppermute | solution.py:277
  572.1 17.4 %collective-permute-done.31 = bf16[128,4608]{0,1:T(8,128)(2,1)S(1)} collective-permute-done((bf16[128,4608]{0,1:T(8,128)(2,1)S(1)}, bf16[128,4608]{0,1:T(8,128)(2,1)S(1)}, u32[]{:S(2)}, u32[]{:S(2)}) %collective-permute-start.31) | collective-permute-done | bytes 1179680 | tf_op jit(solution)/shard_map/ppermute | solution.py:276
  599.4 5.8 fusion.42
  614.1 5.0 add_convert_fusion
  624.7 4.5 collective-permute-done.44
  639.6 3.4 collective-permute-done.46
  646.6 32.5 %collective-permute-done.36 = bf16[512,2048]{1,0:T(8,128)(2,1)S(1)} collective-permute-done((bf16[512,2048]{1,0:T(8,128)(2,1)S(1)}, bf16[512,2048]{1,0:T(8,128)(2,1)S(1)}, u32[]{:S(2)}, u32[]{:S(2)}) %collective-permute-start.36) | collective-permute-done | bytes 2097184 | tf_op jit(solution)/shard_map/ppermute | solution.py:223
  683.6 3.0 copy.258
  686.6 3.0 copy.259
  695.4 4.3 collective-permute-done.48
  704.6 4.2 collective-permute-done.49
  724.7 4.7 fusion.7
  736.2 7.8 %fusion.6 = f32[1024,2048]{1,0:T(8,128)} fusion(f32[1024,2048]{1,0:T(8,128)} %get-tuple-element.47, bf16[1024,2048]{1,0:T(8,128)(2,1)S(1)} %copy-done.3, f32[1024]{0:T(1024)S(1)} %broadcast_multiply_fusion.2, f32[1024]{0:T(1024)S(1)} %copy-done.132, f32[2048]{0:T(1024)S(1)} %copy-done.126, f32[1024]{0:T(1024)S(1)} %copy-done.131, ...), kind=kLoop, calls=%fused_computation.12 | loop fusion | flops 23068672 | bytes 25186304 | tf_op jit(solution)/shard_map/add | solution.py:391
  (575 shorter events, 229.6 us)
Async XLA Ops:
  74.1 48.8 %collective-permute-start.1 = (bf16[512,2048]{1,0:T(8,128)(2,1)S(1)}, bf16[512,2048]{1,0:T(8,128)(2,1)S(1)}, u32[]{:S(2)}, u32[]{:S(2)}) collective-permute-start(bf16[512,2048]{1,0:T(8,128)(2,1)S(1)} %add_convert_fusion.10), channel_id=1, source_target_pairs={{0,2},{1,3},{2,0},{3,1},{4,6},{5,7},{6,4},{7,5},{8,10},{9,11},{10,... | collective-permute-start | bytes 6291464 | tf_op jit(solution)/shard_map/ppermute | solution.py:223
  125.0 32.3 %collective-permute-start.2 = (bf16[512,2048]{1,0:T(8,128)(2,1)}, bf16[512,2048]{1,0:T(8,128)(2,1)}, u32[]{:S(2)}, u32[]{:S(2)}) collective-permute-start(bf16[512,2048]{1,0:T(8,128)(2,1)} %add_convert_fusion.9), channel_id=1, source_target_pairs={{0,1},{1,0},{2,3},{3,2},{4,5},{5,4},{6,7},{7,6},{8,9},{9,8},{10,11... | collective-permute-start | bytes 6291464 | tf_op jit(solution)/shard_map/ppermute | solution.py:225
  240.3 62.5 %collective-permute-start.3 = (bf16[512,2048]{1,0:T(8,128)(2,1)}, bf16[512,2048]{1,0:T(8,128)(2,1)}, u32[]{:S(2)}, u32[]{:S(2)}) collective-permute-start(bf16[512,2048]{1,0:T(8,128)(2,1)} %constant_dynamic-slice_fusion.70), channel_id=1, source_target_pairs={{0,1},{1,0},{2,3},{3,2},{4,5},{5,4},{6,7},{7,6},{8,9},{9,8},{10,11... | collective-permute-start | bytes 6291464 | tf_op jit(solution)/shard_map/ppermute | solution.py:221
  262.5 26.8 %collective-permute-start.10 = (bf16[512,2048]{1,0:T(8,128)(2,1)S(1)}, bf16[512,2048]{1,0:T(8,128)(2,1)}, u32[]{:S(2)}, u32[]{:S(2)}) collective-permute-start(bf16[512,2048]{1,0:T(8,128)(2,1)S(1)} %constant_dynamic-slice_fusion.64), channel_id=1, source_target_pairs={{0,1},{1,0},{2,3},{3,2},{4,5},{5,4},{6,7},{7,6},{8,9},{9,8},{10,11... | collective-permute-start | bytes 6291464 | tf_op jit(solution)/shard_map/ppermute | solution.py:221
  269.3 37.0 %collective-permute-start.6 = (bf16[128,4608]{0,1:T(8,128)(2,1)}, bf16[128,4608]{0,1:T(8,128)(2,1)}, u32[]{:S(2)}, u32[]{:S(2)}) collective-permute-start(bf16[128,4608]{0,1:T(8,128)(2,1)} %pad_maximum_fusion.1), channel_id=1, source_target_pairs={{0,8},{8,16},{16,24},{24,28},{28,20},{20,12},{12,4},{4,0},{1,9},{9... | collective-permute-start | bytes 3538952 | tf_op jit(solution)/shard_map/ppermute | solution.py:276
  272.2 71.4 %collective-permute-start.8 = (bf16[128,4608]{0,1:T(8,128)(2,1)}, bf16[128,4608]{0,1:T(8,128)(2,1)}, u32[]{:S(2)}, u32[]{:S(2)}) collective-permute-start(bf16[128,4608]{0,1:T(8,128)(2,1)} %pad_maximum_fusion.2), channel_id=1, source_target_pairs={{8,0},{16,8},{24,16},{28,24},{20,28},{12,20},{4,12},{0,4},{9,1},{1... | collective-permute-start | bytes 3538952 | tf_op jit(solution)/shard_map/ppermute | solution.py:277
  292.5 48.7 %collective-permute-start.11 = (bf16[512,2048]{1,0:T(8,128)(2,1)S(1)}, bf16[512,2048]{1,0:T(8,128)(2,1)}, u32[]{:S(2)}, u32[]{:S(2)}) collective-permute-start(bf16[512,2048]{1,0:T(8,128)(2,1)S(1)} %add_convert_fusion.6), channel_id=1, source_target_pairs={{0,2},{1,3},{2,0},{3,1},{4,6},{5,7},{6,4},{7,5},{8,10},{9,11},{10,... | collective-permute-start | bytes 6291464 | tf_op jit(solution)/shard_map/ppermute | solution.py:223
  305.9 79.1 %collective-permute-start.4 = (bf16[512,2048]{1,0:T(8,128)(2,1)S(1)}, bf16[512,2048]{1,0:T(8,128)(2,1)S(1)}, u32[]{:S(2)}, u32[]{:S(2)}) collective-permute-start(bf16[512,2048]{1,0:T(8,128)(2,1)S(1)} %add_convert_fusion.8), channel_id=1, source_target_pairs={{0,2},{1,3},{2,0},{3,1},{4,6},{5,7},{6,4},{7,5},{8,10},{9,11},{10,... | collective-permute-start | bytes 6291464 | tf_op jit(solution)/shard_map/ppermute | solution.py:223
  307.8 78.1 %collective-permute-start.7 = (bf16[128,4608]{0,1:T(8,128)(2,1)S(1)}, bf16[128,4608]{0,1:T(8,128)(2,1)S(1)}, u32[]{:S(2)}, u32[]{:S(2)}) collective-permute-start(bf16[128,4608]{0,1:T(8,128)(2,1)S(1)} %fusion.12), channel_id=1, source_target_pairs={{0,8},{8,16},{16,24},{24,28},{28,20},{20,12},{12,4},{4,0},{1,9},{9... | collective-permute-start | bytes 3538952 | tf_op jit(solution)/shard_map/ppermute | solution.py:276
  343.5 45.7 %collective-permute-start.12 = (bf16[512,2048]{1,0:T(8,128)(2,1)S(1)}, bf16[512,2048]{1,0:T(8,128)(2,1)S(1)}, u32[]{:S(2)}, u32[]{:S(2)}) collective-permute-start(bf16[512,2048]{1,0:T(8,128)(2,1)S(1)} %add_convert_fusion.5), channel_id=1, source_target_pairs={{0,1},{1,0},{2,3},{3,2},{4,5},{5,4},{6,7},{7,6},{8,9},{9,8},{10,11... | collective-permute-start | bytes 6291464 | tf_op jit(solution)/shard_map/ppermute | solution.py:225
  345.1 42.4 %collective-permute-start.9 = (bf16[128,4608]{0,1:T(8,128)(2,1)S(1)}, bf16[128,4608]{0,1:T(8,128)(2,1)S(1)}, u32[]{:S(2)}, u32[]{:S(2)}) collective-permute-start(bf16[128,4608]{0,1:T(8,128)(2,1)S(1)} %fusion.13), channel_id=1, source_target_pairs={{8,0},{16,8},{24,16},{28,24},{20,28},{12,20},{4,12},{0,4},{9,1},{1... | collective-permute-start | bytes 3538952 | tf_op jit(solution)/shard_map/ppermute | solution.py:277
  423.5 35.6 %collective-permute-start.15 = (bf16[128,4608]{0,1:T(8,128)(2,1)}, bf16[128,4608]{0,1:T(8,128)(2,1)S(1)}, u32[]{:S(2)}, u32[]{:S(2)}) collective-permute-start(bf16[128,4608]{0,1:T(8,128)(2,1)} %fusion.14), channel_id=1, source_target_pairs={{0,8},{8,16},{16,24},{24,28},{28,20},{20,12},{12,4},{4,0},{1,9},{9... | collective-permute-start | bytes 3538952 | tf_op jit(solution)/shard_map/ppermute | solution.py:276
  426.2 33.1 %collective-permute-start.16 = (bf16[128,4608]{0,1:T(8,128)(2,1)}, bf16[128,4608]{0,1:T(8,128)(2,1)}, u32[]{:S(2)}, u32[]{:S(2)}) collective-permute-start(bf16[128,4608]{0,1:T(8,128)(2,1)} %fusion.15), channel_id=1, source_target_pairs={{8,0},{16,8},{24,16},{28,24},{20,28},{12,20},{4,12},{0,4},{9,1},{1... | collective-permute-start | bytes 3538952 | tf_op jit(solution)/shard_map/ppermute | solution.py:277
  428.5 28.0 %collective-permute-start.18 = (bf16[128,512]{1,0:T(8,128)(2,1)S(1)}, bf16[128,512]{1,0:T(8,128)(2,1)}, u32[]{:S(2)}, u32[]{:S(2)}) collective-permute-start(bf16[128,512]{1,0:T(8,128)(2,1)S(1)} %get-tuple-element.266), channel_id=1, source_target_pairs={{8,0},{16,8},{24,16},{28,24},{20,28},{12,20},{4,12},{0,4},{9,1},{1... | collective-permute-start | bytes 393224 | tf_op jit(solution)/shard_map/ppermute | solution.py:277
  430.1 27.4 %collective-permute-start.17 = (bf16[128,512]{1,0:T(8,128)(2,1)}, bf16[128,512]{1,0:T(8,128)(2,1)}, u32[]{:S(2)}, u32[]{:S(2)}) collective-permute-start(bf16[128,512]{1,0:T(8,128)(2,1)} %get-tuple-element.267), channel_id=1, source_target_pairs={{0,8},{8,16},{16,24},{24,28},{28,20},{20,12},{12,4},{4,0},{1,9},{9... | collective-permute-start | bytes 393224 | tf_op jit(solution)/shard_map/ppermute | solution.py:276
  462.5 31.5 %collective-permute-start.19 = (bf16[128,4608]{0,1:T(8,128)(2,1)}, bf16[128,4608]{0,1:T(8,128)(2,1)}, u32[]{:S(2)}, u32[]{:S(2)}) collective-permute-start(bf16[128,4608]{0,1:T(8,128)(2,1)} %fusion.16), channel_id=1, source_target_pairs={{0,8},{8,16},{16,24},{24,28},{28,20},{20,12},{12,4},{4,0},{1,9},{9... | collective-permute-start | bytes 3538952 | tf_op jit(solution)/shard_map/ppermute | solution.py:276
  464.5 30.9 %collective-permute-start.20 = (bf16[128,4608]{0,1:T(8,128)(2,1)}, bf16[128,4608]{0,1:T(8,128)(2,1)}, u32[]{:S(2)}, u32[]{:S(2)}) collective-permute-start(bf16[128,4608]{0,1:T(8,128)(2,1)} %fusion.17), channel_id=1, source_target_pairs={{8,0},{16,8},{24,16},{28,24},{20,28},{12,20},{4,12},{0,4},{9,1},{1... | collective-permute-start | bytes 3538952 | tf_op jit(solution)/shard_map/ppermute | solution.py:277
  472.6 21.3 %collective-permute-start.22 = (bf16[128,512]{1,0:T(8,128)(2,1)S(1)}, bf16[128,512]{1,0:T(8,128)(2,1)S(1)}, u32[]{:S(2)}, u32[]{:S(2)}) collective-permute-start(bf16[128,512]{1,0:T(8,128)(2,1)S(1)} %get-tuple-element.264), channel_id=1, source_target_pairs={{8,0},{16,8},{24,16},{28,24},{20,28},{12,20},{4,12},{0,4},{9,1},{1... | collective-permute-start | bytes 393224 | tf_op jit(solution)/shard_map/ppermute | solution.py:277
  474.3 19.7 %collective-permute-start.21 = (bf16[128,512]{1,0:T(8,128)(2,1)S(1)}, bf16[128,512]{1,0:T(8,128)(2,1)S(1)}, u32[]{:S(2)}, u32[]{:S(2)}) collective-permute-start(bf16[128,512]{1,0:T(8,128)(2,1)S(1)} %get-tuple-element.265), channel_id=1, source_target_pairs={{0,8},{8,16},{16,24},{24,28},{28,20},{20,12},{12,4},{4,0},{1,9},{9... | collective-permute-start | bytes 393224 | tf_op jit(solution)/shard_map/ppermute | solution.py:276
  497.6 30.1 %collective-permute-start.24 = (bf16[128,4608]{0,1:T(8,128)(2,1)S(1)}, bf16[128,4608]{0,1:T(8,128)(2,1)S(1)}, u32[]{:S(2)}, u32[]{:S(2)}) collective-permute-start(bf16[128,4608]{0,1:T(8,128)(2,1)S(1)} %fusion.19), channel_id=1, source_target_pairs={{8,0},{16,8},{24,16},{28,24},{20,28},{12,20},{4,12},{0,4},{9,1},{1... | collective-permute-start | bytes 3538952 | tf_op jit(solution)/shard_map/ppermute | solution.py:277
  499.5 28.4 %collective-permute-start.23 = (bf16[128,4608]{0,1:T(8,128)(2,1)S(1)}, bf16[128,4608]{0,1:T(8,128)(2,1)S(1)}, u32[]{:S(2)}, u32[]{:S(2)}) collective-permute-start(bf16[128,4608]{0,1:T(8,128)(2,1)S(1)} %fusion.18), channel_id=1, source_target_pairs={{0,8},{8,16},{16,24},{24,28},{28,20},{20,12},{12,4},{4,0},{1,9},{9... | collective-permute-start | bytes 3538952 | tf_op jit(solution)/shard_map/ppermute | solution.py:276
  505.4 20.7 %collective-permute-start.26 = (bf16[128,512]{1,0:T(8,128)(2,1)S(1)}, bf16[128,512]{1,0:T(8,128)(2,1)S(1)}, u32[]{:S(2)}, u32[]{:S(2)}) collective-permute-start(bf16[128,512]{1,0:T(8,128)(2,1)S(1)} %get-tuple-element.262), channel_id=1, source_target_pairs={{8,0},{16,8},{24,16},{28,24},{20,28},{12,20},{4,12},{0,4},{9,1},{1... | collective-permute-start | bytes 393224 | tf_op jit(solution)/shard_map/ppermute | solution.py:277
  507.0 20.7 %collective-permute-start.25 = (bf16[128,512]{1,0:T(8,128)(2,1)S(1)}, bf16[128,512]{1,0:T(8,128)(2,1)S(1)}, u32[]{:S(2)}, u32[]{:S(2)}) collective-permute-start(bf16[128,512]{1,0:T(8,128)(2,1)S(1)} %get-tuple-element.263), channel_id=1, source_target_pairs={{0,8},{8,16},{16,24},{24,28},{28,20},{20,12},{12,4},{4,0},{1,9},{9... | collective-permute-start | bytes 393224 | tf_op jit(solution)/shard_map/ppermute | solution.py:276
  529.9 29.0 %collective-permute-start.27 = (bf16[128,4608]{0,1:T(8,128)(2,1)S(1)}, bf16[128,4608]{0,1:T(8,128)(2,1)S(1)}, u32[]{:S(2)}, u32[]{:S(2)}) collective-permute-start(bf16[128,4608]{0,1:T(8,128)(2,1)S(1)} %fusion.20), channel_id=1, source_target_pairs={{0,8},{8,16},{16,24},{24,28},{28,20},{20,12},{12,4},{4,0},{1,9},{9... | collective-permute-start | bytes 3538952 | tf_op jit(solution)/shard_map/ppermute | solution.py:276
  531.5 27.6 %collective-permute-start.28 = (bf16[128,4608]{0,1:T(8,128)(2,1)S(1)}, bf16[128,4608]{0,1:T(8,128)(2,1)S(1)}, u32[]{:S(2)}, u32[]{:S(2)}) collective-permute-start(bf16[128,4608]{0,1:T(8,128)(2,1)S(1)} %fusion.21), channel_id=1, source_target_pairs={{8,0},{16,8},{24,16},{28,24},{20,28},{12,20},{4,12},{0,4},{9,1},{1... | collective-permute-start | bytes 3538952 | tf_op jit(solution)/shard_map/ppermute | solution.py:277
  537.1 21.7 %collective-permute-start.30 = (bf16[128,512]{1,0:T(8,128)(2,1)S(1)}, bf16[128,512]{1,0:T(8,128)(2,1)S(1)}, u32[]{:S(2)}, u32[]{:S(2)}) collective-permute-start(bf16[128,512]{1,0:T(8,128)(2,1)S(1)} %get-tuple-element.260), channel_id=1, source_target_pairs={{8,0},{16,8},{24,16},{28,24},{20,28},{12,20},{4,12},{0,4},{9,1},{1... | collective-permute-start | bytes 393224 | tf_op jit(solution)/shard_map/ppermute | solution.py:277
  538.7 20.1 %collective-permute-start.29 = (bf16[128,512]{1,0:T(8,128)(2,1)S(1)}, bf16[128,512]{1,0:T(8,128)(2,1)S(1)}, u32[]{:S(2)}, u32[]{:S(2)}) collective-permute-start(bf16[128,512]{1,0:T(8,128)(2,1)S(1)} %get-tuple-element.261), channel_id=1, source_target_pairs={{0,8},{8,16},{16,24},{24,28},{28,20},{20,12},{12,4},{4,0},{1,9},{9... | collective-permute-start | bytes 393224 | tf_op jit(solution)/shard_map/ppermute | solution.py:276
  560.4 11.6 %collective-permute-start.34 = (bf16[128,512]{1,0:T(8,128)(2,1)S(1)}, bf16[128,512]{1,0:T(8,128)(2,1)S(1)}, u32[]{:S(2)}, u32[]{:S(2)}) collective-permute-start(bf16[128,512]{1,0:T(8,128)(2,1)S(1)} %get-tuple-element.258), channel_id=1, source_target_pairs={{8,0},{16,8},{24,16},{28,24},{20,28},{12,20},{4,12},{0,4},{9,1},{1... | collective-permute-start | bytes 393224 | tf_op jit(solution)/shard_map/ppermute | solution.py:277
  562.0 10.0 %collective-permute-start.33 = (bf16[128,512]{1,0:T(8,128)(2,1)S(1)}, bf16[128,512]{1,0:T(8,128)(2,1)S(1)}, u32[]{:S(2)}, u32[]{:S(2)}) collective-permute-start(bf16[128,512]{1,0:T(8,128)(2,1)S(1)} %get-tuple-element.259), channel_id=1, source_target_pairs={{0,8},{8,16},{16,24},{24,28},{28,20},{20,12},{12,4},{4,0},{1,9},{9... | collective-permute-start | bytes 393224 | tf_op jit(solution)/shard_map/ppermute | solution.py:276
  564.5 24.9 %collective-permute-start.31 = (bf16[128,4608]{0,1:T(8,128)(2,1)S(1)}, bf16[128,4608]{0,1:T(8,128)(2,1)S(1)}, u32[]{:S(2)}, u32[]{:S(2)}) collective-permute-start(bf16[128,4608]{0,1:T(8,128)(2,1)S(1)} %fusion.22), channel_id=1, source_target_pairs={{0,8},{8,16},{16,24},{24,28},{28,20},{20,12},{12,4},{4,0},{1,9},{9... | collective-permute-start | bytes 3538952 | tf_op jit(solution)/shard_map/ppermute | solution.py:276
  566.6 24.1 %collective-permute-start.32 = (bf16[128,4608]{0,1:T(8,128)(2,1)S(1)}, bf16[128,4608]{0,1:T(8,128)(2,1)S(1)}, u32[]{:S(2)}, u32[]{:S(2)}) collective-permute-start(bf16[128,4608]{0,1:T(8,128)(2,1)S(1)} %fusion.23), channel_id=1, source_target_pairs={{8,0},{16,8},{24,16},{28,24},{20,28},{12,20},{4,12},{0,4},{9,1},{1... | collective-permute-start | bytes 3538952 | tf_op jit(solution)/shard_map/ppermute | solution.py:277
  608.4 85.8 %collective-permute-start.57 = (bf16[128,512]{1,0:T(8,128)(2,1)}, bf16[128,512]{1,0:T(8,128)(2,1)}, u32[]{:S(2)}, u32[]{:S(2)}) collective-permute-start(bf16[128,512]{1,0:T(8,128)(2,1)} %get-tuple-element.238), channel_id=1, source_target_pairs={{0,8},{8,16},{16,24},{24,28},{28,20},{20,12},{12,4},{4,0},{1,9},{9... | collective-permute-start | bytes 393224 | tf_op jit(solution)/shard_map/ppermute | solution.py:276
  609.5 84.7 %collective-permute-start.58 = (bf16[128,512]{1,0:T(8,128)(2,1)}, bf16[128,512]{1,0:T(8,128)(2,1)}, u32[]{:S(2)}, u32[]{:S(2)}) collective-permute-start(bf16[128,512]{1,0:T(8,128)(2,1)} %get-tuple-element.239), channel_id=1, source_target_pairs={{8,0},{16,8},{24,16},{28,24},{20,28},{12,20},{4,12},{0,4},{9,1},{1... | collective-permute-start | bytes 393224 | tf_op jit(solution)/shard_map/ppermute | solution.py:277
  611.4 8.1 %collective-permute-start.43 = (bf16[128,1024]{0,1:T(8,128)(2,1)}, bf16[128,1024]{0,1:T(8,128)(2,1)}, u32[]{:S(2)}, u32[]{:S(2)}) collective-permute-start(bf16[128,1024]{0,1:T(8,128)(2,1)} %pad_maximum_fusion.4), channel_id=1, source_target_pairs={{0,8},{8,16},{16,24},{24,28},{28,20},{20,12},{12,4},{4,0},{1,9},{9... | collective-permute-start | bytes 786440 | tf_op jit(solution)/shard_map/ppermute | solution.py:276
  613.2 9.2 %collective-permute-start.50 = (bf16[128,1024]{0,1:T(8,128)(2,1)}, bf16[128,1024]{0,1:T(8,128)(2,1)}, u32[]{:S(2)}, u32[]{:S(2)}) collective-permute-start(bf16[128,1024]{0,1:T(8,128)(2,1)} %pad_maximum_fusion.5), channel_id=1, source_target_pairs={{8,0},{16,8},{24,16},{28,24},{20,28},{12,20},{4,12},{0,4},{9,1},{1... | collective-permute-start | bytes 786440 | tf_op jit(solution)/shard_map/ppermute | solution.py:277
  619.4 12.9 %collective-permute-start.35 = (bf16[512,2048]{1,0:T(8,128)(2,1)S(1)}, bf16[512,2048]{1,0:T(8,128)(2,1)S(1)}, u32[]{:S(2)}, u32[]{:S(2)}) collective-permute-start(bf16[512,2048]{1,0:T(8,128)(2,1)S(1)} %constant_dynamic-slice_fusion.62), channel_id=1, source_target_pairs={{0,1},{1,0},{2,3},{3,2},{4,5},{5,4},{6,7},{7,6},{8,9},{9,8},{10,11... | collective-permute-start | bytes 6291464 | tf_op jit(solution)/shard_map/ppermute | solution.py:221
  621.3 8.0 %collective-permute-start.44 = (bf16[128,1024]{0,1:T(8,128)(2,1)S(1)}, bf16[128,1024]{0,1:T(8,128)(2,1)S(1)}, u32[]{:S(2)}, u32[]{:S(2)}) collective-permute-start(bf16[128,1024]{0,1:T(8,128)(2,1)S(1)} %fusion.65), channel_id=1, source_target_pairs={{0,8},{8,16},{16,24},{24,28},{28,20},{20,12},{12,4},{4,0},{1,9},{9... | collective-permute-start | bytes 786440 | tf_op jit(solution)/shard_map/ppermute | solution.py:276
  623.5 7.7 %collective-permute-start.51 = (bf16[128,1024]{0,1:T(8,128)(2,1)S(1)}, bf16[128,1024]{0,1:T(8,128)(2,1)S(1)}, u32[]{:S(2)}, u32[]{:S(2)}) collective-permute-start(bf16[128,1024]{0,1:T(8,128)(2,1)S(1)} %fusion.71), channel_id=1, source_target_pairs={{8,0},{16,8},{24,16},{28,24},{20,28},{12,20},{4,12},{0,4},{9,1},{1... | collective-permute-start | bytes 786440 | tf_op jit(solution)/shard_map/ppermute | solution.py:277
  629.4 7.2 collective-permute-start.45
  633.1 45.9 %collective-permute-start.36 = (bf16[512,2048]{1,0:T(8,128)(2,1)S(1)}, bf16[512,2048]{1,0:T(8,128)(2,1)S(1)}, u32[]{:S(2)}, u32[]{:S(2)}) collective-permute-start(bf16[512,2048]{1,0:T(8,128)(2,1)S(1)} %add_convert_fusion.4), channel_id=1, source_target_pairs={{0,2},{1,3},{2,0},{3,1},{4,6},{5,7},{6,4},{7,5},{8,10},{9,11},{10,... | collective-permute-start | bytes 6291464 | tf_op jit(solution)/shard_map/ppermute | solution.py:223
  643.8 45.9 %collective-permute-start.47 = (bf16[128,1024]{0,1:T(8,128)(2,1)}, bf16[128,1024]{0,1:T(8,128)(2,1)}, u32[]{:S(2)}, u32[]{:S(2)}) collective-permute-start(bf16[128,1024]{0,1:T(8,128)(2,1)} %fusion.68), channel_id=1, source_target_pairs={{0,8},{8,16},{16,24},{24,28},{28,20},{20,12},{12,4},{4,0},{1,9},{9... | collective-permute-start | bytes 786440 | tf_op jit(solution)/shard_map/ppermute | solution.py:276
  645.7 46.4 %collective-permute-start.54 = (bf16[128,1024]{0,1:T(8,128)(2,1)}, bf16[128,1024]{0,1:T(8,128)(2,1)}, u32[]{:S(2)}, u32[]{:S(2)}) collective-permute-start(bf16[128,1024]{0,1:T(8,128)(2,1)} %fusion.74), channel_id=1, source_target_pairs={{8,0},{16,8},{24,16},{28,24},{20,28},{12,20},{4,12},{0,4},{9,1},{1... | collective-permute-start | bytes 786440 | tf_op jit(solution)/shard_map/ppermute | solution.py:277
  681.3 30.3 %collective-permute-start.37 = (bf16[512,2048]{1,0:T(8,128)(2,1)}, bf16[512,2048]{1,0:T(8,128)(2,1)}, u32[]{:S(2)}, u32[]{:S(2)}) collective-permute-start(bf16[512,2048]{1,0:T(8,128)(2,1)} %add_convert_fusion.3), channel_id=1, source_target_pairs={{0,1},{1,0},{2,3},{3,2},{4,5},{5,4},{6,7},{7,6},{8,9},{9,8},{10,11... | collective-permute-start | bytes 6291464 | tf_op jit(solution)/shard_map/ppermute | solution.py:225
  690.9 8.8 %collective-permute-start.48 = (bf16[128,1024]{0,1:T(8,128)(2,1)S(1)}, bf16[128,1024]{0,1:T(8,128)(2,1)S(1)}, u32[]{:S(2)}, u32[]{:S(2)}) collective-permute-start(bf16[128,1024]{0,1:T(8,128)(2,1)S(1)} %fusion.69), channel_id=1, source_target_pairs={{0,8},{8,16},{16,24},{24,28},{28,20},{20,12},{12,4},{4,0},{1,9},{9... | collective-permute-start | bytes 786440 | tf_op jit(solution)/shard_map/ppermute | solution.py:276
  693.2 8.5 %collective-permute-start.55 = (bf16[128,1024]{0,1:T(8,128)(2,1)S(1)}, bf16[128,1024]{0,1:T(8,128)(2,1)S(1)}, u32[]{:S(2)}, u32[]{:S(2)}) collective-permute-start(bf16[128,1024]{0,1:T(8,128)(2,1)S(1)} %fusion.75), channel_id=1, source_target_pairs={{8,0},{16,8},{24,16},{28,24},{20,28},{12,20},{4,12},{0,4},{9,1},{1... | collective-permute-start | bytes 786440 | tf_op jit(solution)/shard_map/ppermute | solution.py:277
  700.5 8.3 %collective-permute-start.49 = (bf16[128,1024]{0,1:T(8,128)(2,1)}, bf16[128,1024]{0,1:T(8,128)(2,1)}, u32[]{:S(2)}, u32[]{:S(2)}) collective-permute-start(bf16[128,1024]{0,1:T(8,128)(2,1)} %fusion.70), channel_id=1, source_target_pairs={{0,8},{8,16},{16,24},{24,28},{28,20},{20,12},{12,4},{4,0},{1,9},{9... | collective-permute-start | bytes 786440 | tf_op jit(solution)/shard_map/ppermute | solution.py:276
  702.5 8.1 %collective-permute-start.56 = (bf16[128,1024]{0,1:T(8,128)(2,1)}, bf16[128,1024]{0,1:T(8,128)(2,1)}, u32[]{:S(2)}, u32[]{:S(2)}) collective-permute-start(bf16[128,1024]{0,1:T(8,128)(2,1)} %fusion.76), channel_id=1, source_target_pairs={{8,0},{16,8},{24,16},{28,24},{20,28},{12,20},{4,12},{0,4},{9,1},{1... | collective-permute-start | bytes 786440 | tf_op jit(solution)/shard_map/ppermute | solution.py:277
  733.3 10.7 %collective-permute-start.42 = (f32[4352]{0:T(1024)S(1)}, f32[4352]{0:T(1024)S(1)}, u32[]{:S(2)}, u32[]{:S(2)}) collective-permute-start(f32[4352]{0:T(1024)S(1)} %add.1473), channel_id=1, source_target_pairs={{0,16},{4,20},{8,24},{12,28},{16,0},{20,4},{24,8},{28,12},{1,17},{... | collective-permute-start | bytes 52232 | tf_op jit(solution)/shard_map/ppermute | solution.py:243
  (158 other events, 1008.2 us)

commit v5 on v4

--- a/solution.py
+++ b/solution.py
@@ -324,21 +324,32 @@
         gate = matmul(normed_mid, w_gate)
         upper = matmul(normed_mid, w_up)
         hidden = swiglu(gate, upper).astype(jnp.bfloat16)
+        down_grad_t = inner_rows(cotangent, hidden)
+        down = Ring(plan, [down_grad_t])
+        down.step()
         mlp_part = matmul(hidden, w_down).astype(jnp.bfloat16)
         mixed = (resid + plan.tp_sum(mlp_part).astype(jnp.float32)).astype(jnp.bfloat16)
-        down_grad_t = inner_rows(cotangent, hidden)
-        hidden_grad = outer_cols(cotangent, w_down)
+
+        def down_hook(values):
+            if down.done < down.steps:
+                down.step()
+            down.state, values = lax.optimization_barrier((down.state, values))
+            return values
+
+        hidden_grad = down_hook(outer_cols(cotangent, w_down))
         _, pull = jax.vjp(swiglu, gate, upper)
         gate_grad, upper_grad = pull(hidden_grad)
         gate_grad = gate_grad.astype(jnp.bfloat16)
         upper_grad = upper_grad.astype(jnp.bfloat16)
+        gate_grad, upper_grad = down_hook((gate_grad, upper_grad))
         mid_part = (outer_cols(gate_grad, w_gate) + outer_cols(upper_grad, w_up)).astype(
             jnp.bfloat16
         )
+        mid_part, gate_grad, upper_grad = down_hook((mid_part, gate_grad, upper_grad))
         mid_sum = plan.tp_sum(mid_part)
-        gate_w_grad = inner_rows(normed_mid, gate_grad)
-        up_w_grad = inner_rows(normed_mid, upper_grad)
-        big = Ring(plan, [down_grad_t, gate_w_grad, up_w_grad])
+        gate_w_grad = down_hook(inner_rows(normed_mid, gate_grad))
+        up_w_grad = down_hook(inner_rows(normed_mid, upper_grad))
+        big = Ring(plan, [gate_w_grad, up_w_grad])
         big.step()
         mid_grad = mid_sum.astype(jnp.float32)
         resid_grad = cotangent.astype(jnp.float32) + norm_back(resid, mlp_gain, mid_grad)
@@ -353,8 +364,10 @@
                 big.step()
             if small.done < small.steps:
                 small.step()
-            big.state, small.state, values = lax.optimization_barrier(
-                (big.state, small.state, values)
+            if down.done < down.steps:
+                down.step()
+            down.state, big.state, small.state, values = lax.optimization_barrier(
+                (down.state, big.state, small.state, values)
             )
             return values
 
@@ -377,6 +390,10 @@
             + outer_cols(k_grad, key_matrix)
             + outer_cols(v_grad, value_matrix)
         ).astype(jnp.bfloat16)
+        in_part, q_grad, k_grad, v_grad = lax.optimization_barrier(
+            (in_part, q_grad, k_grad, v_grad)
+        )
+        in_sum = plan.tp_sum(in_part)
         query_w_grad = inner_rows(normed_in, q_grad)
         key_w_grad = inner_rows(normed_in, k_grad)
         value_w_grad = inner_rows(normed_in, v_grad)
@@ -384,8 +401,11 @@
             big.step()
         while small.done < small.steps:
             small.step()
-        in_grad = plan.tp_sum(in_part).astype(jnp.float32)
-        down_sum, gate_sum, up_sum = big.result()
+        while down.done < down.steps:
+            down.step()
+        in_grad = in_sum.astype(jnp.float32)
+        (down_sum,) = down.result()
+        gate_sum, up_sum = big.result()
         (out_sum,) = small.result()
         query_sum, key_sum, value_sum = plan.dp_rs([query_w_grad, key_w_grad, value_w_grad])
         input_grad = resid_grad + norm_back(stream, attn_gain, in_grad)

time: 755 us -> 709 us (0.939)
  waiting for transfers between devices: 270 us -> 237 us
  matrix products: 147 us -> 133 us
  local copies, waits for them, and re-layouts: 98.5 us -> 87 us
    ppermute x4, waiting for transfers between devices: 148 us -> 129 us  [tp_sum(): other = lax.ppermute(chip_sum, 'tensor', self.chip_pairs)]
    dynamic_slice x7 -> x5, local copies, waits for them, and re-layouts: 31 us -> 19 us  [piece(): parts = [lax.dynamic_slice_in_dim(g, start, half, 0) for g in self.grads]]
    ppermute x21 -> x28, starting transfers between devices: 20.2 us -> 30.9 us  [step(): got_a = lax.ppermute(send_a.astype(jnp.bfloat16), 'dp', self.plan.cw)]
    ppermute x21 -> x28, waiting for transfers between devices: 76.4 us -> 66.6 us  [step(): got_b = lax.ppermute(send_b.astype(jnp.bfloat16), 'dp', self.plan.ccw)]
    convert_element_type x1 -> x2, other arithmetic: 0.9 us -> 8.78 us  [the longest x1 7.88 us: body(): upper_grad = upper_grad.astype(jnp.bfloat16)]
    ppermute x21 -> x28, waiting for transfers between devices: 38.6 us -> 33.8 us  [step(): got_a = lax.ppermute(send_a.astype(jnp.bfloat16), 'dp', self.plan.cw)]
    ppermute x21 -> x28, starting transfers between devices: 27.5 us -> 29.3 us  [step(): got_b = lax.ppermute(send_b.astype(jnp.bfloat16), 'dp', self.plan.ccw)]
    convert_element_type x17 -> x23, other arithmetic: 13.9 us -> 15.4 us  [step(): got_b = lax.ppermute(send_b.astype(jnp.bfloat16), 'dp', self.plan.ccw)]
  transfers between devices with their start and end apart: 59 -> 73, of which waited for: 25 -> 27; matrix products, arithmetic and copies ran while one was open for 23% -> 27% of each run, Pallas kernels for 0% -> 0%
where the time goes in v5:
time: 709 us; the launch traced here: 700 us
  waiting for transfers between devices  237 us (33%)
  other arithmetic  149 us (21%)
  matrix products  133 us (19%)
  local copies, waits for them, and re-layouts  87 us (12%)
  starting transfers between devices  71.1 us (10%)
  between operations  23.7 us (3%)
    ppermute x4, waiting for transfers between devices, tp_sum(): other = lax.ppermute(chip_sum, 'tensor', self.chip_pairs)  129 us
    ppermute x28, waiting for transfers between devices, step(): got_b = lax.ppermute(send_b.astype(jnp.bfloat16), 'dp', self.plan.ccw)  66.6 us
    dot_general x7, matrix products, outer_cols(): lax.dot_general(left, right, (((1,), (1,)), ((), ())), preferred_element_...  46.4 us
    dot_general x7, matrix products, matmul(): return jnp.dot(left, right, preferred_element_type=jnp.float32)  45.7 us
    dot_general x7, matrix products, inner_rows(): lax.dot_general(left, right, (((0,), (0,)), ((), ())), preferred_element_...  38.3 us
    ppermute x28, waiting for transfers between devices, step(): got_a = lax.ppermute(send_a.astype(jnp.bfloat16), 'dp', self.plan.cw)  33.8 us
    ppermute x28, starting transfers between devices, step(): got_a = lax.ppermute(send_a.astype(jnp.bfloat16), 'dp', self.plan.cw)  30.9 us
    unnamed x267, local copies, waits for them, and re-layouts  29.6 us
  transfers between devices with their start and end apart: 73, of which 27 were waited for; matrix products, arithmetic and copies ran while one was open for 27% of the time, Pallas kernels for 0%

profile of v5, /device:TPU:0, one launch (start us, length us, event | category | flops | bytes accessed | tf_op | source)
XLA Modules:
  0.0 700.4 jit_solution(8393646822146307737)
XLA Ops:
  0.7 3.2 fusion.1
  15.9 6.9 fusion.93
  25.7 3.5 reshape.555
  32.2 3.5 copy.263
  36.9 4.5 convolution_convert_fusion.3
  46.7 4.6 copy.219
  67.6 3.5 collective-permute-done
  77.0 45.9 %collective-permute-done.1 = bf16[512,2048]{1,0:T(8,128)(2,1)S(1)} collective-permute-done((bf16[512,2048]{1,0:T(8,128)(2,1)S(1)}, bf16[512,2048]{1,0:T(8,128)(2,1)S(1)}, u32[]{:S(2)}, u32[]{:S(2)}) %collective-permute-start.1) | collective-permute-done | bytes 2097184 | tf_op jit(solution)/shard_map/ppermute | solution.py:223
  141.2 4.7 convert_add_fusion
  146.5 5.9 multiply_convert_fusion
  152.5 6.7 fusion.94
  159.2 13.4 %multiply_convert_fusion.2 = (bf16[1024,1536]{1,0:T(8,128)(2,1)S(1)}, f32[1024,1536]{1,0:T(8,128)}) fusion(f32[1024,1536]{1,0:T(8,128)S(1)} %fusion.94, bf16[1024,2048]{1,0:T(8,128)(2,1)S(1)} %multiply_convert_fusion, bf16[2048,1536]{1,0:T(8,128)(2,1)} %param.35), kind=kOutput, calls=%fused_computation.25 | convolution fusion | flops 6451888128 | bytes 26214400 | tf_op jit(solution)/shard_map/dot_general | solution.py:23
  172.6 6.9 fusion.95
  179.5 4.6 copy-done.24
  186.4 8.6 %fusion.96 = f32[1024,1536]{1,0:T(8,128)} fusion(bf16[1024,2048]{1,0:T(8,128)(2,1)S(1)} %copy-done.42, bf16[1536,2048]{1,0:T(8,128)(2,1)S(1)} %bitcast.226), kind=kOutput, calls=%fused_computation.344 | convolution fusion | flops 6442450944 | bytes 16777216 | tf_op jit(solution)/shard_map/dot_general | solution.py:33
  206.7 9.5 %convolution_convert_fusion = bf16[1024,2048]{1,0:T(8,128)(2,1)S(1)} fusion(bf16[1024,1536]{1,0:T(8,128)(2,1)S(1)} %copy-done.120, bf16[1536,2048]{1,0:T(8,128)(2,1)} %param.36), kind=kOutput, calls=%fused_computation.38 | convolution fusion | flops 6444548096 | bytes 13631488 | tf_op jit(solution)/shard_map/dot_general | solution.py:23
  221.6 7.9 %multiply_convert_fusion.1 = (bf16[1024,1536]{1,0:T(8,128)(2,1)S(1)}, bf16[1024,1536]{1,0:T(8,128)(2,1)}) fusion(f32[1024,1536]{1,0:T(8,128)} %fusion.96, f32[1024,1536]{1,0:T(8,128)S(1)} %bitcast.208, f32[1024,1536]{1,0:T(8,128)} %get-tuple-element.411), kind=kLoop, calls=%fused_computation.24 | loop fusion | flops 22020096 | bytes 25165824 | tf_op jit(solution)/shard_map/convert_element_type | solution.py:343
  234.0 10.9 %fusion.97 = f32[1024,2048]{1,0:T(8,128)} fusion(bf16[1024,1536]{1,0:T(8,128)(2,1)S(1)} %get-tuple-element.93, bf16[2048,1536]{1,0:T(8,128)(2,1)} %param.35), kind=kOutput, calls=%fused_computation.345 | convolution fusion | flops 6442450944 | bytes 17825792 | tf_op jit(solution)/shard_map/dot_general | solution.py:33
  244.9 10.9 %add_convert_fusion.1 = bf16[1024,2048]{1,0:T(8,128)(2,1)S(1)} fusion(f32[1024,2048]{1,0:T(8,128)} %fusion.97, bf16[1024,1536]{1,0:T(8,128)(2,1)S(1)} %copy-done.72, bf16[2048,1536]{1,0:T(8,128)(2,1)} %param.34), kind=kOutput, calls=%fused_computation.17 | convolution fusion | flops 6446645248 | bytes 22020096 | tf_op jit(solution)/shard_map/dot_general | solution.py:33
  259.9 9.7 %fusion.98 = f32[2048,1536]{1,0:T(8,128)} fusion(bf16[1024,2048]{1,0:T(8,128)(2,1)S(1)} %copy-done.36, bf16[1024,1536]{1,0:T(8,128)(2,1)S(1)} %copy-done.73), kind=kOutput, calls=%fused_computation.346 | convolution fusion | flops 6442450944 | bytes 19922944 | tf_op jit(solution)/shard_map/dot_general | solution.py:27
  269.6 9.5 %fusion.99 = f32[2048,1536]{1,0:T(8,128)} fusion(bf16[1024,2048]{1,0:T(8,128)(2,1)S(1)} %copy-done.36, bf16[1024,1536]{1,0:T(8,128)(2,1)S(1)} %copy-done.71), kind=kOutput, calls=%fused_computation.347 | convolution fusion | flops 6442450944 | bytes 19922944 | tf_op jit(solution)/shard_map/dot_general | solution.py:27
  282.3 8.6 %constant_dynamic-slice_fusion.70 = (f32[128,1536]{1,0:T(8,128)}, f32[128,1536]{1,0:T(8,128)}, f32[128,1536]{1,0:T(8,128)}, f32[128,1536]{1,0:T(8,128)}, f32[128...) fusion(f32[2048,1536]{1,0:T(8,128)} %fusion.98, ...), kind=kLoop, calls=%fused_computation.307 | loop fusion | bytes 22020152 | tf_op jit(solution)/shard_map/dynamic_slice | solution.py:265
  309.9 8.1 %constant_dynamic-slice_fusion.71 = (f32[128,1536]{1,0:T(8,128)}, f32[128,1536]{1,0:T(8,128)}, f32[128,1536]{1,0:T(8,128)}, f32[128,1536]{1,0:T(8,128)}, f32[128...) fusion(f32[2048,1536]{1,0:T(8,128)} %fusion.99, ...), kind=kLoop, calls=%fused_computation.308 | loop fusion | bytes 22020152 | tf_op jit(solution)/shard_map/dynamic_slice | solution.py:265
  318.0 5.8 collective-permute-done.20
  325.7 17.9 %collective-permute-done.4 = bf16[512,2048]{1,0:T(8,128)(2,1)} collective-permute-done((bf16[512,2048]{1,0:T(8,128)(2,1)S(1)}, bf16[512,2048]{1,0:T(8,128)(2,1)}, u32[]{:S(2)}, u32[]{:S(2)}) %collective-permute-start.4) | collective-permute-done | bytes 2097184 | tf_op jit(solution)/shard_map/ppermute | solution.py:223
  346.0 41.2 %collective-permute-done.25 = bf16[512,2048]{1,0:T(8,128)(2,1)S(1)} collective-permute-done((bf16[512,2048]{1,0:T(8,128)(2,1)S(1)}, bf16[512,2048]{1,0:T(8,128)(2,1)S(1)}, u32[]{:S(2)}, u32[]{:S(2)}) %collective-permute-start.25) | collective-permute-done | bytes 2097184 | tf_op jit(solution)/shard_map/ppermute | solution.py:223
  392.5 8.8 %collective-permute-done.18 = bf16[128,1536]{0,1:T(8,128)(2,1)S(1)} collective-permute-done((bf16[128,1536]{0,1:T(8,128)(2,1)S(1)}, bf16[128,1536]{0,1:T(8,128)(2,1)S(1)}, u32[]{:S(2)}, u32[]{:S(2)}) %collective-permute-start.18) | collective-permute-done | bytes 393248 | tf_op jit(solution)/shard_map/ppermute | solution.py:276
  403.6 4.7 collective-permute-done.23
  411.1 3.4 copy-done.3
  418.0 14.5 %subtract_add_fusion = (f32[1024,2048]{1,0:T(8,128)}, bf16[1024,2048]{1,0:T(8,128)(2,1)}) fusion(bf16[1024,2048]{1,0:T(8,128)(2,1)} %param.37, f32[1024]{0:T(1024)S(1)} %broadcast_multiply_fusion.3, f32[1024]{0:T(1024)S(1)} %copy-done.110, f32[2048]{0:T(1024)S(1)} %copy-done.104, f32[1024]{0:T(1024)S(1)} %copy-done.106, bf16[512,2048]{1,0:T(8,128)(2,1)} %copy-done.16, ...), kind=kLoop, calls=%fused_computation.15 | loop fusion | flops 48234496 | bytes 33574912 | tf_op jit(solution)/shard_map/add | solution.py:355
  432.4 6.2 fusion.17
  441.4 3.4 fusion.34
  450.9 6.6 convert_element_type.522
  466.9 4.1 collective-permute-done.32
  481.5 15.6 %collective-permute-done.36 = bf16[128,512]{1,0:T(8,128)(2,1)S(1)} collective-permute-done((bf16[128,512]{1,0:T(8,128)(2,1)S(1)}, bf16[128,512]{1,0:T(8,128)(2,1)S(1)}, u32[]{:S(2)}, u32[]{:S(2)}) %collective-permute-start.36) | collective-permute-done | bytes 131104 | tf_op jit(solution)/shard_map/ppermute | solution.py:277
  504.7 13.8 %collective-permute-done.40 = bf16[128,512]{1,0:T(8,128)(2,1)S(1)} collective-permute-done((bf16[128,512]{1,0:T(8,128)(2,1)S(1)}, bf16[128,512]{1,0:T(8,128)(2,1)S(1)}, u32[]{:S(2)}, u32[]{:S(2)}) %collective-permute-start.40) | collective-permute-done | bytes 131104 | tf_op jit(solution)/shard_map/ppermute | solution.py:277
  528.7 11.0 %collective-permute-done.44 = bf16[128,512]{1,0:T(8,128)(2,1)S(1)} collective-permute-done((bf16[128,512]{1,0:T(8,128)(2,1)S(1)}, bf16[128,512]{1,0:T(8,128)(2,1)S(1)}, u32[]{:S(2)}, u32[]{:S(2)}) %collective-permute-start.44) | collective-permute-done | bytes 131104 | tf_op jit(solution)/shard_map/ppermute | solution.py:277
  552.7 5.3 collective-permute-done.45
  561.9 5.8 fusion.85
  570.2 5.5 add_convert_fusion
  604.3 3.2 collective-permute-done.59
  611.6 4.3 collective-permute-done.60
  617.5 24.0 %collective-permute-done.50 = bf16[512,2048]{1,0:T(8,128)(2,1)S(1)} collective-permute-done((bf16[512,2048]{1,0:T(8,128)(2,1)S(1)}, bf16[512,2048]{1,0:T(8,128)(2,1)S(1)}, u32[]{:S(2)}, u32[]{:S(2)}) %collective-permute-start.50) | collective-permute-done | bytes 2097184 | tf_op jit(solution)/shard_map/ppermute | solution.py:223
  647.1 5.3 collective-permute-done.68
  656.5 3.9 collective-permute-done.69
  663.9 5.0 collective-permute-done.70
  682.1 4.4 fusion.7
  691.1 7.8 %fusion.6 = f32[1024,2048]{1,0:T(8,128)} fusion(f32[1024,2048]{1,0:T(8,128)} %get-tuple-element.99, bf16[1024,2048]{1,0:T(8,128)(2,1)S(1)} %copy-done.4, f32[1024]{0:T(1024)S(1)} %broadcast_multiply_fusion.2, f32[1024]{0:T(1024)S(1)} %copy-done.109, f32[2048]{0:T(1024)S(1)} %copy-done.100, f32[1024]{0:T(1024)S(1)} %copy-done.108, ...), kind=kLoop, calls=%fused_computation.12 | loop fusion | flops 23068672 | bytes 25186304 | tf_op jit(solution)/shard_map/add | solution.py:411
  (592 shorter events, 243.6 us)
Async XLA Ops:
  74.1 48.8 %collective-permute-start.1 = (bf16[512,2048]{1,0:T(8,128)(2,1)S(1)}, bf16[512,2048]{1,0:T(8,128)(2,1)S(1)}, u32[]{:S(2)}, u32[]{:S(2)}) collective-permute-start(bf16[512,2048]{1,0:T(8,128)(2,1)S(1)} %add_convert_fusion.10), channel_id=1, source_target_pairs={{0,2},{1,3},{2,0},{3,1},{4,6},{5,7},{6,4},{7,5},{8,10},{9,11},{10,... | collective-permute-start | bytes 6291464 | tf_op jit(solution)/shard_map/ppermute | solution.py:223
  125.1 12.6 %collective-permute-start.2 = (bf16[512,2048]{1,0:T(8,128)(2,1)}, bf16[512,2048]{1,0:T(8,128)(2,1)}, u32[]{:S(2)}, u32[]{:S(2)}) collective-permute-start(bf16[512,2048]{1,0:T(8,128)(2,1)} %add_convert_fusion.9), channel_id=1, source_target_pairs={{0,1},{1,0},{2,3},{3,2},{4,5},{5,4},{6,7},{7,6},{8,9},{9,8},{10,11... | collective-permute-start | bytes 6291464 | tf_op jit(solution)/shard_map/ppermute | solution.py:225
  184.3 18.5 %collective-permute-start.8 = (bf16[128,1536]{0,1:T(8,128)(2,1)S(1)}, bf16[128,1536]{0,1:T(8,128)(2,1)S(1)}, u32[]{:S(2)}, u32[]{:S(2)}) collective-permute-start(bf16[128,1536]{0,1:T(8,128)(2,1)S(1)} %get-tuple-element.294), channel_id=1, source_target_pairs={{8,0},{16,8},{24,16},{28,24},{20,28},{12,20},{4,12},{0,4},{9,1},{1... | collective-permute-start | bytes 1179656 | tf_op jit(solution)/shard_map/ppermute | solution.py:277
  186.1 16.7 %collective-permute-start.6 = (bf16[128,1536]{0,1:T(8,128)(2,1)S(1)}, bf16[128,1536]{0,1:T(8,128)(2,1)}, u32[]{:S(2)}, u32[]{:S(2)}) collective-permute-start(bf16[128,1536]{0,1:T(8,128)(2,1)S(1)} %get-tuple-element.295), channel_id=1, source_target_pairs={{0,8},{8,16},{16,24},{24,28},{28,20},{20,12},{12,4},{4,0},{1,9},{9... | collective-permute-start | bytes 1179656 | tf_op jit(solution)/shard_map/ppermute | solution.py:276
  204.6 13.3 %collective-permute-start.9 = (bf16[128,1536]{0,1:T(8,128)(2,1)S(1)}, bf16[128,1536]{0,1:T(8,128)(2,1)S(1)}, u32[]{:S(2)}, u32[]{:S(2)}) collective-permute-start(bf16[128,1536]{0,1:T(8,128)(2,1)S(1)} %get-tuple-element.292), channel_id=1, source_target_pairs={{8,0},{16,8},{24,16},{28,24},{20,28},{12,20},{4,12},{0,4},{9,1},{1... | collective-permute-start | bytes 1179656 | tf_op jit(solution)/shard_map/ppermute | solution.py:277
  206.4 11.6 %collective-permute-start.7 = (bf16[128,1536]{0,1:T(8,128)(2,1)S(1)}, bf16[128,1536]{0,1:T(8,128)(2,1)S(1)}, u32[]{:S(2)}, u32[]{:S(2)}) collective-permute-start(bf16[128,1536]{0,1:T(8,128)(2,1)S(1)} %get-tuple-element.293), channel_id=1, source_target_pairs={{0,8},{8,16},{16,24},{24,28},{28,20},{20,12},{12,4},{4,0},{1,9},{9... | collective-permute-start | bytes 1179656 | tf_op jit(solution)/shard_map/ppermute | solution.py:276
  217.9 74.5 %collective-permute-start.3 = (bf16[512,2048]{1,0:T(8,128)(2,1)}, bf16[512,2048]{1,0:T(8,128)(2,1)}, u32[]{:S(2)}, u32[]{:S(2)}) collective-permute-start(bf16[512,2048]{1,0:T(8,128)(2,1)} %constant_dynamic-slice_fusion.72), channel_id=1, source_target_pairs={{0,1},{1,0},{2,3},{3,2},{4,5},{5,4},{6,7},{7,6},{8,9},{9,8},{10,11... | collective-permute-start | bytes 6291464 | tf_op jit(solution)/shard_map/ppermute | solution.py:221
  219.3 11.2 %collective-permute-start.11 = (bf16[128,1536]{0,1:T(8,128)(2,1)S(1)}, bf16[128,1536]{0,1:T(8,128)(2,1)S(1)}, u32[]{:S(2)}, u32[]{:S(2)}) collective-permute-start(bf16[128,1536]{0,1:T(8,128)(2,1)S(1)} %get-tuple-element.290), channel_id=1, source_target_pairs={{8,0},{16,8},{24,16},{28,24},{20,28},{12,20},{4,12},{0,4},{9,1},{1... | collective-permute-start | bytes 1179656 | tf_op jit(solution)/shard_map/ppermute | solution.py:277
  221.2 10.4 %collective-permute-start.10 = (bf16[128,1536]{0,1:T(8,128)(2,1)S(1)}, bf16[128,1536]{0,1:T(8,128)(2,1)S(1)}, u32[]{:S(2)}, u32[]{:S(2)}) collective-permute-start(bf16[128,1536]{0,1:T(8,128)(2,1)S(1)} %get-tuple-element.291), channel_id=1, source_target_pairs={{0,8},{8,16},{16,24},{24,28},{28,20},{20,12},{12,4},{4,0},{1,9},{9... | collective-permute-start | bytes 1179656 | tf_op jit(solution)/shard_map/ppermute | solution.py:276
  231.9 23.9 %collective-permute-start.13 = (bf16[128,1536]{0,1:T(8,128)(2,1)S(1)}, bf16[128,1536]{0,1:T(8,128)(2,1)S(1)}, u32[]{:S(2)}, u32[]{:S(2)}) collective-permute-start(bf16[128,1536]{0,1:T(8,128)(2,1)S(1)} %get-tuple-element.286), channel_id=1, source_target_pairs={{8,0},{16,8},{24,16},{28,24},{20,28},{12,20},{4,12},{0,4},{9,1},{1... | collective-permute-start | bytes 1179656 | tf_op jit(solution)/shard_map/ppermute | solution.py:277
  233.5 22.4 %collective-permute-start.12 = (bf16[128,1536]{0,1:T(8,128)(2,1)S(1)}, bf16[128,1536]{0,1:T(8,128)(2,1)S(1)}, u32[]{:S(2)}, u32[]{:S(2)}) collective-permute-start(bf16[128,1536]{0,1:T(8,128)(2,1)S(1)} %get-tuple-element.287), channel_id=1, source_target_pairs={{0,8},{8,16},{16,24},{24,28},{28,20},{20,12},{12,4},{4,0},{1,9},{9... | collective-permute-start | bytes 1179656 | tf_op jit(solution)/shard_map/ppermute | solution.py:276
  256.3 22.9 %collective-permute-start.15 = (bf16[128,1536]{0,1:T(8,128)(2,1)S(1)}, bf16[128,1536]{0,1:T(8,128)(2,1)S(1)}, u32[]{:S(2)}, u32[]{:S(2)}) collective-permute-start(bf16[128,1536]{0,1:T(8,128)(2,1)S(1)} %get-tuple-element.284), channel_id=1, source_target_pairs={{8,0},{16,8},{24,16},{28,24},{20,28},{12,20},{4,12},{0,4},{9,1},{1... | collective-permute-start | bytes 1179656 | tf_op jit(solution)/shard_map/ppermute | solution.py:277
  257.8 21.4 %collective-permute-start.14 = (bf16[128,1536]{0,1:T(8,128)(2,1)S(1)}, bf16[128,1536]{0,1:T(8,128)(2,1)S(1)}, u32[]{:S(2)}, u32[]{:S(2)}) collective-permute-start(bf16[128,1536]{0,1:T(8,128)(2,1)S(1)} %get-tuple-element.285), channel_id=1, source_target_pairs={{0,8},{8,16},{16,24},{24,28},{28,20},{20,12},{12,4},{4,0},{1,9},{9... | collective-permute-start | bytes 1179656 | tf_op jit(solution)/shard_map/ppermute | solution.py:276
  259.9 45.4 %collective-permute-start.24 = (bf16[512,2048]{1,0:T(8,128)(2,1)}, bf16[512,2048]{1,0:T(8,128)(2,1)}, u32[]{:S(2)}, u32[]{:S(2)}) collective-permute-start(bf16[512,2048]{1,0:T(8,128)(2,1)} %constant_dynamic-slice_fusion.52), channel_id=1, source_target_pairs={{0,1},{1,0},{2,3},{3,2},{4,5},{5,4},{6,7},{7,6},{8,9},{9,8},{10,11... | collective-permute-start | bytes 6291464 | tf_op jit(solution)/shard_map/ppermute | solution.py:221
  280.3 16.1 %collective-permute-start.17 = (bf16[128,1536]{0,1:T(8,128)(2,1)}, bf16[128,1536]{0,1:T(8,128)(2,1)}, u32[]{:S(2)}, u32[]{:S(2)}) collective-permute-start(bf16[128,1536]{0,1:T(8,128)(2,1)} %get-tuple-element.282), channel_id=1, source_target_pairs={{8,0},{16,8},{24,16},{28,24},{20,28},{12,20},{4,12},{0,4},{9,1},{1... | collective-permute-start | bytes 1179656 | tf_op jit(solution)/shard_map/ppermute | solution.py:277
  281.8 15.7 %collective-permute-start.16 = (bf16[128,1536]{0,1:T(8,128)(2,1)S(1)}, bf16[128,1536]{0,1:T(8,128)(2,1)}, u32[]{:S(2)}, u32[]{:S(2)}) collective-permute-start(bf16[128,1536]{0,1:T(8,128)(2,1)S(1)} %get-tuple-element.283), channel_id=1, source_target_pairs={{0,8},{8,16},{16,24},{24,28},{28,20},{20,12},{12,4},{4,0},{1,9},{9... | collective-permute-start | bytes 1179656 | tf_op jit(solution)/shard_map/ppermute | solution.py:276
  294.9 48.7 %collective-permute-start.4 = (bf16[512,2048]{1,0:T(8,128)(2,1)S(1)}, bf16[512,2048]{1,0:T(8,128)(2,1)}, u32[]{:S(2)}, u32[]{:S(2)}) collective-permute-start(bf16[512,2048]{1,0:T(8,128)(2,1)S(1)} %add_convert_fusion.8), channel_id=1, source_target_pairs={{0,2},{1,3},{2,0},{3,1},{4,6},{5,7},{6,4},{7,5},{8,10},{9,11},{10,... | collective-permute-start | bytes 6291464 | tf_op jit(solution)/shard_map/ppermute | solution.py:223
  300.9 89.0 %collective-permute-start.19 = (bf16[128,1536]{0,1:T(8,128)(2,1)}, bf16[128,1536]{0,1:T(8,128)(2,1)}, u32[]{:S(2)}, u32[]{:S(2)}) collective-permute-start(bf16[128,1536]{0,1:T(8,128)(2,1)} %get-tuple-element.280), channel_id=1, source_target_pairs={{8,0},{16,8},{24,16},{28,24},{20,28},{12,20},{4,12},{0,4},{9,1},{1... | collective-permute-start | bytes 1179656 | tf_op jit(solution)/shard_map/ppermute | solution.py:277
  304.7 19.1 %collective-permute-start.20 = (bf16[128,3072]{1,0:T(8,128)(2,1)}, bf16[128,3072]{1,0:T(8,128)(2,1)}, u32[]{:S(2)}, u32[]{:S(2)}) collective-permute-start(bf16[128,3072]{1,0:T(8,128)(2,1)} %pad_maximum_fusion.1), channel_id=1, source_target_pairs={{0,8},{8,16},{16,24},{24,28},{28,20},{20,12},{12,4},{4,0},{1,9},{9... | collective-permute-start | bytes 2359304 | tf_op jit(solution)/shard_map/ppermute | solution.py:276
  307.8 79.4 %collective-permute-start.25 = (bf16[512,2048]{1,0:T(8,128)(2,1)S(1)}, bf16[512,2048]{1,0:T(8,128)(2,1)S(1)}, u32[]{:S(2)}, u32[]{:S(2)}) collective-permute-start(bf16[512,2048]{1,0:T(8,128)(2,1)S(1)} %add_convert_fusion.6), channel_id=1, source_target_pairs={{0,2},{1,3},{2,0},{3,1},{4,6},{5,7},{6,4},{7,5},{8,10},{9,11},{10,... | collective-permute-start | bytes 6291464 | tf_op jit(solution)/shard_map/ppermute | solution.py:223
  308.5 79.6 %collective-permute-start.22 = (bf16[128,3072]{1,0:T(8,128)(2,1)S(1)}, bf16[128,3072]{1,0:T(8,128)(2,1)S(1)}, u32[]{:S(2)}, u32[]{:S(2)}) collective-permute-start(bf16[128,3072]{1,0:T(8,128)(2,1)S(1)} %pad_maximum_fusion.2), channel_id=1, source_target_pairs={{8,0},{16,8},{24,16},{28,24},{20,28},{12,20},{4,12},{0,4},{9,1},{1... | collective-permute-start | bytes 2359304 | tf_op jit(solution)/shard_map/ppermute | solution.py:277
  325.1 77.2 %collective-permute-start.21 = (bf16[128,3072]{1,0:T(8,128)(2,1)S(1)}, bf16[128,3072]{1,0:T(8,128)(2,1)S(1)}, u32[]{:S(2)}, u32[]{:S(2)}) collective-permute-start(bf16[128,3072]{1,0:T(8,128)(2,1)S(1)} %fusion.22), channel_id=1, source_target_pairs={{0,8},{8,16},{16,24},{24,28},{28,20},{20,12},{12,4},{4,0},{1,9},{9... | collective-permute-start | bytes 2359304 | tf_op jit(solution)/shard_map/ppermute | solution.py:276
  346.0 62.5 %collective-permute-start.5 = (bf16[512,2048]{1,0:T(8,128)(2,1)S(1)}, bf16[512,2048]{1,0:T(8,128)(2,1)S(1)}, u32[]{:S(2)}, u32[]{:S(2)}) collective-permute-start(bf16[512,2048]{1,0:T(8,128)(2,1)S(1)} %add_convert_fusion.7), channel_id=1, source_target_pairs={{0,1},{1,0},{2,3},{3,2},{4,5},{5,4},{6,7},{7,6},{8,9},{9,8},{10,11... | collective-permute-start | bytes 6291464 | tf_op jit(solution)/shard_map/ppermute | solution.py:225
  388.0 22.7 %collective-permute-start.26 = (bf16[512,2048]{1,0:T(8,128)(2,1)S(1)}, bf16[512,2048]{1,0:T(8,128)(2,1)S(1)}, u32[]{:S(2)}, u32[]{:S(2)}) collective-permute-start(bf16[512,2048]{1,0:T(8,128)(2,1)S(1)} %add_convert_fusion.5), channel_id=1, source_target_pairs={{0,1},{1,0},{2,3},{3,2},{4,5},{5,4},{6,7},{7,6},{8,9},{9,8},{10,11... | collective-permute-start | bytes 6291464 | tf_op jit(solution)/shard_map/ppermute | solution.py:225
  388.3 20.0 %collective-permute-start.23 = (bf16[128,3072]{1,0:T(8,128)(2,1)S(1)}, bf16[128,3072]{1,0:T(8,128)(2,1)S(1)}, u32[]{:S(2)}, u32[]{:S(2)}) collective-permute-start(bf16[128,3072]{1,0:T(8,128)(2,1)S(1)} %fusion.23), channel_id=1, source_target_pairs={{8,0},{16,8},{24,16},{28,24},{20,28},{12,20},{4,12},{0,4},{9,1},{1... | collective-permute-start | bytes 2359304 | tf_op jit(solution)/shard_map/ppermute | solution.py:277
  389.9 11.4 %collective-permute-start.18 = (bf16[128,1536]{0,1:T(8,128)(2,1)S(1)}, bf16[128,1536]{0,1:T(8,128)(2,1)S(1)}, u32[]{:S(2)}, u32[]{:S(2)}) collective-permute-start(bf16[128,1536]{0,1:T(8,128)(2,1)S(1)} %get-tuple-element.281), channel_id=1, source_target_pairs={{0,8},{8,16},{16,24},{24,28},{28,20},{20,12},{12,4},{4,0},{1,9},{9... | collective-permute-start | bytes 1179656 | tf_op jit(solution)/shard_map/ppermute | solution.py:276
  447.4 24.6 %collective-permute-start.29 = (bf16[128,3072]{1,0:T(8,128)(2,1)}, bf16[128,3072]{1,0:T(8,128)(2,1)}, u32[]{:S(2)}, u32[]{:S(2)}) collective-permute-start(bf16[128,3072]{1,0:T(8,128)(2,1)} %fusion.24), channel_id=1, source_target_pairs={{0,8},{8,16},{16,24},{24,28},{28,20},{20,12},{12,4},{4,0},{1,9},{9... | collective-permute-start | bytes 2359304 | tf_op jit(solution)/shard_map/ppermute | solution.py:276
  449.3 24.0 %collective-permute-start.30 = (bf16[128,3072]{1,0:T(8,128)(2,1)}, bf16[128,3072]{1,0:T(8,128)(2,1)}, u32[]{:S(2)}, u32[]{:S(2)}) collective-permute-start(bf16[128,3072]{1,0:T(8,128)(2,1)} %fusion.25), channel_id=1, source_target_pairs={{8,0},{16,8},{24,16},{28,24},{20,28},{12,20},{4,12},{0,4},{9,1},{1... | collective-permute-start | bytes 2359304 | tf_op jit(solution)/shard_map/ppermute | solution.py:277
  475.0 22.1 %collective-permute-start.33 = (bf16[128,3072]{1,0:T(8,128)(2,1)S(1)}, bf16[128,3072]{1,0:T(8,128)(2,1)S(1)}, u32[]{:S(2)}, u32[]{:S(2)}) collective-permute-start(bf16[128,3072]{1,0:T(8,128)(2,1)S(1)} %fusion.26), channel_id=1, source_target_pairs={{0,8},{8,16},{16,24},{24,28},{28,20},{20,12},{12,4},{4,0},{1,9},{9... | collective-permute-start | bytes 2359304 | tf_op jit(solution)/shard_map/ppermute | solution.py:276
  476.9 20.5 %collective-permute-start.34 = (bf16[128,3072]{1,0:T(8,128)(2,1)S(1)}, bf16[128,3072]{1,0:T(8,128)(2,1)S(1)}, u32[]{:S(2)}, u32[]{:S(2)}) collective-permute-start(bf16[128,3072]{1,0:T(8,128)(2,1)S(1)} %fusion.27), channel_id=1, source_target_pairs={{8,0},{16,8},{24,16},{28,24},{20,28},{12,20},{4,12},{0,4},{9,1},{1... | collective-permute-start | bytes 2359304 | tf_op jit(solution)/shard_map/ppermute | solution.py:277
  478.9 18.1 %collective-permute-start.36 = (bf16[128,512]{1,0:T(8,128)(2,1)S(1)}, bf16[128,512]{1,0:T(8,128)(2,1)S(1)}, u32[]{:S(2)}, u32[]{:S(2)}) collective-permute-start(bf16[128,512]{1,0:T(8,128)(2,1)S(1)} %get-tuple-element.328), channel_id=1, source_target_pairs={{8,0},{16,8},{24,16},{28,24},{20,28},{12,20},{4,12},{0,4},{9,1},{1... | collective-permute-start | bytes 393224 | tf_op jit(solution)/shard_map/ppermute | solution.py:277
  479.9 17.2 %collective-permute-start.35 = (bf16[128,512]{1,0:T(8,128)(2,1)S(1)}, bf16[128,512]{1,0:T(8,128)(2,1)S(1)}, u32[]{:S(2)}, u32[]{:S(2)}) collective-permute-start(bf16[128,512]{1,0:T(8,128)(2,1)S(1)} %get-tuple-element.329), channel_id=1, source_target_pairs={{0,8},{8,16},{16,24},{24,28},{28,20},{20,12},{12,4},{4,0},{1,9},{9... | collective-permute-start | bytes 393224 | tf_op jit(solution)/shard_map/ppermute | solution.py:276
  497.7 20.9 %collective-permute-start.37 = (bf16[128,3072]{1,0:T(8,128)(2,1)S(1)}, bf16[128,3072]{1,0:T(8,128)(2,1)S(1)}, u32[]{:S(2)}, u32[]{:S(2)}) collective-permute-start(bf16[128,3072]{1,0:T(8,128)(2,1)S(1)} %fusion.28), channel_id=1, source_target_pairs={{0,8},{8,16},{16,24},{24,28},{28,20},{20,12},{12,4},{4,0},{1,9},{9... | collective-permute-start | bytes 2359304 | tf_op jit(solution)/shard_map/ppermute | solution.py:276
  499.4 19.3 %collective-permute-start.38 = (bf16[128,3072]{1,0:T(8,128)(2,1)S(1)}, bf16[128,3072]{1,0:T(8,128)(2,1)S(1)}, u32[]{:S(2)}, u32[]{:S(2)}) collective-permute-start(bf16[128,3072]{1,0:T(8,128)(2,1)S(1)} %fusion.29), channel_id=1, source_target_pairs={{8,0},{16,8},{24,16},{28,24},{20,28},{12,20},{4,12},{0,4},{9,1},{1... | collective-permute-start | bytes 2359304 | tf_op jit(solution)/shard_map/ppermute | solution.py:277
  502.1 16.4 %collective-permute-start.40 = (bf16[128,512]{1,0:T(8,128)(2,1)S(1)}, bf16[128,512]{1,0:T(8,128)(2,1)S(1)}, u32[]{:S(2)}, u32[]{:S(2)}) collective-permute-start(bf16[128,512]{1,0:T(8,128)(2,1)S(1)} %get-tuple-element.326), channel_id=1, source_target_pairs={{8,0},{16,8},{24,16},{28,24},{20,28},{12,20},{4,12},{0,4},{9,1},{1... | collective-permute-start | bytes 393224 | tf_op jit(solution)/shard_map/ppermute | solution.py:277
  502.4 16.1 %collective-permute-start.39 = (bf16[128,512]{1,0:T(8,128)(2,1)S(1)}, bf16[128,512]{1,0:T(8,128)(2,1)S(1)}, u32[]{:S(2)}, u32[]{:S(2)}) collective-permute-start(bf16[128,512]{1,0:T(8,128)(2,1)S(1)} %get-tuple-element.327), channel_id=1, source_target_pairs={{0,8},{8,16},{16,24},{24,28},{28,20},{20,12},{12,4},{4,0},{1,9},{9... | collective-permute-start | bytes 393224 | tf_op jit(solution)/shard_map/ppermute | solution.py:276
  519.1 20.7 %collective-permute-start.41 = (bf16[128,3072]{1,0:T(8,128)(2,1)S(1)}, bf16[128,3072]{1,0:T(8,128)(2,1)S(1)}, u32[]{:S(2)}, u32[]{:S(2)}) collective-permute-start(bf16[128,3072]{1,0:T(8,128)(2,1)S(1)} %fusion.30), channel_id=1, source_target_pairs={{0,8},{8,16},{16,24},{24,28},{28,20},{20,12},{12,4},{4,0},{1,9},{9... | collective-permute-start | bytes 2359304 | tf_op jit(solution)/shard_map/ppermute | solution.py:276
  521.0 19.1 %collective-permute-start.42 = (bf16[128,3072]{1,0:T(8,128)(2,1)S(1)}, bf16[128,3072]{1,0:T(8,128)(2,1)S(1)}, u32[]{:S(2)}, u32[]{:S(2)}) collective-permute-start(bf16[128,3072]{1,0:T(8,128)(2,1)S(1)} %fusion.31), channel_id=1, source_target_pairs={{8,0},{16,8},{24,16},{28,24},{20,28},{12,20},{4,12},{0,4},{9,1},{1... | collective-permute-start | bytes 2359304 | tf_op jit(solution)/shard_map/ppermute | solution.py:277
  525.7 14.0 %collective-permute-start.44 = (bf16[128,512]{1,0:T(8,128)(2,1)S(1)}, bf16[128,512]{1,0:T(8,128)(2,1)S(1)}, u32[]{:S(2)}, u32[]{:S(2)}) collective-permute-start(bf16[128,512]{1,0:T(8,128)(2,1)S(1)} %get-tuple-element.324), channel_id=1, source_target_pairs={{8,0},{16,8},{24,16},{28,24},{20,28},{12,20},{4,12},{0,4},{9,1},{1... | collective-permute-start | bytes 393224 | tf_op jit(solution)/shard_map/ppermute | solution.py:277
  526.3 13.5 %collective-permute-start.43 = (bf16[128,512]{1,0:T(8,128)(2,1)S(1)}, bf16[128,512]{1,0:T(8,128)(2,1)S(1)}, u32[]{:S(2)}, u32[]{:S(2)}) collective-permute-start(bf16[128,512]{1,0:T(8,128)(2,1)S(1)} %get-tuple-element.325), channel_id=1, source_target_pairs={{0,8},{8,16},{16,24},{24,28},{28,20},{20,12},{12,4},{4,0},{1,9},{9... | collective-permute-start | bytes 393224 | tf_op jit(solution)/shard_map/ppermute | solution.py:276
  543.7 14.3 %collective-permute-start.45 = (bf16[128,3072]{1,0:T(8,128)(2,1)S(1)}, bf16[128,3072]{1,0:T(8,128)(2,1)S(1)}, u32[]{:S(2)}, u32[]{:S(2)}) collective-permute-start(bf16[128,3072]{1,0:T(8,128)(2,1)S(1)} %fusion.32), channel_id=1, source_target_pairs={{0,8},{8,16},{16,24},{24,28},{28,20},{20,12},{12,4},{4,0},{1,9},{9... | collective-permute-start | bytes 2359304 | tf_op jit(solution)/shard_map/ppermute | solution.py:276
  545.2 14.6 %collective-permute-start.46 = (bf16[128,3072]{1,0:T(8,128)(2,1)S(1)}, bf16[128,3072]{1,0:T(8,128)(2,1)S(1)}, u32[]{:S(2)}, u32[]{:S(2)}) collective-permute-start(bf16[128,3072]{1,0:T(8,128)(2,1)S(1)} %fusion.33), channel_id=1, source_target_pairs={{8,0},{16,8},{24,16},{28,24},{20,28},{12,20},{4,12},{0,4},{9,1},{1... | collective-permute-start | bytes 2359304 | tf_op jit(solution)/shard_map/ppermute | solution.py:277
  580.3 72.6 %collective-permute-start.71 = (bf16[128,512]{1,0:T(8,128)(2,1)S(1)}, bf16[128,512]{1,0:T(8,128)(2,1)S(1)}, u32[]{:S(2)}, u32[]{:S(2)}) collective-permute-start(bf16[128,512]{1,0:T(8,128)(2,1)S(1)} %get-tuple-element.302), channel_id=1, source_target_pairs={{0,8},{8,16},{16,24},{24,28},{28,20},{20,12},{12,4},{4,0},{1,9},{9... | collective-permute-start | bytes 393224 | tf_op jit(solution)/shard_map/ppermute | solution.py:276
  581.8 71.1 %collective-permute-start.72 = (bf16[128,512]{1,0:T(8,128)(2,1)S(1)}, bf16[128,512]{1,0:T(8,128)(2,1)S(1)}, u32[]{:S(2)}, u32[]{:S(2)}) collective-permute-start(bf16[128,512]{1,0:T(8,128)(2,1)S(1)} %get-tuple-element.303), channel_id=1, source_target_pairs={{8,0},{16,8},{24,16},{28,24},{20,28},{12,20},{4,12},{0,4},{9,1},{1... | collective-permute-start | bytes 393224 | tf_op jit(solution)/shard_map/ppermute | solution.py:277
  595.4 46.0 %collective-permute-start.50 = (bf16[512,2048]{1,0:T(8,128)(2,1)S(1)}, bf16[512,2048]{1,0:T(8,128)(2,1)S(1)}, u32[]{:S(2)}, u32[]{:S(2)}) collective-permute-start(bf16[512,2048]{1,0:T(8,128)(2,1)S(1)} %add_convert_fusion.4), channel_id=1, source_target_pairs={{0,2},{1,3},{2,0},{3,1},{4,6},{5,7},{6,4},{7,5},{8,10},{9,11},{10,... | collective-permute-start | bytes 6291464 | tf_op jit(solution)/shard_map/ppermute | solution.py:223
  611.0 32.6 %collective-permute-start.67 = (bf16[128,1024]{0,1:T(8,128)(2,1)S(1)}, bf16[128,1024]{0,1:T(8,128)(2,1)S(1)}, u32[]{:S(2)}, u32[]{:S(2)}) collective-permute-start(bf16[128,1024]{0,1:T(8,128)(2,1)S(1)} %fusion.70), channel_id=1, source_target_pairs={{8,0},{16,8},{24,16},{28,24},{20,28},{12,20},{4,12},{0,4},{9,1},{1... | collective-permute-start | bytes 786440 | tf_op jit(solution)/shard_map/ppermute | solution.py:277
  616.0 29.3 %collective-permute-start.61 = (bf16[128,1024]{0,1:T(8,128)(2,1)S(1)}, bf16[128,1024]{0,1:T(8,128)(2,1)S(1)}, u32[]{:S(2)}, u32[]{:S(2)}) collective-permute-start(bf16[128,1024]{0,1:T(8,128)(2,1)S(1)} %fusion.65), channel_id=1, source_target_pairs={{0,8},{8,16},{16,24},{24,28},{28,20},{20,12},{12,4},{4,0},{1,9},{9... | collective-permute-start | bytes 786440 | tf_op jit(solution)/shard_map/ppermute | solution.py:276
  643.6 26.3 %collective-permute-start.51 = (bf16[512,2048]{1,0:T(8,128)(2,1)}, bf16[512,2048]{1,0:T(8,128)(2,1)}, u32[]{:S(2)}, u32[]{:S(2)}) collective-permute-start(bf16[512,2048]{1,0:T(8,128)(2,1)} %add_convert_fusion.3), channel_id=1, source_target_pairs={{0,1},{1,0},{2,3},{3,2},{4,5},{5,4},{6,7},{7,6},{8,9},{9,8},{10,11... | collective-permute-start | bytes 6291464 | tf_op jit(solution)/shard_map/ppermute | solution.py:225
  (155 other events, 1143.6 us)

commit v6 on v5

--- a/solution.py
+++ b/solution.py
@@ -314,21 +314,33 @@
         q_raw = matmul(normed_in, w_query)
         k_raw = matmul(normed_in, key_matrix)
         v_raw = matmul(normed_in, value_matrix)
-        attended, logsum, queries, keys_rot, values = attend(
-            q_raw, k_raw, v_raw, query_gain, key_gain, seqs
-        )
-        attn_part = matmul(attended, w_out).astype(jnp.bfloat16)
-        resid = stream + plan.tp_sum(attn_part).astype(jnp.float32)
+        halves = 2 if seqs % 2 == 0 else 1
+        rows = count // halves
+        outs = []
+        for c in range(halves):
+            span = slice(c * rows, (c + 1) * rows)
+            att_c, logsum_c, queries_c, keys_c, values_c = attend(
+                q_raw[span], k_raw[span], v_raw[span], query_gain, key_gain, seqs // halves
+            )
+            attn_part = matmul(att_c, w_out).astype(jnp.bfloat16)
+            resid_c = stream[span] + plan.tp_sum(attn_part).astype(jnp.float32)
+            normed_mid_c = rms_scale(resid_c, mlp_gain).astype(jnp.bfloat16)
+            gate_c = matmul(normed_mid_c, w_gate)
+            upper_c = matmul(normed_mid_c, w_up)
+            hidden_c = swiglu(gate_c, upper_c).astype(jnp.bfloat16)
+            mlp_part = matmul(hidden_c, w_down).astype(jnp.bfloat16)
+            mlp_sum_c = plan.tp_sum(mlp_part)
+            outs.append(
+                (att_c, logsum_c, queries_c, keys_c, values_c, resid_c, normed_mid_c, gate_c,
+                 upper_c, hidden_c, mlp_sum_c)
+            )
+        joined = [jnp.concatenate(parts, 0) for parts in zip(*outs)]
+        (attended, logsum, queries, keys_rot, values, resid, normed_mid, gate, upper, hidden,
+         mlp_sum) = joined
         resid_rows = lax.dynamic_slice_in_dim(resid, offset, share, 0)
-        normed_mid = rms_scale(resid, mlp_gain).astype(jnp.bfloat16)
-        gate = matmul(normed_mid, w_gate)
-        upper = matmul(normed_mid, w_up)
-        hidden = swiglu(gate, upper).astype(jnp.bfloat16)
         down_grad_t = inner_rows(cotangent, hidden)
         down = Ring(plan, [down_grad_t])
         down.step()
-        mlp_part = matmul(hidden, w_down).astype(jnp.bfloat16)
-        mixed = (resid + plan.tp_sum(mlp_part).astype(jnp.float32)).astype(jnp.bfloat16)
 
         def down_hook(values):
             if down.done < down.steps:
@@ -341,7 +353,8 @@
         gate_grad, upper_grad = pull(hidden_grad)
         gate_grad = gate_grad.astype(jnp.bfloat16)
         upper_grad = upper_grad.astype(jnp.bfloat16)
-        gate_grad, upper_grad = down_hook((gate_grad, upper_grad))
+        gate_grad, upper_grad, mlp_sum = down_hook((gate_grad, upper_grad, mlp_sum))
+        mixed = (resid + mlp_sum.astype(jnp.float32)).astype(jnp.bfloat16)
         mid_part = (outer_cols(gate_grad, w_gate) + outer_cols(upper_grad, w_up)).astype(
             jnp.bfloat16
         )

time: 709 us -> 757 us (1.068)
  other arithmetic: 149 us -> 188 us
  local copies, waits for them, and re-layouts: 87 us -> 112 us
  waiting for transfers between devices: 237 us -> 212 us
    ppermute x28, waiting for transfers between devices: 33.8 us -> 12.5 us  [step(): got_a = lax.ppermute(send_a.astype(jnp.bfloat16), 'dp', self.plan.cw)]
    ppermute x4 -> x6, waiting for transfers between devices: 129 us -> 116 us  [tp_sum(): other = lax.ppermute(chip_sum, 'tensor', self.chip_pairs)]
    ppermute x28, waiting for transfers between devices: 66.6 us -> 79.1 us  [step(): got_b = lax.ppermute(send_b.astype(jnp.bfloat16), 'dp', self.plan.ccw)]
    convert_element_type x36, other arithmetic: 14 us -> 26.4 us  [step(): self.state = (got_a.astype(jnp.float32), got_b.astype(jnp.float32))]
    concatenate x0 -> x6, local copies, waits for them, and re-layouts: none -> 11.2 us  [the longest x4 9.75 us: head_prep(): turned = jnp.concatenate([-normed[..., half:], normed[..., :half]], -1)]
    ppermute x28, starting transfers between devices: 30.9 us -> 22.1 us  [step(): got_a = lax.ppermute(send_a.astype(jnp.bfloat16), 'dp', self.plan.cw)]
    reshape x0 -> x5, local copies, waits for them, and re-layouts: none -> 8.29 us  [the longest x1 3.04 us: attend_back(): query_in = q_raw.reshape(seqs, length, heads, HEAD_SIZE)]
    reshape x5 -> x6, local copies, waits for them, and re-layouts: 17.5 us -> 11.5 us  [attend(): q_raw.reshape(seqs, length, heads, HEAD_SIZE)]
  transfers between devices with their start and end apart: 73 -> 79, of which waited for: 27 -> 23; matrix products, arithmetic and copies ran while one was open for 27% -> 36% of each run, Pallas kernels for 0% -> 0%
where the time goes in v6:
time: 757 us; the launch traced here: 746 us
  waiting for transfers between devices  212 us (28%)
  other arithmetic  188 us (25%)
  matrix products  139 us (18%)
  local copies, waits for them, and re-layouts  112 us (15%)
  starting transfers between devices  69.7 us (9%)
  between operations  25 us (3%)
    ppermute x6, waiting for transfers between devices, tp_sum(): other = lax.ppermute(chip_sum, 'tensor', self.chip_pairs)  116 us
    ppermute x28, waiting for transfers between devices, step(): got_b = lax.ppermute(send_b.astype(jnp.bfloat16), 'dp', self.plan.ccw)  79.1 us
    dot_general x11, matrix products, matmul(): return jnp.dot(left, right, preferred_element_type=jnp.float32)  46.5 us
    dot_general x7, matrix products, outer_cols(): lax.dot_general(left, right, (((1,), (1,)), ((), ())), preferred_element_...  44.6 us
    dot_general x7, matrix products, inner_rows(): lax.dot_general(left, right, (((0,), (0,)), ((), ())), preferred_element_...  39.4 us
    ppermute x28, starting transfers between devices, step(): got_b = lax.ppermute(send_b.astype(jnp.bfloat16), 'dp', self.plan.ccw)  33.7 us
    unnamed x333, local copies, waits for them, and re-layouts  28.5 us
    convert_element_type x36, other arithmetic, step(): self.state = (got_a.astype(jnp.float32), got_b.astype(jnp.float32))  26.4 us
  transfers between devices with their start and end apart: 79, of which 23 were waited for; matrix products, arithmetic and copies ran while one was open for 36% of the time, Pallas kernels for 0%

profile of v6, /device:TPU:0, one launch (start us, length us, event | category | flops | bytes accessed | tf_op | source)
XLA Modules:
  0.0 745.7 jit_solution(16136958867515332001)
XLA Ops:
  0.7 3.2 multiply_reduce_fusion.3
  25.9 3.8 convolution_convert_fusion.6
  31.6 3.5 fusion.123
  85.3 22.3 %collective-permute-done.4 = bf16[256,2048]{1,0:T(8,128)(2,1)S(1)} collective-permute-done((bf16[256,2048]{1,0:T(8,128)(2,1)S(1)}, bf16[256,2048]{1,0:T(8,128)(2,1)S(1)}, u32[]{:S(2)}, u32[]{:S(2)}) %collective-permute-start.4) | collective-permute-done | bytes 1048608 | tf_op jit(solution)/shard_map/ppermute | solution.py:223
  109.0 20.9 %collective-permute-done.1 = bf16[256,2048]{1,0:T(8,128)(2,1)S(1)} collective-permute-done((bf16[256,2048]{1,0:T(8,128)(2,1)S(1)}, bf16[256,2048]{1,0:T(8,128)(2,1)S(1)}, u32[]{:S(2)}, u32[]{:S(2)}) %collective-permute-start.1) | collective-permute-done | bytes 1048608 | tf_op jit(solution)/shard_map/ppermute | solution.py:223
  131.3 10.6 %fusion.127 = f32[1024,1536]{1,0:T(8,128)} fusion(bf16[1024,2048]{1,0:T(8,128)(2,1)S(1)} %copy-done.44, bf16[1536,2048]{1,0:T(8,128)(2,1)} %param.38), kind=kOutput, calls=%fused_computation.427 | convolution fusion | flops 6442450944 | bytes 16777216 | tf_op jit(solution)/shard_map/dot_general | solution.py:33
  156.9 3.0 reshape.688
  159.9 6.7 convert_element_type.590
  167.3 3.6 multiply_reduce_fusion.12
  182.1 7.1 fusion.125
  189.3 3.4 fusion.126
  192.8 5.2 multiply_convert_fusion.4
  198.0 3.8 convolution_convert_fusion
  202.5 5.2 multiply_convert_fusion.5
  207.8 8.2 %fusion.4 = f32[1536,2048]{1,0:T(8,128)S(1)} fusion(bf16[1024,2048]{1,0:T(8,128)(2,1)S(1)} %copy-done.45, bf16[512,1536]{1,0:T(8,128)(2,1)} %copy-done.150, bf16[512,1536]{1,0:T(8,128)(2,1)S(1)} %get-tuple-element.446), kind=kOutput, calls=%fused_computation.36 | convolution fusion | flops 6448742400 | bytes 19922944 | tf_op jit(solution)/shard_map/dot_general | solution.py:27
  218.2 8.4 %convolution_convert_fusion.1 = bf16[512,2048]{1,0:T(8,128)(2,1)S(1)} fusion(bf16[512,1536]{1,0:T(8,128)(2,1)S(1)} %get-tuple-element.446, bf16[1536,2048]{1,0:T(8,128)(2,1)} %param.38), kind=kOutput, calls=%fused_computation.46 | convolution fusion | flops 3222274048 | bytes 9961472 | tf_op jit(solution)/shard_map/dot_general | solution.py:23
  253.8 6.2 collective-permute-done.16
  262.0 18.5 %collective-permute-done.13 = bf16[256,2048]{1,0:T(8,128)(2,1)S(1)} collective-permute-done((bf16[256,2048]{1,0:T(8,128)(2,1)S(1)}, bf16[256,2048]{1,0:T(8,128)(2,1)S(1)}, u32[]{:S(2)}, u32[]{:S(2)}) %collective-permute-start.13) | collective-permute-done | bytes 1048608 | tf_op jit(solution)/shard_map/ppermute | solution.py:223
  281.1 7.1 multiply_convert_fusion.1
  299.5 9.0 %fusion.128 = f32[1024,2048]{1,0:T(8,128)} fusion(bf16[1024,1536]{1,0:T(8,128)(2,1)S(1)} %copy-done.77, bf16[2048,1536]{1,0:T(8,128)(2,1)S(1)} %bitcast.267), kind=kOutput, calls=%fused_computation.428 | convolution fusion | flops 6442450944 | bytes 17825792 | tf_op jit(solution)/shard_map/dot_general | solution.py:33
  308.5 9.2 %add_convert_fusion.1 = bf16[1024,2048]{1,0:T(8,128)(2,1)S(1)} fusion(f32[1024,2048]{1,0:T(8,128)} %fusion.128, bf16[1024,1536]{1,0:T(8,128)(2,1)S(1)} %copy-done.78, bf16[2048,1536]{1,0:T(8,128)(2,1)S(1)} %bitcast.271), kind=kOutput, calls=%fused_computation.11 | convolution fusion | flops 6446645248 | bytes 22020096 | tf_op jit(solution)/shard_map/dot_general | solution.py:33
  322.2 9.5 %fusion.9 = f32[2048,1536]{1,0:T(8,128)} fusion(bf16[1024,1536]{1,0:T(8,128)(2,1)S(1)} %copy-done.78, bf16[512,2048]{1,0:T(8,128)(2,1)S(1)} %copy-done.92, bf16[512,2048]{1,0:T(8,128)(2,1)S(1)} %copy-done.90), kind=kOutput, calls=%fused_computation.50 | convolution fusion | flops 6450839552 | bytes 19922944 | tf_op jit(solution)/shard_map/dot_general | solution.py:27
  331.7 9.6 %fusion.8 = f32[2048,1536]{1,0:T(8,128)} fusion(bf16[1024,1536]{1,0:T(8,128)(2,1)S(1)} %copy-done.77, bf16[512,2048]{1,0:T(8,128)(2,1)S(1)} %copy-done.92, bf16[512,2048]{1,0:T(8,128)(2,1)S(1)} %copy-done.90), kind=kOutput, calls=%fused_computation.49 | convolution fusion | flops 6450839552 | bytes 19922944 | tf_op jit(solution)/shard_map/dot_general | solution.py:27
  348.2 7.8 %constant_dynamic-slice_fusion.72 = (f32[128,1536]{1,0:T(8,128)}, f32[128,1536]{1,0:T(8,128)}, f32[128,1536]{1,0:T(8,128)}, f32[128,1536]{1,0:T(8,128)}, f32[128...) fusion(f32[2048,1536]{1,0:T(8,128)} %fusion.9, ...), kind=kLoop, calls=%fused_computation.373 | loop fusion | bytes 22020152 | tf_op jit(solution)/shard_map/dynamic_slice | solution.py:265
  362.6 7.8 %constant_dynamic-slice_fusion.73 = (f32[128,1536]{1,0:T(8,128)}, f32[128,1536]{1,0:T(8,128)}, f32[128,1536]{1,0:T(8,128)}, f32[128,1536]{1,0:T(8,128)}, f32[128...) fusion(f32[2048,1536]{1,0:T(8,128)} %fusion.8, ...), kind=kLoop, calls=%fused_computation.374 | loop fusion | bytes 22020152 | tf_op jit(solution)/shard_map/dynamic_slice | solution.py:265
  371.0 23.0 %collective-permute-done.31 = bf16[512,2048]{1,0:T(8,128)(2,1)S(1)} collective-permute-done((bf16[512,2048]{1,0:T(8,128)(2,1)S(1)}, bf16[512,2048]{1,0:T(8,128)(2,1)S(1)}, u32[]{:S(2)}, u32[]{:S(2)}) %collective-permute-start.31) | collective-permute-done | bytes 2097184 | tf_op jit(solution)/shard_map/ppermute | solution.py:223
  406.2 3.2 fusion.12
  409.3 20.3 %collective-permute-done.25 = bf16[128,1536]{0,1:T(8,128)(2,1)} collective-permute-done((bf16[128,1536]{0,1:T(8,128)(2,1)}, bf16[128,1536]{0,1:T(8,128)(2,1)}, u32[]{:S(2)}, u32[]{:S(2)}) %collective-permute-start.25) | collective-permute-done | bytes 393248 | tf_op jit(solution)/shard_map/ppermute | solution.py:277
  446.6 13.0 %subtract_add_fusion.1 = (f32[1024,2048]{1,0:T(8,128)}, bf16[1024,2048]{1,0:T(8,128)(2,1)}) fusion(bf16[1024,2048]{1,0:T(8,128)(2,1)} %param.39, f32[1024]{0:T(1024)S(1)} %broadcast_multiply_fusion.3, f32[1024]{0:T(1024)S(1)} %get-tuple-element.419, f32[2048]{0:T(1024)S(1)} %copy-done.132, f32[1024]{0:T(1024)S(1)} %get-tuple-element.418, ...), kind=kLoop, calls=%fused_computation.8 | loop fusion | flops 31457280 | bytes 33574912 | tf_op jit(solution)/shard_map/add | solution.py:368
  459.7 6.0 fusion.16
  469.3 3.4 fusion.33
  495.8 3.4 collective-permute-done.38
  510.5 15.3 %collective-permute-done.42 = bf16[128,512]{1,0:T(8,128)(2,1)S(1)} collective-permute-done((bf16[128,512]{1,0:T(8,128)(2,1)S(1)}, bf16[128,512]{1,0:T(8,128)(2,1)S(1)}, u32[]{:S(2)}, u32[]{:S(2)}) %collective-permute-start.42) | collective-permute-done | bytes 131104 | tf_op jit(solution)/shard_map/ppermute | solution.py:277
  533.2 14.6 %collective-permute-done.46 = bf16[128,512]{1,0:T(8,128)(2,1)S(1)} collective-permute-done((bf16[128,512]{1,0:T(8,128)(2,1)S(1)}, bf16[128,512]{1,0:T(8,128)(2,1)S(1)}, u32[]{:S(2)}, u32[]{:S(2)}) %collective-permute-start.46) | collective-permute-done | bytes 131104 | tf_op jit(solution)/shard_map/ppermute | solution.py:277
  559.4 9.3 %collective-permute-done.50 = bf16[128,512]{1,0:T(8,128)(2,1)S(1)} collective-permute-done((bf16[128,512]{1,0:T(8,128)(2,1)S(1)}, bf16[128,512]{1,0:T(8,128)(2,1)S(1)}, u32[]{:S(2)}, u32[]{:S(2)}) %collective-permute-start.50) | collective-permute-done | bytes 131104 | tf_op jit(solution)/shard_map/ppermute | solution.py:277
  578.3 2.9 copy.323
  585.5 5.4 multiply_reduce_fusion.6
  593.1 5.5 add_add_fusion
  606.2 5.6 fusion.112
  614.4 5.5 add_convert_fusion
  655.9 4.3 collective-permute-done.66
  660.3 25.4 %collective-permute-done.56 = bf16[512,2048]{1,0:T(8,128)(2,1)S(1)} collective-permute-done((bf16[512,2048]{1,0:T(8,128)(2,1)S(1)}, bf16[512,2048]{1,0:T(8,128)(2,1)S(1)}, u32[]{:S(2)}, u32[]{:S(2)}) %collective-permute-start.56) | collective-permute-done | bytes 2097184 | tf_op jit(solution)/shard_map/ppermute | solution.py:223
  691.4 5.3 collective-permute-done.74
  700.8 3.9 collective-permute-done.75
  709.0 4.1 collective-permute-done.76
  727.4 4.8 multiply_reduce_fusion
  733.0 3.1 collective-permute-done.61
  736.3 7.8 %subtract_add_fusion = f32[1024,2048]{1,0:T(8,128)} fusion(f32[1024,2048]{1,0:T(8,128)} %get-tuple-element.101, bf16[1024,2048]{1,0:T(8,128)(2,1)S(1)} %copy-done.8, f32[1024]{0:T(1024)S(1)} %broadcast_multiply_fusion.2, f32[1024]{0:T(1024)S(1)} %copy-done.135, f32[2048]{0:T(1024)S(1)} %copy-done.124, f32[1024]{0:T(1024)S(1)} %copy-done.134, ...), kind=kLoop, calls=%fused_computation.5 | loop fusion | flops 23068672 | bytes 25186304 | tf_op jit(solution)/shard_map/add | solution.py:424
  (724 shorter events, 322.0 us)
Async XLA Ops:
  81.0 26.6 %collective-permute-start.4 = (bf16[256,2048]{1,0:T(8,128)(2,1)S(1)}, bf16[256,2048]{1,0:T(8,128)(2,1)S(1)}, u32[]{:S(2)}, u32[]{:S(2)}) collective-permute-start(bf16[256,2048]{1,0:T(8,128)(2,1)S(1)} %add_convert_fusion.12), channel_id=1, source_target_pairs={{0,2},{1,3},{2,0},{3,1},{4,6},{5,7},{6,4},{7,5},{8,10},{9,11},{10,... | collective-permute-start | bytes 3145736 | tf_op jit(solution)/shard_map/ppermute | solution.py:223
  85.2 44.7 %collective-permute-start.1 = (bf16[256,2048]{1,0:T(8,128)(2,1)S(1)}, bf16[256,2048]{1,0:T(8,128)(2,1)S(1)}, u32[]{:S(2)}, u32[]{:S(2)}) collective-permute-start(bf16[256,2048]{1,0:T(8,128)(2,1)S(1)} %add_convert_fusion.14), channel_id=1, source_target_pairs={{0,2},{1,3},{2,0},{3,1},{4,6},{5,7},{6,4},{7,5},{8,10},{9,11},{10,... | collective-permute-start | bytes 3145736 | tf_op jit(solution)/shard_map/ppermute | solution.py:223
  109.0 63.7 %collective-permute-start.5 = (bf16[256,2048]{1,0:T(8,128)(2,1)}, bf16[256,2048]{1,0:T(8,128)(2,1)}, u32[]{:S(2)}, u32[]{:S(2)}) collective-permute-start(bf16[256,2048]{1,0:T(8,128)(2,1)} %add_convert_fusion.11), channel_id=1, source_target_pairs={{0,1},{1,0},{2,3},{3,2},{4,5},{5,4},{6,7},{7,6},{8,9},{9,8},{10,11... | collective-permute-start | bytes 3145736 | tf_op jit(solution)/shard_map/ppermute | solution.py:225
  131.3 43.3 %collective-permute-start.2 = (bf16[256,2048]{1,0:T(8,128)(2,1)}, bf16[256,2048]{1,0:T(8,128)(2,1)}, u32[]{:S(2)}, u32[]{:S(2)}) collective-permute-start(bf16[256,2048]{1,0:T(8,128)(2,1)} %add_convert_fusion.13), channel_id=1, source_target_pairs={{0,1},{1,0},{2,3},{3,2},{4,5},{5,4},{6,7},{7,6},{8,9},{9,8},{10,11... | collective-permute-start | bytes 3145736 | tf_op jit(solution)/shard_map/ppermute | solution.py:225
  202.0 30.3 %collective-permute-start.15 = (bf16[256,2048]{1,0:T(8,128)(2,1)S(1)}, bf16[256,2048]{1,0:T(8,128)(2,1)S(1)}, u32[]{:S(2)}, u32[]{:S(2)}) collective-permute-start(bf16[256,2048]{1,0:T(8,128)(2,1)S(1)} %constant_dynamic-slice_fusion.68), channel_id=1, source_target_pairs={{0,1},{1,0},{2,3},{3,2},{4,5},{5,4},{6,7},{7,6},{8,9},{9,8},{10,11... | collective-permute-start | bytes 3145736 | tf_op jit(solution)/shard_map/ppermute | solution.py:221
  227.8 18.9 %collective-permute-start.12 = (bf16[256,2048]{1,0:T(8,128)(2,1)}, bf16[256,2048]{1,0:T(8,128)(2,1)}, u32[]{:S(2)}, u32[]{:S(2)}) collective-permute-start(bf16[256,2048]{1,0:T(8,128)(2,1)} %constant_dynamic-slice_fusion.71), channel_id=1, source_target_pairs={{0,1},{1,0},{2,3},{3,2},{4,5},{5,4},{6,7},{7,6},{8,9},{9,8},{10,11... | collective-permute-start | bytes 3145736 | tf_op jit(solution)/shard_map/ppermute | solution.py:221
  229.9 15.6 %collective-permute-start.9 = (bf16[128,1536]{0,1:T(8,128)(2,1)}, bf16[128,1536]{0,1:T(8,128)(2,1)}, u32[]{:S(2)}, u32[]{:S(2)}) collective-permute-start(bf16[128,1536]{0,1:T(8,128)(2,1)} %get-tuple-element.300), channel_id=1, source_target_pairs={{8,0},{16,8},{24,16},{28,24},{20,28},{12,20},{4,12},{0,4},{9,1},{1... | collective-permute-start | bytes 1179656 | tf_op jit(solution)/shard_map/ppermute | solution.py:277
  231.4 15.2 %collective-permute-start.7 = (bf16[128,1536]{0,1:T(8,128)(2,1)}, bf16[128,1536]{0,1:T(8,128)(2,1)S(1)}, u32[]{:S(2)}, u32[]{:S(2)}) collective-permute-start(bf16[128,1536]{0,1:T(8,128)(2,1)} %get-tuple-element.301), channel_id=1, source_target_pairs={{0,8},{8,16},{16,24},{24,28},{28,20},{20,12},{12,4},{4,0},{1,9},{9... | collective-permute-start | bytes 1179656 | tf_op jit(solution)/shard_map/ppermute | solution.py:276
  233.6 26.3 %collective-permute-start.16 = (bf16[256,2048]{1,0:T(8,128)(2,1)}, bf16[256,2048]{1,0:T(8,128)(2,1)}, u32[]{:S(2)}, u32[]{:S(2)}) collective-permute-start(bf16[256,2048]{1,0:T(8,128)(2,1)} %add_convert_fusion.8), channel_id=1, source_target_pairs={{0,2},{1,3},{2,0},{3,1},{4,6},{5,7},{6,4},{7,5},{8,10},{9,11},{10,... | collective-permute-start | bytes 3145736 | tf_op jit(solution)/shard_map/ppermute | solution.py:223
  248.8 31.7 %collective-permute-start.13 = (bf16[256,2048]{1,0:T(8,128)(2,1)S(1)}, bf16[256,2048]{1,0:T(8,128)(2,1)S(1)}, u32[]{:S(2)}, u32[]{:S(2)}) collective-permute-start(bf16[256,2048]{1,0:T(8,128)(2,1)S(1)} %add_convert_fusion.10), channel_id=1, source_target_pairs={{0,2},{1,3},{2,0},{3,1},{4,6},{5,7},{6,4},{7,5},{8,10},{9,11},{10,... | collective-permute-start | bytes 3145736 | tf_op jit(solution)/shard_map/ppermute | solution.py:223
  251.8 36.3 %collective-permute-start.11 = (bf16[128,1536]{0,1:T(8,128)(2,1)}, bf16[128,1536]{0,1:T(8,128)(2,1)}, u32[]{:S(2)}, u32[]{:S(2)}) collective-permute-start(bf16[128,1536]{0,1:T(8,128)(2,1)} %get-tuple-element.298), channel_id=1, source_target_pairs={{8,0},{16,8},{24,16},{28,24},{20,28},{12,20},{4,12},{0,4},{9,1},{1... | collective-permute-start | bytes 1179656 | tf_op jit(solution)/shard_map/ppermute | solution.py:277
  253.4 35.8 %collective-permute-start.10 = (bf16[128,1536]{0,1:T(8,128)(2,1)S(1)}, bf16[128,1536]{0,1:T(8,128)(2,1)}, u32[]{:S(2)}, u32[]{:S(2)}) collective-permute-start(bf16[128,1536]{0,1:T(8,128)(2,1)S(1)} %get-tuple-element.299), channel_id=1, source_target_pairs={{0,8},{8,16},{16,24},{24,28},{28,20},{20,12},{12,4},{4,0},{1,9},{9... | collective-permute-start | bytes 1179656 | tf_op jit(solution)/shard_map/ppermute | solution.py:276
  261.9 28.3 %collective-permute-start.17 = (bf16[256,2048]{1,0:T(8,128)(2,1)S(1)}, bf16[256,2048]{1,0:T(8,128)(2,1)}, u32[]{:S(2)}, u32[]{:S(2)}) collective-permute-start(bf16[256,2048]{1,0:T(8,128)(2,1)S(1)} %add_convert_fusion.7), channel_id=1, source_target_pairs={{0,1},{1,0},{2,3},{3,2},{4,5},{5,4},{6,7},{7,6},{8,9},{9,8},{10,11... | collective-permute-start | bytes 3145736 | tf_op jit(solution)/shard_map/ppermute | solution.py:225
  297.4 20.3 %collective-permute-start.19 = (bf16[128,1536]{0,1:T(8,128)(2,1)S(1)}, bf16[128,1536]{0,1:T(8,128)(2,1)S(1)}, u32[]{:S(2)}, u32[]{:S(2)}) collective-permute-start(bf16[128,1536]{0,1:T(8,128)(2,1)S(1)} %get-tuple-element.294), channel_id=1, source_target_pairs={{8,0},{16,8},{24,16},{28,24},{20,28},{12,20},{4,12},{0,4},{9,1},{1... | collective-permute-start | bytes 1179656 | tf_op jit(solution)/shard_map/ppermute | solution.py:277
  299.2 18.6 %collective-permute-start.18 = (bf16[128,1536]{0,1:T(8,128)(2,1)S(1)}, bf16[128,1536]{0,1:T(8,128)(2,1)S(1)}, u32[]{:S(2)}, u32[]{:S(2)}) collective-permute-start(bf16[128,1536]{0,1:T(8,128)(2,1)S(1)} %get-tuple-element.295), channel_id=1, source_target_pairs={{0,8},{8,16},{16,24},{24,28},{28,20},{20,12},{12,4},{4,0},{1,9},{9... | collective-permute-start | bytes 1179656 | tf_op jit(solution)/shard_map/ppermute | solution.py:276
  319.6 21.6 %collective-permute-start.21 = (bf16[128,1536]{0,1:T(8,128)(2,1)S(1)}, bf16[128,1536]{0,1:T(8,128)(2,1)S(1)}, u32[]{:S(2)}, u32[]{:S(2)}) collective-permute-start(bf16[128,1536]{0,1:T(8,128)(2,1)S(1)} %get-tuple-element.292), channel_id=1, source_target_pairs={{8,0},{16,8},{24,16},{28,24},{20,28},{12,20},{4,12},{0,4},{9,1},{1... | collective-permute-start | bytes 1179656 | tf_op jit(solution)/shard_map/ppermute | solution.py:277
  321.3 20.0 %collective-permute-start.20 = (bf16[128,1536]{0,1:T(8,128)(2,1)S(1)}, bf16[128,1536]{0,1:T(8,128)(2,1)S(1)}, u32[]{:S(2)}, u32[]{:S(2)}) collective-permute-start(bf16[128,1536]{0,1:T(8,128)(2,1)S(1)} %get-tuple-element.293), channel_id=1, source_target_pairs={{0,8},{8,16},{16,24},{24,28},{28,20},{20,12},{12,4},{4,0},{1,9},{9... | collective-permute-start | bytes 1179656 | tf_op jit(solution)/shard_map/ppermute | solution.py:276
  322.1 23.6 %collective-permute-start.30 = (bf16[512,2048]{1,0:T(8,128)(2,1)S(1)}, bf16[512,2048]{1,0:T(8,128)(2,1)S(1)}, u32[]{:S(2)}, u32[]{:S(2)}) collective-permute-start(bf16[512,2048]{1,0:T(8,128)(2,1)S(1)} %constant_dynamic-slice_fusion.51), channel_id=1, source_target_pairs={{0,1},{1,0},{2,3},{3,2},{4,5},{5,4},{6,7},{7,6},{8,9},{9,8},{10,11... | collective-permute-start | bytes 6291464 | tf_op jit(solution)/shard_map/ppermute | solution.py:221
  346.5 47.5 %collective-permute-start.31 = (bf16[512,2048]{1,0:T(8,128)(2,1)S(1)}, bf16[512,2048]{1,0:T(8,128)(2,1)S(1)}, u32[]{:S(2)}, u32[]{:S(2)}) collective-permute-start(bf16[512,2048]{1,0:T(8,128)(2,1)S(1)} %add_convert_fusion.6), channel_id=1, source_target_pairs={{0,2},{1,3},{2,0},{3,1},{4,6},{5,7},{6,4},{7,5},{8,10},{9,11},{10,... | collective-permute-start | bytes 6291464 | tf_op jit(solution)/shard_map/ppermute | solution.py:223
  361.1 35.1 %collective-permute-start.26 = (bf16[128,3072]{1,0:T(8,128)(2,1)}, bf16[128,3072]{1,0:T(8,128)(2,1)}, u32[]{:S(2)}, u32[]{:S(2)}) collective-permute-start(bf16[128,3072]{1,0:T(8,128)(2,1)} %pad_maximum_fusion.8), channel_id=1, source_target_pairs={{0,8},{8,16},{16,24},{24,28},{28,20},{20,12},{12,4},{4,0},{1,9},{9... | collective-permute-start | bytes 2359304 | tf_op jit(solution)/shard_map/ppermute | solution.py:276
  370.5 29.7 %collective-permute-start.28 = (bf16[128,3072]{1,0:T(8,128)(2,1)S(1)}, bf16[128,3072]{1,0:T(8,128)(2,1)S(1)}, u32[]{:S(2)}, u32[]{:S(2)}) collective-permute-start(bf16[128,3072]{1,0:T(8,128)(2,1)S(1)} %pad_maximum_fusion.9), channel_id=1, source_target_pairs={{8,0},{16,8},{24,16},{28,24},{20,28},{12,20},{4,12},{0,4},{9,1},{1... | collective-permute-start | bytes 2359304 | tf_op jit(solution)/shard_map/ppermute | solution.py:277
  396.2 42.2 %collective-permute-start.32 = (bf16[512,2048]{1,0:T(8,128)(2,1)}, bf16[512,2048]{1,0:T(8,128)(2,1)}, u32[]{:S(2)}, u32[]{:S(2)}) collective-permute-start(bf16[512,2048]{1,0:T(8,128)(2,1)} %add_convert_fusion.5), channel_id=1, source_target_pairs={{0,1},{1,0},{2,3},{3,2},{4,5},{5,4},{6,7},{7,6},{8,9},{9,8},{10,11... | collective-permute-start | bytes 6291464 | tf_op jit(solution)/shard_map/ppermute | solution.py:225
  398.4 35.1 %collective-permute-start.27 = (bf16[128,3072]{1,0:T(8,128)(2,1)}, bf16[128,3072]{1,0:T(8,128)(2,1)}, u32[]{:S(2)}, u32[]{:S(2)}) collective-permute-start(bf16[128,3072]{1,0:T(8,128)(2,1)} %fusion.21), channel_id=1, source_target_pairs={{0,8},{8,16},{16,24},{24,28},{28,20},{20,12},{12,4},{4,0},{1,9},{9... | collective-permute-start | bytes 2359304 | tf_op jit(solution)/shard_map/ppermute | solution.py:276
  401.2 34.8 %collective-permute-start.29 = (bf16[128,3072]{1,0:T(8,128)(2,1)}, bf16[128,3072]{1,0:T(8,128)(2,1)}, u32[]{:S(2)}, u32[]{:S(2)}) collective-permute-start(bf16[128,3072]{1,0:T(8,128)(2,1)} %fusion.22), channel_id=1, source_target_pairs={{8,0},{16,8},{24,16},{28,24},{20,28},{12,20},{4,12},{0,4},{9,1},{1... | collective-permute-start | bytes 2359304 | tf_op jit(solution)/shard_map/ppermute | solution.py:277
  403.9 25.7 %collective-permute-start.25 = (bf16[128,1536]{0,1:T(8,128)(2,1)}, bf16[128,1536]{0,1:T(8,128)(2,1)}, u32[]{:S(2)}, u32[]{:S(2)}) collective-permute-start(bf16[128,1536]{0,1:T(8,128)(2,1)} %get-tuple-element.288), channel_id=1, source_target_pairs={{8,0},{16,8},{24,16},{28,24},{20,28},{12,20},{4,12},{0,4},{9,1},{1... | collective-permute-start | bytes 1179656 | tf_op jit(solution)/shard_map/ppermute | solution.py:277
  405.6 26.0 %collective-permute-start.24 = (bf16[128,1536]{0,1:T(8,128)(2,1)}, bf16[128,1536]{0,1:T(8,128)(2,1)}, u32[]{:S(2)}, u32[]{:S(2)}) collective-permute-start(bf16[128,1536]{0,1:T(8,128)(2,1)} %get-tuple-element.289), channel_id=1, source_target_pairs={{0,8},{8,16},{16,24},{24,28},{28,20},{20,12},{12,4},{4,0},{1,9},{9... | collective-permute-start | bytes 1179656 | tf_op jit(solution)/shard_map/ppermute | solution.py:276
  475.2 25.9 %collective-permute-start.35 = (bf16[128,3072]{1,0:T(8,128)(2,1)}, bf16[128,3072]{1,0:T(8,128)(2,1)}, u32[]{:S(2)}, u32[]{:S(2)}) collective-permute-start(bf16[128,3072]{1,0:T(8,128)(2,1)} %fusion.23), channel_id=1, source_target_pairs={{0,8},{8,16},{16,24},{24,28},{28,20},{20,12},{12,4},{4,0},{1,9},{9... | collective-permute-start | bytes 2359304 | tf_op jit(solution)/shard_map/ppermute | solution.py:276
  477.9 24.6 %collective-permute-start.36 = (bf16[128,3072]{1,0:T(8,128)(2,1)}, bf16[128,3072]{1,0:T(8,128)(2,1)}, u32[]{:S(2)}, u32[]{:S(2)}) collective-permute-start(bf16[128,3072]{1,0:T(8,128)(2,1)} %fusion.24), channel_id=1, source_target_pairs={{8,0},{16,8},{24,16},{28,24},{20,28},{12,20},{4,12},{0,4},{9,1},{1... | collective-permute-start | bytes 2359304 | tf_op jit(solution)/shard_map/ppermute | solution.py:277
  504.1 21.8 %collective-permute-start.39 = (bf16[128,3072]{1,0:T(8,128)(2,1)S(1)}, bf16[128,3072]{1,0:T(8,128)(2,1)S(1)}, u32[]{:S(2)}, u32[]{:S(2)}) collective-permute-start(bf16[128,3072]{1,0:T(8,128)(2,1)S(1)} %fusion.25), channel_id=1, source_target_pairs={{0,8},{8,16},{16,24},{24,28},{28,20},{20,12},{12,4},{4,0},{1,9},{9... | collective-permute-start | bytes 2359304 | tf_op jit(solution)/shard_map/ppermute | solution.py:276
  505.9 20.2 %collective-permute-start.40 = (bf16[128,3072]{1,0:T(8,128)(2,1)S(1)}, bf16[128,3072]{1,0:T(8,128)(2,1)S(1)}, u32[]{:S(2)}, u32[]{:S(2)}) collective-permute-start(bf16[128,3072]{1,0:T(8,128)(2,1)S(1)} %fusion.26), channel_id=1, source_target_pairs={{8,0},{16,8},{24,16},{28,24},{20,28},{12,20},{4,12},{0,4},{9,1},{1... | collective-permute-start | bytes 2359304 | tf_op jit(solution)/shard_map/ppermute | solution.py:277
  507.9 17.9 %collective-permute-start.42 = (bf16[128,512]{1,0:T(8,128)(2,1)S(1)}, bf16[128,512]{1,0:T(8,128)(2,1)S(1)}, u32[]{:S(2)}, u32[]{:S(2)}) collective-permute-start(bf16[128,512]{1,0:T(8,128)(2,1)S(1)} %get-tuple-element.336), channel_id=1, source_target_pairs={{8,0},{16,8},{24,16},{28,24},{20,28},{12,20},{4,12},{0,4},{9,1},{1... | collective-permute-start | bytes 393224 | tf_op jit(solution)/shard_map/ppermute | solution.py:277
  508.5 17.4 %collective-permute-start.41 = (bf16[128,512]{1,0:T(8,128)(2,1)S(1)}, bf16[128,512]{1,0:T(8,128)(2,1)S(1)}, u32[]{:S(2)}, u32[]{:S(2)}) collective-permute-start(bf16[128,512]{1,0:T(8,128)(2,1)S(1)} %get-tuple-element.337), channel_id=1, source_target_pairs={{0,8},{8,16},{16,24},{24,28},{28,20},{20,12},{12,4},{4,0},{1,9},{9... | collective-permute-start | bytes 393224 | tf_op jit(solution)/shard_map/ppermute | solution.py:276
  526.4 21.4 %collective-permute-start.43 = (bf16[128,3072]{1,0:T(8,128)(2,1)S(1)}, bf16[128,3072]{1,0:T(8,128)(2,1)S(1)}, u32[]{:S(2)}, u32[]{:S(2)}) collective-permute-start(bf16[128,3072]{1,0:T(8,128)(2,1)S(1)} %fusion.27), channel_id=1, source_target_pairs={{0,8},{8,16},{16,24},{24,28},{28,20},{20,12},{12,4},{4,0},{1,9},{9... | collective-permute-start | bytes 2359304 | tf_op jit(solution)/shard_map/ppermute | solution.py:276
  528.5 19.5 %collective-permute-start.44 = (bf16[128,3072]{1,0:T(8,128)(2,1)}, bf16[128,3072]{1,0:T(8,128)(2,1)S(1)}, u32[]{:S(2)}, u32[]{:S(2)}) collective-permute-start(bf16[128,3072]{1,0:T(8,128)(2,1)} %fusion.28), channel_id=1, source_target_pairs={{8,0},{16,8},{24,16},{28,24},{20,28},{12,20},{4,12},{0,4},{9,1},{1... | collective-permute-start | bytes 2359304 | tf_op jit(solution)/shard_map/ppermute | solution.py:277
  530.6 17.2 %collective-permute-start.46 = (bf16[128,512]{1,0:T(8,128)(2,1)S(1)}, bf16[128,512]{1,0:T(8,128)(2,1)S(1)}, u32[]{:S(2)}, u32[]{:S(2)}) collective-permute-start(bf16[128,512]{1,0:T(8,128)(2,1)S(1)} %get-tuple-element.334), channel_id=1, source_target_pairs={{8,0},{16,8},{24,16},{28,24},{20,28},{12,20},{4,12},{0,4},{9,1},{1... | collective-permute-start | bytes 393224 | tf_op jit(solution)/shard_map/ppermute | solution.py:277
  531.1 16.6 %collective-permute-start.45 = (bf16[128,512]{1,0:T(8,128)(2,1)S(1)}, bf16[128,512]{1,0:T(8,128)(2,1)S(1)}, u32[]{:S(2)}, u32[]{:S(2)}) collective-permute-start(bf16[128,512]{1,0:T(8,128)(2,1)S(1)} %get-tuple-element.335), channel_id=1, source_target_pairs={{0,8},{8,16},{16,24},{24,28},{28,20},{20,12},{12,4},{4,0},{1,9},{9... | collective-permute-start | bytes 393224 | tf_op jit(solution)/shard_map/ppermute | solution.py:276
  548.4 20.4 %collective-permute-start.47 = (bf16[128,3072]{1,0:T(8,128)(2,1)S(1)}, bf16[128,3072]{1,0:T(8,128)(2,1)S(1)}, u32[]{:S(2)}, u32[]{:S(2)}) collective-permute-start(bf16[128,3072]{1,0:T(8,128)(2,1)S(1)} %fusion.29), channel_id=1, source_target_pairs={{0,8},{8,16},{16,24},{24,28},{28,20},{20,12},{12,4},{4,0},{1,9},{9... | collective-permute-start | bytes 2359304 | tf_op jit(solution)/shard_map/ppermute | solution.py:276
  549.5 19.4 %collective-permute-start.48 = (bf16[128,3072]{1,0:T(8,128)(2,1)S(1)}, bf16[128,3072]{1,0:T(8,128)(2,1)S(1)}, u32[]{:S(2)}, u32[]{:S(2)}) collective-permute-start(bf16[128,3072]{1,0:T(8,128)(2,1)S(1)} %fusion.30), channel_id=1, source_target_pairs={{8,0},{16,8},{24,16},{28,24},{20,28},{12,20},{4,12},{0,4},{9,1},{1... | collective-permute-start | bytes 2359304 | tf_op jit(solution)/shard_map/ppermute | solution.py:277
  569.9 29.1 %collective-permute-start.54 = (bf16[128,512]{1,0:T(8,128)(2,1)}, bf16[128,512]{1,0:T(8,128)(2,1)}, u32[]{:S(2)}, u32[]{:S(2)}) collective-permute-start(bf16[128,512]{1,0:T(8,128)(2,1)} %get-tuple-element.330), channel_id=1, source_target_pairs={{8,0},{16,8},{24,16},{28,24},{20,28},{12,20},{4,12},{0,4},{9,1},{1... | collective-permute-start | bytes 393224 | tf_op jit(solution)/shard_map/ppermute | solution.py:277
  571.0 29.6 %collective-permute-start.53 = (bf16[128,512]{1,0:T(8,128)(2,1)S(1)}, bf16[128,512]{1,0:T(8,128)(2,1)}, u32[]{:S(2)}, u32[]{:S(2)}) collective-permute-start(bf16[128,512]{1,0:T(8,128)(2,1)S(1)} %get-tuple-element.331), channel_id=1, source_target_pairs={{0,8},{8,16},{16,24},{24,28},{28,20},{20,12},{12,4},{4,0},{1,9},{9... | collective-permute-start | bytes 393224 | tf_op jit(solution)/shard_map/ppermute | solution.py:276
  573.0 29.3 %collective-permute-start.51 = (bf16[128,3072]{1,0:T(8,128)(2,1)}, bf16[128,3072]{1,0:T(8,128)(2,1)}, u32[]{:S(2)}, u32[]{:S(2)}) collective-permute-start(bf16[128,3072]{1,0:T(8,128)(2,1)} %fusion.31), channel_id=1, source_target_pairs={{0,8},{8,16},{16,24},{24,28},{28,20},{20,12},{12,4},{4,0},{1,9},{9... | collective-permute-start | bytes 2359304 | tf_op jit(solution)/shard_map/ppermute | solution.py:276
  574.3 29.4 %collective-permute-start.52 = (bf16[128,3072]{1,0:T(8,128)(2,1)}, bf16[128,3072]{1,0:T(8,128)(2,1)}, u32[]{:S(2)}, u32[]{:S(2)}) collective-permute-start(bf16[128,3072]{1,0:T(8,128)(2,1)} %fusion.32), channel_id=1, source_target_pairs={{8,0},{16,8},{24,16},{28,24},{20,28},{12,20},{4,12},{0,4},{9,1},{1... | collective-permute-start | bytes 2359304 | tf_op jit(solution)/shard_map/ppermute | solution.py:277
  624.4 73.6 %collective-permute-start.77 = (bf16[128,512]{1,0:T(8,128)(2,1)S(1)}, bf16[128,512]{1,0:T(8,128)(2,1)S(1)}, u32[]{:S(2)}, u32[]{:S(2)}) collective-permute-start(bf16[128,512]{1,0:T(8,128)(2,1)S(1)} %get-tuple-element.310), channel_id=1, source_target_pairs={{0,8},{8,16},{16,24},{24,28},{28,20},{20,12},{12,4},{4,0},{1,9},{9... | collective-permute-start | bytes 393224 | tf_op jit(solution)/shard_map/ppermute | solution.py:276
  624.7 73.3 %collective-permute-start.78 = (bf16[128,512]{1,0:T(8,128)(2,1)S(1)}, bf16[128,512]{1,0:T(8,128)(2,1)S(1)}, u32[]{:S(2)}, u32[]{:S(2)}) collective-permute-start(bf16[128,512]{1,0:T(8,128)(2,1)S(1)} %get-tuple-element.311), channel_id=1, source_target_pairs={{8,0},{16,8},{24,16},{28,24},{20,28},{12,20},{4,12},{0,4},{9,1},{1... | collective-permute-start | bytes 393224 | tf_op jit(solution)/shard_map/ppermute | solution.py:277
  638.5 47.3 %collective-permute-start.56 = (bf16[512,2048]{1,0:T(8,128)(2,1)S(1)}, bf16[512,2048]{1,0:T(8,128)(2,1)S(1)}, u32[]{:S(2)}, u32[]{:S(2)}) collective-permute-start(bf16[512,2048]{1,0:T(8,128)(2,1)S(1)} %add_convert_fusion.4), channel_id=1, source_target_pairs={{0,2},{1,3},{2,0},{3,1},{4,6},{5,7},{6,4},{7,5},{8,10},{9,11},{10,... | collective-permute-start | bytes 6291464 | tf_op jit(solution)/shard_map/ppermute | solution.py:223
  654.6 33.3 %collective-permute-start.73 = (bf16[128,1024]{0,1:T(8,128)(2,1)S(1)}, bf16[128,1024]{0,1:T(8,128)(2,1)S(1)}, u32[]{:S(2)}, u32[]{:S(2)}) collective-permute-start(bf16[128,1024]{0,1:T(8,128)(2,1)S(1)} %fusion.83), channel_id=1, source_target_pairs={{8,0},{16,8},{24,16},{28,24},{20,28},{12,20},{4,12},{0,4},{9,1},{1... | collective-permute-start | bytes 786440 | tf_op jit(solution)/shard_map/ppermute | solution.py:277
  660.3 30.2 %collective-permute-start.67 = (bf16[128,1024]{0,1:T(8,128)(2,1)S(1)}, bf16[128,1024]{0,1:T(8,128)(2,1)S(1)}, u32[]{:S(2)}, u32[]{:S(2)}) collective-permute-start(bf16[128,1024]{0,1:T(8,128)(2,1)S(1)} %fusion.78), channel_id=1, source_target_pairs={{0,8},{8,16},{16,24},{24,28},{28,20},{20,12},{12,4},{4,0},{1,9},{9... | collective-permute-start | bytes 786440 | tf_op jit(solution)/shard_map/ppermute | solution.py:276
  687.9 26.1 %collective-permute-start.57 = (bf16[512,2048]{1,0:T(8,128)(2,1)}, bf16[512,2048]{1,0:T(8,128)(2,1)}, u32[]{:S(2)}, u32[]{:S(2)}) collective-permute-start(bf16[512,2048]{1,0:T(8,128)(2,1)} %add_convert_fusion.3), channel_id=1, source_target_pairs={{0,1},{1,0},{2,3},{3,2},{4,5},{5,4},{6,7},{7,6},{8,9},{9,8},{10,11... | collective-permute-start | bytes 6291464 | tf_op jit(solution)/shard_map/ppermute | solution.py:225
  (194 other events, 1597.5 us)

commit v7 on v5

--- a/solution.py
+++ b/solution.py
@@ -209,18 +209,19 @@
                 self.half_of = [0 if t < same[t][0] else 1 for t in range(4)]
                 self.tp_ok = True
 
-    def tp_sum(self, part):
+    def tp_sum(self, part, ties=()):
         if not self.tp_ok:
             return lax.psum(part.astype(jnp.float32), "tensor").astype(jnp.bfloat16)
+        ties = list(ties) + [lambda x: x] * (2 - len(ties))
         rows = part.shape[0]
         h = rows // 2
         t = lax.axis_index("tensor")
         half = jnp.array(self.half_of, jnp.int32)[t]
         keep = lax.dynamic_slice_in_dim(part, half * h, h, 0)
         give = lax.dynamic_slice_in_dim(part, (1 - half) * h, h, 0)
-        got = lax.ppermute(give, "tensor", self.core_pairs)
+        got = ties[0](lax.ppermute(give, "tensor", self.core_pairs))
         chip_sum = (keep.astype(jnp.float32) + got.astype(jnp.float32)).astype(jnp.bfloat16)
-        other = lax.ppermute(chip_sum, "tensor", self.chip_pairs)
+        other = ties[1](lax.ppermute(chip_sum, "tensor", self.chip_pairs))
         done = (chip_sum.astype(jnp.float32) + other.astype(jnp.float32)).astype(jnp.bfloat16)
         partner = lax.ppermute(done, "tensor", self.core_pairs)
         first = jnp.where(half == 0, done, partner)
@@ -328,7 +329,7 @@
         down = Ring(plan, [down_grad_t])
         down.step()
         mlp_part = matmul(hidden, w_down).astype(jnp.bfloat16)
-        mixed = (resid + plan.tp_sum(mlp_part).astype(jnp.float32)).astype(jnp.bfloat16)
+        mlp_sum = plan.tp_sum(mlp_part)
 
         def down_hook(values):
             if down.done < down.steps:
@@ -341,14 +342,24 @@
         gate_grad, upper_grad = pull(hidden_grad)
         gate_grad = gate_grad.astype(jnp.bfloat16)
         upper_grad = upper_grad.astype(jnp.bfloat16)
-        gate_grad, upper_grad = down_hook((gate_grad, upper_grad))
+        gate_grad, upper_grad, mlp_sum = down_hook((gate_grad, upper_grad, mlp_sum))
+        mixed = (resid + mlp_sum.astype(jnp.float32)).astype(jnp.bfloat16)
         mid_part = (outer_cols(gate_grad, w_gate) + outer_cols(upper_grad, w_up)).astype(
             jnp.bfloat16
         )
         mid_part, gate_grad, upper_grad = down_hook((mid_part, gate_grad, upper_grad))
-        mid_sum = plan.tp_sum(mid_part)
-        gate_w_grad = down_hook(inner_rows(normed_mid, gate_grad))
-        up_w_grad = down_hook(inner_rows(normed_mid, upper_grad))
+        held = {}
+
+        def tie_gate(got):
+            held["gate"], got = down_hook((inner_rows(normed_mid, gate_grad), got))
+            return got
+
+        def tie_up(got):
+            held["up"], got = down_hook((inner_rows(normed_mid, upper_grad), got))
+            return got
+
+        mid_sum = plan.tp_sum(mid_part, (tie_gate, tie_up))
+        gate_w_grad, up_w_grad = held["gate"], held["up"]
         big = Ring(plan, [gate_w_grad, up_w_grad])
         big.step()
         mid_grad = mid_sum.astype(jnp.float32)
@@ -393,10 +404,19 @@
         in_part, q_grad, k_grad, v_grad = lax.optimization_barrier(
             (in_part, q_grad, k_grad, v_grad)
         )
-        in_sum = plan.tp_sum(in_part)
-        query_w_grad = inner_rows(normed_in, q_grad)
-        key_w_grad = inner_rows(normed_in, k_grad)
-        value_w_grad = inner_rows(normed_in, v_grad)
+
+        def tie_query(got):
+            held["query"], got = lax.optimization_barrier((inner_rows(normed_in, q_grad), got))
+            return got
+
+        def tie_kv(got):
+            held["key"], held["value"], got = lax.optimization_barrier(
+                (inner_rows(normed_in, k_grad), inner_rows(normed_in, v_grad), got)
+            )
+            return got
+
+        in_sum = plan.tp_sum(in_part, (tie_query, tie_kv))
+        query_w_grad, key_w_grad, value_w_grad = held["query"], held["key"], held["value"]
         while big.done < big.steps:
             big.step()
         while small.done < small.steps:

time: 709 us -> 718 us (1.013)
  waiting for transfers between devices: 237 us -> 247 us
  local copies, waits for them, and re-layouts: 87 us -> 78.1 us
    unnamed x267 -> x244, local copies, waits for them, and re-layouts: 29.6 us -> 22.5 us
  transfers between devices with their start and end apart: 73 -> 73, of which waited for: 27 -> 34; matrix products, arithmetic and copies ran while one was open for 27% -> 24% of each run, Pallas kernels for 0% -> 0%
where the time goes in v7:
time: 718 us; the launch traced here: 710 us
  waiting for transfers between devices  247 us (34%)
  other arithmetic  149 us (21%)
  matrix products  137 us (19%)
  local copies, waits for them, and re-layouts  78.1 us (11%)
  starting transfers between devices  74.8 us (10%)
  between operations  23.6 us (3%)
    ppermute x4, waiting for transfers between devices, tp_sum(): other = ties[1](lax.ppermute(chip_sum, 'tensor', self.chip_pairs))  133 us
    ppermute x28, waiting for transfers between devices, step(): got_b = lax.ppermute(send_b.astype(jnp.bfloat16), 'dp', self.plan.ccw)  69.5 us
    dot_general x7, matrix products, outer_cols(): lax.dot_general(left, right, (((1,), (1,)), ((), ())), preferred_element_...  48.4 us
    dot_general x7, matrix products, matmul(): return jnp.dot(left, right, preferred_element_type=jnp.float32)  44.5 us
    dot_general x7, matrix products, inner_rows(): lax.dot_general(left, right, (((0,), (0,)), ((), ())), preferred_element_...  39.1 us
    ppermute x28, waiting for transfers between devices, step(): got_a = lax.ppermute(send_a.astype(jnp.bfloat16), 'dp', self.plan.cw)  36.2 us
    ppermute x28, starting transfers between devices, step(): got_b = lax.ppermute(send_b.astype(jnp.bfloat16), 'dp', self.plan.ccw)  33.5 us
    ppermute x28, starting transfers between devices, step(): got_a = lax.ppermute(send_a.astype(jnp.bfloat16), 'dp', self.plan.cw)  26 us
  transfers between devices with their start and end apart: 73, of which 34 were waited for; matrix products, arithmetic and copies ran while one was open for 24% of the time, Pallas kernels for 0%

profile of v7, /device:TPU:0, one launch (start us, length us, event | category | flops | bytes accessed | tf_op | source)
XLA Modules:
  0.0 709.6 jit_solution(15154432725561612762)
XLA Ops:
  0.7 3.2 fusion.1
  16.0 6.9 fusion.93
  25.7 3.5 reshape.555
  32.1 3.5 copy.242
  36.9 4.5 convolution_convert_fusion.3
  46.7 4.6 copy.201
  67.6 3.5 collective-permute-done
  77.0 45.9 %collective-permute-done.1 = bf16[512,2048]{1,0:T(8,128)(2,1)S(1)} collective-permute-done((bf16[512,2048]{1,0:T(8,128)(2,1)S(1)}, bf16[512,2048]{1,0:T(8,128)(2,1)S(1)}, u32[]{:S(2)}, u32[]{:S(2)}) %collective-permute-start.1) | collective-permute-done | bytes 2097184 | tf_op jit(solution)/shard_map/ppermute | solution.py:224
  142.4 3.9 convert_add_fusion
  146.9 5.9 multiply_convert_fusion
  152.9 10.3 %fusion.94 = f32[1024,1536]{1,0:T(8,128)S(1)} fusion(bf16[1024,2048]{1,0:T(8,128)(2,1)S(1)} %multiply_convert_fusion, bf16[2048,1536]{1,0:T(8,128)(2,1)} %param.34), kind=kOutput, calls=%fused_computation.343 | convolution fusion | flops 6442450944 | bytes 16777216 | tf_op jit(solution)/shard_map/dot_general | solution.py:23
  163.3 9.6 %multiply_convert_fusion.2 = (bf16[1024,1536]{1,0:T(8,128)(2,1)}, f32[1024,1536]{1,0:T(8,128)}) fusion(f32[1024,1536]{1,0:T(8,128)S(1)} %fusion.94, bf16[1024,2048]{1,0:T(8,128)(2,1)S(1)} %multiply_convert_fusion, bf16[2048,1536]{1,0:T(8,128)(2,1)S(1)} %bitcast.230), kind=kOutput, calls=%fused_computation.25 | convolution fusion | flops 6451888128 | bytes 26214400 | tf_op jit(solution)/shard_map/dot_general | solution.py:23
  172.9 8.7 %convolution_convert_fusion = bf16[1024,2048]{1,0:T(8,128)(2,1)S(1)} fusion(bf16[1024,1536]{1,0:T(8,128)(2,1)} %get-tuple-element.426, bf16[1536,2048]{1,0:T(8,128)(2,1)S(1)} %bitcast.228), kind=kOutput, calls=%fused_computation.39 | convolution fusion | flops 6444548096 | bytes 13631488 | tf_op jit(solution)/shard_map/dot_general | solution.py:23
  183.7 8.7 %fusion.95 = f32[1536,2048]{1,0:T(8,128)S(1)} fusion(bf16[1024,1536]{1,0:T(8,128)(2,1)} %get-tuple-element.426, bf16[1024,2048]{1,0:T(8,128)(2,1)S(1)} %copy-done.40), kind=kOutput, calls=%fused_computation.344 | convolution fusion | flops 6442450944 | bytes 19922944 | tf_op jit(solution)/shard_map/dot_general | solution.py:27
  194.8 3.1 add_convert_fusion.8
  199.7 4.7 collective-permute-done.5
  208.8 9.0 %fusion.96 = f32[1024,1536]{1,0:T(8,128)} fusion(bf16[1024,2048]{1,0:T(8,128)(2,1)S(1)} %copy-done.40, bf16[1536,2048]{1,0:T(8,128)(2,1)S(1)} %bitcast.228), kind=kOutput, calls=%fused_computation.345 | convolution fusion | flops 6442450944 | bytes 16777216 | tf_op jit(solution)/shard_map/dot_general | solution.py:33
  224.3 21.4 %collective-permute-done.10 = bf16[512,2048]{1,0:T(8,128)(2,1)} collective-permute-done((bf16[512,2048]{1,0:T(8,128)(2,1)}, bf16[512,2048]{1,0:T(8,128)(2,1)}, u32[]{:S(2)}, u32[]{:S(2)}) %collective-permute-start.10) | collective-permute-done | bytes 2097184 | tf_op jit(solution)/shard_map/ppermute | solution.py:224
  252.5 5.9 multiply_convert_fusion.1
  258.4 3.6 collective-permute-done.8
  269.6 10.8 %fusion.97 = f32[1024,2048]{1,0:T(8,128)} fusion(bf16[1024,1536]{1,0:T(8,128)(2,1)S(1)} %get-tuple-element.103, bf16[2048,1536]{1,0:T(8,128)(2,1)} %param.35), kind=kOutput, calls=%fused_computation.346 | convolution fusion | flops 6442450944 | bytes 17825792 | tf_op jit(solution)/shard_map/dot_general | solution.py:33
  280.5 10.9 %add_convert_fusion.1 = bf16[1024,2048]{1,0:T(8,128)(2,1)S(1)} fusion(f32[1024,2048]{1,0:T(8,128)} %fusion.97, bf16[1024,1536]{1,0:T(8,128)(2,1)S(1)} %get-tuple-element.99, bf16[2048,1536]{1,0:T(8,128)(2,1)} %param.34), kind=kOutput, calls=%fused_computation.17 | convolution fusion | flops 6446645248 | bytes 22020096 | tf_op jit(solution)/shard_map/dot_general | solution.py:33
  295.7 9.7 %fusion.98 = f32[2048,1536]{1,0:T(8,128)} fusion(bf16[1024,2048]{1,0:T(8,128)(2,1)S(1)} %copy-done.36, bf16[1024,1536]{1,0:T(8,128)(2,1)S(1)} %get-tuple-element.99), kind=kOutput, calls=%fused_computation.347 | convolution fusion | flops 6442450944 | bytes 19922944 | tf_op jit(solution)/shard_map/dot_general | solution.py:27
  308.8 9.6 %fusion.99 = f32[2048,1536]{1,0:T(8,128)} fusion(bf16[1024,2048]{1,0:T(8,128)(2,1)S(1)} %copy-done.36, bf16[1024,1536]{1,0:T(8,128)(2,1)S(1)} %get-tuple-element.103), kind=kOutput, calls=%fused_computation.348 | convolution fusion | flops 6442450944 | bytes 19922944 | tf_op jit(solution)/shard_map/dot_general | solution.py:27
  322.1 7.6 %constant_dynamic-slice_fusion.69 = (f32[128,1536]{1,0:T(8,128)}, f32[128,1536]{1,0:T(8,128)}, f32[128,1536]{1,0:T(8,128)}, f32[128,1536]{1,0:T(8,128)}, f32[128...) fusion(f32[2048,1536]{1,0:T(8,128)} %fusion.98, ...), kind=kLoop, calls=%fused_computation.307 | loop fusion | bytes 22020152 | tf_op jit(solution)/shard_map/dynamic_slice | solution.py:266
  331.3 22.8 %collective-permute-done.19 = bf16[512,2048]{1,0:T(8,128)(2,1)S(1)} collective-permute-done((bf16[512,2048]{1,0:T(8,128)(2,1)S(1)}, bf16[512,2048]{1,0:T(8,128)(2,1)S(1)}, u32[]{:S(2)}, u32[]{:S(2)}) %collective-permute-start.19) | collective-permute-done | bytes 2097184 | tf_op jit(solution)/shard_map/ppermute | solution.py:224
  358.6 7.8 %constant_dynamic-slice_fusion.71 = (f32[128,1536]{1,0:T(8,128)}, f32[128,1536]{1,0:T(8,128)}, f32[128,1536]{1,0:T(8,128)}, f32[128,1536]{1,0:T(8,128)}, f32[128...) fusion(f32[2048,1536]{1,0:T(8,128)} %fusion.99, ...), kind=kLoop, calls=%fused_computation.309 | loop fusion | bytes 22020152 | tf_op jit(solution)/shard_map/dynamic_slice | solution.py:266
  366.4 7.9 %collective-permute-done.22 = bf16[128,3072]{1,0:T(8,128)(2,1)} collective-permute-done((bf16[128,3072]{1,0:T(8,128)(2,1)S(1)}, bf16[128,3072]{1,0:T(8,128)(2,1)}, u32[]{:S(2)}, u32[]{:S(2)}) %collective-permute-start.22) | collective-permute-done | bytes 786464 | tf_op jit(solution)/shard_map/ppermute | solution.py:277
  382.6 20.6 %collective-permute-done.21 = bf16[128,1536]{0,1:T(8,128)(2,1)S(1)} collective-permute-done((bf16[128,1536]{0,1:T(8,128)(2,1)S(1)}, bf16[128,1536]{0,1:T(8,128)(2,1)S(1)}, u32[]{:S(2)}, u32[]{:S(2)}) %collective-permute-start.21) | collective-permute-done | bytes 393248 | tf_op jit(solution)/shard_map/ppermute | solution.py:278
  408.1 3.4 copy-done.3
  415.3 13.9 %subtract_add_fusion = (f32[1024,2048]{1,0:T(8,128)}, bf16[1024,2048]{1,0:T(8,128)(2,1)}) fusion(bf16[1024,2048]{1,0:T(8,128)(2,1)} %param.37, f32[1024]{0:T(1024)S(1)} %broadcast_multiply_fusion.3, f32[1024]{0:T(1024)S(1)} %copy-done.101, f32[2048]{0:T(1024)S(1)} %copy-done.95, f32[1024]{0:T(1024)S(1)} %copy-done.97, ...), kind=kLoop, calls=%fused_computation.15 | loop fusion | flops 41943040 | bytes 33574912 | tf_op jit(solution)/shard_map/add | solution.py:366
  429.2 6.0 fusion.17
  437.4 3.4 fusion.34
  449.3 14.0 %collective-permute-done.32 = bf16[128,512]{1,0:T(8,128)(2,1)} collective-permute-done((bf16[128,512]{1,0:T(8,128)(2,1)S(1)}, bf16[128,512]{1,0:T(8,128)(2,1)}, u32[]{:S(2)}, u32[]{:S(2)}) %collective-permute-start.32) | collective-permute-done | bytes 131104 | tf_op jit(solution)/shard_map/ppermute | solution.py:278
  476.0 10.3 %collective-permute-done.36 = bf16[128,512]{1,0:T(8,128)(2,1)S(1)} collective-permute-done((bf16[128,512]{1,0:T(8,128)(2,1)S(1)}, bf16[128,512]{1,0:T(8,128)(2,1)S(1)}, u32[]{:S(2)}, u32[]{:S(2)}) %collective-permute-start.36) | collective-permute-done | bytes 131104 | tf_op jit(solution)/shard_map/ppermute | solution.py:278
  490.8 6.6 convert_element_type.522
  517.5 12.0 %collective-permute-done.44 = bf16[128,512]{1,0:T(8,128)(2,1)S(1)} collective-permute-done((bf16[128,512]{1,0:T(8,128)(2,1)S(1)}, bf16[128,512]{1,0:T(8,128)(2,1)S(1)}, u32[]{:S(2)}, u32[]{:S(2)}) %collective-permute-start.44) | collective-permute-done | bytes 131104 | tf_op jit(solution)/shard_map/ppermute | solution.py:278
  542.2 3.2 collective-permute-done.45
  548.7 5.6 fusion.85
  556.9 7.5 %add_convert_fusion = bf16[1024,2048]{1,0:T(8,128)(2,1)} fusion(f32[1024,2048]{1,0:T(8,128)} %fusion.85, f32[1024,2048]{1,0:T(8,128)S(1)} %fusion.84, bf16[2048,256]{1,0:T(8,128)(2,1)} %param.29, bf16[32,8,8,128]{3,2,1,0:T(8,128)(2,1)S(1)} %bitcast.216), kind=kOutput, calls=%fused_computation.14 | convolution fusion | flops 1080033280 | bytes 22544384 | tf_op jit(solution)/shard_map/dot_general | solution.py:33
  564.4 3.3 constant_dynamic-slice_fusion.15
  583.9 42.6 %collective-permute-done.50 = bf16[512,2048]{1,0:T(8,128)(2,1)S(1)} collective-permute-done((bf16[512,2048]{1,0:T(8,128)(2,1)S(1)}, bf16[512,2048]{1,0:T(8,128)(2,1)S(1)}, u32[]{:S(2)}, u32[]{:S(2)}) %collective-permute-start.50) | collective-permute-done | bytes 2097184 | tf_op jit(solution)/shard_map/ppermute | solution.py:224
  629.7 4.2 collective-permute-done.57
  644.7 3.3 collective-permute-done.59
  658.1 3.2 collective-permute-done.61
  664.6 3.1 collective-permute-done.62
  680.7 4.3 maximum_convert_fusion.1
  702.4 5.7 fusion.6
  (571 shorter events, 252.3 us)
Async XLA Ops:
  74.1 48.8 %collective-permute-start.1 = (bf16[512,2048]{1,0:T(8,128)(2,1)S(1)}, bf16[512,2048]{1,0:T(8,128)(2,1)S(1)}, u32[]{:S(2)}, u32[]{:S(2)}) collective-permute-start(bf16[512,2048]{1,0:T(8,128)(2,1)S(1)} %add_convert_fusion.10), channel_id=1, source_target_pairs={{0,2},{1,3},{2,0},{3,1},{4,6},{5,7},{6,4},{7,5},{8,10},{9,11},{10,... | collective-permute-start | bytes 6291464 | tf_op jit(solution)/shard_map/ppermute | solution.py:224
  125.1 13.8 %collective-permute-start.2 = (bf16[512,2048]{1,0:T(8,128)(2,1)}, bf16[512,2048]{1,0:T(8,128)(2,1)}, u32[]{:S(2)}, u32[]{:S(2)}) collective-permute-start(bf16[512,2048]{1,0:T(8,128)(2,1)} %add_convert_fusion.9), channel_id=1, source_target_pairs={{0,1},{1,0},{2,3},{3,2},{4,5},{5,4},{6,7},{7,6},{8,9},{9,8},{10,11... | collective-permute-start | bytes 6291464 | tf_op jit(solution)/shard_map/ppermute | solution.py:226
  181.8 13.0 %collective-permute-start.9 = (bf16[512,2048]{1,0:T(8,128)(2,1)S(1)}, bf16[512,2048]{1,0:T(8,128)(2,1)S(1)}, u32[]{:S(2)}, u32[]{:S(2)}) collective-permute-start(bf16[512,2048]{1,0:T(8,128)(2,1)S(1)} %constant_dynamic-slice_fusion.72), channel_id=1, source_target_pairs={{0,1},{1,0},{2,3},{3,2},{4,5},{5,4},{6,7},{7,6},{8,9},{9,8},{10,11... | collective-permute-start | bytes 6291464 | tf_op jit(solution)/shard_map/ppermute | solution.py:222
  192.7 11.7 %collective-permute-start.5 = (bf16[128,1536]{0,1:T(8,128)(2,1)S(1)}, bf16[128,1536]{0,1:T(8,128)(2,1)S(1)}, u32[]{:S(2)}, u32[]{:S(2)}) collective-permute-start(bf16[128,1536]{0,1:T(8,128)(2,1)S(1)} %get-tuple-element.310), channel_id=1, source_target_pairs={{8,0},{16,8},{24,16},{28,24},{20,28},{12,20},{4,12},{0,4},{9,1},{1... | collective-permute-start | bytes 1179656 | tf_op jit(solution)/shard_map/ppermute | solution.py:278
  194.6 11.2 %collective-permute-start.3 = (bf16[128,1536]{0,1:T(8,128)(2,1)S(1)}, bf16[128,1536]{0,1:T(8,128)(2,1)S(1)}, u32[]{:S(2)}, u32[]{:S(2)}) collective-permute-start(bf16[128,1536]{0,1:T(8,128)(2,1)S(1)} %get-tuple-element.311), channel_id=1, source_target_pairs={{0,8},{8,16},{16,24},{24,28},{28,20},{20,12},{12,4},{4,0},{1,9},{9... | collective-permute-start | bytes 1179656 | tf_op jit(solution)/shard_map/ppermute | solution.py:277
  198.0 47.8 %collective-permute-start.10 = (bf16[512,2048]{1,0:T(8,128)(2,1)}, bf16[512,2048]{1,0:T(8,128)(2,1)}, u32[]{:S(2)}, u32[]{:S(2)}) collective-permute-start(bf16[512,2048]{1,0:T(8,128)(2,1)} %add_convert_fusion.8), channel_id=1, source_target_pairs={{0,2},{1,3},{2,0},{3,1},{4,6},{5,7},{6,4},{7,5},{8,10},{9,11},{10,... | collective-permute-start | bytes 6291464 | tf_op jit(solution)/shard_map/ppermute | solution.py:224
  206.8 17.3 %collective-permute-start.6 = (bf16[128,1536]{0,1:T(8,128)(2,1)}, bf16[128,1536]{0,1:T(8,128)(2,1)S(1)}, u32[]{:S(2)}, u32[]{:S(2)}) collective-permute-start(bf16[128,1536]{0,1:T(8,128)(2,1)} %get-tuple-element.308), channel_id=1, source_target_pairs={{8,0},{16,8},{24,16},{28,24},{20,28},{12,20},{4,12},{0,4},{9,1},{1... | collective-permute-start | bytes 1179656 | tf_op jit(solution)/shard_map/ppermute | solution.py:278
  208.4 15.9 %collective-permute-start.4 = (bf16[128,1536]{0,1:T(8,128)(2,1)S(1)}, bf16[128,1536]{0,1:T(8,128)(2,1)S(1)}, u32[]{:S(2)}, u32[]{:S(2)}) collective-permute-start(bf16[128,1536]{0,1:T(8,128)(2,1)S(1)} %get-tuple-element.309), channel_id=1, source_target_pairs={{0,8},{8,16},{16,24},{24,28},{28,20},{20,12},{12,4},{4,0},{1,9},{9... | collective-permute-start | bytes 1179656 | tf_op jit(solution)/shard_map/ppermute | solution.py:277
  248.8 14.6 %collective-permute-start.11 = (bf16[512,2048]{1,0:T(8,128)(2,1)S(1)}, bf16[512,2048]{1,0:T(8,128)(2,1)S(1)}, u32[]{:S(2)}, u32[]{:S(2)}) collective-permute-start(bf16[512,2048]{1,0:T(8,128)(2,1)S(1)} %add_convert_fusion.7), channel_id=1, source_target_pairs={{0,1},{1,0},{2,3},{3,2},{4,5},{5,4},{6,7},{7,6},{8,9},{9,8},{10,11... | collective-permute-start | bytes 6291464 | tf_op jit(solution)/shard_map/ppermute | solution.py:226
  250.4 11.6 %collective-permute-start.8 = (bf16[128,1536]{0,1:T(8,128)(2,1)S(1)}, bf16[128,1536]{0,1:T(8,128)(2,1)S(1)}, u32[]{:S(2)}, u32[]{:S(2)}) collective-permute-start(bf16[128,1536]{0,1:T(8,128)(2,1)S(1)} %get-tuple-element.306), channel_id=1, source_target_pairs={{8,0},{16,8},{24,16},{28,24},{20,28},{12,20},{4,12},{0,4},{9,1},{1... | collective-permute-start | bytes 1179656 | tf_op jit(solution)/shard_map/ppermute | solution.py:278
  252.0 11.2 %collective-permute-start.7 = (bf16[128,1536]{0,1:T(8,128)(2,1)S(1)}, bf16[128,1536]{0,1:T(8,128)(2,1)S(1)}, u32[]{:S(2)}, u32[]{:S(2)}) collective-permute-start(bf16[128,1536]{0,1:T(8,128)(2,1)S(1)} %get-tuple-element.307), channel_id=1, source_target_pairs={{0,8},{8,16},{16,24},{24,28},{28,20},{20,12},{12,4},{4,0},{1,9},{9... | collective-permute-start | bytes 1179656 | tf_op jit(solution)/shard_map/ppermute | solution.py:277
  267.6 23.8 %collective-permute-start.13 = (bf16[128,1536]{0,1:T(8,128)(2,1)S(1)}, bf16[128,1536]{0,1:T(8,128)(2,1)S(1)}, u32[]{:S(2)}, u32[]{:S(2)}) collective-permute-start(bf16[128,1536]{0,1:T(8,128)(2,1)S(1)} %get-tuple-element.302), channel_id=1, source_target_pairs={{8,0},{16,8},{24,16},{28,24},{20,28},{12,20},{4,12},{0,4},{9,1},{1... | collective-permute-start | bytes 1179656 | tf_op jit(solution)/shard_map/ppermute | solution.py:278
  269.2 22.2 %collective-permute-start.12 = (bf16[128,1536]{0,1:T(8,128)(2,1)S(1)}, bf16[128,1536]{0,1:T(8,128)(2,1)S(1)}, u32[]{:S(2)}, u32[]{:S(2)}) collective-permute-start(bf16[128,1536]{0,1:T(8,128)(2,1)S(1)} %get-tuple-element.303), channel_id=1, source_target_pairs={{0,8},{8,16},{16,24},{24,28},{28,20},{20,12},{12,4},{4,0},{1,9},{9... | collective-permute-start | bytes 1179656 | tf_op jit(solution)/shard_map/ppermute | solution.py:277
  291.8 14.6 %collective-permute-start.16 = (bf16[512,2048]{1,0:T(8,128)(2,1)S(1)}, bf16[512,2048]{1,0:T(8,128)(2,1)S(1)}, u32[]{:S(2)}, u32[]{:S(2)}) collective-permute-start(bf16[512,2048]{1,0:T(8,128)(2,1)S(1)} %constant_dynamic-slice_fusion.70), channel_id=1, source_target_pairs={{0,1},{1,0},{2,3},{3,2},{4,5},{5,4},{6,7},{7,6},{8,9},{9,8},{10,11... | collective-permute-start | bytes 6291464 | tf_op jit(solution)/shard_map/ppermute | solution.py:222
  293.6 11.8 %collective-permute-start.15 = (bf16[128,1536]{0,1:T(8,128)(2,1)S(1)}, bf16[128,1536]{0,1:T(8,128)(2,1)S(1)}, u32[]{:S(2)}, u32[]{:S(2)}) collective-permute-start(bf16[128,1536]{0,1:T(8,128)(2,1)S(1)} %get-tuple-element.300), channel_id=1, source_target_pairs={{8,0},{16,8},{24,16},{28,24},{20,28},{12,20},{4,12},{0,4},{9,1},{1... | collective-permute-start | bytes 1179656 | tf_op jit(solution)/shard_map/ppermute | solution.py:278
  295.2 11.0 %collective-permute-start.14 = (bf16[128,1536]{0,1:T(8,128)(2,1)S(1)}, bf16[128,1536]{0,1:T(8,128)(2,1)S(1)}, u32[]{:S(2)}, u32[]{:S(2)}) collective-permute-start(bf16[128,1536]{0,1:T(8,128)(2,1)S(1)} %get-tuple-element.301), channel_id=1, source_target_pairs={{0,8},{8,16},{16,24},{24,28},{28,20},{20,12},{12,4},{4,0},{1,9},{9... | collective-permute-start | bytes 1179656 | tf_op jit(solution)/shard_map/ppermute | solution.py:277
  307.3 46.8 %collective-permute-start.19 = (bf16[512,2048]{1,0:T(8,128)(2,1)S(1)}, bf16[512,2048]{1,0:T(8,128)(2,1)S(1)}, u32[]{:S(2)}, u32[]{:S(2)}) collective-permute-start(bf16[512,2048]{1,0:T(8,128)(2,1)S(1)} %add_convert_fusion.6), channel_id=1, source_target_pairs={{0,2},{1,3},{2,0},{3,1},{4,6},{5,7},{6,4},{7,5},{8,10},{9,11},{10,... | collective-permute-start | bytes 6291464 | tf_op jit(solution)/shard_map/ppermute | solution.py:224
  320.0 11.2 %collective-permute-start.18 = (bf16[128,1536]{0,1:T(8,128)(2,1)S(1)}, bf16[128,1536]{0,1:T(8,128)(2,1)S(1)}, u32[]{:S(2)}, u32[]{:S(2)}) collective-permute-start(bf16[128,1536]{0,1:T(8,128)(2,1)S(1)} %get-tuple-element.298), channel_id=1, source_target_pairs={{8,0},{16,8},{24,16},{28,24},{20,28},{12,20},{4,12},{0,4},{9,1},{1... | collective-permute-start | bytes 1179656 | tf_op jit(solution)/shard_map/ppermute | solution.py:278
  321.6 9.6 %collective-permute-start.17 = (bf16[128,1536]{0,1:T(8,128)(2,1)S(1)}, bf16[128,1536]{0,1:T(8,128)(2,1)S(1)}, u32[]{:S(2)}, u32[]{:S(2)}) collective-permute-start(bf16[128,1536]{0,1:T(8,128)(2,1)S(1)} %get-tuple-element.299), channel_id=1, source_target_pairs={{0,8},{8,16},{16,24},{24,28},{28,20},{20,12},{12,4},{4,0},{1,9},{9... | collective-permute-start | bytes 1179656 | tf_op jit(solution)/shard_map/ppermute | solution.py:277
  356.4 17.9 %collective-permute-start.22 = (bf16[128,3072]{1,0:T(8,128)(2,1)S(1)}, bf16[128,3072]{1,0:T(8,128)(2,1)}, u32[]{:S(2)}, u32[]{:S(2)}) collective-permute-start(bf16[128,3072]{1,0:T(8,128)(2,1)S(1)} %pad_maximum_fusion.2), channel_id=1, source_target_pairs={{0,8},{8,16},{16,24},{24,28},{28,20},{20,12},{12,4},{4,0},{1,9},{9... | collective-permute-start | bytes 2359304 | tf_op jit(solution)/shard_map/ppermute | solution.py:277
  357.0 19.1 %collective-permute-start.24 = (bf16[128,3072]{1,0:T(8,128)(2,1)S(1)}, bf16[128,3072]{1,0:T(8,128)(2,1)}, u32[]{:S(2)}, u32[]{:S(2)}) collective-permute-start(bf16[128,3072]{1,0:T(8,128)(2,1)S(1)} %pad_maximum_fusion.3), channel_id=1, source_target_pairs={{8,0},{16,8},{24,16},{28,24},{20,28},{12,20},{4,12},{0,4},{9,1},{1... | collective-permute-start | bytes 2359304 | tf_op jit(solution)/shard_map/ppermute | solution.py:278
  366.4 41.4 %collective-permute-start.26 = (bf16[512,2048]{1,0:T(8,128)(2,1)S(1)}, bf16[512,2048]{1,0:T(8,128)(2,1)S(1)}, u32[]{:S(2)}, u32[]{:S(2)}) collective-permute-start(bf16[512,2048]{1,0:T(8,128)(2,1)S(1)} %add_convert_fusion.5), channel_id=1, source_target_pairs={{0,1},{1,0},{2,3},{3,2},{4,5},{5,4},{6,7},{7,6},{8,9},{9,8},{10,11... | collective-permute-start | bytes 6291464 | tf_op jit(solution)/shard_map/ppermute | solution.py:226
  375.6 29.6 %collective-permute-start.23 = (bf16[128,3072]{1,0:T(8,128)(2,1)S(1)}, bf16[128,3072]{1,0:T(8,128)(2,1)S(1)}, u32[]{:S(2)}, u32[]{:S(2)}) collective-permute-start(bf16[128,3072]{1,0:T(8,128)(2,1)S(1)} %fusion.22), channel_id=1, source_target_pairs={{0,8},{8,16},{16,24},{24,28},{28,20},{20,12},{12,4},{4,0},{1,9},{9... | collective-permute-start | bytes 2359304 | tf_op jit(solution)/shard_map/ppermute | solution.py:277
  377.4 29.1 %collective-permute-start.25 = (bf16[128,3072]{1,0:T(8,128)(2,1)S(1)}, bf16[128,3072]{1,0:T(8,128)(2,1)S(1)}, u32[]{:S(2)}, u32[]{:S(2)}) collective-permute-start(bf16[128,3072]{1,0:T(8,128)(2,1)S(1)} %fusion.23), channel_id=1, source_target_pairs={{8,0},{16,8},{24,16},{28,24},{20,28},{12,20},{4,12},{0,4},{9,1},{1... | collective-permute-start | bytes 2359304 | tf_op jit(solution)/shard_map/ppermute | solution.py:278
  380.6 22.7 %collective-permute-start.21 = (bf16[128,1536]{0,1:T(8,128)(2,1)S(1)}, bf16[128,1536]{0,1:T(8,128)(2,1)S(1)}, u32[]{:S(2)}, u32[]{:S(2)}) collective-permute-start(bf16[128,1536]{0,1:T(8,128)(2,1)S(1)} %get-tuple-element.296), channel_id=1, source_target_pairs={{8,0},{16,8},{24,16},{28,24},{20,28},{12,20},{4,12},{0,4},{9,1},{1... | collective-permute-start | bytes 1179656 | tf_op jit(solution)/shard_map/ppermute | solution.py:278
  382.2 22.0 %collective-permute-start.20 = (bf16[128,1536]{0,1:T(8,128)(2,1)S(1)}, bf16[128,1536]{0,1:T(8,128)(2,1)S(1)}, u32[]{:S(2)}, u32[]{:S(2)}) collective-permute-start(bf16[128,1536]{0,1:T(8,128)(2,1)S(1)} %get-tuple-element.297), channel_id=1, source_target_pairs={{0,8},{8,16},{16,24},{24,28},{28,20},{20,12},{12,4},{4,0},{1,9},{9... | collective-permute-start | bytes 1179656 | tf_op jit(solution)/shard_map/ppermute | solution.py:277
  442.2 22.1 %collective-permute-start.29 = (bf16[128,3072]{1,0:T(8,128)(2,1)}, bf16[128,3072]{1,0:T(8,128)(2,1)}, u32[]{:S(2)}, u32[]{:S(2)}) collective-permute-start(bf16[128,3072]{1,0:T(8,128)(2,1)} %fusion.24), channel_id=1, source_target_pairs={{0,8},{8,16},{16,24},{24,28},{28,20},{20,12},{12,4},{4,0},{1,9},{9... | collective-permute-start | bytes 2359304 | tf_op jit(solution)/shard_map/ppermute | solution.py:277
  444.7 20.9 %collective-permute-start.30 = (bf16[128,3072]{1,0:T(8,128)(2,1)}, bf16[128,3072]{1,0:T(8,128)(2,1)}, u32[]{:S(2)}, u32[]{:S(2)}) collective-permute-start(bf16[128,3072]{1,0:T(8,128)(2,1)} %fusion.25), channel_id=1, source_target_pairs={{8,0},{16,8},{24,16},{28,24},{20,28},{12,20},{4,12},{0,4},{9,1},{1... | collective-permute-start | bytes 2359304 | tf_op jit(solution)/shard_map/ppermute | solution.py:278
  445.6 17.7 %collective-permute-start.32 = (bf16[128,512]{1,0:T(8,128)(2,1)S(1)}, bf16[128,512]{1,0:T(8,128)(2,1)}, u32[]{:S(2)}, u32[]{:S(2)}) collective-permute-start(bf16[128,512]{1,0:T(8,128)(2,1)S(1)} %get-tuple-element.346), channel_id=1, source_target_pairs={{8,0},{16,8},{24,16},{28,24},{20,28},{12,20},{4,12},{0,4},{9,1},{1... | collective-permute-start | bytes 393224 | tf_op jit(solution)/shard_map/ppermute | solution.py:278
  448.0 16.3 %collective-permute-start.31 = (bf16[128,512]{1,0:T(8,128)(2,1)S(1)}, bf16[128,512]{1,0:T(8,128)(2,1)S(1)}, u32[]{:S(2)}, u32[]{:S(2)}) collective-permute-start(bf16[128,512]{1,0:T(8,128)(2,1)S(1)} %get-tuple-element.347), channel_id=1, source_target_pairs={{0,8},{8,16},{16,24},{24,28},{28,20},{20,12},{12,4},{4,0},{1,9},{9... | collective-permute-start | bytes 393224 | tf_op jit(solution)/shard_map/ppermute | solution.py:277
  467.2 19.1 %collective-permute-start.33 = (bf16[128,3072]{1,0:T(8,128)(2,1)S(1)}, bf16[128,3072]{1,0:T(8,128)(2,1)S(1)}, u32[]{:S(2)}, u32[]{:S(2)}) collective-permute-start(bf16[128,3072]{1,0:T(8,128)(2,1)S(1)} %fusion.26), channel_id=1, source_target_pairs={{0,8},{8,16},{16,24},{24,28},{28,20},{20,12},{12,4},{4,0},{1,9},{9... | collective-permute-start | bytes 2359304 | tf_op jit(solution)/shard_map/ppermute | solution.py:277
  469.0 17.5 %collective-permute-start.34 = (bf16[128,3072]{1,0:T(8,128)(2,1)S(1)}, bf16[128,3072]{1,0:T(8,128)(2,1)S(1)}, u32[]{:S(2)}, u32[]{:S(2)}) collective-permute-start(bf16[128,3072]{1,0:T(8,128)(2,1)S(1)} %fusion.27), channel_id=1, source_target_pairs={{8,0},{16,8},{24,16},{28,24},{20,28},{12,20},{4,12},{0,4},{9,1},{1... | collective-permute-start | bytes 2359304 | tf_op jit(solution)/shard_map/ppermute | solution.py:278
  472.4 13.8 %collective-permute-start.36 = (bf16[128,512]{1,0:T(8,128)(2,1)S(1)}, bf16[128,512]{1,0:T(8,128)(2,1)S(1)}, u32[]{:S(2)}, u32[]{:S(2)}) collective-permute-start(bf16[128,512]{1,0:T(8,128)(2,1)S(1)} %get-tuple-element.344), channel_id=1, source_target_pairs={{8,0},{16,8},{24,16},{28,24},{20,28},{12,20},{4,12},{0,4},{9,1},{1... | collective-permute-start | bytes 393224 | tf_op jit(solution)/shard_map/ppermute | solution.py:278
  473.0 13.3 %collective-permute-start.35 = (bf16[128,512]{1,0:T(8,128)(2,1)S(1)}, bf16[128,512]{1,0:T(8,128)(2,1)S(1)}, u32[]{:S(2)}, u32[]{:S(2)}) collective-permute-start(bf16[128,512]{1,0:T(8,128)(2,1)S(1)} %get-tuple-element.345), channel_id=1, source_target_pairs={{0,8},{8,16},{16,24},{24,28},{28,20},{20,12},{12,4},{4,0},{1,9},{9... | collective-permute-start | bytes 393224 | tf_op jit(solution)/shard_map/ppermute | solution.py:277
  487.7 19.8 %collective-permute-start.37 = (bf16[128,3072]{1,0:T(8,128)(2,1)}, bf16[128,3072]{1,0:T(8,128)(2,1)S(1)}, u32[]{:S(2)}, u32[]{:S(2)}) collective-permute-start(bf16[128,3072]{1,0:T(8,128)(2,1)} %fusion.28), channel_id=1, source_target_pairs={{0,8},{8,16},{16,24},{24,28},{28,20},{20,12},{12,4},{4,0},{1,9},{9... | collective-permute-start | bytes 2359304 | tf_op jit(solution)/shard_map/ppermute | solution.py:277
  490.3 17.3 %collective-permute-start.38 = (bf16[128,3072]{1,0:T(8,128)(2,1)}, bf16[128,3072]{1,0:T(8,128)(2,1)}, u32[]{:S(2)}, u32[]{:S(2)}) collective-permute-start(bf16[128,3072]{1,0:T(8,128)(2,1)} %fusion.29), channel_id=1, source_target_pairs={{8,0},{16,8},{24,16},{28,24},{20,28},{12,20},{4,12},{0,4},{9,1},{1... | collective-permute-start | bytes 2359304 | tf_op jit(solution)/shard_map/ppermute | solution.py:278
  509.3 20.3 %collective-permute-start.41 = (bf16[128,3072]{1,0:T(8,128)(2,1)S(1)}, bf16[128,3072]{1,0:T(8,128)(2,1)S(1)}, u32[]{:S(2)}, u32[]{:S(2)}) collective-permute-start(bf16[128,3072]{1,0:T(8,128)(2,1)S(1)} %fusion.30), channel_id=1, source_target_pairs={{0,8},{8,16},{16,24},{24,28},{28,20},{20,12},{12,4},{4,0},{1,9},{9... | collective-permute-start | bytes 2359304 | tf_op jit(solution)/shard_map/ppermute | solution.py:277
  510.9 18.8 %collective-permute-start.42 = (bf16[128,3072]{1,0:T(8,128)(2,1)S(1)}, bf16[128,3072]{1,0:T(8,128)(2,1)S(1)}, u32[]{:S(2)}, u32[]{:S(2)}) collective-permute-start(bf16[128,3072]{1,0:T(8,128)(2,1)S(1)} %fusion.31), channel_id=1, source_target_pairs={{8,0},{16,8},{24,16},{28,24},{20,28},{12,20},{4,12},{0,4},{9,1},{1... | collective-permute-start | bytes 2359304 | tf_op jit(solution)/shard_map/ppermute | solution.py:278
  514.5 15.0 %collective-permute-start.44 = (bf16[128,512]{1,0:T(8,128)(2,1)S(1)}, bf16[128,512]{1,0:T(8,128)(2,1)S(1)}, u32[]{:S(2)}, u32[]{:S(2)}) collective-permute-start(bf16[128,512]{1,0:T(8,128)(2,1)S(1)} %get-tuple-element.340), channel_id=1, source_target_pairs={{8,0},{16,8},{24,16},{28,24},{20,28},{12,20},{4,12},{0,4},{9,1},{1... | collective-permute-start | bytes 393224 | tf_op jit(solution)/shard_map/ppermute | solution.py:278
  515.6 13.9 %collective-permute-start.43 = (bf16[128,512]{1,0:T(8,128)(2,1)S(1)}, bf16[128,512]{1,0:T(8,128)(2,1)S(1)}, u32[]{:S(2)}, u32[]{:S(2)}) collective-permute-start(bf16[128,512]{1,0:T(8,128)(2,1)S(1)} %get-tuple-element.341), channel_id=1, source_target_pairs={{0,8},{8,16},{16,24},{24,28},{28,20},{20,12},{12,4},{4,0},{1,9},{9... | collective-permute-start | bytes 393224 | tf_op jit(solution)/shard_map/ppermute | solution.py:277
  531.2 9.6 %collective-permute-start.48 = (bf16[128,512]{1,0:T(8,128)(2,1)S(1)}, bf16[128,512]{1,0:T(8,128)(2,1)S(1)}, u32[]{:S(2)}, u32[]{:S(2)}) collective-permute-start(bf16[128,512]{1,0:T(8,128)(2,1)S(1)} %get-tuple-element.338), channel_id=1, source_target_pairs={{8,0},{16,8},{24,16},{28,24},{20,28},{12,20},{4,12},{0,4},{9,1},{1... | collective-permute-start | bytes 393224 | tf_op jit(solution)/shard_map/ppermute | solution.py:278
  531.5 10.0 %collective-permute-start.47 = (bf16[128,512]{1,0:T(8,128)(2,1)S(1)}, bf16[128,512]{1,0:T(8,128)(2,1)S(1)}, u32[]{:S(2)}, u32[]{:S(2)}) collective-permute-start(bf16[128,512]{1,0:T(8,128)(2,1)S(1)} %get-tuple-element.339), channel_id=1, source_target_pairs={{0,8},{8,16},{16,24},{24,28},{28,20},{20,12},{12,4},{4,0},{1,9},{9... | collective-permute-start | bytes 393224 | tf_op jit(solution)/shard_map/ppermute | solution.py:277
  533.4 12.0 %collective-permute-start.45 = (bf16[128,3072]{1,0:T(8,128)(2,1)S(1)}, bf16[128,3072]{1,0:T(8,128)(2,1)S(1)}, u32[]{:S(2)}, u32[]{:S(2)}) collective-permute-start(bf16[128,3072]{1,0:T(8,128)(2,1)S(1)} %fusion.32), channel_id=1, source_target_pairs={{0,8},{8,16},{16,24},{24,28},{28,20},{20,12},{12,4},{4,0},{1,9},{9... | collective-permute-start | bytes 2359304 | tf_op jit(solution)/shard_map/ppermute | solution.py:277
  534.6 12.0 %collective-permute-start.46 = (bf16[128,3072]{1,0:T(8,128)(2,1)S(1)}, bf16[128,3072]{1,0:T(8,128)(2,1)S(1)}, u32[]{:S(2)}, u32[]{:S(2)}) collective-permute-start(bf16[128,3072]{1,0:T(8,128)(2,1)S(1)} %fusion.33), channel_id=1, source_target_pairs={{8,0},{16,8},{24,16},{28,24},{20,28},{12,20},{4,12},{0,4},{9,1},{1... | collective-permute-start | bytes 2359304 | tf_op jit(solution)/shard_map/ppermute | solution.py:278
  570.5 93.1 %collective-permute-start.71 = (bf16[128,512]{1,0:T(8,128)(2,1)S(1)}, bf16[128,512]{1,0:T(8,128)(2,1)S(1)}, u32[]{:S(2)}, u32[]{:S(2)}) collective-permute-start(bf16[128,512]{1,0:T(8,128)(2,1)S(1)} %get-tuple-element.318), channel_id=1, source_target_pairs={{0,8},{8,16},{16,24},{24,28},{28,20},{20,12},{12,4},{4,0},{1,9},{9... | collective-permute-start | bytes 393224 | tf_op jit(solution)/shard_map/ppermute | solution.py:277
  571.4 92.1 %collective-permute-start.72 = (bf16[128,512]{1,0:T(8,128)(2,1)S(1)}, bf16[128,512]{1,0:T(8,128)(2,1)S(1)}, u32[]{:S(2)}, u32[]{:S(2)}) collective-permute-start(bf16[128,512]{1,0:T(8,128)(2,1)S(1)} %get-tuple-element.319), channel_id=1, source_target_pairs={{8,0},{16,8},{24,16},{28,24},{20,28},{12,20},{4,12},{0,4},{9,1},{1... | collective-permute-start | bytes 393224 | tf_op jit(solution)/shard_map/ppermute | solution.py:278
  579.0 47.5 %collective-permute-start.50 = (bf16[512,2048]{1,0:T(8,128)(2,1)S(1)}, bf16[512,2048]{1,0:T(8,128)(2,1)S(1)}, u32[]{:S(2)}, u32[]{:S(2)}) collective-permute-start(bf16[512,2048]{1,0:T(8,128)(2,1)S(1)} %add_convert_fusion.4), channel_id=1, source_target_pairs={{0,2},{1,3},{2,0},{3,1},{4,6},{5,7},{6,4},{7,5},{8,10},{9,11},{10,... | collective-permute-start | bytes 6291464 | tf_op jit(solution)/shard_map/ppermute | solution.py:224
  652.4 25.7 %collective-permute-start.51 = (bf16[512,2048]{1,0:T(8,128)(2,1)}, bf16[512,2048]{1,0:T(8,128)(2,1)}, u32[]{:S(2)}, u32[]{:S(2)}) collective-permute-start(bf16[512,2048]{1,0:T(8,128)(2,1)} %add_convert_fusion.3), channel_id=1, source_target_pairs={{0,1},{1,0},{2,3},{3,2},{4,5},{5,4},{6,7},{7,6},{8,9},{9,8},{10,11... | collective-permute-start | bytes 6291464 | tf_op jit(solution)/shard_map/ppermute | solution.py:226
  (145 other events, 1032.2 us)

commit v8 on v5

--- a/solution.py
+++ b/solution.py
@@ -227,8 +227,8 @@
         second = jnp.where(half == 0, partner, done)
         return jnp.concatenate([first, second], 0)
 
-    def dp_rs(self, grads):
-        ring = Ring(self, grads)
+    def dp_rs(self, lhs, rhs):
+        ring = Ring(self, lhs, rhs)
         for _ in range(ring.steps):
             ring.step()
         return ring.result()
@@ -246,23 +246,37 @@
 
 
 class Ring:
-    def __init__(self, plan, grads):
+    def __init__(self, plan, lhs, rhs):
         self.plan = plan
         self.n = n = plan.n_dp
         self.me = lax.axis_index("dp")
         self.pos = jnp.array(plan.pos, jnp.int32)[self.me]
         self.order = jnp.array(plan.ring, jnp.int32)
-        self.widths = [g.shape[1] for g in grads]
-        self.grads = grads
-        self.rows = grads[0].shape[0] // n
+        self.lhs = lhs
+        self.rhs = rhs
+        self.rows = lhs.shape[1] // n
+        self.widths = [r.shape[1] for r in rhs]
+        total = sum(self.widths)
+        cut = total // 2
+        self.sides = ([], [])
+        start = 0
+        for i, w in enumerate(self.widths):
+            lo, hi = start, start + w
+            if lo < cut:
+                self.sides[0].append((i, 0, min(hi, cut) - lo))
+            if hi > cut:
+                self.sides[1].append((i, max(lo, cut) - lo, w))
+            start = hi
         self.steps = n - 1
         self.done = 0
         self.state = None
 
     def piece(self, index, side):
-        half = self.rows // 2
-        start = index * self.rows + side * half
-        parts = [lax.dynamic_slice_in_dim(g, start, half, 0) for g in self.grads]
+        block = lax.dynamic_slice_in_dim(self.lhs, index * self.rows, self.rows, 1)
+        parts = [
+            inner_rows(block, self.rhs[i] if (lo, hi) == (0, self.widths[i]) else self.rhs[i][:, lo:hi])
+            for i, lo, hi in self.sides[side]
+        ]
         return parts[0] if len(parts) == 1 else jnp.concatenate(parts, 1)
 
     def step(self):
@@ -280,7 +294,7 @@
 
     def result(self):
         acc_a, acc_b = self.state
-        total = jnp.concatenate([acc_a + self.piece(self.me, 0), acc_b + self.piece(self.me, 1)], 0)
+        total = jnp.concatenate([acc_a + self.piece(self.me, 0), acc_b + self.piece(self.me, 1)], 1)
         out, start = [], 0
         for w in self.widths:
             out.append(total[:, start : start + w])
@@ -324,8 +338,7 @@
         gate = matmul(normed_mid, w_gate)
         upper = matmul(normed_mid, w_up)
         hidden = swiglu(gate, upper).astype(jnp.bfloat16)
-        down_grad_t = inner_rows(cotangent, hidden)
-        down = Ring(plan, [down_grad_t])
+        down = Ring(plan, cotangent, [hidden])
         down.step()
         mlp_part = matmul(hidden, w_down).astype(jnp.bfloat16)
         mixed = (resid + plan.tp_sum(mlp_part).astype(jnp.float32)).astype(jnp.bfloat16)
@@ -347,17 +360,14 @@
         )
         mid_part, gate_grad, upper_grad = down_hook((mid_part, gate_grad, upper_grad))
         mid_sum = plan.tp_sum(mid_part)
-        gate_w_grad = down_hook(inner_rows(normed_mid, gate_grad))
-        up_w_grad = down_hook(inner_rows(normed_mid, upper_grad))
-        big = Ring(plan, [gate_w_grad, up_w_grad])
+        big = Ring(plan, normed_mid, [gate_grad, upper_grad])
         big.step()
         mid_grad = mid_sum.astype(jnp.float32)
         resid_grad = cotangent.astype(jnp.float32) + norm_back(resid, mlp_gain, mid_grad)
         mlp_gain_part = gain_term(resid_rows, lax.dynamic_slice_in_dim(mid_grad, offset, share, 0))
         resid_low = resid_grad.astype(jnp.bfloat16)
-        out_w_grad_t = inner_rows(resid_low, attended)
         attended_grad = outer_cols(resid_low, w_out).astype(jnp.bfloat16)
-        small = Ring(plan, [out_w_grad_t])
+        small = Ring(plan, resid_low, [attended])
 
         def hook(values):
             if big.done < big.steps:
@@ -394,9 +404,6 @@
             (in_part, q_grad, k_grad, v_grad)
         )
         in_sum = plan.tp_sum(in_part)
-        query_w_grad = inner_rows(normed_in, q_grad)
-        key_w_grad = inner_rows(normed_in, k_grad)
-        value_w_grad = inner_rows(normed_in, v_grad)
         while big.done < big.steps:
             big.step()
         while small.done < small.steps:
@@ -407,7 +414,7 @@
         (down_sum,) = down.result()
         gate_sum, up_sum = big.result()
         (out_sum,) = small.result()
-        query_sum, key_sum, value_sum = plan.dp_rs([query_w_grad, key_w_grad, value_w_grad])
+        query_sum, key_sum, value_sum = plan.dp_rs(normed_in, [q_grad, k_grad, v_grad])
         input_grad = resid_grad + norm_back(stream, attn_gain, in_grad)
         attn_gain_part = gain_term(stream_rows, lax.dynamic_slice_in_dim(in_grad, offset, share, 0))
         gains = plan.all_sum(jnp.concatenate([attn_gain_part, mlp_gain_part, qg_part, kg_part]))

time: 709 us -> 780 us (1.10)
  matrix products: 133 us -> 195 us
  waiting for transfers between devices: 237 us -> 271 us
  local copies, waits for them, and re-layouts: 87 us -> 57.1 us
    ppermute x28, waiting for transfers between devices: 33.8 us -> 90.2 us  [step(): got_a = lax.ppermute(send_a.astype(jnp.bfloat16), 'dp', self.plan.cw)]
    dot_general x7 -> x72, matrix products: 38.3 us -> 89.8 us  [inner_rows(): lax.dot_general(left, right, (((0,), (0,)), ((), ())), preferred_element_...]
    ppermute x28, waiting for transfers between devices: 66.6 us -> 34.7 us  [step(): got_b = lax.ppermute(send_b.astype(jnp.bfloat16), 'dp', self.plan.ccw)]
    dynamic_slice x5 -> x0, local copies, waits for them, and re-layouts: 19 us -> none  [piece(): parts = [lax.dynamic_slice_in_dim(g, start, half, 0) for g in self.grads]]
    add x1 -> x0, other arithmetic: 14.5 us -> none  [body(): cotangent.astype(jnp.float32) + norm_back(resid, mlp_gain, mid_grad)]
    convert_element_type x0 -> x1, other arithmetic: none -> 11 us  [body(): resid_low = resid_grad.astype(jnp.bfloat16)]
    ppermute x28, starting transfers between devices: 29.3 us -> 39 us  [step(): got_b = lax.ppermute(send_b.astype(jnp.bfloat16), 'dp', self.plan.ccw)]
    ppermute x28, starting transfers between devices: 30.9 us -> 22.2 us  [step(): got_a = lax.ppermute(send_a.astype(jnp.bfloat16), 'dp', self.plan.cw)]
  transfers between devices with their start and end apart: 73 -> 73, of which waited for: 27 -> 28; matrix products, arithmetic and copies ran while one was open for 27% -> 26% of each run, Pallas kernels for 0% -> 0%
where the time goes in v8:
time: 780 us; the launch traced here: 771 us
  waiting for transfers between devices  271 us (35%)
  matrix products  195 us (25%)
  other arithmetic  152 us (19%)
  starting transfers between devices  73.8 us (9%)
  local copies, waits for them, and re-layouts  57.1 us (7%)
  between operations  23.3 us (3%)
    ppermute x4, waiting for transfers between devices, tp_sum(): other = lax.ppermute(chip_sum, 'tensor', self.chip_pairs)  137 us
    ppermute x28, waiting for transfers between devices, step(): got_a = lax.ppermute(send_a.astype(jnp.bfloat16), 'dp', self.plan.cw)  90.2 us
    dot_general x72, matrix products, inner_rows(): lax.dot_general(left, right, (((0,), (0,)), ((), ())), preferred_element_...  89.8 us
    dot_general x7, matrix products, outer_cols(): lax.dot_general(left, right, (((1,), (1,)), ((), ())), preferred_element_...  53.6 us
    dot_general x7, matrix products, matmul(): return jnp.dot(left, right, preferred_element_type=jnp.float32)  45.8 us
    ppermute x28, starting transfers between devices, step(): got_b = lax.ppermute(send_b.astype(jnp.bfloat16), 'dp', self.plan.ccw)  39 us
    ppermute x28, waiting for transfers between devices, step(): got_b = lax.ppermute(send_b.astype(jnp.bfloat16), 'dp', self.plan.ccw)  34.7 us
    ppermute x28, starting transfers between devices, step(): got_a = lax.ppermute(send_a.astype(jnp.bfloat16), 'dp', self.plan.cw)  22.2 us
  transfers between devices with their start and end apart: 73, of which 28 were waited for; matrix products, arithmetic and copies ran while one was open for 26% of the time, Pallas kernels for 0%

profile of v8, /device:TPU:0, one launch (start us, length us, event | category | flops | bytes accessed | tf_op | source)
XLA Modules:
  0.0 771.5 jit_solution(5194200720712057046)
XLA Ops:
  0.7 3.2 fusion.1
  15.9 6.9 fusion.306
  22.8 2.9 reshape.457
  25.7 3.5 copy.279
  29.2 2.9 copy.233
  32.0 3.5 reshape.443
  42.0 4.3 copy.231
  61.1 5.6 convolution_convert_fusion.1
  66.7 3.2 constant_dynamic-slice_fusion.3
  71.0 3.5 collective-permute-done
  74.5 4.4 add_convert_fusion.10
  78.9 2.9 collective-permute-start.1
  81.8 6.7 convert_element_type.522
  90.3 37.7 %collective-permute-done.1 = bf16[512,2048]{1,0:T(8,128)(2,1)} collective-permute-done((bf16[512,2048]{1,0:T(8,128)(2,1)}, bf16[512,2048]{1,0:T(8,128)(2,1)}, u32[]{:S(2)}, u32[]{:S(2)}) %collective-permute-start.1) | collective-permute-done | bytes 2097184 | tf_op jit(solution)/shard_map/ppermute | solution.py:223
  128.0 4.4 add_convert_fusion.9
  154.5 12.0 %fusion.308 = f32[1024,1536]{1,0:T(8,128)} fusion(bf16[1024,2048]{1,0:T(8,128)(2,1)} %param.37, bf16[1536,2048]{1,0:T(8,128)(2,1)} %param.36), kind=kOutput, calls=%fused_computation.452 | convolution fusion | flops 6442450944 | bytes 16777216 | tf_op jit(solution)/shard_map/dot_general | solution.py:33
  170.0 4.5 convert_add_fusion
  174.5 5.7 multiply_convert_fusion
  180.3 6.7 fusion.307
  186.9 13.2 %multiply_convert_fusion.2 = (bf16[1024,1536]{1,0:T(8,128)(2,1)S(1)}, f32[1024,1536]{1,0:T(8,128)}) fusion(f32[1024,1536]{1,0:T(8,128)S(1)} %fusion.307, bf16[1024,2048]{1,0:T(8,128)(2,1)S(1)} %multiply_convert_fusion, bf16[2048,1536]{1,0:T(8,128)(2,1)} %param.35), kind=kOutput, calls=%fused_computation.25 | convolution fusion | flops 6451888128 | bytes 26214400 | tf_op jit(solution)/shard_map/dot_general | solution.py:23
  200.2 10.0 %convolution_convert_fusion = bf16[1024,2048]{1,0:T(8,128)(2,1)S(1)} fusion(bf16[1024,1536]{1,0:T(8,128)(2,1)S(1)} %get-tuple-element.285, bf16[1536,2048]{1,0:T(8,128)(2,1)} %param.36), kind=kOutput, calls=%fused_computation.38 | convolution fusion | flops 6444548096 | bytes 13631488 | tf_op jit(solution)/shard_map/dot_general | solution.py:23
  235.9 6.8 collective-permute-done.9
  247.2 8.3 %multiply_convert_fusion.1 = (bf16[1024,1536]{1,0:T(8,128)(2,1)S(1)}, bf16[1024,1536]{1,0:T(8,128)(2,1)S(1)}) fusion(f32[1024,1536]{1,0:T(8,128)} %fusion.308, f32[1024,1536]{1,0:T(8,128)} %copy-done.32, f32[1024,1536]{1,0:T(8,128)} %get-tuple-element.286), kind=kLoop, calls=%fused_computation.24 | loop fusion | flops 22020096 | bytes 25165824 | tf_op jit(solution)/shard_map/convert_element_type | solution.py:356
  256.3 10.7 %fusion.309 = f32[1024,2048]{1,0:T(8,128)} fusion(bf16[1024,1536]{1,0:T(8,128)(2,1)S(1)} %get-tuple-element.85, bf16[2048,1536]{1,0:T(8,128)(2,1)} %param.35), kind=kOutput, calls=%fused_computation.453 | convolution fusion | flops 6442450944 | bytes 17825792 | tf_op jit(solution)/shard_map/dot_general | solution.py:33
  271.0 12.4 %add_convert_fusion.1 = bf16[1024,2048]{1,0:T(8,128)(2,1)} fusion(f32[1024,2048]{1,0:T(8,128)} %fusion.309, bf16[1024,1536]{1,0:T(8,128)(2,1)S(1)} %get-tuple-element.84, bf16[2048,1536]{1,0:T(8,128)(2,1)} %param.34), kind=kOutput, calls=%fused_computation.17 | convolution fusion | flops 6446645248 | bytes 22020096 | tf_op jit(solution)/shard_map/dot_general | solution.py:33
  320.9 34.6 %collective-permute-done.4 = bf16[512,2048]{1,0:T(8,128)(2,1)S(1)} collective-permute-done((bf16[512,2048]{1,0:T(8,128)(2,1)S(1)}, bf16[512,2048]{1,0:T(8,128)(2,1)S(1)}, u32[]{:S(2)}, u32[]{:S(2)}) %collective-permute-start.4) | collective-permute-done | bytes 2097184 | tf_op jit(solution)/shard_map/ppermute | solution.py:223
  356.4 43.1 %collective-permute-done.21 = bf16[512,2048]{1,0:T(8,128)(2,1)S(1)} collective-permute-done((bf16[512,2048]{1,0:T(8,128)(2,1)S(1)}, bf16[512,2048]{1,0:T(8,128)(2,1)S(1)}, u32[]{:S(2)}, u32[]{:S(2)}) %collective-permute-start.21) | collective-permute-done | bytes 2097184 | tf_op jit(solution)/shard_map/ppermute | solution.py:223
  412.6 21.8 %collective-permute-done.14 = bf16[256,768]{1,0:T(8,128)(2,1)S(1)} collective-permute-done((bf16[256,768]{1,0:T(8,128)(2,1)S(1)}, bf16[256,768]{1,0:T(8,128)(2,1)S(1)}, u32[]{:S(2)}, u32[]{:S(2)}) %collective-permute-start.14) | collective-permute-done | bytes 393248 | tf_op jit(solution)/shard_map/ppermute | solution.py:290
  436.9 4.2 broadcast_select_fusion.5
  443.9 11.0 %fusion.297 = (bf16[1024,2048]{1,0:T(8,128)(2,1)}, f32[1024,2048]{1,0:T(8,128)}, bf16[1024,2048]{1,0:T(8,128)(2,1)}) fusion(f32[1024]{0:T(1024)S(1)} %broadcast_multiply_fusion.3, f32[1024]{0:T(1024)S(1)} %get-tuple-element.265, bf16[512,2048]{1,0:T(8,128)(2,1)} %copy-done.8, bf16[512,2048]{1,0:T(8,128)(2,1)S(1)} %get-tuple-element.247, ...), kind=kLoop, calls=%fused_computation.441 | loop fusion | flops 50331648 | bytes 37769216 | tf_op jit(solution)/shard_map/convert_element_type | solution.py:368
  459.2 5.7 convolution_convert_fusion.5
  498.2 17.1 %collective-permute-done.29 = bf16[256,256]{1,0:T(8,128)(2,1)S(1)} collective-permute-done((bf16[256,256]{1,0:T(8,128)(2,1)}, bf16[256,256]{1,0:T(8,128)(2,1)S(1)}, u32[]{:S(2)}, u32[]{:S(2)}) %collective-permute-start.29) | collective-permute-done | bytes 131104 | tf_op jit(solution)/shard_map/ppermute | solution.py:290
  529.2 19.5 %collective-permute-done.35 = bf16[256,256]{1,0:T(8,128)(2,1)S(1)} collective-permute-done((bf16[256,256]{1,0:T(8,128)(2,1)S(1)}, bf16[256,256]{1,0:T(8,128)(2,1)S(1)}, u32[]{:S(2)}, u32[]{:S(2)}) %collective-permute-start.35) | collective-permute-done | bytes 131104 | tf_op jit(solution)/shard_map/ppermute | solution.py:290
  557.6 12.7 %collective-permute-done.40 = bf16[256,256]{1,0:T(8,128)(2,1)S(1)} collective-permute-done((bf16[256,256]{1,0:T(8,128)(2,1)S(1)}, bf16[256,256]{1,0:T(8,128)(2,1)S(1)}, u32[]{:S(2)}, u32[]{:S(2)}) %collective-permute-start.40) | collective-permute-done | bytes 131104 | tf_op jit(solution)/shard_map/ppermute | solution.py:291
  578.1 11.1 %collective-permute-done.44 = bf16[256,256]{1,0:T(8,128)(2,1)S(1)} collective-permute-done((bf16[256,256]{1,0:T(8,128)(2,1)S(1)}, bf16[256,256]{1,0:T(8,128)(2,1)S(1)}, u32[]{:S(2)}, u32[]{:S(2)}) %collective-permute-start.44) | collective-permute-done | bytes 131104 | tf_op jit(solution)/shard_map/ppermute | solution.py:291
  603.1 11.7 %collective-permute-done.47 = bf16[256,256]{1,0:T(8,128)(2,1)S(1)} collective-permute-done((bf16[256,256]{1,0:T(8,128)(2,1)S(1)}, bf16[256,256]{1,0:T(8,128)(2,1)S(1)}, u32[]{:S(2)}, u32[]{:S(2)}) %collective-permute-start.47) | collective-permute-done | bytes 131104 | tf_op jit(solution)/shard_map/ppermute | solution.py:290
  618.9 5.8 fusion.296
  627.3 5.7 add_convert_fusion
  666.5 3.0 copy.261
  679.7 2.8 add.1541
  686.2 21.7 %collective-permute-done.50 = bf16[512,2048]{1,0:T(8,128)(2,1)} collective-permute-done((bf16[512,2048]{1,0:T(8,128)(2,1)}, bf16[512,2048]{1,0:T(8,128)(2,1)}, u32[]{:S(2)}, u32[]{:S(2)}) %collective-permute-start.50) | collective-permute-done | bytes 2097184 | tf_op jit(solution)/shard_map/ppermute | solution.py:223
  707.9 4.4 add_convert_fusion.3
  716.1 5.1 collective-permute-done.61
  724.9 4.3 collective-permute-done.62
  734.5 2.8 collective-permute-done.63
  752.6 4.8 fusion.7
  757.8 3.4 collective-permute-done.55
  762.3 7.8 %fusion.6 = f32[1024,2048]{1,0:T(8,128)} fusion(f32[1024,2048]{1,0:T(8,128)} %get-tuple-element.87, bf16[1024,2048]{1,0:T(8,128)(2,1)S(1)} %copy-done.3, f32[1024]{0:T(1024)S(1)} %broadcast_multiply_fusion.2, f32[1024]{0:T(1024)S(1)} %copy-done.105, f32[2048]{0:T(1024)S(1)} %copy-done.100, f32[1024]{0:T(1024)S(1)} %copy-done.104, ...), kind=kLoop, calls=%fused_computation.12 | loop fusion | flops 23068672 | bytes 25186304 | tf_op jit(solution)/shard_map/add | solution.py:418
  (621 shorter events, 298.2 us)
Async XLA Ops:
  78.9 49.1 %collective-permute-start.1 = (bf16[512,2048]{1,0:T(8,128)(2,1)}, bf16[512,2048]{1,0:T(8,128)(2,1)}, u32[]{:S(2)}, u32[]{:S(2)}) collective-permute-start(bf16[512,2048]{1,0:T(8,128)(2,1)} %add_convert_fusion.10), channel_id=1, source_target_pairs={{0,2},{1,3},{2,0},{3,1},{4,6},{5,7},{6,4},{7,5},{8,10},{9,11},{10,... | collective-permute-start | bytes 6291464 | tf_op jit(solution)/shard_map/ppermute | solution.py:223
  132.5 34.1 %collective-permute-start.2 = (bf16[512,2048]{1,0:T(8,128)(2,1)}, bf16[512,2048]{1,0:T(8,128)(2,1)}, u32[]{:S(2)}, u32[]{:S(2)}) collective-permute-start(bf16[512,2048]{1,0:T(8,128)(2,1)} %add_convert_fusion.9), channel_id=1, source_target_pairs={{0,1},{1,0},{2,3},{3,2},{4,5},{5,4},{6,7},{7,6},{8,9},{9,8},{10,11... | collective-permute-start | bytes 6291464 | tf_op jit(solution)/shard_map/ppermute | solution.py:225
  215.2 90.4 %collective-permute-start.3 = (bf16[512,2048]{1,0:T(8,128)(2,1)}, bf16[512,2048]{1,0:T(8,128)(2,1)S(1)}, u32[]{:S(2)}, u32[]{:S(2)}) collective-permute-start(bf16[512,2048]{1,0:T(8,128)(2,1)} %constant_dynamic-slice_fusion.2), channel_id=1, source_target_pairs={{0,1},{1,0},{2,3},{3,2},{4,5},{5,4},{6,7},{7,6},{8,9},{9,8},{10,11... | collective-permute-start | bytes 6291464 | tf_op jit(solution)/shard_map/ppermute | solution.py:221
  217.0 14.0 %collective-permute-start.8 = (bf16[256,768]{1,0:T(8,128)(2,1)S(1)}, bf16[256,768]{1,0:T(8,128)(2,1)S(1)}, u32[]{:S(2)}, u32[]{:S(2)}) collective-permute-start(bf16[256,768]{1,0:T(8,128)(2,1)S(1)} %convolution_convert_fusion.7), channel_id=1, source_target_pairs={{8,0},{16,8},{24,16},{28,24},{20,28},{12,20},{4,12},{0,4},{9,1},{1... | collective-permute-start | bytes 1179656 | tf_op jit(solution)/shard_map/ppermute | solution.py:291
  219.5 14.0 %collective-permute-start.6 = (bf16[256,768]{1,0:T(8,128)(2,1)S(1)}, bf16[256,768]{1,0:T(8,128)(2,1)S(1)}, u32[]{:S(2)}, u32[]{:S(2)}) collective-permute-start(bf16[256,768]{1,0:T(8,128)(2,1)S(1)} %convolution_convert_fusion.8), channel_id=1, source_target_pairs={{0,8},{8,16},{16,24},{24,28},{28,20},{20,12},{12,4},{4,0},{1,9},{9... | collective-permute-start | bytes 1179656 | tf_op jit(solution)/shard_map/ppermute | solution.py:290
  267.9 15.5 %collective-permute-start.13 = (bf16[256,768]{1,0:T(8,128)(2,1)}, bf16[256,768]{1,0:T(8,128)(2,1)}, u32[]{:S(2)}, u32[]{:S(2)}) collective-permute-start(bf16[256,768]{1,0:T(8,128)(2,1)} %add_convert_fusion.29), channel_id=1, source_target_pairs={{8,0},{16,8},{24,16},{28,24},{20,28},{12,20},{4,12},{0,4},{9,1},{1... | collective-permute-start | bytes 1179656 | tf_op jit(solution)/shard_map/ppermute | solution.py:291
  270.4 14.1 %collective-permute-start.12 = (bf16[256,768]{1,0:T(8,128)(2,1)}, bf16[256,768]{1,0:T(8,128)(2,1)}, u32[]{:S(2)}, u32[]{:S(2)}) collective-permute-start(bf16[256,768]{1,0:T(8,128)(2,1)} %add_convert_fusion.30), channel_id=1, source_target_pairs={{0,8},{8,16},{16,24},{24,28},{28,20},{20,12},{12,4},{4,0},{1,9},{9... | collective-permute-start | bytes 1179656 | tf_op jit(solution)/shard_map/ppermute | solution.py:290
  290.7 17.8 %collective-permute-start.20 = (bf16[512,2048]{1,0:T(8,128)(2,1)}, bf16[512,2048]{1,0:T(8,128)(2,1)S(1)}, u32[]{:S(2)}, u32[]{:S(2)}) collective-permute-start(bf16[512,2048]{1,0:T(8,128)(2,1)} %constant_dynamic-slice_fusion.1), channel_id=1, source_target_pairs={{0,1},{1,0},{2,3},{3,2},{4,5},{5,4},{6,7},{7,6},{8,9},{9,8},{10,11... | collective-permute-start | bytes 6291464 | tf_op jit(solution)/shard_map/ppermute | solution.py:221
  290.7 109.6 %collective-permute-start.18 = (bf16[256,1536]{1,0:T(8,128)(2,1)S(1)}, bf16[256,1536]{1,0:T(8,128)(2,1)}, u32[]{:S(2)}, u32[]{:S(2)}) collective-permute-start(bf16[256,1536]{1,0:T(8,128)(2,1)S(1)} %convolution_convert_fusion.2), channel_id=1, source_target_pairs={{8,0},{16,8},{24,16},{28,24},{20,28},{12,20},{4,12},{0,4},{9,1},{1... | collective-permute-start | bytes 2359304 | tf_op jit(solution)/shard_map/ppermute | solution.py:291
  296.4 107.7 %collective-permute-start.16 = (bf16[256,1536]{1,0:T(8,128)(2,1)}, bf16[256,1536]{1,0:T(8,128)(2,1)}, u32[]{:S(2)}, u32[]{:S(2)}) collective-permute-start(bf16[256,1536]{1,0:T(8,128)(2,1)} %convolution_convert_fusion.3), channel_id=1, source_target_pairs={{0,8},{8,16},{16,24},{24,28},{28,20},{20,12},{12,4},{4,0},{1,9},{9... | collective-permute-start | bytes 2359304 | tf_op jit(solution)/shard_map/ppermute | solution.py:290
  307.0 48.6 %collective-permute-start.4 = (bf16[512,2048]{1,0:T(8,128)(2,1)S(1)}, bf16[512,2048]{1,0:T(8,128)(2,1)S(1)}, u32[]{:S(2)}, u32[]{:S(2)}) collective-permute-start(bf16[512,2048]{1,0:T(8,128)(2,1)S(1)} %add_convert_fusion.8), channel_id=1, source_target_pairs={{0,2},{1,3},{2,0},{3,1},{4,6},{5,7},{6,4},{7,5},{8,10},{9,11},{10,... | collective-permute-start | bytes 6291464 | tf_op jit(solution)/shard_map/ppermute | solution.py:223
  309.4 90.0 %collective-permute-start.21 = (bf16[512,2048]{1,0:T(8,128)(2,1)S(1)}, bf16[512,2048]{1,0:T(8,128)(2,1)S(1)}, u32[]{:S(2)}, u32[]{:S(2)}) collective-permute-start(bf16[512,2048]{1,0:T(8,128)(2,1)S(1)} %add_convert_fusion.6), channel_id=1, source_target_pairs={{0,2},{1,3},{2,0},{3,1},{4,6},{5,7},{6,4},{7,5},{8,10},{9,11},{10,... | collective-permute-start | bytes 6291464 | tf_op jit(solution)/shard_map/ppermute | solution.py:223
  310.1 96.8 %collective-permute-start.15 = (bf16[256,768]{1,0:T(8,128)(2,1)S(1)}, bf16[256,768]{1,0:T(8,128)(2,1)S(1)}, u32[]{:S(2)}, u32[]{:S(2)}) collective-permute-start(bf16[256,768]{1,0:T(8,128)(2,1)S(1)} %add_convert_fusion.27), channel_id=1, source_target_pairs={{8,0},{16,8},{24,16},{28,24},{20,28},{12,20},{4,12},{0,4},{9,1},{1... | collective-permute-start | bytes 1179656 | tf_op jit(solution)/shard_map/ppermute | solution.py:291
  356.3 80.6 %collective-permute-start.5 = (bf16[512,2048]{1,0:T(8,128)(2,1)S(1)}, bf16[512,2048]{1,0:T(8,128)(2,1)}, u32[]{:S(2)}, u32[]{:S(2)}) collective-permute-start(bf16[512,2048]{1,0:T(8,128)(2,1)S(1)} %add_convert_fusion.7), channel_id=1, source_target_pairs={{0,1},{1,0},{2,3},{3,2},{4,5},{5,4},{6,7},{7,6},{8,9},{9,8},{10,11... | collective-permute-start | bytes 6291464 | tf_op jit(solution)/shard_map/ppermute | solution.py:225
  400.3 40.8 %collective-permute-start.22 = (bf16[512,2048]{1,0:T(8,128)(2,1)S(1)}, bf16[512,2048]{1,0:T(8,128)(2,1)S(1)}, u32[]{:S(2)}, u32[]{:S(2)}) collective-permute-start(bf16[512,2048]{1,0:T(8,128)(2,1)S(1)} %add_convert_fusion.5), channel_id=1, source_target_pairs={{0,1},{1,0},{2,3},{3,2},{4,5},{5,4},{6,7},{7,6},{8,9},{9,8},{10,11... | collective-permute-start | bytes 6291464 | tf_op jit(solution)/shard_map/ppermute | solution.py:225
  402.5 32.9 %collective-permute-start.19 = (bf16[256,1536]{1,0:T(8,128)(2,1)S(1)}, bf16[256,1536]{1,0:T(8,128)(2,1)S(1)}, u32[]{:S(2)}, u32[]{:S(2)}) collective-permute-start(bf16[256,1536]{1,0:T(8,128)(2,1)S(1)} %add_convert_fusion.21), channel_id=1, source_target_pairs={{8,0},{16,8},{24,16},{28,24},{20,28},{12,20},{4,12},{0,4},{9,1},{1... | collective-permute-start | bytes 2359304 | tf_op jit(solution)/shard_map/ppermute | solution.py:291
  406.3 30.4 %collective-permute-start.17 = (bf16[256,1536]{1,0:T(8,128)(2,1)S(1)}, bf16[256,1536]{1,0:T(8,128)(2,1)S(1)}, u32[]{:S(2)}, u32[]{:S(2)}) collective-permute-start(bf16[256,1536]{1,0:T(8,128)(2,1)S(1)} %add_convert_fusion.22), channel_id=1, source_target_pairs={{0,8},{8,16},{16,24},{24,28},{28,20},{20,12},{12,4},{4,0},{1,9},{9... | collective-permute-start | bytes 2359304 | tf_op jit(solution)/shard_map/ppermute | solution.py:290
  406.9 27.5 %collective-permute-start.14 = (bf16[256,768]{1,0:T(8,128)(2,1)S(1)}, bf16[256,768]{1,0:T(8,128)(2,1)S(1)}, u32[]{:S(2)}, u32[]{:S(2)}) collective-permute-start(bf16[256,768]{1,0:T(8,128)(2,1)S(1)} %add_convert_fusion.28), channel_id=1, source_target_pairs={{0,8},{8,16},{16,24},{24,28},{28,20},{20,12},{12,4},{4,0},{1,9},{9... | collective-permute-start | bytes 1179656 | tf_op jit(solution)/shard_map/ppermute | solution.py:290
  485.4 32.2 %collective-permute-start.28 = (bf16[256,1536]{1,0:T(8,128)(2,1)}, bf16[256,1536]{1,0:T(8,128)(2,1)}, u32[]{:S(2)}, u32[]{:S(2)}) collective-permute-start(bf16[256,1536]{1,0:T(8,128)(2,1)} %add_convert_fusion.19), channel_id=1, source_target_pairs={{8,0},{16,8},{24,16},{28,24},{20,28},{12,20},{4,12},{0,4},{9,1},{1... | collective-permute-start | bytes 2359304 | tf_op jit(solution)/shard_map/ppermute | solution.py:291
  486.9 32.1 %collective-permute-start.27 = (bf16[256,1536]{1,0:T(8,128)(2,1)}, bf16[256,1536]{1,0:T(8,128)(2,1)}, u32[]{:S(2)}, u32[]{:S(2)}) collective-permute-start(bf16[256,1536]{1,0:T(8,128)(2,1)} %add_convert_fusion.20), channel_id=1, source_target_pairs={{0,8},{8,16},{16,24},{24,28},{28,20},{20,12},{12,4},{4,0},{1,9},{9... | collective-permute-start | bytes 2359304 | tf_op jit(solution)/shard_map/ppermute | solution.py:290
  489.4 26.0 %collective-permute-start.26 = (bf16[256,768]{1,0:T(8,128)(2,1)}, bf16[256,768]{1,0:T(8,128)(2,1)}, u32[]{:S(2)}, u32[]{:S(2)}) collective-permute-start(bf16[256,768]{1,0:T(8,128)(2,1)} %add_convert_fusion.25), channel_id=1, source_target_pairs={{8,0},{16,8},{24,16},{28,24},{20,28},{12,20},{4,12},{0,4},{9,1},{1... | collective-permute-start | bytes 1179656 | tf_op jit(solution)/shard_map/ppermute | solution.py:291
  490.6 25.8 %collective-permute-start.25 = (bf16[256,768]{1,0:T(8,128)(2,1)}, bf16[256,768]{1,0:T(8,128)(2,1)}, u32[]{:S(2)}, u32[]{:S(2)}) collective-permute-start(bf16[256,768]{1,0:T(8,128)(2,1)} %add_convert_fusion.26), channel_id=1, source_target_pairs={{0,8},{8,16},{16,24},{24,28},{28,20},{20,12},{12,4},{4,0},{1,9},{9... | collective-permute-start | bytes 1179656 | tf_op jit(solution)/shard_map/ppermute | solution.py:290
  495.0 20.3 %collective-permute-start.29 = (bf16[256,256]{1,0:T(8,128)(2,1)}, bf16[256,256]{1,0:T(8,128)(2,1)S(1)}, u32[]{:S(2)}, u32[]{:S(2)}) collective-permute-start(bf16[256,256]{1,0:T(8,128)(2,1)} %add_convert_fusion.52), channel_id=1, source_target_pairs={{0,8},{8,16},{16,24},{24,28},{28,20},{20,12},{12,4},{4,0},{1,9},{9... | collective-permute-start | bytes 393224 | tf_op jit(solution)/shard_map/ppermute | solution.py:290
  521.1 29.5 %collective-permute-start.34 = (bf16[256,1536]{1,0:T(8,128)(2,1)S(1)}, bf16[256,1536]{1,0:T(8,128)(2,1)S(1)}, u32[]{:S(2)}, u32[]{:S(2)}) collective-permute-start(bf16[256,1536]{1,0:T(8,128)(2,1)S(1)} %add_convert_fusion.17), channel_id=1, source_target_pairs={{8,0},{16,8},{24,16},{28,24},{20,28},{12,20},{4,12},{0,4},{9,1},{1... | collective-permute-start | bytes 2359304 | tf_op jit(solution)/shard_map/ppermute | solution.py:291
  521.8 29.0 %collective-permute-start.33 = (bf16[256,1536]{1,0:T(8,128)(2,1)S(1)}, bf16[256,1536]{1,0:T(8,128)(2,1)S(1)}, u32[]{:S(2)}, u32[]{:S(2)}) collective-permute-start(bf16[256,1536]{1,0:T(8,128)(2,1)S(1)} %add_convert_fusion.18), channel_id=1, source_target_pairs={{0,8},{8,16},{16,24},{24,28},{28,20},{20,12},{12,4},{4,0},{1,9},{9... | collective-permute-start | bytes 2359304 | tf_op jit(solution)/shard_map/ppermute | solution.py:290
  523.6 25.1 %collective-permute-start.32 = (bf16[256,768]{1,0:T(8,128)(2,1)S(1)}, bf16[256,768]{1,0:T(8,128)(2,1)S(1)}, u32[]{:S(2)}, u32[]{:S(2)}) collective-permute-start(bf16[256,768]{1,0:T(8,128)(2,1)S(1)} %add_convert_fusion.23), channel_id=1, source_target_pairs={{8,0},{16,8},{24,16},{28,24},{20,28},{12,20},{4,12},{0,4},{9,1},{1... | collective-permute-start | bytes 1179656 | tf_op jit(solution)/shard_map/ppermute | solution.py:291
  524.1 25.5 %collective-permute-start.31 = (bf16[256,768]{1,0:T(8,128)(2,1)S(1)}, bf16[256,768]{1,0:T(8,128)(2,1)S(1)}, u32[]{:S(2)}, u32[]{:S(2)}) collective-permute-start(bf16[256,768]{1,0:T(8,128)(2,1)S(1)} %add_convert_fusion.24), channel_id=1, source_target_pairs={{0,8},{8,16},{16,24},{24,28},{28,20},{20,12},{12,4},{4,0},{1,9},{9... | collective-permute-start | bytes 1179656 | tf_op jit(solution)/shard_map/ppermute | solution.py:290
  526.9 21.8 %collective-permute-start.35 = (bf16[256,256]{1,0:T(8,128)(2,1)S(1)}, bf16[256,256]{1,0:T(8,128)(2,1)S(1)}, u32[]{:S(2)}, u32[]{:S(2)}) collective-permute-start(bf16[256,256]{1,0:T(8,128)(2,1)S(1)} %add_convert_fusion.50), channel_id=1, source_target_pairs={{0,8},{8,16},{16,24},{24,28},{28,20},{20,12},{12,4},{4,0},{1,9},{9... | collective-permute-start | bytes 393224 | tf_op jit(solution)/shard_map/ppermute | solution.py:290
  551.6 20.2 %collective-permute-start.38 = (bf16[256,1536]{1,0:T(8,128)(2,1)S(1)}, bf16[256,1536]{1,0:T(8,128)(2,1)S(1)}, u32[]{:S(2)}, u32[]{:S(2)}) collective-permute-start(bf16[256,1536]{1,0:T(8,128)(2,1)S(1)} %add_convert_fusion.15), channel_id=1, source_target_pairs={{8,0},{16,8},{24,16},{28,24},{20,28},{12,20},{4,12},{0,4},{9,1},{1... | collective-permute-start | bytes 2359304 | tf_op jit(solution)/shard_map/ppermute | solution.py:291
  553.5 18.4 %collective-permute-start.37 = (bf16[256,1536]{1,0:T(8,128)(2,1)S(1)}, bf16[256,1536]{1,0:T(8,128)(2,1)S(1)}, u32[]{:S(2)}, u32[]{:S(2)}) collective-permute-start(bf16[256,1536]{1,0:T(8,128)(2,1)S(1)} %add_convert_fusion.16), channel_id=1, source_target_pairs={{0,8},{8,16},{16,24},{24,28},{28,20},{20,12},{12,4},{4,0},{1,9},{9... | collective-permute-start | bytes 2359304 | tf_op jit(solution)/shard_map/ppermute | solution.py:290
  554.5 15.8 %collective-permute-start.40 = (bf16[256,256]{1,0:T(8,128)(2,1)S(1)}, bf16[256,256]{1,0:T(8,128)(2,1)S(1)}, u32[]{:S(2)}, u32[]{:S(2)}) collective-permute-start(bf16[256,256]{1,0:T(8,128)(2,1)S(1)} %add_convert_fusion.47), channel_id=1, source_target_pairs={{8,0},{16,8},{24,16},{28,24},{20,28},{12,20},{4,12},{0,4},{9,1},{1... | collective-permute-start | bytes 393224 | tf_op jit(solution)/shard_map/ppermute | solution.py:291
  555.7 16.0 %collective-permute-start.39 = (bf16[256,256]{1,0:T(8,128)(2,1)S(1)}, bf16[256,256]{1,0:T(8,128)(2,1)S(1)}, u32[]{:S(2)}, u32[]{:S(2)}) collective-permute-start(bf16[256,256]{1,0:T(8,128)(2,1)S(1)} %add_convert_fusion.48), channel_id=1, source_target_pairs={{0,8},{8,16},{16,24},{24,28},{28,20},{20,12},{12,4},{4,0},{1,9},{9... | collective-permute-start | bytes 393224 | tf_op jit(solution)/shard_map/ppermute | solution.py:290
  572.4 18.3 %collective-permute-start.42 = (bf16[256,1536]{1,0:T(8,128)(2,1)S(1)}, bf16[256,1536]{1,0:T(8,128)(2,1)S(1)}, u32[]{:S(2)}, u32[]{:S(2)}) collective-permute-start(bf16[256,1536]{1,0:T(8,128)(2,1)S(1)} %add_convert_fusion.13), channel_id=1, source_target_pairs={{8,0},{16,8},{24,16},{28,24},{20,28},{12,20},{4,12},{0,4},{9,1},{1... | collective-permute-start | bytes 2359304 | tf_op jit(solution)/shard_map/ppermute | solution.py:291
  574.3 16.7 %collective-permute-start.41 = (bf16[256,1536]{1,0:T(8,128)(2,1)S(1)}, bf16[256,1536]{1,0:T(8,128)(2,1)S(1)}, u32[]{:S(2)}, u32[]{:S(2)}) collective-permute-start(bf16[256,1536]{1,0:T(8,128)(2,1)S(1)} %add_convert_fusion.14), channel_id=1, source_target_pairs={{0,8},{8,16},{16,24},{24,28},{28,20},{20,12},{12,4},{4,0},{1,9},{9... | collective-permute-start | bytes 2359304 | tf_op jit(solution)/shard_map/ppermute | solution.py:290
  575.0 14.2 %collective-permute-start.44 = (bf16[256,256]{1,0:T(8,128)(2,1)S(1)}, bf16[256,256]{1,0:T(8,128)(2,1)S(1)}, u32[]{:S(2)}, u32[]{:S(2)}) collective-permute-start(bf16[256,256]{1,0:T(8,128)(2,1)S(1)} %add_convert_fusion.45), channel_id=1, source_target_pairs={{8,0},{16,8},{24,16},{28,24},{20,28},{12,20},{4,12},{0,4},{9,1},{1... | collective-permute-start | bytes 393224 | tf_op jit(solution)/shard_map/ppermute | solution.py:291
  576.5 14.2 %collective-permute-start.43 = (bf16[256,256]{1,0:T(8,128)(2,1)S(1)}, bf16[256,256]{1,0:T(8,128)(2,1)S(1)}, u32[]{:S(2)}, u32[]{:S(2)}) collective-permute-start(bf16[256,256]{1,0:T(8,128)(2,1)S(1)} %add_convert_fusion.46), channel_id=1, source_target_pairs={{0,8},{8,16},{16,24},{24,28},{28,20},{20,12},{12,4},{4,0},{1,9},{9... | collective-permute-start | bytes 393224 | tf_op jit(solution)/shard_map/ppermute | solution.py:290
  597.8 17.7 %collective-permute-start.46 = (bf16[256,1536]{1,0:T(8,128)(2,1)S(1)}, bf16[256,1536]{1,0:T(8,128)(2,1)S(1)}, u32[]{:S(2)}, u32[]{:S(2)}) collective-permute-start(bf16[256,1536]{1,0:T(8,128)(2,1)S(1)} %add_convert_fusion.11), channel_id=1, source_target_pairs={{8,0},{16,8},{24,16},{28,24},{20,28},{12,20},{4,12},{0,4},{9,1},{1... | collective-permute-start | bytes 2359304 | tf_op jit(solution)/shard_map/ppermute | solution.py:291
  599.7 17.1 %collective-permute-start.45 = (bf16[256,1536]{1,0:T(8,128)(2,1)S(1)}, bf16[256,1536]{1,0:T(8,128)(2,1)S(1)}, u32[]{:S(2)}, u32[]{:S(2)}) collective-permute-start(bf16[256,1536]{1,0:T(8,128)(2,1)S(1)} %add_convert_fusion.12), channel_id=1, source_target_pairs={{0,8},{8,16},{16,24},{24,28},{28,20},{20,12},{12,4},{4,0},{1,9},{9... | collective-permute-start | bytes 2359304 | tf_op jit(solution)/shard_map/ppermute | solution.py:290
  600.2 14.6 %collective-permute-start.47 = (bf16[256,256]{1,0:T(8,128)(2,1)S(1)}, bf16[256,256]{1,0:T(8,128)(2,1)S(1)}, u32[]{:S(2)}, u32[]{:S(2)}) collective-permute-start(bf16[256,256]{1,0:T(8,128)(2,1)S(1)} %add_convert_fusion.44), channel_id=1, source_target_pairs={{0,8},{8,16},{16,24},{24,28},{28,20},{20,12},{12,4},{4,0},{1,9},{9... | collective-permute-start | bytes 393224 | tf_op jit(solution)/shard_map/ppermute | solution.py:290
  644.5 17.9 %collective-permute-start.64 = (bf16[256,512]{0,1:T(8,128)(2,1)S(1)}, bf16[256,512]{0,1:T(8,128)(2,1)S(1)}, u32[]{:S(2)}, u32[]{:S(2)}) collective-permute-start(bf16[256,512]{0,1:T(8,128)(2,1)S(1)} %pad_maximum_fusion), channel_id=1, source_target_pairs={{8,0},{16,8},{24,16},{28,24},{20,28},{12,20},{4,12},{0,4},{9,1},{1... | collective-permute-start | bytes 786440 | tf_op jit(solution)/shard_map/ppermute | solution.py:291
  646.9 17.8 %collective-permute-start.57 = (bf16[256,512]{1,0:T(8,128)(2,1)S(1)}, bf16[256,512]{1,0:T(8,128)(2,1)S(1)}, u32[]{:S(2)}, u32[]{:S(2)}) collective-permute-start(bf16[256,512]{1,0:T(8,128)(2,1)S(1)} %convolution_convert_fusion.9), channel_id=1, source_target_pairs={{0,8},{8,16},{16,24},{24,28},{28,20},{20,12},{12,4},{4,0},{1,9},{9... | collective-permute-start | bytes 786440 | tf_op jit(solution)/shard_map/ppermute | solution.py:290
  660.0 48.0 %collective-permute-start.50 = (bf16[512,2048]{1,0:T(8,128)(2,1)}, bf16[512,2048]{1,0:T(8,128)(2,1)}, u32[]{:S(2)}, u32[]{:S(2)}) collective-permute-start(bf16[512,2048]{1,0:T(8,128)(2,1)} %add_convert_fusion.4), channel_id=1, source_target_pairs={{0,2},{1,3},{2,0},{3,1},{4,6},{5,7},{6,4},{7,5},{8,10},{9,11},{10,... | collective-permute-start | bytes 6291464 | tf_op jit(solution)/shard_map/ppermute | solution.py:223
  669.6 43.3 %collective-permute-start.71 = (bf16[256,256]{1,0:T(8,128)(2,1)S(1)}, bf16[256,256]{1,0:T(8,128)(2,1)S(1)}, u32[]{:S(2)}, u32[]{:S(2)}) collective-permute-start(bf16[256,256]{1,0:T(8,128)(2,1)S(1)} %add_convert_fusion.42), channel_id=1, source_target_pairs={{0,8},{8,16},{16,24},{24,28},{28,20},{20,12},{12,4},{4,0},{1,9},{9... | collective-permute-start | bytes 393224 | tf_op jit(solution)/shard_map/ppermute | solution.py:290
  678.3 43.4 %collective-permute-start.72 = (bf16[256,256]{1,0:T(8,128)(2,1)S(1)}, bf16[256,256]{1,0:T(8,128)(2,1)S(1)}, u32[]{:S(2)}, u32[]{:S(2)}) collective-permute-start(bf16[256,256]{1,0:T(8,128)(2,1)S(1)} %add_convert_fusion.41), channel_id=1, source_target_pairs={{8,0},{16,8},{24,16},{28,24},{20,28},{12,20},{4,12},{0,4},{9,1},{1... | collective-permute-start | bytes 393224 | tf_op jit(solution)/shard_map/ppermute | solution.py:291
  683.9 30.3 %collective-permute-start.67 = (bf16[256,512]{0,1:T(8,128)(2,1)S(1)}, bf16[256,512]{0,1:T(8,128)(2,1)S(1)}, u32[]{:S(2)}, u32[]{:S(2)}) collective-permute-start(bf16[256,512]{0,1:T(8,128)(2,1)S(1)} %fusion.27), channel_id=1, source_target_pairs={{8,0},{16,8},{24,16},{28,24},{20,28},{12,20},{4,12},{0,4},{9,1},{1... | collective-permute-start | bytes 786440 | tf_op jit(solution)/shard_map/ppermute | solution.py:291
  685.1 27.2 %collective-permute-start.60 = (bf16[256,512]{1,0:T(8,128)(2,1)S(1)}, bf16[256,512]{1,0:T(8,128)(2,1)S(1)}, u32[]{:S(2)}, u32[]{:S(2)}) collective-permute-start(bf16[256,512]{1,0:T(8,128)(2,1)S(1)} %add_convert_fusion.38), channel_id=1, source_target_pairs={{0,8},{8,16},{16,24},{24,28},{28,20},{20,12},{12,4},{4,0},{1,9},{9... | collective-permute-start | bytes 786440 | tf_op jit(solution)/shard_map/ppermute | solution.py:290
  712.4 26.8 %collective-permute-start.51 = (bf16[512,2048]{1,0:T(8,128)(2,1)}, bf16[512,2048]{1,0:T(8,128)(2,1)}, u32[]{:S(2)}, u32[]{:S(2)}) collective-permute-start(bf16[512,2048]{1,0:T(8,128)(2,1)} %add_convert_fusion.3), channel_id=1, source_target_pairs={{0,1},{1,0},{2,3},{3,2},{4,5},{5,4},{6,7},{7,6},{8,9},{9,8},{10,11... | collective-permute-start | bytes 6291464 | tf_op jit(solution)/shard_map/ppermute | solution.py:225
  732.5 13.2 %collective-permute-start.70 = (bf16[256,512]{0,1:T(8,128)(2,1)S(1)}, bf16[256,512]{0,1:T(8,128)(2,1)S(1)}, u32[]{:S(2)}, u32[]{:S(2)}) collective-permute-start(bf16[256,512]{0,1:T(8,128)(2,1)S(1)} %fusion.30), channel_id=1, source_target_pairs={{8,0},{16,8},{24,16},{28,24},{20,28},{12,20},{4,12},{0,4},{9,1},{1... | collective-permute-start | bytes 786440 | tf_op jit(solution)/shard_map/ppermute | solution.py:291
  (143 other events, 1342.2 us)

commit v9 on v5

--- a/solution.py
+++ b/solution.py
@@ -209,18 +209,19 @@
                 self.half_of = [0 if t < same[t][0] else 1 for t in range(4)]
                 self.tp_ok = True
 
-    def tp_sum(self, part):
+    def tp_sum(self, part, ties=()):
         if not self.tp_ok:
             return lax.psum(part.astype(jnp.float32), "tensor").astype(jnp.bfloat16)
+        ties = list(ties) + [lambda x: x] * (2 - len(ties))
         rows = part.shape[0]
         h = rows // 2
         t = lax.axis_index("tensor")
         half = jnp.array(self.half_of, jnp.int32)[t]
         keep = lax.dynamic_slice_in_dim(part, half * h, h, 0)
         give = lax.dynamic_slice_in_dim(part, (1 - half) * h, h, 0)
-        got = lax.ppermute(give, "tensor", self.core_pairs)
+        got = ties[0](lax.ppermute(give, "tensor", self.core_pairs))
         chip_sum = (keep.astype(jnp.float32) + got.astype(jnp.float32)).astype(jnp.bfloat16)
-        other = lax.ppermute(chip_sum, "tensor", self.chip_pairs)
+        other = ties[1](lax.ppermute(chip_sum, "tensor", self.chip_pairs))
         done = (chip_sum.astype(jnp.float32) + other.astype(jnp.float32)).astype(jnp.bfloat16)
         partner = lax.ppermute(done, "tensor", self.core_pairs)
         first = jnp.where(half == 0, done, partner)
@@ -318,7 +319,15 @@
             q_raw, k_raw, v_raw, query_gain, key_gain, seqs
         )
         attn_part = matmul(attended, w_out).astype(jnp.bfloat16)
-        resid = stream + plan.tp_sum(attn_part).astype(jnp.float32)
+        held = {}
+
+        def tie_hidden(got):
+            held["hidden_grad"], got = lax.optimization_barrier(
+                (outer_cols(cotangent, w_down), got)
+            )
+            return got
+
+        resid = stream + plan.tp_sum(attn_part, (lambda x: x, tie_hidden)).astype(jnp.float32)
         resid_rows = lax.dynamic_slice_in_dim(resid, offset, share, 0)
         normed_mid = rms_scale(resid, mlp_gain).astype(jnp.bfloat16)
         gate = matmul(normed_mid, w_gate)
@@ -336,7 +345,7 @@
             down.state, values = lax.optimization_barrier((down.state, values))
             return values
 
-        hidden_grad = down_hook(outer_cols(cotangent, w_down))
+        hidden_grad = down_hook(held["hidden_grad"])
         _, pull = jax.vjp(swiglu, gate, upper)
         gate_grad, upper_grad = pull(hidden_grad)
         gate_grad = gate_grad.astype(jnp.bfloat16)

time: 709 us -> 702 us (level)
  waiting for transfers between devices: 237 us -> 226 us
    ppermute x8, waiting for transfers between devices: 132 us -> 122 us  [the longest x4 118 us: tp_sum(): other = ties[1](lax.ppermute(chip_sum, 'tensor', self.chip_pairs))]
    unnamed x267 -> x259, local copies, waits for them, and re-layouts: 29.6 us -> 29.4 us
  transfers between devices with their start and end apart: 73 -> 73, of which waited for: 27 -> 29; matrix products, arithmetic and copies ran while one was open for 27% -> 27% of each run, Pallas kernels for 0% -> 0%
where the time goes in v9:
time: 702 us; the launch traced here: 693 us
  waiting for transfers between devices  226 us (32%)
  other arithmetic  148 us (21%)
  matrix products  134 us (19%)
  local copies, waits for them, and re-layouts  86.3 us (12%)
  starting transfers between devices  74.8 us (11%)
  between operations  23.8 us (3%)
    ppermute x4, waiting for transfers between devices, tp_sum(): other = ties[1](lax.ppermute(chip_sum, 'tensor', self.chip_pairs))  118 us
    ppermute x28, waiting for transfers between devices, step(): got_b = lax.ppermute(send_b.astype(jnp.bfloat16), 'dp', self.plan.ccw)  66.6 us
    dot_general x7, matrix products, outer_cols(): lax.dot_general(left, right, (((1,), (1,)), ((), ())), preferred_element_...  48.3 us
    dot_general x7, matrix products, matmul(): return jnp.dot(left, right, preferred_element_type=jnp.float32)  44.8 us
    dot_general x7, matrix products, inner_rows(): lax.dot_general(left, right, (((0,), (0,)), ((), ())), preferred_element_...  38.1 us
    ppermute x28, waiting for transfers between devices, step(): got_a = lax.ppermute(send_a.astype(jnp.bfloat16), 'dp', self.plan.cw)  34.7 us
    ppermute x28, starting transfers between devices, step(): got_b = lax.ppermute(send_b.astype(jnp.bfloat16), 'dp', self.plan.ccw)  34.1 us
    unnamed x259, local copies, waits for them, and re-layouts  29.4 us
  transfers between devices with their start and end apart: 73, of which 29 were waited for; matrix products, arithmetic and copies ran while one was open for 27% of the time, Pallas kernels for 0%

profile of v9, /device:TPU:0, one launch (start us, length us, event | category | flops | bytes accessed | tf_op | source)
XLA Modules:
  0.0 693.4 jit_solution(9886572624315094133)
XLA Ops:
  0.7 3.2 fusion.1
  16.0 6.9 fusion.93
  25.7 3.5 reshape.555
  32.1 3.5 copy.263
  36.9 4.5 convolution_convert_fusion.3
  46.6 4.3 copy.219
  67.3 3.5 collective-permute-done
  70.7 3.0 add_convert_fusion.10
  76.7 10.5 %fusion.94 = f32[1024,1536]{1,0:T(8,128)} fusion(bf16[1024,2048]{1,0:T(8,128)(2,1)S(1)} %copy-done.42, bf16[1536,2048]{1,0:T(8,128)(2,1)} %param.36), kind=kOutput, calls=%fused_computation.342 | convolution fusion | flops 6442450944 | bytes 16777216 | tf_op jit(solution)/shard_map/dot_general | solution.py:33
  87.2 35.4 %collective-permute-done.1 = bf16[512,2048]{1,0:T(8,128)(2,1)S(1)} collective-permute-done((bf16[512,2048]{1,0:T(8,128)(2,1)S(1)}, bf16[512,2048]{1,0:T(8,128)(2,1)S(1)}, u32[]{:S(2)}, u32[]{:S(2)}) %collective-permute-start.1) | collective-permute-done | bytes 2097184 | tf_op jit(solution)/shard_map/ppermute | solution.py:224
  140.8 4.2 convert_add_fusion
  145.6 5.7 multiply_convert_fusion
  151.4 10.3 %fusion.95 = f32[1024,1536]{1,0:T(8,128)S(1)} fusion(bf16[1024,2048]{1,0:T(8,128)(2,1)S(1)} %multiply_convert_fusion, bf16[2048,1536]{1,0:T(8,128)(2,1)} %param.34), kind=kOutput, calls=%fused_computation.343 | convolution fusion | flops 6442450944 | bytes 16777216 | tf_op jit(solution)/shard_map/dot_general | solution.py:23
  161.7 9.4 %multiply_convert_fusion.2 = (bf16[1024,1536]{1,0:T(8,128)(2,1)S(1)}, f32[1024,1536]{1,0:T(8,128)}) fusion(f32[1024,1536]{1,0:T(8,128)S(1)} %fusion.95, bf16[1024,2048]{1,0:T(8,128)(2,1)S(1)} %multiply_convert_fusion, bf16[2048,1536]{1,0:T(8,128)(2,1)S(1)} %bitcast.226), kind=kOutput, calls=%fused_computation.25 | convolution fusion | flops 6451888128 | bytes 26214400 | tf_op jit(solution)/shard_map/dot_general | solution.py:23
  171.2 6.9 fusion.96
  178.1 4.5 copy-done.24
  199.8 9.1 %convolution_convert_fusion = bf16[1024,2048]{1,0:T(8,128)(2,1)S(1)} fusion(bf16[1024,1536]{1,0:T(8,128)(2,1)S(1)} %copy-done.118, bf16[1536,2048]{1,0:T(8,128)(2,1)} %param.36), kind=kOutput, calls=%fused_computation.38 | convolution fusion | flops 6444548096 | bytes 13631488 | tf_op jit(solution)/shard_map/dot_general | solution.py:23
  213.9 8.1 %multiply_convert_fusion.1 = (bf16[1024,1536]{1,0:T(8,128)(2,1)S(1)}, bf16[1024,1536]{1,0:T(8,128)(2,1)}) fusion(f32[1024,1536]{1,0:T(8,128)S(1)} %bitcast.208, f32[1024,1536]{1,0:T(8,128)} %copy-done.30, f32[1024,1536]{1,0:T(8,128)} %get-tuple-element.415), kind=kLoop, calls=%fused_computation.24 | loop fusion | flops 22020096 | bytes 25165824 | tf_op jit(solution)/shard_map/convert_element_type | solution.py:352
  226.3 10.9 %fusion.97 = f32[1024,2048]{1,0:T(8,128)} fusion(bf16[1024,1536]{1,0:T(8,128)(2,1)S(1)} %get-tuple-element.97, bf16[2048,1536]{1,0:T(8,128)(2,1)} %param.35), kind=kOutput, calls=%fused_computation.345 | convolution fusion | flops 6442450944 | bytes 17825792 | tf_op jit(solution)/shard_map/dot_general | solution.py:33
  237.2 10.9 %add_convert_fusion.1 = bf16[1024,2048]{1,0:T(8,128)(2,1)S(1)} fusion(f32[1024,2048]{1,0:T(8,128)} %fusion.97, bf16[1024,1536]{1,0:T(8,128)(2,1)S(1)} %copy-done.73, bf16[2048,1536]{1,0:T(8,128)(2,1)} %param.34), kind=kOutput, calls=%fused_computation.17 | convolution fusion | flops 6446645248 | bytes 22020096 | tf_op jit(solution)/shard_map/dot_general | solution.py:33
  252.2 9.5 %fusion.98 = f32[2048,1536]{1,0:T(8,128)} fusion(bf16[1024,2048]{1,0:T(8,128)(2,1)S(1)} %copy-done.36, bf16[1024,1536]{1,0:T(8,128)(2,1)S(1)} %copy-done.74), kind=kOutput, calls=%fused_computation.346 | convolution fusion | flops 6442450944 | bytes 19922944 | tf_op jit(solution)/shard_map/dot_general | solution.py:27
  261.8 9.5 %fusion.99 = f32[2048,1536]{1,0:T(8,128)} fusion(bf16[1024,2048]{1,0:T(8,128)(2,1)S(1)} %copy-done.36, bf16[1024,1536]{1,0:T(8,128)(2,1)S(1)} %copy-done.72), kind=kOutput, calls=%fused_computation.347 | convolution fusion | flops 6442450944 | bytes 19922944 | tf_op jit(solution)/shard_map/dot_general | solution.py:27
  274.9 8.6 %constant_dynamic-slice_fusion.70 = (f32[128,1536]{1,0:T(8,128)}, f32[128,1536]{1,0:T(8,128)}, f32[128,1536]{1,0:T(8,128)}, f32[128,1536]{1,0:T(8,128)}, f32[128...) fusion(f32[2048,1536]{1,0:T(8,128)} %fusion.98, ...), kind=kLoop, calls=%fused_computation.307 | loop fusion | bytes 22020152 | tf_op jit(solution)/shard_map/dynamic_slice | solution.py:266
  303.0 8.0 %constant_dynamic-slice_fusion.71 = (f32[128,1536]{1,0:T(8,128)}, f32[128,1536]{1,0:T(8,128)}, f32[128,1536]{1,0:T(8,128)}, f32[128,1536]{1,0:T(8,128)}, f32[128...) fusion(f32[2048,1536]{1,0:T(8,128)} %fusion.99, ...), kind=kLoop, calls=%fused_computation.308 | loop fusion | bytes 22020152 | tf_op jit(solution)/shard_map/dynamic_slice | solution.py:266
  311.0 5.8 collective-permute-done.20
  318.4 17.7 %collective-permute-done.4 = bf16[512,2048]{1,0:T(8,128)(2,1)} collective-permute-done((bf16[512,2048]{1,0:T(8,128)(2,1)S(1)}, bf16[512,2048]{1,0:T(8,128)(2,1)}, u32[]{:S(2)}, u32[]{:S(2)}) %collective-permute-start.4) | collective-permute-done | bytes 2097184 | tf_op jit(solution)/shard_map/ppermute | solution.py:224
  338.6 41.4 %collective-permute-done.25 = bf16[512,2048]{1,0:T(8,128)(2,1)S(1)} collective-permute-done((bf16[512,2048]{1,0:T(8,128)(2,1)S(1)}, bf16[512,2048]{1,0:T(8,128)(2,1)S(1)}, u32[]{:S(2)}, u32[]{:S(2)}) %collective-permute-start.25) | collective-permute-done | bytes 2097184 | tf_op jit(solution)/shard_map/ppermute | solution.py:224
  385.1 9.0 %collective-permute-done.18 = bf16[128,1536]{0,1:T(8,128)(2,1)S(1)} collective-permute-done((bf16[128,1536]{0,1:T(8,128)(2,1)S(1)}, bf16[128,1536]{0,1:T(8,128)(2,1)S(1)}, u32[]{:S(2)}, u32[]{:S(2)}) %collective-permute-start.18) | collective-permute-done | bytes 393248 | tf_op jit(solution)/shard_map/ppermute | solution.py:277
  396.3 4.7 collective-permute-done.23
  403.8 3.4 copy-done.3
  410.7 14.5 %subtract_add_fusion = (f32[1024,2048]{1,0:T(8,128)}, bf16[1024,2048]{1,0:T(8,128)(2,1)}) fusion(bf16[1024,2048]{1,0:T(8,128)(2,1)} %param.37, f32[1024]{0:T(1024)S(1)} %broadcast_multiply_fusion.3, f32[1024]{0:T(1024)S(1)} %copy-done.108, f32[2048]{0:T(1024)S(1)} %copy-done.104, f32[1024]{0:T(1024)S(1)} %get-tuple-element.395, ...), kind=kLoop, calls=%fused_computation.15 | loop fusion | flops 48234496 | bytes 33574912 | tf_op jit(solution)/shard_map/add | solution.py:364
  425.1 6.2 fusion.17
  433.8 3.4 fusion.34
  443.4 6.6 convert_element_type.522
  459.4 3.5 collective-permute-done.32
  473.3 14.9 %collective-permute-done.36 = bf16[128,512]{1,0:T(8,128)(2,1)S(1)} collective-permute-done((bf16[128,512]{1,0:T(8,128)(2,1)S(1)}, bf16[128,512]{1,0:T(8,128)(2,1)S(1)}, u32[]{:S(2)}, u32[]{:S(2)}) %collective-permute-start.36) | collective-permute-done | bytes 131104 | tf_op jit(solution)/shard_map/ppermute | solution.py:278
  495.8 14.0 %collective-permute-done.40 = bf16[128,512]{1,0:T(8,128)(2,1)S(1)} collective-permute-done((bf16[128,512]{1,0:T(8,128)(2,1)S(1)}, bf16[128,512]{1,0:T(8,128)(2,1)S(1)}, u32[]{:S(2)}, u32[]{:S(2)}) %collective-permute-start.40) | collective-permute-done | bytes 131104 | tf_op jit(solution)/shard_map/ppermute | solution.py:278
  520.1 11.1 %collective-permute-done.44 = bf16[128,512]{1,0:T(8,128)(2,1)S(1)} collective-permute-done((bf16[128,512]{1,0:T(8,128)(2,1)S(1)}, bf16[128,512]{1,0:T(8,128)(2,1)S(1)}, u32[]{:S(2)}, u32[]{:S(2)}) %collective-permute-start.44) | collective-permute-done | bytes 131104 | tf_op jit(solution)/shard_map/ppermute | solution.py:278
  544.1 5.2 collective-permute-done.45
  552.7 5.8 fusion.85
  561.1 5.5 add_convert_fusion
  603.2 3.6 collective-permute-done.60
  608.7 23.7 %collective-permute-done.50 = bf16[512,2048]{1,0:T(8,128)(2,1)S(1)} collective-permute-done((bf16[512,2048]{1,0:T(8,128)(2,1)S(1)}, bf16[512,2048]{1,0:T(8,128)(2,1)S(1)}, u32[]{:S(2)}, u32[]{:S(2)}) %collective-permute-start.50) | collective-permute-done | bytes 2097184 | tf_op jit(solution)/shard_map/ppermute | solution.py:224
  638.0 5.3 collective-permute-done.68
  647.4 3.9 collective-permute-done.69
  655.3 4.5 collective-permute-done.70
  673.4 4.3 fusion.7
  683.9 7.8 %fusion.6 = f32[1024,2048]{1,0:T(8,128)} fusion(f32[1024,2048]{1,0:T(8,128)} %get-tuple-element.103, bf16[1024,2048]{1,0:T(8,128)(2,1)S(1)} %copy-done.4, f32[1024]{0:T(1024)S(1)} %broadcast_multiply_fusion.2, f32[1024]{0:T(1024)S(1)} %copy-done.107, f32[2048]{0:T(1024)S(1)} %copy-done.101, f32[1024]{0:T(1024)S(1)} %copy-done.106, ...), kind=kLoop, calls=%fused_computation.12 | loop fusion | flops 23068672 | bytes 25186304 | tf_op jit(solution)/shard_map/add | solution.py:420
  (583 shorter events, 249.9 us)
Async XLA Ops:
  73.7 48.8 %collective-permute-start.1 = (bf16[512,2048]{1,0:T(8,128)(2,1)S(1)}, bf16[512,2048]{1,0:T(8,128)(2,1)S(1)}, u32[]{:S(2)}, u32[]{:S(2)}) collective-permute-start(bf16[512,2048]{1,0:T(8,128)(2,1)S(1)} %add_convert_fusion.10), channel_id=1, source_target_pairs={{0,2},{1,3},{2,0},{3,1},{4,6},{5,7},{6,4},{7,5},{8,10},{9,11},{10,... | collective-permute-start | bytes 6291464 | tf_op jit(solution)/shard_map/ppermute | solution.py:224
  124.7 12.6 %collective-permute-start.2 = (bf16[512,2048]{1,0:T(8,128)(2,1)}, bf16[512,2048]{1,0:T(8,128)(2,1)}, u32[]{:S(2)}, u32[]{:S(2)}) collective-permute-start(bf16[512,2048]{1,0:T(8,128)(2,1)} %add_convert_fusion.9), channel_id=1, source_target_pairs={{0,1},{1,0},{2,3},{3,2},{4,5},{5,4},{6,7},{7,6},{8,9},{9,8},{10,11... | collective-permute-start | bytes 6291464 | tf_op jit(solution)/shard_map/ppermute | solution.py:226
  182.8 11.7 %collective-permute-start.8 = (bf16[128,1536]{0,1:T(8,128)(2,1)S(1)}, bf16[128,1536]{0,1:T(8,128)(2,1)S(1)}, u32[]{:S(2)}, u32[]{:S(2)}) collective-permute-start(bf16[128,1536]{0,1:T(8,128)(2,1)S(1)} %get-tuple-element.298), channel_id=1, source_target_pairs={{8,0},{16,8},{24,16},{28,24},{20,28},{12,20},{4,12},{0,4},{9,1},{1... | collective-permute-start | bytes 1179656 | tf_op jit(solution)/shard_map/ppermute | solution.py:278
  184.7 11.3 %collective-permute-start.6 = (bf16[128,1536]{0,1:T(8,128)(2,1)S(1)}, bf16[128,1536]{0,1:T(8,128)(2,1)}, u32[]{:S(2)}, u32[]{:S(2)}) collective-permute-start(bf16[128,1536]{0,1:T(8,128)(2,1)S(1)} %get-tuple-element.299), channel_id=1, source_target_pairs={{0,8},{8,16},{16,24},{24,28},{28,20},{20,12},{12,4},{4,0},{1,9},{9... | collective-permute-start | bytes 1179656 | tf_op jit(solution)/shard_map/ppermute | solution.py:277
  197.7 12.8 %collective-permute-start.9 = (bf16[128,1536]{0,1:T(8,128)(2,1)S(1)}, bf16[128,1536]{0,1:T(8,128)(2,1)S(1)}, u32[]{:S(2)}, u32[]{:S(2)}) collective-permute-start(bf16[128,1536]{0,1:T(8,128)(2,1)S(1)} %get-tuple-element.296), channel_id=1, source_target_pairs={{8,0},{16,8},{24,16},{28,24},{20,28},{12,20},{4,12},{0,4},{9,1},{1... | collective-permute-start | bytes 1179656 | tf_op jit(solution)/shard_map/ppermute | solution.py:278
  199.3 11.2 %collective-permute-start.7 = (bf16[128,1536]{0,1:T(8,128)(2,1)S(1)}, bf16[128,1536]{0,1:T(8,128)(2,1)S(1)}, u32[]{:S(2)}, u32[]{:S(2)}) collective-permute-start(bf16[128,1536]{0,1:T(8,128)(2,1)S(1)} %get-tuple-element.297), channel_id=1, source_target_pairs={{0,8},{8,16},{16,24},{24,28},{28,20},{20,12},{12,4},{4,0},{1,9},{9... | collective-permute-start | bytes 1179656 | tf_op jit(solution)/shard_map/ppermute | solution.py:277
  210.5 74.5 %collective-permute-start.3 = (bf16[512,2048]{1,0:T(8,128)(2,1)}, bf16[512,2048]{1,0:T(8,128)(2,1)}, u32[]{:S(2)}, u32[]{:S(2)}) collective-permute-start(bf16[512,2048]{1,0:T(8,128)(2,1)} %constant_dynamic-slice_fusion.72), channel_id=1, source_target_pairs={{0,1},{1,0},{2,3},{3,2},{4,5},{5,4},{6,7},{7,6},{8,9},{9,8},{10,11... | collective-permute-start | bytes 6291464 | tf_op jit(solution)/shard_map/ppermute | solution.py:222
  211.9 10.7 %collective-permute-start.11 = (bf16[128,1536]{0,1:T(8,128)(2,1)S(1)}, bf16[128,1536]{0,1:T(8,128)(2,1)S(1)}, u32[]{:S(2)}, u32[]{:S(2)}) collective-permute-start(bf16[128,1536]{0,1:T(8,128)(2,1)S(1)} %get-tuple-element.294), channel_id=1, source_target_pairs={{8,0},{16,8},{24,16},{28,24},{20,28},{12,20},{4,12},{0,4},{9,1},{1... | collective-permute-start | bytes 1179656 | tf_op jit(solution)/shard_map/ppermute | solution.py:278
  213.5 10.4 %collective-permute-start.10 = (bf16[128,1536]{0,1:T(8,128)(2,1)S(1)}, bf16[128,1536]{0,1:T(8,128)(2,1)S(1)}, u32[]{:S(2)}, u32[]{:S(2)}) collective-permute-start(bf16[128,1536]{0,1:T(8,128)(2,1)S(1)} %get-tuple-element.295), channel_id=1, source_target_pairs={{0,8},{8,16},{16,24},{24,28},{28,20},{20,12},{12,4},{4,0},{1,9},{9... | collective-permute-start | bytes 1179656 | tf_op jit(solution)/shard_map/ppermute | solution.py:277
  224.2 23.9 %collective-permute-start.13 = (bf16[128,1536]{0,1:T(8,128)(2,1)S(1)}, bf16[128,1536]{0,1:T(8,128)(2,1)S(1)}, u32[]{:S(2)}, u32[]{:S(2)}) collective-permute-start(bf16[128,1536]{0,1:T(8,128)(2,1)S(1)} %get-tuple-element.290), channel_id=1, source_target_pairs={{8,0},{16,8},{24,16},{28,24},{20,28},{12,20},{4,12},{0,4},{9,1},{1... | collective-permute-start | bytes 1179656 | tf_op jit(solution)/shard_map/ppermute | solution.py:278
  226.1 22.1 %collective-permute-start.12 = (bf16[128,1536]{0,1:T(8,128)(2,1)S(1)}, bf16[128,1536]{0,1:T(8,128)(2,1)S(1)}, u32[]{:S(2)}, u32[]{:S(2)}) collective-permute-start(bf16[128,1536]{0,1:T(8,128)(2,1)S(1)} %get-tuple-element.291), channel_id=1, source_target_pairs={{0,8},{8,16},{16,24},{24,28},{28,20},{20,12},{12,4},{4,0},{1,9},{9... | collective-permute-start | bytes 1179656 | tf_op jit(solution)/shard_map/ppermute | solution.py:277
  248.6 22.7 %collective-permute-start.15 = (bf16[128,1536]{0,1:T(8,128)(2,1)S(1)}, bf16[128,1536]{0,1:T(8,128)(2,1)S(1)}, u32[]{:S(2)}, u32[]{:S(2)}) collective-permute-start(bf16[128,1536]{0,1:T(8,128)(2,1)S(1)} %get-tuple-element.288), channel_id=1, source_target_pairs={{8,0},{16,8},{24,16},{28,24},{20,28},{12,20},{4,12},{0,4},{9,1},{1... | collective-permute-start | bytes 1179656 | tf_op jit(solution)/shard_map/ppermute | solution.py:278
  250.5 20.9 %collective-permute-start.14 = (bf16[128,1536]{0,1:T(8,128)(2,1)S(1)}, bf16[128,1536]{0,1:T(8,128)(2,1)S(1)}, u32[]{:S(2)}, u32[]{:S(2)}) collective-permute-start(bf16[128,1536]{0,1:T(8,128)(2,1)S(1)} %get-tuple-element.289), channel_id=1, source_target_pairs={{0,8},{8,16},{16,24},{24,28},{28,20},{20,12},{12,4},{4,0},{1,9},{9... | collective-permute-start | bytes 1179656 | tf_op jit(solution)/shard_map/ppermute | solution.py:277
  252.2 45.6 %collective-permute-start.24 = (bf16[512,2048]{1,0:T(8,128)(2,1)}, bf16[512,2048]{1,0:T(8,128)(2,1)}, u32[]{:S(2)}, u32[]{:S(2)}) collective-permute-start(bf16[512,2048]{1,0:T(8,128)(2,1)} %constant_dynamic-slice_fusion.52), channel_id=1, source_target_pairs={{0,1},{1,0},{2,3},{3,2},{4,5},{5,4},{6,7},{7,6},{8,9},{9,8},{10,11... | collective-permute-start | bytes 6291464 | tf_op jit(solution)/shard_map/ppermute | solution.py:222
  272.5 16.4 %collective-permute-start.17 = (bf16[128,1536]{0,1:T(8,128)(2,1)}, bf16[128,1536]{0,1:T(8,128)(2,1)}, u32[]{:S(2)}, u32[]{:S(2)}) collective-permute-start(bf16[128,1536]{0,1:T(8,128)(2,1)} %get-tuple-element.286), channel_id=1, source_target_pairs={{8,0},{16,8},{24,16},{28,24},{20,28},{12,20},{4,12},{0,4},{9,1},{1... | collective-permute-start | bytes 1179656 | tf_op jit(solution)/shard_map/ppermute | solution.py:278
  274.3 15.7 %collective-permute-start.16 = (bf16[128,1536]{0,1:T(8,128)(2,1)S(1)}, bf16[128,1536]{0,1:T(8,128)(2,1)}, u32[]{:S(2)}, u32[]{:S(2)}) collective-permute-start(bf16[128,1536]{0,1:T(8,128)(2,1)S(1)} %get-tuple-element.287), channel_id=1, source_target_pairs={{0,8},{8,16},{16,24},{24,28},{28,20},{20,12},{12,4},{4,0},{1,9},{9... | collective-permute-start | bytes 1179656 | tf_op jit(solution)/shard_map/ppermute | solution.py:277
  287.5 48.7 %collective-permute-start.4 = (bf16[512,2048]{1,0:T(8,128)(2,1)S(1)}, bf16[512,2048]{1,0:T(8,128)(2,1)}, u32[]{:S(2)}, u32[]{:S(2)}) collective-permute-start(bf16[512,2048]{1,0:T(8,128)(2,1)S(1)} %add_convert_fusion.8), channel_id=1, source_target_pairs={{0,2},{1,3},{2,0},{3,1},{4,6},{5,7},{6,4},{7,5},{8,10},{9,11},{10,... | collective-permute-start | bytes 6291464 | tf_op jit(solution)/shard_map/ppermute | solution.py:224
  293.3 89.5 %collective-permute-start.19 = (bf16[128,1536]{0,1:T(8,128)(2,1)}, bf16[128,1536]{0,1:T(8,128)(2,1)}, u32[]{:S(2)}, u32[]{:S(2)}) collective-permute-start(bf16[128,1536]{0,1:T(8,128)(2,1)} %get-tuple-element.284), channel_id=1, source_target_pairs={{8,0},{16,8},{24,16},{28,24},{20,28},{12,20},{4,12},{0,4},{9,1},{1... | collective-permute-start | bytes 1179656 | tf_op jit(solution)/shard_map/ppermute | solution.py:278
  297.8 19.0 %collective-permute-start.20 = (bf16[128,3072]{1,0:T(8,128)(2,1)}, bf16[128,3072]{1,0:T(8,128)(2,1)}, u32[]{:S(2)}, u32[]{:S(2)}) collective-permute-start(bf16[128,3072]{1,0:T(8,128)(2,1)} %pad_maximum_fusion.1), channel_id=1, source_target_pairs={{0,8},{8,16},{16,24},{24,28},{28,20},{20,12},{12,4},{4,0},{1,9},{9... | collective-permute-start | bytes 2359304 | tf_op jit(solution)/shard_map/ppermute | solution.py:277
  300.3 79.6 %collective-permute-start.25 = (bf16[512,2048]{1,0:T(8,128)(2,1)S(1)}, bf16[512,2048]{1,0:T(8,128)(2,1)S(1)}, u32[]{:S(2)}, u32[]{:S(2)}) collective-permute-start(bf16[512,2048]{1,0:T(8,128)(2,1)S(1)} %add_convert_fusion.6), channel_id=1, source_target_pairs={{0,2},{1,3},{2,0},{3,1},{4,6},{5,7},{6,4},{7,5},{8,10},{9,11},{10,... | collective-permute-start | bytes 6291464 | tf_op jit(solution)/shard_map/ppermute | solution.py:224
  301.1 79.8 %collective-permute-start.22 = (bf16[128,3072]{1,0:T(8,128)(2,1)S(1)}, bf16[128,3072]{1,0:T(8,128)(2,1)S(1)}, u32[]{:S(2)}, u32[]{:S(2)}) collective-permute-start(bf16[128,3072]{1,0:T(8,128)(2,1)S(1)} %pad_maximum_fusion.2), channel_id=1, source_target_pairs={{8,0},{16,8},{24,16},{28,24},{20,28},{12,20},{4,12},{0,4},{9,1},{1... | collective-permute-start | bytes 2359304 | tf_op jit(solution)/shard_map/ppermute | solution.py:278
  318.1 76.9 %collective-permute-start.21 = (bf16[128,3072]{1,0:T(8,128)(2,1)S(1)}, bf16[128,3072]{1,0:T(8,128)(2,1)S(1)}, u32[]{:S(2)}, u32[]{:S(2)}) collective-permute-start(bf16[128,3072]{1,0:T(8,128)(2,1)S(1)} %fusion.22), channel_id=1, source_target_pairs={{0,8},{8,16},{16,24},{24,28},{28,20},{20,12},{12,4},{4,0},{1,9},{9... | collective-permute-start | bytes 2359304 | tf_op jit(solution)/shard_map/ppermute | solution.py:277
  338.5 62.6 %collective-permute-start.5 = (bf16[512,2048]{1,0:T(8,128)(2,1)S(1)}, bf16[512,2048]{1,0:T(8,128)(2,1)S(1)}, u32[]{:S(2)}, u32[]{:S(2)}) collective-permute-start(bf16[512,2048]{1,0:T(8,128)(2,1)S(1)} %add_convert_fusion.7), channel_id=1, source_target_pairs={{0,1},{1,0},{2,3},{3,2},{4,5},{5,4},{6,7},{7,6},{8,9},{9,8},{10,11... | collective-permute-start | bytes 6291464 | tf_op jit(solution)/shard_map/ppermute | solution.py:226
  380.8 22.7 %collective-permute-start.26 = (bf16[512,2048]{1,0:T(8,128)(2,1)S(1)}, bf16[512,2048]{1,0:T(8,128)(2,1)S(1)}, u32[]{:S(2)}, u32[]{:S(2)}) collective-permute-start(bf16[512,2048]{1,0:T(8,128)(2,1)S(1)} %add_convert_fusion.5), channel_id=1, source_target_pairs={{0,1},{1,0},{2,3},{3,2},{4,5},{5,4},{6,7},{7,6},{8,9},{9,8},{10,11... | collective-permute-start | bytes 6291464 | tf_op jit(solution)/shard_map/ppermute | solution.py:226
  381.0 20.0 %collective-permute-start.23 = (bf16[128,3072]{1,0:T(8,128)(2,1)S(1)}, bf16[128,3072]{1,0:T(8,128)(2,1)S(1)}, u32[]{:S(2)}, u32[]{:S(2)}) collective-permute-start(bf16[128,3072]{1,0:T(8,128)(2,1)S(1)} %fusion.23), channel_id=1, source_target_pairs={{8,0},{16,8},{24,16},{28,24},{20,28},{12,20},{4,12},{0,4},{9,1},{1... | collective-permute-start | bytes 2359304 | tf_op jit(solution)/shard_map/ppermute | solution.py:278
  382.8 11.2 %collective-permute-start.18 = (bf16[128,1536]{0,1:T(8,128)(2,1)S(1)}, bf16[128,1536]{0,1:T(8,128)(2,1)S(1)}, u32[]{:S(2)}, u32[]{:S(2)}) collective-permute-start(bf16[128,1536]{0,1:T(8,128)(2,1)S(1)} %get-tuple-element.285), channel_id=1, source_target_pairs={{0,8},{8,16},{16,24},{24,28},{28,20},{20,12},{12,4},{4,0},{1,9},{9... | collective-permute-start | bytes 1179656 | tf_op jit(solution)/shard_map/ppermute | solution.py:277
  440.1 23.7 %collective-permute-start.29 = (bf16[128,3072]{1,0:T(8,128)(2,1)}, bf16[128,3072]{1,0:T(8,128)(2,1)}, u32[]{:S(2)}, u32[]{:S(2)}) collective-permute-start(bf16[128,3072]{1,0:T(8,128)(2,1)} %fusion.24), channel_id=1, source_target_pairs={{0,8},{8,16},{16,24},{24,28},{28,20},{20,12},{12,4},{4,0},{1,9},{9... | collective-permute-start | bytes 2359304 | tf_op jit(solution)/shard_map/ppermute | solution.py:277
  441.7 23.5 %collective-permute-start.30 = (bf16[128,3072]{1,0:T(8,128)(2,1)}, bf16[128,3072]{1,0:T(8,128)(2,1)}, u32[]{:S(2)}, u32[]{:S(2)}) collective-permute-start(bf16[128,3072]{1,0:T(8,128)(2,1)} %fusion.25), channel_id=1, source_target_pairs={{8,0},{16,8},{24,16},{28,24},{20,28},{12,20},{4,12},{0,4},{9,1},{1... | collective-permute-start | bytes 2359304 | tf_op jit(solution)/shard_map/ppermute | solution.py:278
  466.8 21.5 %collective-permute-start.33 = (bf16[128,3072]{1,0:T(8,128)(2,1)S(1)}, bf16[128,3072]{1,0:T(8,128)(2,1)S(1)}, u32[]{:S(2)}, u32[]{:S(2)}) collective-permute-start(bf16[128,3072]{1,0:T(8,128)(2,1)S(1)} %fusion.26), channel_id=1, source_target_pairs={{0,8},{8,16},{16,24},{24,28},{28,20},{20,12},{12,4},{4,0},{1,9},{9... | collective-permute-start | bytes 2359304 | tf_op jit(solution)/shard_map/ppermute | solution.py:277
  468.2 20.3 %collective-permute-start.34 = (bf16[128,3072]{1,0:T(8,128)(2,1)S(1)}, bf16[128,3072]{1,0:T(8,128)(2,1)S(1)}, u32[]{:S(2)}, u32[]{:S(2)}) collective-permute-start(bf16[128,3072]{1,0:T(8,128)(2,1)S(1)} %fusion.27), channel_id=1, source_target_pairs={{8,0},{16,8},{24,16},{28,24},{20,28},{12,20},{4,12},{0,4},{9,1},{1... | collective-permute-start | bytes 2359304 | tf_op jit(solution)/shard_map/ppermute | solution.py:278
  470.8 17.5 %collective-permute-start.36 = (bf16[128,512]{1,0:T(8,128)(2,1)S(1)}, bf16[128,512]{1,0:T(8,128)(2,1)S(1)}, u32[]{:S(2)}, u32[]{:S(2)}) collective-permute-start(bf16[128,512]{1,0:T(8,128)(2,1)S(1)} %get-tuple-element.332), channel_id=1, source_target_pairs={{8,0},{16,8},{24,16},{28,24},{20,28},{12,20},{4,12},{0,4},{9,1},{1... | collective-permute-start | bytes 393224 | tf_op jit(solution)/shard_map/ppermute | solution.py:278
  472.4 15.9 %collective-permute-start.35 = (bf16[128,512]{1,0:T(8,128)(2,1)S(1)}, bf16[128,512]{1,0:T(8,128)(2,1)S(1)}, u32[]{:S(2)}, u32[]{:S(2)}) collective-permute-start(bf16[128,512]{1,0:T(8,128)(2,1)S(1)} %get-tuple-element.333), channel_id=1, source_target_pairs={{0,8},{8,16},{16,24},{24,28},{28,20},{20,12},{12,4},{4,0},{1,9},{9... | collective-permute-start | bytes 393224 | tf_op jit(solution)/shard_map/ppermute | solution.py:277
  488.8 21.1 %collective-permute-start.37 = (bf16[128,3072]{1,0:T(8,128)(2,1)S(1)}, bf16[128,3072]{1,0:T(8,128)(2,1)S(1)}, u32[]{:S(2)}, u32[]{:S(2)}) collective-permute-start(bf16[128,3072]{1,0:T(8,128)(2,1)S(1)} %fusion.28), channel_id=1, source_target_pairs={{0,8},{8,16},{16,24},{24,28},{28,20},{20,12},{12,4},{4,0},{1,9},{9... | collective-permute-start | bytes 2359304 | tf_op jit(solution)/shard_map/ppermute | solution.py:277
  490.8 19.3 %collective-permute-start.38 = (bf16[128,3072]{1,0:T(8,128)(2,1)S(1)}, bf16[128,3072]{1,0:T(8,128)(2,1)S(1)}, u32[]{:S(2)}, u32[]{:S(2)}) collective-permute-start(bf16[128,3072]{1,0:T(8,128)(2,1)S(1)} %fusion.29), channel_id=1, source_target_pairs={{8,0},{16,8},{24,16},{28,24},{20,28},{12,20},{4,12},{0,4},{9,1},{1... | collective-permute-start | bytes 2359304 | tf_op jit(solution)/shard_map/ppermute | solution.py:278
  493.2 16.6 %collective-permute-start.40 = (bf16[128,512]{1,0:T(8,128)(2,1)S(1)}, bf16[128,512]{1,0:T(8,128)(2,1)S(1)}, u32[]{:S(2)}, u32[]{:S(2)}) collective-permute-start(bf16[128,512]{1,0:T(8,128)(2,1)S(1)} %get-tuple-element.330), channel_id=1, source_target_pairs={{8,0},{16,8},{24,16},{28,24},{20,28},{12,20},{4,12},{0,4},{9,1},{1... | collective-permute-start | bytes 393224 | tf_op jit(solution)/shard_map/ppermute | solution.py:278
  494.3 15.6 %collective-permute-start.39 = (bf16[128,512]{1,0:T(8,128)(2,1)S(1)}, bf16[128,512]{1,0:T(8,128)(2,1)S(1)}, u32[]{:S(2)}, u32[]{:S(2)}) collective-permute-start(bf16[128,512]{1,0:T(8,128)(2,1)S(1)} %get-tuple-element.331), channel_id=1, source_target_pairs={{0,8},{8,16},{16,24},{24,28},{28,20},{20,12},{12,4},{4,0},{1,9},{9... | collective-permute-start | bytes 393224 | tf_op jit(solution)/shard_map/ppermute | solution.py:277
  510.5 20.8 %collective-permute-start.41 = (bf16[128,3072]{1,0:T(8,128)(2,1)S(1)}, bf16[128,3072]{1,0:T(8,128)(2,1)S(1)}, u32[]{:S(2)}, u32[]{:S(2)}) collective-permute-start(bf16[128,3072]{1,0:T(8,128)(2,1)S(1)} %fusion.30), channel_id=1, source_target_pairs={{0,8},{8,16},{16,24},{24,28},{28,20},{20,12},{12,4},{4,0},{1,9},{9... | collective-permute-start | bytes 2359304 | tf_op jit(solution)/shard_map/ppermute | solution.py:277
  512.3 19.1 %collective-permute-start.42 = (bf16[128,3072]{1,0:T(8,128)(2,1)S(1)}, bf16[128,3072]{1,0:T(8,128)(2,1)S(1)}, u32[]{:S(2)}, u32[]{:S(2)}) collective-permute-start(bf16[128,3072]{1,0:T(8,128)(2,1)S(1)} %fusion.31), channel_id=1, source_target_pairs={{8,0},{16,8},{24,16},{28,24},{20,28},{12,20},{4,12},{0,4},{9,1},{1... | collective-permute-start | bytes 2359304 | tf_op jit(solution)/shard_map/ppermute | solution.py:278
  517.1 14.1 %collective-permute-start.44 = (bf16[128,512]{1,0:T(8,128)(2,1)S(1)}, bf16[128,512]{1,0:T(8,128)(2,1)S(1)}, u32[]{:S(2)}, u32[]{:S(2)}) collective-permute-start(bf16[128,512]{1,0:T(8,128)(2,1)S(1)} %get-tuple-element.328), channel_id=1, source_target_pairs={{8,0},{16,8},{24,16},{28,24},{20,28},{12,20},{4,12},{0,4},{9,1},{1... | collective-permute-start | bytes 393224 | tf_op jit(solution)/shard_map/ppermute | solution.py:278
  517.4 13.8 %collective-permute-start.43 = (bf16[128,512]{1,0:T(8,128)(2,1)S(1)}, bf16[128,512]{1,0:T(8,128)(2,1)S(1)}, u32[]{:S(2)}, u32[]{:S(2)}) collective-permute-start(bf16[128,512]{1,0:T(8,128)(2,1)S(1)} %get-tuple-element.329), channel_id=1, source_target_pairs={{0,8},{8,16},{16,24},{24,28},{28,20},{20,12},{12,4},{4,0},{1,9},{9... | collective-permute-start | bytes 393224 | tf_op jit(solution)/shard_map/ppermute | solution.py:277
  535.1 14.2 %collective-permute-start.45 = (bf16[128,3072]{1,0:T(8,128)(2,1)S(1)}, bf16[128,3072]{1,0:T(8,128)(2,1)S(1)}, u32[]{:S(2)}, u32[]{:S(2)}) collective-permute-start(bf16[128,3072]{1,0:T(8,128)(2,1)S(1)} %fusion.32), channel_id=1, source_target_pairs={{0,8},{8,16},{16,24},{24,28},{28,20},{20,12},{12,4},{4,0},{1,9},{9... | collective-permute-start | bytes 2359304 | tf_op jit(solution)/shard_map/ppermute | solution.py:277
  536.6 14.0 %collective-permute-start.46 = (bf16[128,3072]{1,0:T(8,128)(2,1)S(1)}, bf16[128,3072]{1,0:T(8,128)(2,1)S(1)}, u32[]{:S(2)}, u32[]{:S(2)}) collective-permute-start(bf16[128,3072]{1,0:T(8,128)(2,1)S(1)} %fusion.33), channel_id=1, source_target_pairs={{8,0},{16,8},{24,16},{28,24},{20,28},{12,20},{4,12},{0,4},{9,1},{1... | collective-permute-start | bytes 2359304 | tf_op jit(solution)/shard_map/ppermute | solution.py:278
  571.2 73.1 %collective-permute-start.71 = (bf16[128,512]{1,0:T(8,128)(2,1)S(1)}, bf16[128,512]{1,0:T(8,128)(2,1)S(1)}, u32[]{:S(2)}, u32[]{:S(2)}) collective-permute-start(bf16[128,512]{1,0:T(8,128)(2,1)S(1)} %get-tuple-element.306), channel_id=1, source_target_pairs={{0,8},{8,16},{16,24},{24,28},{28,20},{20,12},{12,4},{4,0},{1,9},{9... | collective-permute-start | bytes 393224 | tf_op jit(solution)/shard_map/ppermute | solution.py:277
  572.9 71.4 %collective-permute-start.72 = (bf16[128,512]{1,0:T(8,128)(2,1)S(1)}, bf16[128,512]{1,0:T(8,128)(2,1)S(1)}, u32[]{:S(2)}, u32[]{:S(2)}) collective-permute-start(bf16[128,512]{1,0:T(8,128)(2,1)S(1)} %get-tuple-element.307), channel_id=1, source_target_pairs={{8,0},{16,8},{24,16},{28,24},{20,28},{12,20},{4,12},{0,4},{9,1},{1... | collective-permute-start | bytes 393224 | tf_op jit(solution)/shard_map/ppermute | solution.py:278
  586.6 45.8 %collective-permute-start.50 = (bf16[512,2048]{1,0:T(8,128)(2,1)S(1)}, bf16[512,2048]{1,0:T(8,128)(2,1)S(1)}, u32[]{:S(2)}, u32[]{:S(2)}) collective-permute-start(bf16[512,2048]{1,0:T(8,128)(2,1)S(1)} %add_convert_fusion.4), channel_id=1, source_target_pairs={{0,2},{1,3},{2,0},{3,1},{4,6},{5,7},{6,4},{7,5},{8,10},{9,11},{10,... | collective-permute-start | bytes 6291464 | tf_op jit(solution)/shard_map/ppermute | solution.py:224
  602.1 32.4 %collective-permute-start.67 = (bf16[128,1024]{0,1:T(8,128)(2,1)S(1)}, bf16[128,1024]{0,1:T(8,128)(2,1)S(1)}, u32[]{:S(2)}, u32[]{:S(2)}) collective-permute-start(bf16[128,1024]{0,1:T(8,128)(2,1)S(1)} %fusion.70), channel_id=1, source_target_pairs={{8,0},{16,8},{24,16},{28,24},{20,28},{12,20},{4,12},{0,4},{9,1},{1... | collective-permute-start | bytes 786440 | tf_op jit(solution)/shard_map/ppermute | solution.py:278
  606.9 29.8 %collective-permute-start.61 = (bf16[128,1024]{0,1:T(8,128)(2,1)S(1)}, bf16[128,1024]{0,1:T(8,128)(2,1)S(1)}, u32[]{:S(2)}, u32[]{:S(2)}) collective-permute-start(bf16[128,1024]{0,1:T(8,128)(2,1)S(1)} %fusion.65), channel_id=1, source_target_pairs={{0,8},{8,16},{16,24},{24,28},{28,20},{20,12},{12,4},{4,0},{1,9},{9... | collective-permute-start | bytes 786440 | tf_op jit(solution)/shard_map/ppermute | solution.py:277
  634.5 26.3 %collective-permute-start.51 = (bf16[512,2048]{1,0:T(8,128)(2,1)}, bf16[512,2048]{1,0:T(8,128)(2,1)}, u32[]{:S(2)}, u32[]{:S(2)}) collective-permute-start(bf16[512,2048]{1,0:T(8,128)(2,1)} %add_convert_fusion.3), channel_id=1, source_target_pairs={{0,1},{1,0},{2,3},{3,2},{4,5},{5,4},{6,7},{7,6},{8,9},{9,8},{10,11... | collective-permute-start | bytes 6291464 | tf_op jit(solution)/shard_map/ppermute | solution.py:226
  (151 other events, 1054.6 us)

commit v10 on v9

--- a/solution.py
+++ b/solution.py
@@ -209,24 +209,46 @@
                 self.half_of = [0 if t < same[t][0] else 1 for t in range(4)]
                 self.tp_ok = True
 
-    def tp_sum(self, part, ties=()):
+    def tp_begin(self, part):
         if not self.tp_ok:
-            return lax.psum(part.astype(jnp.float32), "tensor").astype(jnp.bfloat16)
-        ties = list(ties) + [lambda x: x] * (2 - len(ties))
+            total = lax.psum(part.astype(jnp.float32), "tensor").astype(jnp.bfloat16)
+            return {"got": total, "other": total}
         rows = part.shape[0]
         h = rows // 2
         t = lax.axis_index("tensor")
         half = jnp.array(self.half_of, jnp.int32)[t]
         keep = lax.dynamic_slice_in_dim(part, half * h, h, 0)
         give = lax.dynamic_slice_in_dim(part, (1 - half) * h, h, 0)
-        got = ties[0](lax.ppermute(give, "tensor", self.core_pairs))
-        chip_sum = (keep.astype(jnp.float32) + got.astype(jnp.float32)).astype(jnp.bfloat16)
-        other = ties[1](lax.ppermute(chip_sum, "tensor", self.chip_pairs))
-        done = (chip_sum.astype(jnp.float32) + other.astype(jnp.float32)).astype(jnp.bfloat16)
+        got = lax.ppermute(give, "tensor", self.core_pairs)
+        return {"half": half, "keep": keep, "got": got}
+
+    def tp_mid(self, st):
+        if not self.tp_ok:
+            return
+        st["chip_sum"] = (st["keep"].astype(jnp.float32) + st["got"].astype(jnp.float32)).astype(
+            jnp.bfloat16
+        )
+        st["other"] = lax.ppermute(st["chip_sum"], "tensor", self.chip_pairs)
+
+    def tp_end(self, st):
+        if not self.tp_ok:
+            return st["other"]
+        half = st["half"]
+        done = (st["chip_sum"].astype(jnp.float32) + st["other"].astype(jnp.float32)).astype(
+            jnp.bfloat16
+        )
         partner = lax.ppermute(done, "tensor", self.core_pairs)
         first = jnp.where(half == 0, done, partner)
         second = jnp.where(half == 0, partner, done)
         return jnp.concatenate([first, second], 0)
+
+    def tp_sum(self, part, ties=()):
+        ties = list(ties) + [lambda x: x] * (2 - len(ties))
+        st = self.tp_begin(part)
+        st["got"] = ties[0](st["got"])
+        self.tp_mid(st)
+        st["other"] = ties[1](st["other"])
+        return self.tp_end(st)
 
     def dp_rs(self, grads):
         ring = Ring(self, grads)
@@ -337,7 +359,7 @@
         down = Ring(plan, [down_grad_t])
         down.step()
         mlp_part = matmul(hidden, w_down).astype(jnp.bfloat16)
-        mixed = (resid + plan.tp_sum(mlp_part).astype(jnp.float32)).astype(jnp.bfloat16)
+        mlp_st = plan.tp_begin(mlp_part)
 
         def down_hook(values):
             if down.done < down.steps:
@@ -345,7 +367,8 @@
             down.state, values = lax.optimization_barrier((down.state, values))
             return values
 
-        hidden_grad = down_hook(held["hidden_grad"])
+        hidden_grad, mlp_st["got"] = down_hook((held["hidden_grad"], mlp_st["got"]))
+        plan.tp_mid(mlp_st)
         _, pull = jax.vjp(swiglu, gate, upper)
         gate_grad, upper_grad = pull(hidden_grad)
         gate_grad = gate_grad.astype(jnp.bfloat16)
@@ -354,7 +377,10 @@
         mid_part = (outer_cols(gate_grad, w_gate) + outer_cols(upper_grad, w_up)).astype(
             jnp.bfloat16
         )
-        mid_part, gate_grad, upper_grad = down_hook((mid_part, gate_grad, upper_grad))
+        mid_part, gate_grad, upper_grad, mlp_st["other"] = down_hook(
+            (mid_part, gate_grad, upper_grad, mlp_st["other"])
+        )
+        mixed = (resid + plan.tp_end(mlp_st).astype(jnp.float32)).astype(jnp.bfloat16)
         mid_sum = plan.tp_sum(mid_part)
         gate_w_grad = down_hook(inner_rows(normed_mid, gate_grad))
         up_w_grad = down_hook(inner_rows(normed_mid, upper_grad))

time: 702 us -> 690 us (0.983)
  waiting for transfers between devices: 226 us -> 208 us
    ppermute x12, waiting for transfers between devices: 122 us -> 99.4 us  [the longest x4 95.9 us: tp_mid(): st['other'] = lax.ppermute(st['chip_sum'], 'tensor', self.chip_pairs)]
    ppermute x28, waiting for transfers between devices: 66.6 us -> 80.1 us  [step(): got_b = lax.ppermute(send_b.astype(jnp.bfloat16), 'dp', self.plan.ccw)]
    ppermute x28, waiting for transfers between devices: 34.7 us -> 24.3 us  [step(): got_a = lax.ppermute(send_a.astype(jnp.bfloat16), 'dp', self.plan.cw)]
    unnamed x259 -> x245, local copies, waits for them, and re-layouts: 29.4 us -> 31.8 us
  transfers between devices with their start and end apart: 73 -> 73, of which waited for: 29 -> 30; matrix products, arithmetic and copies ran while one was open for 27% -> 27% of each run, Pallas kernels for 0% -> 0%
where the time goes in v10:
time: 690 us; the launch traced here: 681 us
  waiting for transfers between devices  208 us (30%)
  other arithmetic  155 us (22%)
  matrix products  132 us (19%)
  local copies, waits for them, and re-layouts  87.6 us (13%)
  starting transfers between devices  74.8 us (11%)
  between operations  23.6 us (3%)
    ppermute x4, waiting for transfers between devices, tp_mid(): st['other'] = lax.ppermute(st['chip_sum'], 'tensor', self.chip_pairs)  95.9 us
    ppermute x28, waiting for transfers between devices, step(): got_b = lax.ppermute(send_b.astype(jnp.bfloat16), 'dp', self.plan.ccw)  80.1 us
    dot_general x7, matrix products, outer_cols(): lax.dot_general(left, right, (((1,), (1,)), ((), ())), preferred_element_...  48.3 us
    dot_general x7, matrix products, matmul(): return jnp.dot(left, right, preferred_element_type=jnp.float32)  42.7 us
    dot_general x7, matrix products, inner_rows(): lax.dot_general(left, right, (((0,), (0,)), ((), ())), preferred_element_...  38.1 us
    unnamed x245, local copies, waits for them, and re-layouts  31.8 us
    ppermute x28, starting transfers between devices, step(): got_b = lax.ppermute(send_b.astype(jnp.bfloat16), 'dp', self.plan.ccw)  31.6 us
    ppermute x28, starting transfers between devices, step(): got_a = lax.ppermute(send_a.astype(jnp.bfloat16), 'dp', self.plan.cw)  29.8 us
  transfers between devices with their start and end apart: 73, of which 30 were waited for; matrix products, arithmetic and copies ran while one was open for 27% of the time, Pallas kernels for 0%

profile of v10, /device:TPU:0, one launch (start us, length us, event | category | flops | bytes accessed | tf_op | source)
XLA Modules:
  0.0 680.7 jit_solution(15247256903071636230)
XLA Ops:
  0.7 3.2 fusion.1
  16.0 6.9 %fusion.93 = f32[1024,512]{1,0:T(8,128)} fusion(bf16[1024,2048]{1,0:T(8,128)(2,1)} %copy-done.39, bf16[2048,512]{1,0:T(8,128)(2,1)} %param.27), kind=kOutput, calls=%fused_computation.341 | convolution fusion | flops 2147483648 | bytes 8388608 | tf_op jit(solution)/shard_map/dot_general | solution.py:23
  25.7 3.5 reshape.555
  32.1 3.5 copy.263
  36.9 4.5 convolution_convert_fusion.3
  46.7 4.3 copy.219
  67.3 3.5 collective-permute-done
  76.7 10.6 %fusion.94 = f32[1024,1536]{1,0:T(8,128)} fusion(bf16[1024,2048]{1,0:T(8,128)(2,1)S(1)} %copy-done.41, bf16[1536,2048]{1,0:T(8,128)(2,1)} %param.36), kind=kOutput, calls=%fused_computation.342 | convolution fusion | flops 6442450944 | bytes 16777216 | tf_op jit(solution)/shard_map/dot_general | solution.py:33
  87.3 35.4 %collective-permute-done.1 = bf16[512,2048]{1,0:T(8,128)(2,1)S(1)} collective-permute-done((bf16[512,2048]{1,0:T(8,128)(2,1)S(1)}, bf16[512,2048]{1,0:T(8,128)(2,1)S(1)}, u32[]{:S(2)}, u32[]{:S(2)}) %collective-permute-start.1) | collective-permute-done | bytes 2097184 | tf_op jit(solution)/shard_map/ppermute | solution.py:231
  140.8 4.2 convert_add_fusion
  145.6 5.7 multiply_convert_fusion
  151.4 10.3 %fusion.95 = f32[1024,1536]{1,0:T(8,128)S(1)} fusion(bf16[1024,2048]{1,0:T(8,128)(2,1)S(1)} %multiply_convert_fusion, bf16[2048,1536]{1,0:T(8,128)(2,1)} %param.34), kind=kOutput, calls=%fused_computation.343 | convolution fusion | flops 6442450944 | bytes 16777216 | tf_op jit(solution)/shard_map/dot_general | solution.py:23
  161.8 9.0 %multiply_convert_fusion.2 = (bf16[1024,1536]{1,0:T(8,128)(2,1)S(1)}, f32[1024,1536]{1,0:T(8,128)}) fusion(f32[1024,1536]{1,0:T(8,128)S(1)} %fusion.95, bf16[1024,2048]{1,0:T(8,128)(2,1)S(1)} %multiply_convert_fusion, bf16[2048,1536]{1,0:T(8,128)(2,1)S(1)} %bitcast.226), kind=kOutput, calls=%fused_computation.25 | convolution fusion | flops 6451888128 | bytes 26214400 | tf_op jit(solution)/shard_map/dot_general | solution.py:23
  170.9 7.3 %convolution_convert_fusion = bf16[1024,2048]{1,0:T(8,128)(2,1)S(1)} fusion(bf16[1024,1536]{1,0:T(8,128)(2,1)S(1)} %get-tuple-element.418, bf16[1536,2048]{1,0:T(8,128)(2,1)S(1)} %bitcast.224), kind=kOutput, calls=%fused_computation.38 | convolution fusion | flops 6444548096 | bytes 13631488 | tf_op jit(solution)/shard_map/dot_general | solution.py:23
  182.6 6.8 fusion.96
  189.4 4.5 copy-done.24
  197.5 8.4 %collective-permute-done.5 = bf16[128,1536]{0,1:T(8,128)(2,1)S(1)} collective-permute-done((bf16[128,1536]{0,1:T(8,128)(2,1)S(1)}, bf16[128,1536]{0,1:T(8,128)(2,1)S(1)}, u32[]{:S(2)}, u32[]{:S(2)}) %collective-permute-start.5) | collective-permute-done | bytes 393248 | tf_op jit(solution)/shard_map/ppermute | solution.py:300
  221.6 3.2 add_convert_fusion.8
  229.9 6.7 multiply_convert_fusion.1
  241.4 10.9 %fusion.97 = f32[1024,2048]{1,0:T(8,128)} fusion(bf16[1024,1536]{1,0:T(8,128)(2,1)S(1)} %get-tuple-element.101, bf16[2048,1536]{1,0:T(8,128)(2,1)} %param.35), kind=kOutput, calls=%fused_computation.345 | convolution fusion | flops 6442450944 | bytes 17825792 | tf_op jit(solution)/shard_map/dot_general | solution.py:33
  252.4 10.9 %add_convert_fusion.2 = bf16[1024,2048]{1,0:T(8,128)(2,1)S(1)} fusion(f32[1024,2048]{1,0:T(8,128)} %fusion.97, bf16[1024,1536]{1,0:T(8,128)(2,1)S(1)} %get-tuple-element.98, bf16[2048,1536]{1,0:T(8,128)(2,1)} %param.34), kind=kOutput, calls=%fused_computation.18 | convolution fusion | flops 6446645248 | bytes 22020096 | tf_op jit(solution)/shard_map/dot_general | solution.py:33
  263.4 10.3 %collective-permute-done.12 = bf16[512,2048]{1,0:T(8,128)(2,1)S(1)} collective-permute-done((bf16[512,2048]{1,0:T(8,128)(2,1)S(1)}, bf16[512,2048]{1,0:T(8,128)(2,1)S(1)}, u32[]{:S(2)}, u32[]{:S(2)}) %collective-permute-start.12) | collective-permute-done | bytes 2097184 | tf_op jit(solution)/shard_map/ppermute | solution.py:231
  280.4 9.4 %fusion.98 = f32[2048,1536]{1,0:T(8,128)} fusion(bf16[1024,2048]{1,0:T(8,128)(2,1)S(1)} %copy-done.36, bf16[1024,1536]{1,0:T(8,128)(2,1)S(1)} %copy-done.69), kind=kOutput, calls=%fused_computation.346 | convolution fusion | flops 6442450944 | bytes 19922944 | tf_op jit(solution)/shard_map/dot_general | solution.py:27
  289.8 9.6 %fusion.99 = f32[2048,1536]{1,0:T(8,128)} fusion(bf16[1024,2048]{1,0:T(8,128)(2,1)S(1)} %copy-done.36, bf16[1024,1536]{1,0:T(8,128)(2,1)S(1)} %get-tuple-element.101), kind=kOutput, calls=%fused_computation.347 | convolution fusion | flops 6442450944 | bytes 19922944 | tf_op jit(solution)/shard_map/dot_general | solution.py:27
  303.2 7.8 %constant_dynamic-slice_fusion.70 = (f32[128,1536]{1,0:T(8,128)}, f32[128,1536]{1,0:T(8,128)}, f32[128,1536]{1,0:T(8,128)}, f32[128,1536]{1,0:T(8,128)}, f32[128...) fusion(f32[2048,1536]{1,0:T(8,128)} %fusion.98, ...), kind=kLoop, calls=%fused_computation.307 | loop fusion | bytes 22020152 | tf_op jit(solution)/shard_map/dynamic_slice | solution.py:288
  326.4 7.8 %constant_dynamic-slice_fusion.71 = (f32[128,1536]{1,0:T(8,128)}, f32[128,1536]{1,0:T(8,128)}, f32[128,1536]{1,0:T(8,128)}, f32[128,1536]{1,0:T(8,128)}, f32[128...) fusion(f32[2048,1536]{1,0:T(8,128)} %fusion.99, ...), kind=kLoop, calls=%fused_computation.308 | loop fusion | bytes 22020152 | tf_op jit(solution)/shard_map/dynamic_slice | solution.py:288
  334.2 26.3 %collective-permute-done.25 = bf16[512,2048]{1,0:T(8,128)(2,1)S(1)} collective-permute-done((bf16[512,2048]{1,0:T(8,128)(2,1)S(1)}, bf16[512,2048]{1,0:T(8,128)(2,1)S(1)}, u32[]{:S(2)}, u32[]{:S(2)}) %collective-permute-start.25) | collective-permute-done | bytes 2097184 | tf_op jit(solution)/shard_map/ppermute | solution.py:231
  364.3 14.3 %collective-permute-done.22 = bf16[128,3072]{1,0:T(8,128)(2,1)S(1)} collective-permute-done((bf16[128,3072]{1,0:T(8,128)(2,1)S(1)}, bf16[128,3072]{1,0:T(8,128)(2,1)S(1)}, u32[]{:S(2)}, u32[]{:S(2)}) %collective-permute-start.22) | collective-permute-done | bytes 786464 | tf_op jit(solution)/shard_map/ppermute | solution.py:300
  384.9 3.9 broadcast_select_fusion.5
  388.9 6.9 %collective-permute-done.21 = bf16[128,3072]{1,0:T(8,128)(2,1)S(1)} collective-permute-done((bf16[128,3072]{1,0:T(8,128)(2,1)S(1)}, bf16[128,3072]{1,0:T(8,128)(2,1)S(1)}, u32[]{:S(2)}, u32[]{:S(2)}) %collective-permute-start.21) | collective-permute-done | bytes 786464 | tf_op jit(solution)/shard_map/ppermute | solution.py:299
  397.6 3.4 copy-done.3
  404.4 14.5 %subtract_add_fusion = (f32[1024,2048]{1,0:T(8,128)}, bf16[1024,2048]{1,0:T(8,128)(2,1)}) fusion(bf16[1024,2048]{1,0:T(8,128)(2,1)} %param.37, f32[1024]{0:T(1024)S(1)} %broadcast_multiply_fusion.3, f32[1024]{0:T(1024)S(1)} %copy-done.104, f32[2048]{0:T(1024)S(1)} %copy-done.100, f32[1024]{0:T(1024)S(1)} %get-tuple-element.399, ...), kind=kLoop, calls=%fused_computation.15 | loop fusion | flops 48234496 | bytes 33574912 | tf_op jit(solution)/shard_map/add | solution.py:390
  418.9 6.2 fusion.17
  428.6 3.4 fusion.34
  437.4 6.6 convert_element_type.522
  466.0 13.5 %collective-permute-done.36 = bf16[128,512]{1,0:T(8,128)(2,1)S(1)} collective-permute-done((bf16[128,512]{1,0:T(8,128)(2,1)S(1)}, bf16[128,512]{1,0:T(8,128)(2,1)S(1)}, u32[]{:S(2)}, u32[]{:S(2)}) %collective-permute-start.36) | collective-permute-done | bytes 131104 | tf_op jit(solution)/shard_map/ppermute | solution.py:300
  487.2 13.3 %collective-permute-done.40 = bf16[128,512]{1,0:T(8,128)(2,1)S(1)} collective-permute-done((bf16[128,512]{1,0:T(8,128)(2,1)S(1)}, bf16[128,512]{1,0:T(8,128)(2,1)S(1)}, u32[]{:S(2)}, u32[]{:S(2)}) %collective-permute-start.40) | collective-permute-done | bytes 131104 | tf_op jit(solution)/shard_map/ppermute | solution.py:300
  510.7 10.5 %collective-permute-done.44 = bf16[128,512]{1,0:T(8,128)(2,1)S(1)} collective-permute-done((bf16[128,512]{1,0:T(8,128)(2,1)S(1)}, bf16[128,512]{1,0:T(8,128)(2,1)S(1)}, u32[]{:S(2)}, u32[]{:S(2)}) %collective-permute-start.44) | collective-permute-done | bytes 131104 | tf_op jit(solution)/shard_map/ppermute | solution.py:300
  541.0 5.8 fusion.85
  549.3 5.5 add_convert_fusion
  590.7 4.3 collective-permute-done.60
  596.6 23.9 %collective-permute-done.50 = bf16[512,2048]{1,0:T(8,128)(2,1)S(1)} collective-permute-done((bf16[512,2048]{1,0:T(8,128)(2,1)S(1)}, bf16[512,2048]{1,0:T(8,128)(2,1)S(1)}, u32[]{:S(2)}, u32[]{:S(2)}) %collective-permute-start.50) | collective-permute-done | bytes 2097184 | tf_op jit(solution)/shard_map/ppermute | solution.py:231
  626.2 5.3 collective-permute-done.68
  635.6 3.9 collective-permute-done.69
  643.3 4.6 collective-permute-done.70
  661.7 4.6 fusion.7
  666.9 3.3 collective-permute-done.55
  671.5 7.8 %fusion.6 = f32[1024,2048]{1,0:T(8,128)} fusion(f32[1024,2048]{1,0:T(8,128)} %get-tuple-element.107, bf16[1024,2048]{1,0:T(8,128)(2,1)S(1)} %copy-done.4, f32[1024]{0:T(1024)S(1)} %broadcast_multiply_fusion.2, f32[1024]{0:T(1024)S(1)} %copy-done.103, f32[2048]{0:T(1024)S(1)} %copy-done.97, f32[1024]{0:T(1024)S(1)} %copy-done.102, ...), kind=kLoop, calls=%fused_computation.12 | loop fusion | flops 23068672 | bytes 25186304 | tf_op jit(solution)/shard_map/add | solution.py:446
  (569 shorter events, 257.0 us)
Async XLA Ops:
  73.8 48.8 %collective-permute-start.1 = (bf16[512,2048]{1,0:T(8,128)(2,1)S(1)}, bf16[512,2048]{1,0:T(8,128)(2,1)S(1)}, u32[]{:S(2)}, u32[]{:S(2)}) collective-permute-start(bf16[512,2048]{1,0:T(8,128)(2,1)S(1)} %add_convert_fusion.10), channel_id=1, source_target_pairs={{0,2},{1,3},{2,0},{3,1},{4,6},{5,7},{6,4},{7,5},{8,10},{9,11},{10,... | collective-permute-start | bytes 6291464 | tf_op jit(solution)/shard_map/ppermute | solution.py:231
  124.8 12.6 %collective-permute-start.2 = (bf16[512,2048]{1,0:T(8,128)(2,1)}, bf16[512,2048]{1,0:T(8,128)(2,1)}, u32[]{:S(2)}, u32[]{:S(2)}) collective-permute-start(bf16[512,2048]{1,0:T(8,128)(2,1)} %add_convert_fusion.9), channel_id=1, source_target_pairs={{0,1},{1,0},{2,3},{3,2},{4,5},{5,4},{6,7},{7,6},{8,9},{9,8},{10,11... | collective-permute-start | bytes 6291464 | tf_op jit(solution)/shard_map/ppermute | solution.py:240
  181.3 40.3 %collective-permute-start.7 = (bf16[512,2048]{1,0:T(8,128)(2,1)}, bf16[512,2048]{1,0:T(8,128)(2,1)}, u32[]{:S(2)}, u32[]{:S(2)}) collective-permute-start(bf16[512,2048]{1,0:T(8,128)(2,1)} %constant_dynamic-slice_fusion.72), channel_id=1, source_target_pairs={{0,1},{1,0},{2,3},{3,2},{4,5},{5,4},{6,7},{7,6},{8,9},{9,8},{10,11... | collective-permute-start | bytes 6291464 | tf_op jit(solution)/shard_map/ppermute | solution.py:222
  194.2 11.7 %collective-permute-start.5 = (bf16[128,1536]{0,1:T(8,128)(2,1)S(1)}, bf16[128,1536]{0,1:T(8,128)(2,1)S(1)}, u32[]{:S(2)}, u32[]{:S(2)}) collective-permute-start(bf16[128,1536]{0,1:T(8,128)(2,1)S(1)} %get-tuple-element.302), channel_id=1, source_target_pairs={{8,0},{16,8},{24,16},{28,24},{20,28},{12,20},{4,12},{0,4},{9,1},{1... | collective-permute-start | bytes 1179656 | tf_op jit(solution)/shard_map/ppermute | solution.py:300
  196.0 11.4 %collective-permute-start.3 = (bf16[128,1536]{0,1:T(8,128)(2,1)S(1)}, bf16[128,1536]{0,1:T(8,128)(2,1)}, u32[]{:S(2)}, u32[]{:S(2)}) collective-permute-start(bf16[128,1536]{0,1:T(8,128)(2,1)S(1)} %get-tuple-element.303), channel_id=1, source_target_pairs={{0,8},{8,16},{16,24},{24,28},{28,20},{20,12},{12,4},{4,0},{1,9},{9... | collective-permute-start | bytes 1179656 | tf_op jit(solution)/shard_map/ppermute | solution.py:299
  209.9 10.6 %collective-permute-start.6 = (bf16[128,1536]{0,1:T(8,128)(2,1)}, bf16[128,1536]{0,1:T(8,128)(2,1)S(1)}, u32[]{:S(2)}, u32[]{:S(2)}) collective-permute-start(bf16[128,1536]{0,1:T(8,128)(2,1)} %get-tuple-element.300), channel_id=1, source_target_pairs={{8,0},{16,8},{24,16},{28,24},{20,28},{12,20},{4,12},{0,4},{9,1},{1... | collective-permute-start | bytes 1179656 | tf_op jit(solution)/shard_map/ppermute | solution.py:300
  211.4 10.1 %collective-permute-start.4 = (bf16[128,1536]{0,1:T(8,128)(2,1)S(1)}, bf16[128,1536]{0,1:T(8,128)(2,1)S(1)}, u32[]{:S(2)}, u32[]{:S(2)}) collective-permute-start(bf16[128,1536]{0,1:T(8,128)(2,1)S(1)} %get-tuple-element.301), channel_id=1, source_target_pairs={{0,8},{8,16},{16,24},{24,28},{28,20},{20,12},{12,4},{4,0},{1,9},{9... | collective-permute-start | bytes 1179656 | tf_op jit(solution)/shard_map/ppermute | solution.py:299
  226.4 10.3 %collective-permute-start.9 = (bf16[128,1536]{0,1:T(8,128)(2,1)S(1)}, bf16[128,1536]{0,1:T(8,128)(2,1)S(1)}, u32[]{:S(2)}, u32[]{:S(2)}) collective-permute-start(bf16[128,1536]{0,1:T(8,128)(2,1)S(1)} %get-tuple-element.298), channel_id=1, source_target_pairs={{8,0},{16,8},{24,16},{28,24},{20,28},{12,20},{4,12},{0,4},{9,1},{1... | collective-permute-start | bytes 1179656 | tf_op jit(solution)/shard_map/ppermute | solution.py:300
  228.4 45.2 %collective-permute-start.12 = (bf16[512,2048]{1,0:T(8,128)(2,1)S(1)}, bf16[512,2048]{1,0:T(8,128)(2,1)S(1)}, u32[]{:S(2)}, u32[]{:S(2)}) collective-permute-start(bf16[512,2048]{1,0:T(8,128)(2,1)S(1)} %add_convert_fusion.8), channel_id=1, source_target_pairs={{0,2},{1,3},{2,0},{3,1},{4,6},{5,7},{6,4},{7,5},{8,10},{9,11},{10,... | collective-permute-start | bytes 6291464 | tf_op jit(solution)/shard_map/ppermute | solution.py:231
  239.4 23.9 %collective-permute-start.11 = (bf16[128,1536]{0,1:T(8,128)(2,1)S(1)}, bf16[128,1536]{0,1:T(8,128)(2,1)S(1)}, u32[]{:S(2)}, u32[]{:S(2)}) collective-permute-start(bf16[128,1536]{0,1:T(8,128)(2,1)S(1)} %get-tuple-element.294), channel_id=1, source_target_pairs={{8,0},{16,8},{24,16},{28,24},{20,28},{12,20},{4,12},{0,4},{9,1},{1... | collective-permute-start | bytes 1179656 | tf_op jit(solution)/shard_map/ppermute | solution.py:300
  241.0 22.3 %collective-permute-start.10 = (bf16[128,1536]{0,1:T(8,128)(2,1)S(1)}, bf16[128,1536]{0,1:T(8,128)(2,1)S(1)}, u32[]{:S(2)}, u32[]{:S(2)}) collective-permute-start(bf16[128,1536]{0,1:T(8,128)(2,1)S(1)} %get-tuple-element.295), channel_id=1, source_target_pairs={{0,8},{8,16},{16,24},{24,28},{28,20},{20,12},{12,4},{4,0},{1,9},{9... | collective-permute-start | bytes 1179656 | tf_op jit(solution)/shard_map/ppermute | solution.py:299
  276.2 23.2 %collective-permute-start.15 = (bf16[128,1536]{0,1:T(8,128)(2,1)S(1)}, bf16[128,1536]{0,1:T(8,128)(2,1)S(1)}, u32[]{:S(2)}, u32[]{:S(2)}) collective-permute-start(bf16[128,1536]{0,1:T(8,128)(2,1)S(1)} %get-tuple-element.292), channel_id=1, source_target_pairs={{8,0},{16,8},{24,16},{28,24},{20,28},{12,20},{4,12},{0,4},{9,1},{1... | collective-permute-start | bytes 1179656 | tf_op jit(solution)/shard_map/ppermute | solution.py:300
  277.8 21.6 %collective-permute-start.14 = (bf16[128,1536]{0,1:T(8,128)(2,1)S(1)}, bf16[128,1536]{0,1:T(8,128)(2,1)S(1)}, u32[]{:S(2)}, u32[]{:S(2)}) collective-permute-start(bf16[128,1536]{0,1:T(8,128)(2,1)S(1)} %get-tuple-element.293), channel_id=1, source_target_pairs={{0,8},{8,16},{16,24},{24,28},{28,20},{20,12},{12,4},{4,0},{1,9},{9... | collective-permute-start | bytes 1179656 | tf_op jit(solution)/shard_map/ppermute | solution.py:299
  279.8 31.1 %collective-permute-start.24 = (bf16[512,2048]{1,0:T(8,128)(2,1)}, bf16[512,2048]{1,0:T(8,128)(2,1)}, u32[]{:S(2)}, u32[]{:S(2)}) collective-permute-start(bf16[512,2048]{1,0:T(8,128)(2,1)} %constant_dynamic-slice_fusion.52), channel_id=1, source_target_pairs={{0,1},{1,0},{2,3},{3,2},{4,5},{5,4},{6,7},{7,6},{8,9},{9,8},{10,11... | collective-permute-start | bytes 6291464 | tf_op jit(solution)/shard_map/ppermute | solution.py:222
  279.8 105.1 %collective-permute-start.13 = (bf16[512,2048]{1,0:T(8,128)(2,1)S(1)}, bf16[512,2048]{1,0:T(8,128)(2,1)}, u32[]{:S(2)}, u32[]{:S(2)}) collective-permute-start(bf16[512,2048]{1,0:T(8,128)(2,1)S(1)} %add_convert_fusion.7), channel_id=1, source_target_pairs={{0,1},{1,0},{2,3},{3,2},{4,5},{5,4},{6,7},{7,6},{8,9},{9,8},{10,11... | collective-permute-start | bytes 6291464 | tf_op jit(solution)/shard_map/ppermute | solution.py:240
  301.1 15.3 %collective-permute-start.17 = (bf16[128,1536]{0,1:T(8,128)(2,1)S(1)}, bf16[128,1536]{0,1:T(8,128)(2,1)}, u32[]{:S(2)}, u32[]{:S(2)}) collective-permute-start(bf16[128,1536]{0,1:T(8,128)(2,1)S(1)} %get-tuple-element.290), channel_id=1, source_target_pairs={{8,0},{16,8},{24,16},{28,24},{20,28},{12,20},{4,12},{0,4},{9,1},{1... | collective-permute-start | bytes 1179656 | tf_op jit(solution)/shard_map/ppermute | solution.py:300
  302.8 14.8 %collective-permute-start.16 = (bf16[128,1536]{0,1:T(8,128)(2,1)S(1)}, bf16[128,1536]{0,1:T(8,128)(2,1)}, u32[]{:S(2)}, u32[]{:S(2)}) collective-permute-start(bf16[128,1536]{0,1:T(8,128)(2,1)S(1)} %get-tuple-element.291), channel_id=1, source_target_pairs={{0,8},{8,16},{16,24},{24,28},{28,20},{20,12},{12,4},{4,0},{1,9},{9... | collective-permute-start | bytes 1179656 | tf_op jit(solution)/shard_map/ppermute | solution.py:299
  313.5 47.1 %collective-permute-start.25 = (bf16[512,2048]{1,0:T(8,128)(2,1)S(1)}, bf16[512,2048]{1,0:T(8,128)(2,1)S(1)}, u32[]{:S(2)}, u32[]{:S(2)}) collective-permute-start(bf16[512,2048]{1,0:T(8,128)(2,1)S(1)} %add_convert_fusion.6), channel_id=1, source_target_pairs={{0,2},{1,3},{2,0},{3,1},{4,6},{5,7},{6,4},{7,5},{8,10},{9,11},{10,... | collective-permute-start | bytes 6291464 | tf_op jit(solution)/shard_map/ppermute | solution.py:231
  320.9 58.9 %collective-permute-start.19 = (bf16[128,1536]{0,1:T(8,128)(2,1)}, bf16[128,1536]{0,1:T(8,128)(2,1)}, u32[]{:S(2)}, u32[]{:S(2)}) collective-permute-start(bf16[128,1536]{0,1:T(8,128)(2,1)} %get-tuple-element.288), channel_id=1, source_target_pairs={{8,0},{16,8},{24,16},{28,24},{20,28},{12,20},{4,12},{0,4},{9,1},{1... | collective-permute-start | bytes 1179656 | tf_op jit(solution)/shard_map/ppermute | solution.py:300
  322.5 60.5 %collective-permute-start.18 = (bf16[128,1536]{0,1:T(8,128)(2,1)S(1)}, bf16[128,1536]{0,1:T(8,128)(2,1)}, u32[]{:S(2)}, u32[]{:S(2)}) collective-permute-start(bf16[128,1536]{0,1:T(8,128)(2,1)S(1)} %get-tuple-element.289), channel_id=1, source_target_pairs={{0,8},{8,16},{16,24},{24,28},{28,20},{20,12},{12,4},{4,0},{1,9},{9... | collective-permute-start | bytes 1179656 | tf_op jit(solution)/shard_map/ppermute | solution.py:299
  325.3 37.6 %collective-permute-start.20 = (bf16[128,3072]{1,0:T(8,128)(2,1)}, bf16[128,3072]{1,0:T(8,128)(2,1)}, u32[]{:S(2)}, u32[]{:S(2)}) collective-permute-start(bf16[128,3072]{1,0:T(8,128)(2,1)} %pad_maximum_fusion.1), channel_id=1, source_target_pairs={{0,8},{8,16},{16,24},{24,28},{28,20},{20,12},{12,4},{4,0},{1,9},{9... | collective-permute-start | bytes 2359304 | tf_op jit(solution)/shard_map/ppermute | solution.py:299
  360.5 18.1 %collective-permute-start.22 = (bf16[128,3072]{1,0:T(8,128)(2,1)S(1)}, bf16[128,3072]{1,0:T(8,128)(2,1)S(1)}, u32[]{:S(2)}, u32[]{:S(2)}) collective-permute-start(bf16[128,3072]{1,0:T(8,128)(2,1)S(1)} %pad_maximum_fusion.2), channel_id=1, source_target_pairs={{8,0},{16,8},{24,16},{28,24},{20,28},{12,20},{4,12},{0,4},{9,1},{1... | collective-permute-start | bytes 2359304 | tf_op jit(solution)/shard_map/ppermute | solution.py:300
  362.9 34.3 %collective-permute-start.26 = (bf16[512,2048]{1,0:T(8,128)(2,1)S(1)}, bf16[512,2048]{1,0:T(8,128)(2,1)S(1)}, u32[]{:S(2)}, u32[]{:S(2)}) collective-permute-start(bf16[512,2048]{1,0:T(8,128)(2,1)S(1)} %add_convert_fusion.5), channel_id=1, source_target_pairs={{0,1},{1,0},{2,3},{3,2},{4,5},{5,4},{6,7},{7,6},{8,9},{9,8},{10,11... | collective-permute-start | bytes 6291464 | tf_op jit(solution)/shard_map/ppermute | solution.py:240
  378.6 17.2 %collective-permute-start.21 = (bf16[128,3072]{1,0:T(8,128)(2,1)S(1)}, bf16[128,3072]{1,0:T(8,128)(2,1)S(1)}, u32[]{:S(2)}, u32[]{:S(2)}) collective-permute-start(bf16[128,3072]{1,0:T(8,128)(2,1)S(1)} %fusion.22), channel_id=1, source_target_pairs={{0,8},{8,16},{16,24},{24,28},{28,20},{20,12},{12,4},{4,0},{1,9},{9... | collective-permute-start | bytes 2359304 | tf_op jit(solution)/shard_map/ppermute | solution.py:299
  379.8 17.3 %collective-permute-start.23 = (bf16[128,3072]{1,0:T(8,128)(2,1)S(1)}, bf16[128,3072]{1,0:T(8,128)(2,1)S(1)}, u32[]{:S(2)}, u32[]{:S(2)}) collective-permute-start(bf16[128,3072]{1,0:T(8,128)(2,1)S(1)} %fusion.23), channel_id=1, source_target_pairs={{8,0},{16,8},{24,16},{28,24},{20,28},{12,20},{4,12},{0,4},{9,1},{1... | collective-permute-start | bytes 2359304 | tf_op jit(solution)/shard_map/ppermute | solution.py:300
  433.9 22.7 %collective-permute-start.29 = (bf16[128,3072]{1,0:T(8,128)(2,1)}, bf16[128,3072]{1,0:T(8,128)(2,1)}, u32[]{:S(2)}, u32[]{:S(2)}) collective-permute-start(bf16[128,3072]{1,0:T(8,128)(2,1)} %fusion.24), channel_id=1, source_target_pairs={{0,8},{8,16},{16,24},{24,28},{28,20},{20,12},{12,4},{4,0},{1,9},{9... | collective-permute-start | bytes 2359304 | tf_op jit(solution)/shard_map/ppermute | solution.py:299
  436.4 21.4 %collective-permute-start.30 = (bf16[128,3072]{1,0:T(8,128)(2,1)}, bf16[128,3072]{1,0:T(8,128)(2,1)}, u32[]{:S(2)}, u32[]{:S(2)}) collective-permute-start(bf16[128,3072]{1,0:T(8,128)(2,1)} %fusion.25), channel_id=1, source_target_pairs={{8,0},{16,8},{24,16},{28,24},{20,28},{12,20},{4,12},{0,4},{9,1},{1... | collective-permute-start | bytes 2359304 | tf_op jit(solution)/shard_map/ppermute | solution.py:300
  459.5 20.1 %collective-permute-start.33 = (bf16[128,3072]{1,0:T(8,128)(2,1)S(1)}, bf16[128,3072]{1,0:T(8,128)(2,1)S(1)}, u32[]{:S(2)}, u32[]{:S(2)}) collective-permute-start(bf16[128,3072]{1,0:T(8,128)(2,1)S(1)} %fusion.26), channel_id=1, source_target_pairs={{0,8},{8,16},{16,24},{24,28},{28,20},{20,12},{12,4},{4,0},{1,9},{9... | collective-permute-start | bytes 2359304 | tf_op jit(solution)/shard_map/ppermute | solution.py:299
  461.2 18.6 %collective-permute-start.34 = (bf16[128,3072]{1,0:T(8,128)(2,1)S(1)}, bf16[128,3072]{1,0:T(8,128)(2,1)S(1)}, u32[]{:S(2)}, u32[]{:S(2)}) collective-permute-start(bf16[128,3072]{1,0:T(8,128)(2,1)S(1)} %fusion.27), channel_id=1, source_target_pairs={{8,0},{16,8},{24,16},{28,24},{20,28},{12,20},{4,12},{0,4},{9,1},{1... | collective-permute-start | bytes 2359304 | tf_op jit(solution)/shard_map/ppermute | solution.py:300
  463.4 16.1 %collective-permute-start.36 = (bf16[128,512]{1,0:T(8,128)(2,1)S(1)}, bf16[128,512]{1,0:T(8,128)(2,1)S(1)}, u32[]{:S(2)}, u32[]{:S(2)}) collective-permute-start(bf16[128,512]{1,0:T(8,128)(2,1)S(1)} %get-tuple-element.336), channel_id=1, source_target_pairs={{8,0},{16,8},{24,16},{28,24},{20,28},{12,20},{4,12},{0,4},{9,1},{1... | collective-permute-start | bytes 393224 | tf_op jit(solution)/shard_map/ppermute | solution.py:300
  465.1 14.6 %collective-permute-start.35 = (bf16[128,512]{1,0:T(8,128)(2,1)S(1)}, bf16[128,512]{1,0:T(8,128)(2,1)S(1)}, u32[]{:S(2)}, u32[]{:S(2)}) collective-permute-start(bf16[128,512]{1,0:T(8,128)(2,1)S(1)} %get-tuple-element.337), channel_id=1, source_target_pairs={{0,8},{8,16},{16,24},{24,28},{28,20},{20,12},{12,4},{4,0},{1,9},{9... | collective-permute-start | bytes 393224 | tf_op jit(solution)/shard_map/ppermute | solution.py:299
  480.2 20.3 %collective-permute-start.37 = (bf16[128,3072]{1,0:T(8,128)(2,1)S(1)}, bf16[128,3072]{1,0:T(8,128)(2,1)S(1)}, u32[]{:S(2)}, u32[]{:S(2)}) collective-permute-start(bf16[128,3072]{1,0:T(8,128)(2,1)S(1)} %fusion.28), channel_id=1, source_target_pairs={{0,8},{8,16},{16,24},{24,28},{28,20},{20,12},{12,4},{4,0},{1,9},{9... | collective-permute-start | bytes 2359304 | tf_op jit(solution)/shard_map/ppermute | solution.py:299
  482.0 18.7 %collective-permute-start.38 = (bf16[128,3072]{1,0:T(8,128)(2,1)S(1)}, bf16[128,3072]{1,0:T(8,128)(2,1)S(1)}, u32[]{:S(2)}, u32[]{:S(2)}) collective-permute-start(bf16[128,3072]{1,0:T(8,128)(2,1)S(1)} %fusion.29), channel_id=1, source_target_pairs={{8,0},{16,8},{24,16},{28,24},{20,28},{12,20},{4,12},{0,4},{9,1},{1... | collective-permute-start | bytes 2359304 | tf_op jit(solution)/shard_map/ppermute | solution.py:300
  484.6 15.8 %collective-permute-start.40 = (bf16[128,512]{1,0:T(8,128)(2,1)S(1)}, bf16[128,512]{1,0:T(8,128)(2,1)S(1)}, u32[]{:S(2)}, u32[]{:S(2)}) collective-permute-start(bf16[128,512]{1,0:T(8,128)(2,1)S(1)} %get-tuple-element.334), channel_id=1, source_target_pairs={{8,0},{16,8},{24,16},{28,24},{20,28},{12,20},{4,12},{0,4},{9,1},{1... | collective-permute-start | bytes 393224 | tf_op jit(solution)/shard_map/ppermute | solution.py:300
  486.1 14.3 %collective-permute-start.39 = (bf16[128,512]{1,0:T(8,128)(2,1)S(1)}, bf16[128,512]{1,0:T(8,128)(2,1)S(1)}, u32[]{:S(2)}, u32[]{:S(2)}) collective-permute-start(bf16[128,512]{1,0:T(8,128)(2,1)S(1)} %get-tuple-element.335), channel_id=1, source_target_pairs={{0,8},{8,16},{16,24},{24,28},{28,20},{20,12},{12,4},{4,0},{1,9},{9... | collective-permute-start | bytes 393224 | tf_op jit(solution)/shard_map/ppermute | solution.py:299
  501.1 20.2 %collective-permute-start.41 = (bf16[128,3072]{1,0:T(8,128)(2,1)S(1)}, bf16[128,3072]{1,0:T(8,128)(2,1)S(1)}, u32[]{:S(2)}, u32[]{:S(2)}) collective-permute-start(bf16[128,3072]{1,0:T(8,128)(2,1)S(1)} %fusion.30), channel_id=1, source_target_pairs={{0,8},{8,16},{16,24},{24,28},{28,20},{20,12},{12,4},{4,0},{1,9},{9... | collective-permute-start | bytes 2359304 | tf_op jit(solution)/shard_map/ppermute | solution.py:299
  502.7 18.7 %collective-permute-start.42 = (bf16[128,3072]{1,0:T(8,128)(2,1)S(1)}, bf16[128,3072]{1,0:T(8,128)(2,1)S(1)}, u32[]{:S(2)}, u32[]{:S(2)}) collective-permute-start(bf16[128,3072]{1,0:T(8,128)(2,1)S(1)} %fusion.31), channel_id=1, source_target_pairs={{8,0},{16,8},{24,16},{28,24},{20,28},{12,20},{4,12},{0,4},{9,1},{1... | collective-permute-start | bytes 2359304 | tf_op jit(solution)/shard_map/ppermute | solution.py:300
  507.7 13.5 %collective-permute-start.44 = (bf16[128,512]{1,0:T(8,128)(2,1)S(1)}, bf16[128,512]{1,0:T(8,128)(2,1)S(1)}, u32[]{:S(2)}, u32[]{:S(2)}) collective-permute-start(bf16[128,512]{1,0:T(8,128)(2,1)S(1)} %get-tuple-element.332), channel_id=1, source_target_pairs={{8,0},{16,8},{24,16},{28,24},{20,28},{12,20},{4,12},{0,4},{9,1},{1... | collective-permute-start | bytes 393224 | tf_op jit(solution)/shard_map/ppermute | solution.py:300
  508.8 12.4 %collective-permute-start.43 = (bf16[128,512]{1,0:T(8,128)(2,1)S(1)}, bf16[128,512]{1,0:T(8,128)(2,1)S(1)}, u32[]{:S(2)}, u32[]{:S(2)}) collective-permute-start(bf16[128,512]{1,0:T(8,128)(2,1)S(1)} %get-tuple-element.333), channel_id=1, source_target_pairs={{0,8},{8,16},{16,24},{24,28},{28,20},{20,12},{12,4},{4,0},{1,9},{9... | collective-permute-start | bytes 393224 | tf_op jit(solution)/shard_map/ppermute | solution.py:299
  523.2 10.1 %collective-permute-start.47 = (bf16[128,512]{1,0:T(8,128)(2,1)S(1)}, bf16[128,512]{1,0:T(8,128)(2,1)S(1)}, u32[]{:S(2)}, u32[]{:S(2)}) collective-permute-start(bf16[128,512]{1,0:T(8,128)(2,1)S(1)} %get-tuple-element.331), channel_id=1, source_target_pairs={{0,8},{8,16},{16,24},{24,28},{28,20},{20,12},{12,4},{4,0},{1,9},{9... | collective-permute-start | bytes 393224 | tf_op jit(solution)/shard_map/ppermute | solution.py:299
  525.1 12.0 %collective-permute-start.45 = (bf16[128,3072]{1,0:T(8,128)(2,1)S(1)}, bf16[128,3072]{1,0:T(8,128)(2,1)S(1)}, u32[]{:S(2)}, u32[]{:S(2)}) collective-permute-start(bf16[128,3072]{1,0:T(8,128)(2,1)S(1)} %fusion.32), channel_id=1, source_target_pairs={{0,8},{8,16},{16,24},{24,28},{28,20},{20,12},{12,4},{4,0},{1,9},{9... | collective-permute-start | bytes 2359304 | tf_op jit(solution)/shard_map/ppermute | solution.py:299
  526.7 12.2 %collective-permute-start.46 = (bf16[128,3072]{1,0:T(8,128)(2,1)S(1)}, bf16[128,3072]{1,0:T(8,128)(2,1)S(1)}, u32[]{:S(2)}, u32[]{:S(2)}) collective-permute-start(bf16[128,3072]{1,0:T(8,128)(2,1)S(1)} %fusion.33), channel_id=1, source_target_pairs={{8,0},{16,8},{24,16},{28,24},{20,28},{12,20},{4,12},{0,4},{9,1},{1... | collective-permute-start | bytes 2359304 | tf_op jit(solution)/shard_map/ppermute | solution.py:300
  559.4 72.9 %collective-permute-start.71 = (bf16[128,512]{1,0:T(8,128)(2,1)S(1)}, bf16[128,512]{1,0:T(8,128)(2,1)S(1)}, u32[]{:S(2)}, u32[]{:S(2)}) collective-permute-start(bf16[128,512]{1,0:T(8,128)(2,1)S(1)} %get-tuple-element.310), channel_id=1, source_target_pairs={{0,8},{8,16},{16,24},{24,28},{28,20},{20,12},{12,4},{4,0},{1,9},{9... | collective-permute-start | bytes 393224 | tf_op jit(solution)/shard_map/ppermute | solution.py:299
  560.9 71.4 %collective-permute-start.72 = (bf16[128,512]{1,0:T(8,128)(2,1)S(1)}, bf16[128,512]{1,0:T(8,128)(2,1)S(1)}, u32[]{:S(2)}, u32[]{:S(2)}) collective-permute-start(bf16[128,512]{1,0:T(8,128)(2,1)S(1)} %get-tuple-element.311), channel_id=1, source_target_pairs={{8,0},{16,8},{24,16},{28,24},{20,28},{12,20},{4,12},{0,4},{9,1},{1... | collective-permute-start | bytes 393224 | tf_op jit(solution)/shard_map/ppermute | solution.py:300
  574.5 46.0 %collective-permute-start.50 = (bf16[512,2048]{1,0:T(8,128)(2,1)S(1)}, bf16[512,2048]{1,0:T(8,128)(2,1)S(1)}, u32[]{:S(2)}, u32[]{:S(2)}) collective-permute-start(bf16[512,2048]{1,0:T(8,128)(2,1)S(1)} %add_convert_fusion.4), channel_id=1, source_target_pairs={{0,2},{1,3},{2,0},{3,1},{4,6},{5,7},{6,4},{7,5},{8,10},{9,11},{10,... | collective-permute-start | bytes 6291464 | tf_op jit(solution)/shard_map/ppermute | solution.py:231
  590.1 32.6 %collective-permute-start.67 = (bf16[128,1024]{0,1:T(8,128)(2,1)S(1)}, bf16[128,1024]{0,1:T(8,128)(2,1)S(1)}, u32[]{:S(2)}, u32[]{:S(2)}) collective-permute-start(bf16[128,1024]{0,1:T(8,128)(2,1)S(1)} %fusion.70), channel_id=1, source_target_pairs={{8,0},{16,8},{24,16},{28,24},{20,28},{12,20},{4,12},{0,4},{9,1},{1... | collective-permute-start | bytes 786440 | tf_op jit(solution)/shard_map/ppermute | solution.py:300
  595.1 29.6 %collective-permute-start.61 = (bf16[128,1024]{0,1:T(8,128)(2,1)S(1)}, bf16[128,1024]{0,1:T(8,128)(2,1)S(1)}, u32[]{:S(2)}, u32[]{:S(2)}) collective-permute-start(bf16[128,1024]{0,1:T(8,128)(2,1)S(1)} %fusion.65), channel_id=1, source_target_pairs={{0,8},{8,16},{16,24},{24,28},{28,20},{20,12},{12,4},{4,0},{1,9},{9... | collective-permute-start | bytes 786440 | tf_op jit(solution)/shard_map/ppermute | solution.py:299
  622.7 26.3 %collective-permute-start.51 = (bf16[512,2048]{1,0:T(8,128)(2,1)}, bf16[512,2048]{1,0:T(8,128)(2,1)}, u32[]{:S(2)}, u32[]{:S(2)}) collective-permute-start(bf16[512,2048]{1,0:T(8,128)(2,1)} %add_convert_fusion.3), channel_id=1, source_target_pairs={{0,1},{1,0},{2,3},{3,2},{4,5},{5,4},{6,7},{7,6},{8,9},{9,8},{10,11... | collective-permute-start | bytes 6291464 | tf_op jit(solution)/shard_map/ppermute | solution.py:240
  (144 other events, 929.7 us)

commit v11 on v10

--- a/solution.py
+++ b/solution.py
@@ -332,7 +332,6 @@
         share = count // lax.axis_size("tensor")
         offset = lax.axis_index("tensor") * share
         stream = tokens.astype(jnp.float32)
-        stream_rows = lax.dynamic_slice_in_dim(stream, offset, share, 0)
         normed_in = rms_scale(stream, attn_gain).astype(jnp.bfloat16)
         q_raw = matmul(normed_in, w_query)
         k_raw = matmul(normed_in, key_matrix)
@@ -427,6 +426,10 @@
         ).astype(jnp.bfloat16)
         in_part, q_grad, k_grad, v_grad = lax.optimization_barrier(
             (in_part, q_grad, k_grad, v_grad)
+        )
+        attn_gain_part = gain_term(stream, in_part.astype(jnp.float32))
+        gains = plan.all_sum(
+            jnp.concatenate([attn_gain_part, mlp_gain_part, qg_part, kg_part])
         )
         in_sum = plan.tp_sum(in_part)
         query_w_grad = inner_rows(normed_in, q_grad)
@@ -444,8 +447,6 @@
         (out_sum,) = small.result()
         query_sum, key_sum, value_sum = plan.dp_rs([query_w_grad, key_w_grad, value_w_grad])
         input_grad = resid_grad + norm_back(stream, attn_gain, in_grad)
-        attn_gain_part = gain_term(stream_rows, lax.dynamic_slice_in_dim(in_grad, offset, share, 0))
-        gains = plan.all_sum(jnp.concatenate([attn_gain_part, mlp_gain_part, qg_part, kg_part]))
         width = attn_gain_part.shape[0]
         head = qg_part.shape[0]
         attn_gain_grad = gains[:width]

time: 690 us -> 696 us (level)
  other arithmetic: 155 us -> 141 us
  waiting for transfers between devices: 208 us -> 219 us
  local copies, waits for them, and re-layouts: 87.6 us -> 95.6 us
    convert_element_type x3 -> x0, other arithmetic: 13.2 us -> none  [the longest x1 6.56 us: body(): stream = tokens.astype(jnp.float32)]
    ppermute x28, waiting for transfers between devices: 24.3 us -> 33.9 us  [step(): got_a = lax.ppermute(send_a.astype(jnp.bfloat16), 'dp', self.plan.cw)]
    unnamed x245 -> x241, local copies, waits for them, and re-layouts: 31.8 us -> 39.1 us
  transfers between devices with their start and end apart: 73 -> 73, of which waited for: 30 -> 28; matrix products, arithmetic and copies ran while one was open for 27% -> 27% of each run, Pallas kernels for 0% -> 0%
where the time goes in v11:
time: 696 us; the launch traced here: 687 us
  waiting for transfers between devices  219 us (31%)
  other arithmetic  141 us (20%)
  matrix products  132 us (19%)
  local copies, waits for them, and re-layouts  95.6 us (14%)
  starting transfers between devices  75.7 us (11%)
  between operations  23.6 us (3%)
    ppermute x4, waiting for transfers between devices, tp_mid(): st['other'] = lax.ppermute(st['chip_sum'], 'tensor', self.chip_pairs)  100 us
    ppermute x28, waiting for transfers between devices, step(): got_b = lax.ppermute(send_b.astype(jnp.bfloat16), 'dp', self.plan.ccw)  76 us
    dot_general x7, matrix products, outer_cols(): lax.dot_general(left, right, (((1,), (1,)), ((), ())), preferred_element_...  48.1 us
    dot_general x7, matrix products, matmul(): return jnp.dot(left, right, preferred_element_type=jnp.float32)  42.7 us
    unnamed x241, local copies, waits for them, and re-layouts  39.1 us
    dot_general x7, matrix products, inner_rows(): lax.dot_general(left, right, (((0,), (0,)), ((), ())), preferred_element_...  38.1 us
    ppermute x28, waiting for transfers between devices, step(): got_a = lax.ppermute(send_a.astype(jnp.bfloat16), 'dp', self.plan.cw)  33.9 us
    ppermute x28, starting transfers between devices, step(): got_a = lax.ppermute(send_a.astype(jnp.bfloat16), 'dp', self.plan.cw)  33.2 us
  transfers between devices with their start and end apart: 73, of which 28 were waited for; matrix products, arithmetic and copies ran while one was open for 27% of the time, Pallas kernels for 0%

profile of v11, /device:TPU:0, one launch (start us, length us, event | category | flops | bytes accessed | tf_op | source)
XLA Modules:
  0.0 687.3 jit_solution(3955149795930354038)
XLA Ops:
  0.7 3.2 fusion.1
  16.0 6.9 fusion.95
  25.7 3.5 reshape.547
  32.1 3.5 copy.263
  36.9 4.5 convolution_convert_fusion.3
  46.6 4.3 copy.219
  67.2 3.5 collective-permute-done
  76.6 10.5 %fusion.96 = f32[1024,1536]{1,0:T(8,128)} fusion(bf16[1024,2048]{1,0:T(8,128)(2,1)S(1)} %copy-done.41, bf16[1536,2048]{1,0:T(8,128)(2,1)} %param.36), kind=kOutput, calls=%fused_computation.343 | convolution fusion | flops 6442450944 | bytes 16777216 | tf_op jit(solution)/shard_map/dot_general | solution.py:33
  87.1 35.4 %collective-permute-done.1 = bf16[512,2048]{1,0:T(8,128)(2,1)S(1)} collective-permute-done((bf16[512,2048]{1,0:T(8,128)(2,1)S(1)}, bf16[512,2048]{1,0:T(8,128)(2,1)S(1)}, u32[]{:S(2)}, u32[]{:S(2)}) %collective-permute-start.1) | collective-permute-done | bytes 2097184 | tf_op jit(solution)/shard_map/ppermute | solution.py:231
  143.1 7.8 %convert_add_fusion = (f32[1024,2048]{1,0:T(8,128)}, bf16[1024,2048]{1,0:T(8,128)(2,1)S(1)}) fusion(bf16[1024,2048]{1,0:T(8,128)(2,1)S(1)} %copy-done.2, bf16[512,2048]{1,0:T(8,128)(2,1)S(1)} %get-tuple-element.349, bf16[512,2048]{1,0:T(8,128)(2,1)S(1)} %get-tuple-element.348, f32[2048]{0:T(1024)S(1)} %copy-done.99, f32[1024]{0:T(1024)S(1)} %get-tuple-element.401), kind=kLoop, calls=%fused_computation.4 | loop fusion | flops 18874368 | bytes 20983808 | tf_op jit(solution)/shard_map/add | solution.py:351
  150.9 10.3 %fusion.97 = f32[1024,1536]{1,0:T(8,128)S(1)} fusion(bf16[1024,2048]{1,0:T(8,128)(2,1)S(1)} %get-tuple-element.307, bf16[2048,1536]{1,0:T(8,128)(2,1)} %param.34), kind=kOutput, calls=%fused_computation.344 | convolution fusion | flops 6442450944 | bytes 16777216 | tf_op jit(solution)/shard_map/dot_general | solution.py:23
  161.3 9.0 %multiply_convert_fusion.2 = (bf16[1024,1536]{1,0:T(8,128)(2,1)S(1)}, f32[1024,1536]{1,0:T(8,128)}) fusion(f32[1024,1536]{1,0:T(8,128)S(1)} %fusion.97, bf16[1024,2048]{1,0:T(8,128)(2,1)S(1)} %get-tuple-element.307, bf16[2048,1536]{1,0:T(8,128)(2,1)S(1)} %bitcast.226), kind=kOutput, calls=%fused_computation.29 | convolution fusion | flops 6451888128 | bytes 26214400 | tf_op jit(solution)/shard_map/dot_general | solution.py:23
  170.3 7.3 %convolution_convert_fusion = bf16[1024,2048]{1,0:T(8,128)(2,1)S(1)} fusion(bf16[1024,1536]{1,0:T(8,128)(2,1)S(1)} %get-tuple-element.420, bf16[1536,2048]{1,0:T(8,128)(2,1)S(1)} %bitcast.224), kind=kOutput, calls=%fused_computation.42 | convolution fusion | flops 6444548096 | bytes 13631488 | tf_op jit(solution)/shard_map/dot_general | solution.py:23
  182.1 6.8 fusion.98
  188.9 4.6 copy-done.24
  197.1 8.3 %collective-permute-done.5 = bf16[128,1536]{0,1:T(8,128)(2,1)S(1)} collective-permute-done((bf16[128,1536]{0,1:T(8,128)(2,1)S(1)}, bf16[128,1536]{0,1:T(8,128)(2,1)S(1)}, u32[]{:S(2)}, u32[]{:S(2)}) %collective-permute-start.5) | collective-permute-done | bytes 393248 | tf_op jit(solution)/shard_map/ppermute | solution.py:300
  221.1 3.2 add_convert_fusion.8
  229.4 6.7 multiply_convert_fusion.1
  240.9 10.9 %fusion.99 = f32[1024,2048]{1,0:T(8,128)} fusion(bf16[1024,1536]{1,0:T(8,128)(2,1)S(1)} %get-tuple-element.101, bf16[2048,1536]{1,0:T(8,128)(2,1)} %param.35), kind=kOutput, calls=%fused_computation.346 | convolution fusion | flops 6442450944 | bytes 17825792 | tf_op jit(solution)/shard_map/dot_general | solution.py:33
  251.8 10.9 %add_convert_fusion.2 = bf16[1024,2048]{1,0:T(8,128)(2,1)S(1)} fusion(f32[1024,2048]{1,0:T(8,128)} %fusion.99, bf16[1024,1536]{1,0:T(8,128)(2,1)S(1)} %get-tuple-element.98, bf16[2048,1536]{1,0:T(8,128)(2,1)} %param.34), kind=kOutput, calls=%fused_computation.22 | convolution fusion | flops 6446645248 | bytes 22020096 | tf_op jit(solution)/shard_map/dot_general | solution.py:33
  262.9 10.3 %collective-permute-done.12 = bf16[512,2048]{1,0:T(8,128)(2,1)S(1)} collective-permute-done((bf16[512,2048]{1,0:T(8,128)(2,1)S(1)}, bf16[512,2048]{1,0:T(8,128)(2,1)S(1)}, u32[]{:S(2)}, u32[]{:S(2)}) %collective-permute-start.12) | collective-permute-done | bytes 2097184 | tf_op jit(solution)/shard_map/ppermute | solution.py:231
  279.9 9.5 %fusion.100 = f32[2048,1536]{1,0:T(8,128)} fusion(bf16[1024,2048]{1,0:T(8,128)(2,1)S(1)} %copy-done.40, bf16[1024,1536]{1,0:T(8,128)(2,1)S(1)} %copy-done.70), kind=kOutput, calls=%fused_computation.347 | convolution fusion | flops 6442450944 | bytes 19922944 | tf_op jit(solution)/shard_map/dot_general | solution.py:27
  289.4 9.5 %fusion.101 = f32[2048,1536]{1,0:T(8,128)} fusion(bf16[1024,2048]{1,0:T(8,128)(2,1)S(1)} %copy-done.40, bf16[1024,1536]{1,0:T(8,128)(2,1)S(1)} %get-tuple-element.101), kind=kOutput, calls=%fused_computation.348 | convolution fusion | flops 6442450944 | bytes 19922944 | tf_op jit(solution)/shard_map/dot_general | solution.py:27
  302.7 7.7 %constant_dynamic-slice_fusion.70 = (f32[128,1536]{1,0:T(8,128)}, f32[128,1536]{1,0:T(8,128)}, f32[128,1536]{1,0:T(8,128)}, f32[128,1536]{1,0:T(8,128)}, f32[128...) fusion(f32[2048,1536]{1,0:T(8,128)} %fusion.100, ...), kind=kLoop, calls=%fused_computation.309 | loop fusion | bytes 22020152 | tf_op jit(solution)/shard_map/dynamic_slice | solution.py:288
  325.9 7.8 %constant_dynamic-slice_fusion.71 = (f32[128,1536]{1,0:T(8,128)}, f32[128,1536]{1,0:T(8,128)}, f32[128,1536]{1,0:T(8,128)}, f32[128,1536]{1,0:T(8,128)}, f32[128...) fusion(f32[2048,1536]{1,0:T(8,128)} %fusion.101, ...), kind=kLoop, calls=%fused_computation.310 | loop fusion | bytes 22020152 | tf_op jit(solution)/shard_map/dynamic_slice | solution.py:288
  333.8 26.2 %collective-permute-done.25 = bf16[512,2048]{1,0:T(8,128)(2,1)S(1)} collective-permute-done((bf16[512,2048]{1,0:T(8,128)(2,1)S(1)}, bf16[512,2048]{1,0:T(8,128)(2,1)S(1)}, u32[]{:S(2)}, u32[]{:S(2)}) %collective-permute-start.25) | collective-permute-done | bytes 2097184 | tf_op jit(solution)/shard_map/ppermute | solution.py:231
  363.7 14.3 %collective-permute-done.22 = bf16[128,3072]{1,0:T(8,128)(2,1)S(1)} collective-permute-done((bf16[128,3072]{1,0:T(8,128)(2,1)S(1)}, bf16[128,3072]{1,0:T(8,128)(2,1)S(1)}, u32[]{:S(2)}, u32[]{:S(2)}) %collective-permute-start.22) | collective-permute-done | bytes 786464 | tf_op jit(solution)/shard_map/ppermute | solution.py:300
  384.4 3.9 broadcast_select_fusion.5
  388.3 6.9 %collective-permute-done.21 = bf16[128,3072]{1,0:T(8,128)(2,1)S(1)} collective-permute-done((bf16[128,3072]{1,0:T(8,128)(2,1)S(1)}, bf16[128,3072]{1,0:T(8,128)(2,1)S(1)}, u32[]{:S(2)}, u32[]{:S(2)}) %collective-permute-start.21) | collective-permute-done | bytes 786464 | tf_op jit(solution)/shard_map/ppermute | solution.py:299
  397.0 3.4 copy-done.3
  403.9 14.5 %subtract_add_fusion = (f32[1024,2048]{1,0:T(8,128)}, bf16[1024,2048]{1,0:T(8,128)(2,1)}) fusion(bf16[1024,2048]{1,0:T(8,128)(2,1)} %param.37, f32[1024]{0:T(1024)S(1)} %broadcast_multiply_fusion.3, f32[1024]{0:T(1024)S(1)} %copy-done.103, f32[2048]{0:T(1024)S(1)} %copy-done.99, f32[1024]{0:T(1024)S(1)} %get-tuple-element.401, ...), kind=kLoop, calls=%fused_computation.19 | loop fusion | flops 48234496 | bytes 33574912 | tf_op jit(solution)/shard_map/add | solution.py:389
  418.3 6.2 fusion.19
  428.1 3.4 fusion.36
  444.0 10.6 %collective-permute-done.32 = bf16[128,512]{1,0:T(8,128)(2,1)} collective-permute-done((bf16[128,512]{1,0:T(8,128)(2,1)}, bf16[128,512]{1,0:T(8,128)(2,1)}, u32[]{:S(2)}, u32[]{:S(2)}) %collective-permute-start.32) | collective-permute-done | bytes 131104 | tf_op jit(solution)/shard_map/ppermute | solution.py:300
  465.1 14.0 %collective-permute-done.36 = bf16[128,512]{1,0:T(8,128)(2,1)S(1)} collective-permute-done((bf16[128,512]{1,0:T(8,128)(2,1)S(1)}, bf16[128,512]{1,0:T(8,128)(2,1)S(1)}, u32[]{:S(2)}, u32[]{:S(2)}) %collective-permute-start.36) | collective-permute-done | bytes 131104 | tf_op jit(solution)/shard_map/ppermute | solution.py:300
  486.7 13.1 %collective-permute-done.40 = bf16[128,512]{1,0:T(8,128)(2,1)S(1)} collective-permute-done((bf16[128,512]{1,0:T(8,128)(2,1)S(1)}, bf16[128,512]{1,0:T(8,128)(2,1)S(1)}, u32[]{:S(2)}, u32[]{:S(2)}) %collective-permute-start.40) | collective-permute-done | bytes 131104 | tf_op jit(solution)/shard_map/ppermute | solution.py:300
  509.4 12.0 %collective-permute-done.44 = bf16[128,512]{1,0:T(8,128)(2,1)S(1)} collective-permute-done((bf16[128,512]{1,0:T(8,128)(2,1)S(1)}, bf16[128,512]{1,0:T(8,128)(2,1)S(1)}, u32[]{:S(2)}, u32[]{:S(2)}) %collective-permute-start.44) | collective-permute-done | bytes 131104 | tf_op jit(solution)/shard_map/ppermute | solution.py:300
  531.8 4.4 collective-permute-done.45
  539.8 5.8 fusion.87
  551.2 5.4 add_convert_fusion
  556.7 3.5 copy-done.38
  579.7 4.4 collective-permute-done.58
  588.3 3.3 collective-permute-done.59
  593.8 28.3 %collective-permute-done.50 = bf16[512,2048]{1,0:T(8,128)(2,1)S(1)} collective-permute-done((bf16[512,2048]{1,0:T(8,128)(2,1)S(1)}, bf16[512,2048]{1,0:T(8,128)(2,1)S(1)}, u32[]{:S(2)}, u32[]{:S(2)}) %collective-permute-start.50) | collective-permute-done | bytes 2097184 | tf_op jit(solution)/shard_map/ppermute | solution.py:231
  627.8 5.3 collective-permute-done.61
  636.4 4.6 collective-permute-done.62
  656.4 5.6 fusion.9
  676.1 9.7 %fusion.6 = f32[1024,2048]{1,0:T(8,128)} fusion(f32[1024,2048]{1,0:T(8,128)} %get-tuple-element.107, bf16[1024,2048]{1,0:T(8,128)(2,1)} %param.25, f32[1024]{0:T(1024)S(1)} %broadcast_multiply_fusion.2, f32[1024]{0:T(1024)S(1)} %copy-done.102, f32[2048]{0:T(1024)S(1)} %copy-done.98, f32[1024]{0:T(1024)S(1)} %copy-done.101, bf16[512,2048]{1,0:T(8,128)(2,1)} %copy-done.23, ...), kind=kLoop, calls=%fused_computation.13 | loop fusion | flops 23068672 | bytes 25186304 | tf_op jit(solution)/shard_map/add | solution.py:449
  (560 shorter events, 248.9 us)
Async XLA Ops:
  73.7 48.8 %collective-permute-start.1 = (bf16[512,2048]{1,0:T(8,128)(2,1)S(1)}, bf16[512,2048]{1,0:T(8,128)(2,1)S(1)}, u32[]{:S(2)}, u32[]{:S(2)}) collective-permute-start(bf16[512,2048]{1,0:T(8,128)(2,1)S(1)} %add_convert_fusion.10), channel_id=1, source_target_pairs={{0,2},{1,3},{2,0},{3,1},{4,6},{5,7},{6,4},{7,5},{8,10},{9,11},{10,... | collective-permute-start | bytes 6291464 | tf_op jit(solution)/shard_map/ppermute | solution.py:231
  124.7 12.6 %collective-permute-start.2 = (bf16[512,2048]{1,0:T(8,128)(2,1)}, bf16[512,2048]{1,0:T(8,128)(2,1)}, u32[]{:S(2)}, u32[]{:S(2)}) collective-permute-start(bf16[512,2048]{1,0:T(8,128)(2,1)} %add_convert_fusion.9), channel_id=1, source_target_pairs={{0,1},{1,0},{2,3},{3,2},{4,5},{5,4},{6,7},{7,6},{8,9},{9,8},{10,11... | collective-permute-start | bytes 6291464 | tf_op jit(solution)/shard_map/ppermute | solution.py:240
  180.8 40.3 %collective-permute-start.7 = (bf16[512,2048]{1,0:T(8,128)(2,1)}, bf16[512,2048]{1,0:T(8,128)(2,1)}, u32[]{:S(2)}, u32[]{:S(2)}) collective-permute-start(bf16[512,2048]{1,0:T(8,128)(2,1)} %constant_dynamic-slice_fusion.72), channel_id=1, source_target_pairs={{0,1},{1,0},{2,3},{3,2},{4,5},{5,4},{6,7},{7,6},{8,9},{9,8},{10,11... | collective-permute-start | bytes 6291464 | tf_op jit(solution)/shard_map/ppermute | solution.py:222
  193.7 11.7 %collective-permute-start.5 = (bf16[128,1536]{0,1:T(8,128)(2,1)S(1)}, bf16[128,1536]{0,1:T(8,128)(2,1)S(1)}, u32[]{:S(2)}, u32[]{:S(2)}) collective-permute-start(bf16[128,1536]{0,1:T(8,128)(2,1)S(1)} %get-tuple-element.304), channel_id=1, source_target_pairs={{8,0},{16,8},{24,16},{28,24},{20,28},{12,20},{4,12},{0,4},{9,1},{1... | collective-permute-start | bytes 1179656 | tf_op jit(solution)/shard_map/ppermute | solution.py:300
  195.5 11.4 %collective-permute-start.3 = (bf16[128,1536]{0,1:T(8,128)(2,1)S(1)}, bf16[128,1536]{0,1:T(8,128)(2,1)}, u32[]{:S(2)}, u32[]{:S(2)}) collective-permute-start(bf16[128,1536]{0,1:T(8,128)(2,1)S(1)} %get-tuple-element.305), channel_id=1, source_target_pairs={{0,8},{8,16},{16,24},{24,28},{28,20},{20,12},{12,4},{4,0},{1,9},{9... | collective-permute-start | bytes 1179656 | tf_op jit(solution)/shard_map/ppermute | solution.py:299
  227.9 45.2 %collective-permute-start.12 = (bf16[512,2048]{1,0:T(8,128)(2,1)S(1)}, bf16[512,2048]{1,0:T(8,128)(2,1)S(1)}, u32[]{:S(2)}, u32[]{:S(2)}) collective-permute-start(bf16[512,2048]{1,0:T(8,128)(2,1)S(1)} %add_convert_fusion.8), channel_id=1, source_target_pairs={{0,2},{1,3},{2,0},{3,1},{4,6},{5,7},{6,4},{7,5},{8,10},{9,11},{10,... | collective-permute-start | bytes 6291464 | tf_op jit(solution)/shard_map/ppermute | solution.py:231
  238.9 23.9 %collective-permute-start.11 = (bf16[128,1536]{0,1:T(8,128)(2,1)S(1)}, bf16[128,1536]{0,1:T(8,128)(2,1)S(1)}, u32[]{:S(2)}, u32[]{:S(2)}) collective-permute-start(bf16[128,1536]{0,1:T(8,128)(2,1)S(1)} %get-tuple-element.296), channel_id=1, source_target_pairs={{8,0},{16,8},{24,16},{28,24},{20,28},{12,20},{4,12},{0,4},{9,1},{1... | collective-permute-start | bytes 1179656 | tf_op jit(solution)/shard_map/ppermute | solution.py:300
  240.5 22.3 %collective-permute-start.10 = (bf16[128,1536]{0,1:T(8,128)(2,1)S(1)}, bf16[128,1536]{0,1:T(8,128)(2,1)S(1)}, u32[]{:S(2)}, u32[]{:S(2)}) collective-permute-start(bf16[128,1536]{0,1:T(8,128)(2,1)S(1)} %get-tuple-element.297), channel_id=1, source_target_pairs={{0,8},{8,16},{16,24},{24,28},{28,20},{20,12},{12,4},{4,0},{1,9},{9... | collective-permute-start | bytes 1179656 | tf_op jit(solution)/shard_map/ppermute | solution.py:299
  275.7 23.2 %collective-permute-start.15 = (bf16[128,1536]{0,1:T(8,128)(2,1)S(1)}, bf16[128,1536]{0,1:T(8,128)(2,1)S(1)}, u32[]{:S(2)}, u32[]{:S(2)}) collective-permute-start(bf16[128,1536]{0,1:T(8,128)(2,1)S(1)} %get-tuple-element.294), channel_id=1, source_target_pairs={{8,0},{16,8},{24,16},{28,24},{20,28},{12,20},{4,12},{0,4},{9,1},{1... | collective-permute-start | bytes 1179656 | tf_op jit(solution)/shard_map/ppermute | solution.py:300
  277.3 21.6 %collective-permute-start.14 = (bf16[128,1536]{0,1:T(8,128)(2,1)S(1)}, bf16[128,1536]{0,1:T(8,128)(2,1)S(1)}, u32[]{:S(2)}, u32[]{:S(2)}) collective-permute-start(bf16[128,1536]{0,1:T(8,128)(2,1)S(1)} %get-tuple-element.295), channel_id=1, source_target_pairs={{0,8},{8,16},{16,24},{24,28},{28,20},{20,12},{12,4},{4,0},{1,9},{9... | collective-permute-start | bytes 1179656 | tf_op jit(solution)/shard_map/ppermute | solution.py:299
  279.4 31.1 %collective-permute-start.24 = (bf16[512,2048]{1,0:T(8,128)(2,1)}, bf16[512,2048]{1,0:T(8,128)(2,1)}, u32[]{:S(2)}, u32[]{:S(2)}) collective-permute-start(bf16[512,2048]{1,0:T(8,128)(2,1)} %constant_dynamic-slice_fusion.51), channel_id=1, source_target_pairs={{0,1},{1,0},{2,3},{3,2},{4,5},{5,4},{6,7},{7,6},{8,9},{9,8},{10,11... | collective-permute-start | bytes 6291464 | tf_op jit(solution)/shard_map/ppermute | solution.py:222
  279.4 105.0 %collective-permute-start.13 = (bf16[512,2048]{1,0:T(8,128)(2,1)S(1)}, bf16[512,2048]{1,0:T(8,128)(2,1)}, u32[]{:S(2)}, u32[]{:S(2)}) collective-permute-start(bf16[512,2048]{1,0:T(8,128)(2,1)S(1)} %add_convert_fusion.7), channel_id=1, source_target_pairs={{0,1},{1,0},{2,3},{3,2},{4,5},{5,4},{6,7},{7,6},{8,9},{9,8},{10,11... | collective-permute-start | bytes 6291464 | tf_op jit(solution)/shard_map/ppermute | solution.py:240
  300.6 15.3 %collective-permute-start.17 = (bf16[128,1536]{0,1:T(8,128)(2,1)S(1)}, bf16[128,1536]{0,1:T(8,128)(2,1)}, u32[]{:S(2)}, u32[]{:S(2)}) collective-permute-start(bf16[128,1536]{0,1:T(8,128)(2,1)S(1)} %get-tuple-element.292), channel_id=1, source_target_pairs={{8,0},{16,8},{24,16},{28,24},{20,28},{12,20},{4,12},{0,4},{9,1},{1... | collective-permute-start | bytes 1179656 | tf_op jit(solution)/shard_map/ppermute | solution.py:300
  302.2 14.8 %collective-permute-start.16 = (bf16[128,1536]{0,1:T(8,128)(2,1)S(1)}, bf16[128,1536]{0,1:T(8,128)(2,1)}, u32[]{:S(2)}, u32[]{:S(2)}) collective-permute-start(bf16[128,1536]{0,1:T(8,128)(2,1)S(1)} %get-tuple-element.293), channel_id=1, source_target_pairs={{0,8},{8,16},{16,24},{24,28},{28,20},{20,12},{12,4},{4,0},{1,9},{9... | collective-permute-start | bytes 1179656 | tf_op jit(solution)/shard_map/ppermute | solution.py:299
  312.9 47.1 %collective-permute-start.25 = (bf16[512,2048]{1,0:T(8,128)(2,1)S(1)}, bf16[512,2048]{1,0:T(8,128)(2,1)S(1)}, u32[]{:S(2)}, u32[]{:S(2)}) collective-permute-start(bf16[512,2048]{1,0:T(8,128)(2,1)S(1)} %add_convert_fusion.6), channel_id=1, source_target_pairs={{0,2},{1,3},{2,0},{3,1},{4,6},{5,7},{6,4},{7,5},{8,10},{9,11},{10,... | collective-permute-start | bytes 6291464 | tf_op jit(solution)/shard_map/ppermute | solution.py:231
  320.4 58.9 %collective-permute-start.19 = (bf16[128,1536]{0,1:T(8,128)(2,1)}, bf16[128,1536]{0,1:T(8,128)(2,1)}, u32[]{:S(2)}, u32[]{:S(2)}) collective-permute-start(bf16[128,1536]{0,1:T(8,128)(2,1)} %get-tuple-element.290), channel_id=1, source_target_pairs={{8,0},{16,8},{24,16},{28,24},{20,28},{12,20},{4,12},{0,4},{9,1},{1... | collective-permute-start | bytes 1179656 | tf_op jit(solution)/shard_map/ppermute | solution.py:300
  322.0 60.5 %collective-permute-start.18 = (bf16[128,1536]{0,1:T(8,128)(2,1)S(1)}, bf16[128,1536]{0,1:T(8,128)(2,1)}, u32[]{:S(2)}, u32[]{:S(2)}) collective-permute-start(bf16[128,1536]{0,1:T(8,128)(2,1)S(1)} %get-tuple-element.291), channel_id=1, source_target_pairs={{0,8},{8,16},{16,24},{24,28},{28,20},{20,12},{12,4},{4,0},{1,9},{9... | collective-permute-start | bytes 1179656 | tf_op jit(solution)/shard_map/ppermute | solution.py:299
  324.8 37.6 %collective-permute-start.20 = (bf16[128,3072]{1,0:T(8,128)(2,1)}, bf16[128,3072]{1,0:T(8,128)(2,1)}, u32[]{:S(2)}, u32[]{:S(2)}) collective-permute-start(bf16[128,3072]{1,0:T(8,128)(2,1)} %pad_maximum_fusion.2), channel_id=1, source_target_pairs={{0,8},{8,16},{16,24},{24,28},{28,20},{20,12},{12,4},{4,0},{1,9},{9... | collective-permute-start | bytes 2359304 | tf_op jit(solution)/shard_map/ppermute | solution.py:299
  360.0 18.1 %collective-permute-start.22 = (bf16[128,3072]{1,0:T(8,128)(2,1)S(1)}, bf16[128,3072]{1,0:T(8,128)(2,1)S(1)}, u32[]{:S(2)}, u32[]{:S(2)}) collective-permute-start(bf16[128,3072]{1,0:T(8,128)(2,1)S(1)} %pad_maximum_fusion.3), channel_id=1, source_target_pairs={{8,0},{16,8},{24,16},{28,24},{20,28},{12,20},{4,12},{0,4},{9,1},{1... | collective-permute-start | bytes 2359304 | tf_op jit(solution)/shard_map/ppermute | solution.py:300
  362.4 34.4 %collective-permute-start.26 = (bf16[512,2048]{1,0:T(8,128)(2,1)S(1)}, bf16[512,2048]{1,0:T(8,128)(2,1)S(1)}, u32[]{:S(2)}, u32[]{:S(2)}) collective-permute-start(bf16[512,2048]{1,0:T(8,128)(2,1)S(1)} %add_convert_fusion.5), channel_id=1, source_target_pairs={{0,1},{1,0},{2,3},{3,2},{4,5},{5,4},{6,7},{7,6},{8,9},{9,8},{10,11... | collective-permute-start | bytes 6291464 | tf_op jit(solution)/shard_map/ppermute | solution.py:240
  378.0 17.2 %collective-permute-start.21 = (bf16[128,3072]{1,0:T(8,128)(2,1)S(1)}, bf16[128,3072]{1,0:T(8,128)(2,1)S(1)}, u32[]{:S(2)}, u32[]{:S(2)}) collective-permute-start(bf16[128,3072]{1,0:T(8,128)(2,1)S(1)} %fusion.24), channel_id=1, source_target_pairs={{0,8},{8,16},{16,24},{24,28},{28,20},{20,12},{12,4},{4,0},{1,9},{9... | collective-permute-start | bytes 2359304 | tf_op jit(solution)/shard_map/ppermute | solution.py:299
  379.3 17.3 %collective-permute-start.23 = (bf16[128,3072]{1,0:T(8,128)(2,1)S(1)}, bf16[128,3072]{1,0:T(8,128)(2,1)S(1)}, u32[]{:S(2)}, u32[]{:S(2)}) collective-permute-start(bf16[128,3072]{1,0:T(8,128)(2,1)S(1)} %fusion.25), channel_id=1, source_target_pairs={{8,0},{16,8},{24,16},{28,24},{20,28},{12,20},{4,12},{0,4},{9,1},{1... | collective-permute-start | bytes 2359304 | tf_op jit(solution)/shard_map/ppermute | solution.py:300
  433.4 22.1 %collective-permute-start.29 = (bf16[128,3072]{1,0:T(8,128)(2,1)}, bf16[128,3072]{1,0:T(8,128)(2,1)}, u32[]{:S(2)}, u32[]{:S(2)}) collective-permute-start(bf16[128,3072]{1,0:T(8,128)(2,1)} %fusion.26), channel_id=1, source_target_pairs={{0,8},{8,16},{16,24},{24,28},{28,20},{20,12},{12,4},{4,0},{1,9},{9... | collective-permute-start | bytes 2359304 | tf_op jit(solution)/shard_map/ppermute | solution.py:299
  436.0 20.9 %collective-permute-start.30 = (bf16[128,3072]{1,0:T(8,128)(2,1)}, bf16[128,3072]{1,0:T(8,128)(2,1)}, u32[]{:S(2)}, u32[]{:S(2)}) collective-permute-start(bf16[128,3072]{1,0:T(8,128)(2,1)} %fusion.27), channel_id=1, source_target_pairs={{8,0},{16,8},{24,16},{28,24},{20,28},{12,20},{4,12},{0,4},{9,1},{1... | collective-permute-start | bytes 2359304 | tf_op jit(solution)/shard_map/ppermute | solution.py:300
  440.2 14.4 %collective-permute-start.32 = (bf16[128,512]{1,0:T(8,128)(2,1)}, bf16[128,512]{1,0:T(8,128)(2,1)}, u32[]{:S(2)}, u32[]{:S(2)}) collective-permute-start(bf16[128,512]{1,0:T(8,128)(2,1)} %get-tuple-element.340), channel_id=1, source_target_pairs={{8,0},{16,8},{24,16},{28,24},{20,28},{12,20},{4,12},{0,4},{9,1},{1... | collective-permute-start | bytes 393224 | tf_op jit(solution)/shard_map/ppermute | solution.py:300
  441.8 13.7 %collective-permute-start.31 = (bf16[128,512]{1,0:T(8,128)(2,1)S(1)}, bf16[128,512]{1,0:T(8,128)(2,1)S(1)}, u32[]{:S(2)}, u32[]{:S(2)}) collective-permute-start(bf16[128,512]{1,0:T(8,128)(2,1)S(1)} %get-tuple-element.341), channel_id=1, source_target_pairs={{0,8},{8,16},{16,24},{24,28},{28,20},{20,12},{12,4},{4,0},{1,9},{9... | collective-permute-start | bytes 393224 | tf_op jit(solution)/shard_map/ppermute | solution.py:299
  458.5 20.6 %collective-permute-start.33 = (bf16[128,3072]{1,0:T(8,128)(2,1)S(1)}, bf16[128,3072]{1,0:T(8,128)(2,1)S(1)}, u32[]{:S(2)}, u32[]{:S(2)}) collective-permute-start(bf16[128,3072]{1,0:T(8,128)(2,1)S(1)} %fusion.28), channel_id=1, source_target_pairs={{0,8},{8,16},{16,24},{24,28},{28,20},{20,12},{12,4},{4,0},{1,9},{9... | collective-permute-start | bytes 2359304 | tf_op jit(solution)/shard_map/ppermute | solution.py:299
  460.3 19.0 %collective-permute-start.34 = (bf16[128,3072]{1,0:T(8,128)(2,1)S(1)}, bf16[128,3072]{1,0:T(8,128)(2,1)S(1)}, u32[]{:S(2)}, u32[]{:S(2)}) collective-permute-start(bf16[128,3072]{1,0:T(8,128)(2,1)S(1)} %fusion.29), channel_id=1, source_target_pairs={{8,0},{16,8},{24,16},{28,24},{20,28},{12,20},{4,12},{0,4},{9,1},{1... | collective-permute-start | bytes 2359304 | tf_op jit(solution)/shard_map/ppermute | solution.py:300
  462.5 16.6 %collective-permute-start.36 = (bf16[128,512]{1,0:T(8,128)(2,1)S(1)}, bf16[128,512]{1,0:T(8,128)(2,1)S(1)}, u32[]{:S(2)}, u32[]{:S(2)}) collective-permute-start(bf16[128,512]{1,0:T(8,128)(2,1)S(1)} %get-tuple-element.338), channel_id=1, source_target_pairs={{8,0},{16,8},{24,16},{28,24},{20,28},{12,20},{4,12},{0,4},{9,1},{1... | collective-permute-start | bytes 393224 | tf_op jit(solution)/shard_map/ppermute | solution.py:300
  463.0 16.1 %collective-permute-start.35 = (bf16[128,512]{1,0:T(8,128)(2,1)S(1)}, bf16[128,512]{1,0:T(8,128)(2,1)S(1)}, u32[]{:S(2)}, u32[]{:S(2)}) collective-permute-start(bf16[128,512]{1,0:T(8,128)(2,1)S(1)} %get-tuple-element.339), channel_id=1, source_target_pairs={{0,8},{8,16},{16,24},{24,28},{28,20},{20,12},{12,4},{4,0},{1,9},{9... | collective-permute-start | bytes 393224 | tf_op jit(solution)/shard_map/ppermute | solution.py:299
  479.7 20.1 %collective-permute-start.37 = (bf16[128,3072]{1,0:T(8,128)(2,1)S(1)}, bf16[128,3072]{1,0:T(8,128)(2,1)S(1)}, u32[]{:S(2)}, u32[]{:S(2)}) collective-permute-start(bf16[128,3072]{1,0:T(8,128)(2,1)S(1)} %fusion.30), channel_id=1, source_target_pairs={{0,8},{8,16},{16,24},{24,28},{28,20},{20,12},{12,4},{4,0},{1,9},{9... | collective-permute-start | bytes 2359304 | tf_op jit(solution)/shard_map/ppermute | solution.py:299
  481.3 18.7 %collective-permute-start.38 = (bf16[128,3072]{1,0:T(8,128)(2,1)S(1)}, bf16[128,3072]{1,0:T(8,128)(2,1)S(1)}, u32[]{:S(2)}, u32[]{:S(2)}) collective-permute-start(bf16[128,3072]{1,0:T(8,128)(2,1)S(1)} %fusion.31), channel_id=1, source_target_pairs={{8,0},{16,8},{24,16},{28,24},{20,28},{12,20},{4,12},{0,4},{9,1},{1... | collective-permute-start | bytes 2359304 | tf_op jit(solution)/shard_map/ppermute | solution.py:300
  484.1 15.7 %collective-permute-start.40 = (bf16[128,512]{1,0:T(8,128)(2,1)S(1)}, bf16[128,512]{1,0:T(8,128)(2,1)S(1)}, u32[]{:S(2)}, u32[]{:S(2)}) collective-permute-start(bf16[128,512]{1,0:T(8,128)(2,1)S(1)} %get-tuple-element.336), channel_id=1, source_target_pairs={{8,0},{16,8},{24,16},{28,24},{20,28},{12,20},{4,12},{0,4},{9,1},{1... | collective-permute-start | bytes 393224 | tf_op jit(solution)/shard_map/ppermute | solution.py:300
  484.4 15.4 %collective-permute-start.39 = (bf16[128,512]{1,0:T(8,128)(2,1)S(1)}, bf16[128,512]{1,0:T(8,128)(2,1)S(1)}, u32[]{:S(2)}, u32[]{:S(2)}) collective-permute-start(bf16[128,512]{1,0:T(8,128)(2,1)S(1)} %get-tuple-element.337), channel_id=1, source_target_pairs={{0,8},{8,16},{16,24},{24,28},{28,20},{20,12},{12,4},{4,0},{1,9},{9... | collective-permute-start | bytes 393224 | tf_op jit(solution)/shard_map/ppermute | solution.py:299
  500.4 21.1 %collective-permute-start.41 = (bf16[128,3072]{1,0:T(8,128)(2,1)S(1)}, bf16[128,3072]{1,0:T(8,128)(2,1)S(1)}, u32[]{:S(2)}, u32[]{:S(2)}) collective-permute-start(bf16[128,3072]{1,0:T(8,128)(2,1)S(1)} %fusion.32), channel_id=1, source_target_pairs={{0,8},{8,16},{16,24},{24,28},{28,20},{20,12},{12,4},{4,0},{1,9},{9... | collective-permute-start | bytes 2359304 | tf_op jit(solution)/shard_map/ppermute | solution.py:299
  501.8 19.8 %collective-permute-start.42 = (bf16[128,3072]{1,0:T(8,128)(2,1)S(1)}, bf16[128,3072]{1,0:T(8,128)(2,1)S(1)}, u32[]{:S(2)}, u32[]{:S(2)}) collective-permute-start(bf16[128,3072]{1,0:T(8,128)(2,1)S(1)} %fusion.33), channel_id=1, source_target_pairs={{8,0},{16,8},{24,16},{28,24},{20,28},{12,20},{4,12},{0,4},{9,1},{1... | collective-permute-start | bytes 2359304 | tf_op jit(solution)/shard_map/ppermute | solution.py:300
  506.4 15.0 %collective-permute-start.44 = (bf16[128,512]{1,0:T(8,128)(2,1)S(1)}, bf16[128,512]{1,0:T(8,128)(2,1)S(1)}, u32[]{:S(2)}, u32[]{:S(2)}) collective-permute-start(bf16[128,512]{1,0:T(8,128)(2,1)S(1)} %get-tuple-element.334), channel_id=1, source_target_pairs={{8,0},{16,8},{24,16},{28,24},{20,28},{12,20},{4,12},{0,4},{9,1},{1... | collective-permute-start | bytes 393224 | tf_op jit(solution)/shard_map/ppermute | solution.py:300
  506.7 14.7 %collective-permute-start.43 = (bf16[128,512]{1,0:T(8,128)(2,1)S(1)}, bf16[128,512]{1,0:T(8,128)(2,1)S(1)}, u32[]{:S(2)}, u32[]{:S(2)}) collective-permute-start(bf16[128,512]{1,0:T(8,128)(2,1)S(1)} %get-tuple-element.335), channel_id=1, source_target_pairs={{0,8},{8,16},{16,24},{24,28},{28,20},{20,12},{12,4},{4,0},{1,9},{9... | collective-permute-start | bytes 393224 | tf_op jit(solution)/shard_map/ppermute | solution.py:299
  524.2 12.0 %collective-permute-start.45 = (bf16[128,3072]{1,0:T(8,128)(2,1)S(1)}, bf16[128,3072]{1,0:T(8,128)(2,1)S(1)}, u32[]{:S(2)}, u32[]{:S(2)}) collective-permute-start(bf16[128,3072]{1,0:T(8,128)(2,1)S(1)} %fusion.34), channel_id=1, source_target_pairs={{0,8},{8,16},{16,24},{24,28},{28,20},{20,12},{12,4},{4,0},{1,9},{9... | collective-permute-start | bytes 2359304 | tf_op jit(solution)/shard_map/ppermute | solution.py:299
  525.5 12.2 %collective-permute-start.46 = (bf16[128,3072]{1,0:T(8,128)(2,1)S(1)}, bf16[128,3072]{1,0:T(8,128)(2,1)S(1)}, u32[]{:S(2)}, u32[]{:S(2)}) collective-permute-start(bf16[128,3072]{1,0:T(8,128)(2,1)S(1)} %fusion.35), channel_id=1, source_target_pairs={{8,0},{16,8},{24,16},{28,24},{20,28},{12,20},{4,12},{0,4},{9,1},{1... | collective-permute-start | bytes 2359304 | tf_op jit(solution)/shard_map/ppermute | solution.py:300
  549.0 85.8 %collective-permute-start.71 = (bf16[128,512]{1,0:T(8,128)(2,1)}, bf16[128,512]{1,0:T(8,128)(2,1)}, u32[]{:S(2)}, u32[]{:S(2)}) collective-permute-start(bf16[128,512]{1,0:T(8,128)(2,1)} %get-tuple-element.312), channel_id=1, source_target_pairs={{0,8},{8,16},{16,24},{24,28},{28,20},{20,12},{12,4},{4,0},{1,9},{9... | collective-permute-start | bytes 393224 | tf_op jit(solution)/shard_map/ppermute | solution.py:299
  550.5 84.2 %collective-permute-start.72 = (bf16[128,512]{1,0:T(8,128)(2,1)}, bf16[128,512]{1,0:T(8,128)(2,1)}, u32[]{:S(2)}, u32[]{:S(2)}) collective-permute-start(bf16[128,512]{1,0:T(8,128)(2,1)} %get-tuple-element.313), channel_id=1, source_target_pairs={{8,0},{16,8},{24,16},{28,24},{20,28},{12,20},{4,12},{0,4},{9,1},{1... | collective-permute-start | bytes 393224 | tf_op jit(solution)/shard_map/ppermute | solution.py:300
  574.3 47.8 %collective-permute-start.50 = (bf16[512,2048]{1,0:T(8,128)(2,1)S(1)}, bf16[512,2048]{1,0:T(8,128)(2,1)S(1)}, u32[]{:S(2)}, u32[]{:S(2)}) collective-permute-start(bf16[512,2048]{1,0:T(8,128)(2,1)S(1)} %add_convert_fusion.4), channel_id=1, source_target_pairs={{0,2},{1,3},{2,0},{3,1},{4,6},{5,7},{6,4},{7,5},{8,10},{9,11},{10,... | collective-permute-start | bytes 6291464 | tf_op jit(solution)/shard_map/ppermute | solution.py:231
  591.6 32.7 %collective-permute-start.60 = (bf16[128,1024]{0,1:T(8,128)(2,1)S(1)}, bf16[128,1024]{0,1:T(8,128)(2,1)S(1)}, u32[]{:S(2)}, u32[]{:S(2)}) collective-permute-start(bf16[128,1024]{0,1:T(8,128)(2,1)S(1)} %fusion.66), channel_id=1, source_target_pairs={{0,8},{8,16},{16,24},{24,28},{28,20},{20,12},{12,4},{4,0},{1,9},{9... | collective-permute-start | bytes 786440 | tf_op jit(solution)/shard_map/ppermute | solution.py:299
  593.2 33.9 %collective-permute-start.67 = (bf16[128,1024]{0,1:T(8,128)(2,1)S(1)}, bf16[128,1024]{0,1:T(8,128)(2,1)S(1)}, u32[]{:S(2)}, u32[]{:S(2)}) collective-permute-start(bf16[128,1024]{0,1:T(8,128)(2,1)S(1)} %fusion.72), channel_id=1, source_target_pairs={{8,0},{16,8},{24,16},{28,24},{20,28},{12,20},{4,12},{0,4},{9,1},{1... | collective-permute-start | bytes 786440 | tf_op jit(solution)/shard_map/ppermute | solution.py:300
  624.3 26.0 %collective-permute-start.51 = (bf16[512,2048]{1,0:T(8,128)(2,1)}, bf16[512,2048]{1,0:T(8,128)(2,1)}, u32[]{:S(2)}, u32[]{:S(2)}) collective-permute-start(bf16[512,2048]{1,0:T(8,128)(2,1)} %add_convert_fusion.3), channel_id=1, source_target_pairs={{0,1},{1,0},{2,3},{3,2},{4,5},{5,4},{6,7},{7,6},{8,9},{9,8},{10,11... | collective-permute-start | bytes 6291464 | tf_op jit(solution)/shard_map/ppermute | solution.py:240
  645.5 16.7 %collective-permute-start.70 = (bf16[128,1024]{0,1:T(8,128)(2,1)S(1)}, bf16[128,1024]{0,1:T(8,128)(2,1)S(1)}, u32[]{:S(2)}, u32[]{:S(2)}) collective-permute-start(bf16[128,1024]{0,1:T(8,128)(2,1)S(1)} %fusion.75), channel_id=1, source_target_pairs={{8,0},{16,8},{24,16},{28,24},{20,28},{12,20},{4,12},{0,4},{9,1},{1... | collective-permute-start | bytes 786440 | tf_op jit(solution)/shard_map/ppermute | solution.py:300
  674.8 11.0 %collective-permute-start.56 = (f32[4352]{0:T(1024)S(1)}, f32[4352]{0:T(1024)S(1)}, u32[]{:S(2)}, u32[]{:S(2)}) collective-permute-start(f32[4352]{0:T(1024)S(1)} %add.1875), channel_id=1, source_target_pairs={{0,16},{4,20},{8,24},{12,28},{16,0},{20,4},{24,8},{28,12},{1,17},{... | collective-permute-start | bytes 52232 | tf_op jit(solution)/shard_map/ppermute | solution.py:266
  (142 other events, 925.7 us)
